TPU v7x, 32 devices: a whole 2x2x4 slice. The times are simulated.
32 devices in a mesh: groups: 2 (over y), dom: 4 (over x, core), sub: 4 (over z).
Axes of the slice: x: 2, y: 2, z: 4, core: 2. Of those that a mesh axis runs over, the one named last changes fastest.
Arguments:
- node_states: float32 [8192, 512], P(('groups', 'dom', 'sub')), parts along dimension 0, may hold values from -6 to 6
- node_pre: float32 [8192, 512], P(('groups', 'dom', 'sub')), parts along dimension 0, may hold values from -6 to 6
- edge_states: float32 [4096, 512], P(('groups', 'dom', 'sub')), parts along dimension 0, may hold values from -6 to 6
- edge_pre: float32 [4096, 512], P(('groups', 'dom', 'sub')), parts along dimension 0, may hold values from -6 to 6
- node_cotangent: float32 [8192, 512], P(('groups', 'dom', 'sub')), parts along dimension 0, may hold values from -6 to 6
- edge_cotangent: float32 [4096, 512], P(('groups', 'dom', 'sub')), parts along dimension 0, may hold values from -6 to 6
- endpoints: int32 [2, 4096], P(None, ('groups', 'dom', 'sub')), parts along dimension 1, may hold values from 0 to 319, as said below
- send_lists: int32 [32, 4, 16], P(('groups', 'dom', 'sub')), parts along dimension 0, may hold values from 0 to 255, as said below
- node_counts: int32 [32], P(('groups', 'dom', 'sub')), parts along dimension 0, may hold values from 128 to 256
- edge_blocks: int32 [32], P(('groups', 'dom', 'sub')), parts along dimension 0, may hold values from 1 to 1
- edge_first: float32 [1536, 512], P(('dom', 'sub')), may hold values from -0.15625 to 0.15625
- edge_second: float32 [512, 512], P(('dom', 'sub')), may hold values from -0.25 to 0.25
- edge_bias: float32 [512], P(('dom', 'sub')), may hold values from -3 to 3
- edge_gain: float32 [512], P(('dom', 'sub')), may hold values from 0.5 to 1.5
- edge_shift: float32 [512], P(('dom', 'sub')), may hold values from -3 to 3
- node_first: float32 [1024, 512], P(('dom', 'sub')), may hold values from -0.1875 to 0.1875
- node_second: float32 [512, 512], P(('dom', 'sub')), may hold values from -0.25 to 0.25
- node_bias: float32 [512], P(('dom', 'sub')), may hold values from -3 to 3
- node_gain: float32 [512], P(('dom', 'sub')), may hold values from 0.5 to 1.5
Outputs:
- edge_grads: float32 [4096, 512], P(('groups', 'dom', 'sub')), parts along dimension 0
- node_grads: float32 [8192, 512], P(('groups', 'dom', 'sub')), parts along dimension 0
- edge_first_grad: float32 [3072, 512], P(('groups', 'dom', 'sub')), parts along dimension 0
- edge_second_grad: float32 [1024, 512], P(('groups', 'dom', 'sub')), parts along dimension 0
- node_first_grad: float32 [2048, 512], P(('groups', 'dom', 'sub')), parts along dimension 0
- node_second_grad: float32 [1024, 512], P(('groups', 'dom', 'sub')), parts along dimension 0
There are 2 independent parts, one for each index of `groups`. A program takes and returns all parts, laid end to end along the dimension named above; an argument that names none is the same for every part. Nothing has to cross between parts.
Inputs may be any that keep to these rules, and one draw needn't show every extreme that they name: `endpoints`: sender slots are a live local node below node_counts of the device, or a ghost slot 256 + k * 16 + j whose neighbour k exists; receiver slots are live local nodes. `send_lists`: every entry is a live node of its device.
All inputs are finite; a program needn't handle non-finite values.
Results may differ from a plain program's by a relative error of at most 0.0003.
Values sent between devices are 32-bit elements; how exact they have to be, the bound alone decides.
No kernel may reach another device: no remote copies, remote signals or barrier semaphores. Data moves between devices by JAX's collectives and lax.ppermute only.
A program may use at most 128 MiB of HBM per device.

v0:
```python
import math

import jax
import jax.numpy as jnp
from jax import lax
from jax.sharding import PartitionSpec as P

EPSILON = 1e-05


def padded(cells, sides, width):
    for axis, dim in sides:
        count = lax.axis_size(axis)
        ends = count - 1
        head = lax.slice_in_dim(cells, 0, width, axis=dim)
        tail = lax.slice_in_dim(cells, cells.shape[dim] - width, cells.shape[dim], axis=dim)
        cells = jnp.concatenate(
            [
                lax.ppermute(tail, axis, [(i, (i + 1) % count) for i in range(ends)]),
                cells,
                lax.ppermute(head, axis, [((i + 1) % count, i) for i in range(ends)]),
            ],
            axis=dim,
        )
    return cells


def matmul(left, right):
    return jnp.dot(left, right, precision=lax.Precision.HIGHEST, preferred_element_type=jnp.float32)


def inner(left, right):
    return lax.dot_general(
        left,
        right,
        (((0,), (0,)), ((), ())),
        precision=lax.Precision.HIGHEST,
        preferred_element_type=jnp.float32,
    )


def outer_back(left, right):
    return lax.dot_general(
        left,
        right,
        (((1,), (1,)), ((), ())),
        precision=lax.Precision.HIGHEST,
        preferred_element_type=jnp.float32,
    )


def layer_norm(values):
    center = values - jnp.mean(values, axis=-1, keepdims=True)
    inverse = 1.0 / jnp.sqrt(jnp.mean(center * center, axis=-1, keepdims=True) + EPSILON)
    return (center * inverse, inverse)


def norm_back(upstream, normed, inverse):
    first = jnp.mean(upstream, axis=-1, keepdims=True)
    second = jnp.mean(upstream * normed, axis=-1, keepdims=True)
    return inverse * (upstream - first - normed * second)


def shards(
    node_states,
    node_pre,
    edge_states,
    edge_pre,
    node_cotangent,
    edge_cotangent,
    endpoints,
    send_lists,
    node_counts,
    edge_blocks,
    edge_first,
    edge_second,
    edge_bias,
    edge_gain,
    edge_shift,
    node_first,
    node_second,
    node_bias,
    node_gain,
):
    node_rows, width = node_states.shape
    edge_rows = edge_states.shape[0]
    ghost = send_lists.shape[2]
    dom_count = lax.axis_size("dom")
    sub_count = lax.axis_size("sub")
    peer_count = dom_count * sub_count
    lists = send_lists[0]
    outgoing = jnp.take(node_states, lists.reshape(-1), axis=0).reshape(4, ghost, width)
    dom_side = padded(jnp.stack([outgoing[1], outgoing[0]]), (("dom", 0),), 1)
    sub_side = padded(jnp.stack([outgoing[3], outgoing[2]]), (("sub", 0),), 1)
    ghosts = jnp.stack([dom_side[0], dom_side[3], sub_side[0], sub_side[3]])
    ghosts = ghosts.reshape(4 * ghost, width)
    full_node_first, full_node_second, full_node_bias, full_node_gain = (
        lax.all_gather(node_first, ("dom", "sub"), axis=0, tiled=True),
        lax.all_gather(node_second, ("dom", "sub"), axis=0, tiled=True),
        lax.all_gather(node_bias, ("dom", "sub"), axis=0, tiled=True),
        lax.all_gather(node_gain, ("dom", "sub"), axis=0, tiled=True),
    )
    full_edge_first, full_edge_second, full_edge_bias, full_edge_gain, full_edge_shift = (
        lax.all_gather(edge_first, ("dom", "sub"), axis=0, tiled=True),
        lax.all_gather(edge_second, ("dom", "sub"), axis=0, tiled=True),
        lax.all_gather(edge_bias, ("dom", "sub"), axis=0, tiled=True),
        lax.all_gather(edge_gain, ("dom", "sub"), axis=0, tiled=True),
        lax.all_gather(edge_shift, ("dom", "sub"), axis=0, tiled=True),
    )
    live_nodes = (jnp.arange(node_rows) < node_counts[0]).astype(jnp.float32)[:, None]
    live_edges = (jnp.arange(edge_rows) < edge_blocks[0] * 128).astype(jnp.float32)[:, None]
    source = endpoints[0]
    target = endpoints[1]
    edge_scale = 1.0 / math.sqrt(edge_rows * peer_count)
    node_scale = 1.0 / math.sqrt(node_rows * peer_count)
    edge_act = jnp.maximum(edge_pre, 0.0)
    edge_normed, edge_inverse = layer_norm(matmul(edge_act, full_edge_second) + full_edge_bias)
    message = (edge_normed * full_edge_gain + full_edge_shift) * live_edges
    aggregate = jax.ops.segment_sum(message, target, node_rows)
    node_act = jnp.maximum(node_pre, 0.0)
    node_normed, node_inverse = layer_norm(matmul(node_act, full_node_second) + full_node_bias)
    node_upstream = node_cotangent * live_nodes
    node_grad_z = norm_back(node_upstream * full_node_gain, node_normed, node_inverse)
    node_grad_pre = outer_back(node_grad_z, full_node_second) * (node_pre > 0).astype(jnp.float32)
    node_input = jnp.concatenate([node_states, aggregate], axis=1)
    node_first_grad, node_second_grad = (
        lax.psum_scatter(
            inner(node_input, node_grad_pre) * node_scale,
            ("dom", "sub"),
            scatter_dimension=0,
            tiled=True,
        ),
        lax.psum_scatter(
            inner(node_act, node_grad_z) * node_scale,
            ("dom", "sub"),
            scatter_dimension=0,
            tiled=True,
        ),
    )
    node_grad_input = outer_back(node_grad_pre, full_node_first)
    state_grads = node_upstream + node_grad_input[:, :width]
    edge_upstream = (
        edge_cotangent + jnp.take(node_grad_input[:, width:], target, axis=0)
    ) * live_edges
    edge_grad_z = norm_back(edge_upstream * full_edge_gain, edge_normed, edge_inverse)
    edge_grad_pre = outer_back(edge_grad_z, full_edge_second) * (edge_pre > 0).astype(jnp.float32)
    edge_second_grad = lax.psum_scatter(
        inner(edge_act, edge_grad_z) * edge_scale, ("dom", "sub"), scatter_dimension=0, tiled=True
    )
    extended = jnp.concatenate([node_states, ghosts], axis=0)
    features = jnp.concatenate(
        [edge_states, jnp.take(extended, source, axis=0), jnp.take(extended, target, axis=0)],
        axis=1,
    )
    edge_first_grad = lax.psum_scatter(
        inner(features, edge_grad_pre) * edge_scale, ("dom", "sub"), scatter_dimension=0, tiled=True
    )
    edge_grad_input = outer_back(edge_grad_pre, full_edge_first)
    edge_grads = (edge_cotangent + edge_grad_input[:, :width]) * live_edges
    extended_grads = jax.ops.segment_sum(
        edge_grad_input[:, width : 2 * width], source, node_rows + 4 * ghost
    )
    extended_grads = extended_grads + jax.ops.segment_sum(
        edge_grad_input[:, 2 * width :], target, node_rows + 4 * ghost
    )
    state_grads = state_grads + extended_grads[:node_rows]
    ghost_grads = extended_grads[node_rows:].reshape(4, ghost, width)
    dom_back = padded(jnp.stack([ghost_grads[0], ghost_grads[1]]), (("dom", 0),), 1)
    sub_back = padded(jnp.stack([ghost_grads[2], ghost_grads[3]]), (("sub", 0),), 1)
    returned = jnp.stack([dom_back[3], dom_back[0], sub_back[3], sub_back[0]])
    state_grads = state_grads + jax.ops.segment_sum(
        returned.reshape(-1, width), lists.reshape(-1), node_rows
    )
    return (
        edge_grads,
        state_grads,
        edge_first_grad,
        edge_second_grad,
        node_first_grad,
        node_second_grad,
    )


def solution(mesh):
    in_specs = (
        P(("groups", "dom", "sub"), None),
        P(("groups", "dom", "sub"), None),
        P(("groups", "dom", "sub"), None),
        P(("groups", "dom", "sub"), None),
        P(("groups", "dom", "sub"), None),
        P(("groups", "dom", "sub"), None),
        P(None, ("groups", "dom", "sub")),
        P(("groups", "dom", "sub"), None, None),
        P(("groups", "dom", "sub")),
        P(("groups", "dom", "sub")),
        P(("dom", "sub"), None),
        P(("dom", "sub"), None),
        P(("dom", "sub")),
        P(("dom", "sub")),
        P(("dom", "sub")),
        P(("dom", "sub"), None),
        P(("dom", "sub"), None),
        P(("dom", "sub")),
        P(("dom", "sub")),
    )
    out_specs = (
        P(("groups", "dom", "sub"), None),
        P(("groups", "dom", "sub"), None),
        P(("groups", "dom", "sub"), None),
        P(("groups", "dom", "sub"), None),
        P(("groups", "dom", "sub"), None),
        P(("groups", "dom", "sub"), None),
    )
    return jax.shard_map(shards, mesh=mesh, in_specs=in_specs, out_specs=out_specs, check_vma=False)
```

profile of v0, /device:TPU:0, one launch (start us, length us, event | category | flops | bytes accessed | tf_op | source)
XLA Modules:
  0.0 442.2 jit_solution(13776215325105201834)
XLA Ops:
  7.2 0.7 all-gather.7.cloned.1.call-update
  8.0 0.7 all-gather.5.cloned.1.call-update
  8.7 0.7 all-gather.9.cloned.1.call-update
  10.7 1.2 dynamic-slice
  12.6 0.9 dynamic-update-slice
  13.4 0.8 dynamic-update-slice.1
  14.3 0.8 dynamic-update-slice.2
  15.1 0.8 dynamic-update-slice.3
  16.0 0.8 dynamic-update-slice.4
  16.8 63.6 %all-reduce.5 = (f32[512]{0:T(512)S(1)}, f32[512]{0:T(512)S(1)}, f32[512]{0:T(512)S(1)}, f32[512]{0:T(512)S(1)}, f32[512]{0:T(512)S(1)}) all-reduce(f32[512]{0:T(512)S(1)} %dynamic-update-slice.1, f32[512]{0:T(512)S(1)} %dynamic-update-slice.2, f32[512]{0:T(512)S(1)} %dynamic-update-slice.3, ...), channel_id=1, replica_groups=mesh['groups'=2,'dom'=4,'sub'=4] {'dom','sub'}, use_global_device_ids=true, to_apply=%add.1 | all-reduce | flops 2560 | bytes 20480
  80.4 2.5 fusion.44
  83.5 2.4 convolution_multiply_fusion.2
  86.7 3.5 all-gather.5.cloned.1.call-done
  90.2 2.0 fusion.43
  92.5 2.2 scatter_custom_fusion.2
  94.7 2.5 convolution_select_fusion
  97.3 3.2 convolution_multiply_fusion.1
  100.9 0.7 gather_fusion.1
  101.6 31.2 %all-gather.9.cloned.1.call-done = f32[1024,512]{1,0:T(8,128)} async-done(((f32[64,512]{1,0:T(8,128)}), f32[1024,512]{1,0:T(8,128)}) %all-gather.9.cloned.1.call-update) | async-done | bytes 2097168 | tf_op jit(solution)/shard_map/all_gather | solution.py:98
  132.8 3.5 fusion.45
  136.3 1.0 copy-done.5
  137.4 0.8 gather_fusion
  138.4 2.1 convolution_multiply_fusion.3
  140.6 2.2 collective-permute-start.4
  142.8 1.3 collective-permute-start.5
  144.1 2.4 collective-permute-start.6
  146.6 1.3 collective-permute-start.7
  147.9 0.7 collective-permute-done.6
  148.6 4.4 collective-permute-done.7
  153.0 0.8 gather_fusion.2
  153.8 1.5 gather_fusion.3
  155.2 1.1 broadcast_select_fusion
  156.3 1.2 convolution_select_fusion.1
  157.5 4.4 convolution_multiply_fusion
  162.0 17.1 %all-gather.11.cloned.1.call-done = f32[1536,512]{1,0:T(8,128)} async-done(((f32[96,512]{1,0:T(8,128)}), f32[1536,512]{1,0:T(8,128)}) %all-gather.11.cloned.1.call-update) | async-done | bytes 3145744 | tf_op jit(solution)/shard_map/all_gather | solution.py:104
  179.1 5.2 %fusion.46 = f32[128,1536]{1,0:T(8,128)S(1)} fusion(f32[128,512]{1,0:T(8,128)S(1)} %convolution_select_fusion.1, f32[1536,512]{1,0:T(8,128)} %all-gather.11.cloned.1.call-done), kind=kOutput, calls=%fused_computation.115 | convolution fusion | flops 1207959552 | bytes 4194304 | tf_op jit(solution)/shard_map/dot_general | solution.py:43
  184.3 0.8 fusion.42
  185.1 2.3 scatter_custom_fusion
  187.4 1.3 collective-permute-start
  188.7 3.0 collective-permute-start.1
  191.8 1.3 collective-permute-start.2
  193.1 4.5 %collective-permute-start.3 = (f32[1,16,512]{2,1,0:T(8,128)S(1)}, f32[1,16,512]{2,1,0:T(8,128)S(1)}, u32[]{:S(2)}, u32[]{:S(2)}) collective-permute-start(f32[1,16,512]{2,1,0:T(8,128)S(1)} %get-tuple-element.25), channel_id=1, source_target_pairs={{0,1},{1,2},{2,3},{4,5},{5,6},{6,7},{8,9},{9,10},{10,11},{12,13},{... | collective-permute-start | bytes 98312 | tf_op jit(solution)/shard_map/ppermute | solution.py:19
  197.8 1.4 collective-permute-done.3
  199.2 1.2 scatter_fusion
  200.4 38.9 %reduce-scatter.11.cloned.1.call-done = f32[32,512]{1,0:T(8,128)} async-done(((f32[512,512]{1,0:T(8,128)}), f32[32,512]{1,0:T(8,128)}) %reduce-scatter.11.cloned.1.call-update) | async-done | bytes 65552 | tf_op jit(solution)/shard_map/reduce_scatter | solution.py:133
  239.4 65.3 %reduce-scatter.9.cloned.1.call-done = f32[64,512]{1,0:T(8,128)} async-done(((f32[1024,512]{1,0:T(8,128)}), f32[64,512]{1,0:T(8,128)}) %reduce-scatter.9.cloned.1.call-update) | async-done | bytes 131088 | tf_op jit(solution)/shard_map/reduce_scatter | solution.py:127
  304.7 60.6 %reduce-scatter.7.cloned.1.call-done = f32[32,512]{1,0:T(8,128)} async-done(((f32[512,512]{1,0:T(8,128)}), f32[32,512]{1,0:T(8,128)}) %reduce-scatter.7.cloned.1.call-update) | async-done | bytes 65552 | tf_op jit(solution)/shard_map/reduce_scatter | solution.py:147
  365.3 70.1 %reduce-scatter.5.cloned.1.call-done = f32[96,512]{1,0:T(8,128)} async-done(((f32[1536,512]{1,0:T(8,128)}), f32[96,512]{1,0:T(8,128)}) %reduce-scatter.5.cloned.1.call-update) | async-done | bytes 196624 | tf_op jit(solution)/shard_map/reduce_scatter | solution.py:155
  (84 shorter events, 2.7 us)
Async XLA Ops:
  7.2 76.3 %copy-start.2 = (f32[256,512]{1,0:T(8,128)S(1)}, f32[256,512]{1,0:T(8,128)}, u32[]{:S(2)}) copy-start(f32[256,512]{1,0:T(8,128)} %param.22) | copy-start | bytes 1572868
  7.2 76.0 %copy-start.1 = (f32[256,512]{1,0:T(8,128)S(1)}, f32[256,512]{1,0:T(8,128)}, u32[]{:S(2)}) copy-start(f32[256,512]{1,0:T(8,128)} %param.25) | copy-start | bytes 1572868
  7.2 73.2 %all-gather.7.cloned.1.call-start = ((), (), s32[]{:S(2)}) async-start(), calls=%async_computation.5 | async-start | bytes 1114112 | tf_op jit(solution)/shard_map/all_gather | solution.py:99
  7.9 82.3 %all-gather.5.cloned.1.call-start = ((), (), s32[]{:S(2)}) async-start(), calls=%async_computation.4 | async-start | bytes 1114112 | tf_op jit(solution)/shard_map/all_gather | solution.py:105
  8.7 124.1 %all-gather.9.cloned.1.call-start = ((), (), s32[]{:S(2)}) async-start(), calls=%async_computation.6 | async-start | bytes 2228224 | tf_op jit(solution)/shard_map/all_gather | solution.py:98
  9.4 169.7 %all-gather.11.cloned.1.call-start = ((), (), s32[]{:S(2)}) async-start(), calls=%async_computation.7 | async-start | bytes 3342336 | tf_op jit(solution)/shard_map/all_gather | solution.py:104
  10.0 229.4 %reduce-scatter.11.cloned.1.call-start = ((), (), s32[]{:S(2)}) async-start(), calls=%async_computation.11 | async-start | bytes 1114112 | tf_op jit(solution)/shard_map/reduce_scatter | solution.py:133
  82.9 3.0 copy-start.13
  83.0 7.3 %copy-start.7 = (f32[128,512]{1,0:T(8,128)S(1)}, f32[128,512]{1,0:T(8,128)}, u32[]{:S(2)}) copy-start(f32[128,512]{1,0:T(8,128)} %param.24) | copy-start | bytes 786436
  85.9 11.3 %copy-start = (f32[256,512]{1,0:T(8,128)S(1)}, f32[256,512]{1,0:T(8,128)}, u32[]{:S(2)}) copy-start(f32[256,512]{1,0:T(8,128)} %param.21) | copy-start | bytes 1572868
  85.9 218.7 %reduce-scatter.9.cloned.1.call-start = ((), (), s32[]{:S(2)}) async-start(), calls=%async_computation.10 | async-start | bytes 2228224 | tf_op jit(solution)/shard_map/reduce_scatter | solution.py:127
  94.7 2.5 copy-start.8
  97.2 3.5 copy-start.12
  100.5 264.8 %reduce-scatter.7.cloned.1.call-start = ((), (), s32[]{:S(2)}) async-start(), calls=%async_computation.9 | async-start | bytes 1114112 | tf_op jit(solution)/shard_map/reduce_scatter | solution.py:147
  101.6 36.5 %copy-start.9 = (f32[128,512]{1,0:T(8,128)S(1)}, f32[128,512]{1,0:T(8,128)}, u32[]{:S(2)}) copy-start(f32[128,512]{1,0:T(8,128)} %param.26) | copy-start | bytes 786436
  136.3 1.0 copy-start.5
  140.5 294.9 %reduce-scatter.5.cloned.1.call-start = ((), (), s32[]{:S(2)}) async-start(), calls=%async_computation.8 | async-start | bytes 3342336 | tf_op jit(solution)/shard_map/reduce_scatter | solution.py:155
  140.6 7.2 %collective-permute-start.4 = (f32[1,16,512]{2,1,0:T(8,128)S(1)}, f32[1,16,512]{2,1,0:T(8,128)S(1)}, u32[]{:S(2)}, u32[]{:S(2)}) collective-permute-start(f32[1,16,512]{2,1,0:T(8,128)S(1)} %get-tuple-element.28), channel_id=1, source_target_pairs={{0,4},{4,8},{8,12},{1,5},{5,9},{9,13},{2,6},{6,10},{10,14},{3,7},{... | collective-permute-start | bytes 98312 | tf_op jit(solution)/shard_map/ppermute | solution.py:19
  142.8 5.1 %collective-permute-start.5 = (f32[1,16,512]{2,1,0:T(8,128)S(1)}, f32[1,16,512]{2,1,0:T(8,128)S(1)}, u32[]{:S(2)}, u32[]{:S(2)}) collective-permute-start(f32[1,16,512]{2,1,0:T(8,128)S(1)} %get-tuple-element.31), channel_id=1, source_target_pairs={{4,0},{8,4},{12,8},{5,1},{9,5},{13,9},{6,2},{10,6},{14,10},{7,3},{... | collective-permute-start | bytes 98312 | tf_op jit(solution)/shard_map/ppermute | solution.py:21
  144.1 4.4 %collective-permute-start.6 = (f32[1,16,512]{2,1,0:T(8,128)S(1)}, f32[1,16,512]{2,1,0:T(8,128)S(1)}, u32[]{:S(2)}, u32[]{:S(2)}) collective-permute-start(f32[1,16,512]{2,1,0:T(8,128)S(1)} %get-tuple-element.30), channel_id=1, source_target_pairs={{0,1},{1,2},{2,3},{4,5},{5,6},{6,7},{8,9},{9,10},{10,11},{12,13},{... | collective-permute-start | bytes 98312 | tf_op jit(solution)/shard_map/ppermute | solution.py:19
  146.6 6.4 %collective-permute-start.7 = (f32[1,16,512]{2,1,0:T(8,128)S(1)}, f32[1,16,512]{2,1,0:T(8,128)S(1)}, u32[]{:S(2)}, u32[]{:S(2)}) collective-permute-start(f32[1,16,512]{2,1,0:T(8,128)S(1)} %get-tuple-element.29), channel_id=1, source_target_pairs={{1,0},{2,1},{3,2},{5,4},{6,5},{7,6},{9,8},{10,9},{11,10},{13,12},{... | collective-permute-start | bytes 98312 | tf_op jit(solution)/shard_map/ppermute | solution.py:21
  153.0 3.3 copy-start.4
  155.2 2.3 copy-start.11
  161.9 22.4 %copy-start.10 = (f32[128,512]{1,0:T(8,128)S(1)}, f32[128,512]{1,0:T(8,128)}, u32[]{:S(2)}) copy-start(f32[128,512]{1,0:T(8,128)} %param.26) | copy-start | bytes 786436
  162.0 35.7 %copy-start.6 = (f32[256,1024]{1,0:T(8,128)S(1)}, f32[256,1024]{1,0:T(8,128)}, u32[]{:S(2)}) copy-start(f32[256,1024]{1,0:T(8,128)} %copy-done.5) | copy-start | bytes 3145732
  187.4 10.3 %collective-permute-start = (f32[1,16,512]{2,1,0:T(8,128)S(1)}, f32[1,16,512]{2,1,0:T(8,128)S(1)}, u32[]{:S(2)}, u32[]{:S(2)}) collective-permute-start(f32[1,16,512]{2,1,0:T(8,128)S(1)} %get-tuple-element.24), channel_id=1, source_target_pairs={{4,0},{8,4},{12,8},{5,1},{9,5},{13,9},{6,2},{10,6},{14,10},{7,3},{... | collective-permute-start | bytes 98312 | tf_op jit(solution)/shard_map/ppermute | solution.py:21
  188.7 9.1 %collective-permute-start.1 = (f32[1,16,512]{2,1,0:T(8,128)S(1)}, f32[1,16,512]{2,1,0:T(8,128)S(1)}, u32[]{:S(2)}, u32[]{:S(2)}) collective-permute-start(f32[1,16,512]{2,1,0:T(8,128)S(1)} %get-tuple-element.27), channel_id=1, source_target_pairs={{0,4},{4,8},{8,12},{1,5},{5,9},{9,13},{2,6},{6,10},{10,14},{3,7},{... | collective-permute-start | bytes 98312 | tf_op jit(solution)/shard_map/ppermute | solution.py:19
  191.8 6.0 %collective-permute-start.2 = (f32[1,16,512]{2,1,0:T(8,128)S(1)}, f32[1,16,512]{2,1,0:T(8,128)S(1)}, u32[]{:S(2)}, u32[]{:S(2)}) collective-permute-start(f32[1,16,512]{2,1,0:T(8,128)S(1)} %get-tuple-element.26), channel_id=1, source_target_pairs={{1,0},{2,1},{3,2},{5,4},{6,5},{7,6},{9,8},{10,9},{11,10},{13,12},{... | collective-permute-start | bytes 98312 | tf_op jit(solution)/shard_map/ppermute | solution.py:21
  193.1 6.1 %collective-permute-start.3 = (f32[1,16,512]{2,1,0:T(8,128)S(1)}, f32[1,16,512]{2,1,0:T(8,128)S(1)}, u32[]{:S(2)}, u32[]{:S(2)}) collective-permute-start(f32[1,16,512]{2,1,0:T(8,128)S(1)} %get-tuple-element.25), channel_id=1, source_target_pairs={{0,1},{1,2},{2,3},{4,5},{5,6},{6,7},{8,9},{9,10},{10,11},{12,13},{... | collective-permute-start | bytes 98312 | tf_op jit(solution)/shard_map/ppermute | solution.py:19
  200.4 235.0 %copy-start.3 = (f32[256,512]{1,0:T(8,128)}, f32[256,512]{1,0:T(8,128)S(1)}, u32[]{:S(2)}) copy-start(f32[256,512]{1,0:T(8,128)S(1)} %scatter_fusion) | copy-start | bytes 1572868
Sparse Core Ops, SparseCore 0:
  10.2 40.7 all-gather.6
  53.2 36.9 all-gather.4
  92.4 40.3 all-gather.8
  135.0 44.1 all-gather.10
  183.2 56.1 reduce-scatter.10
  244.0 60.6 reduce-scatter.8
  308.9 56.3 reduce-scatter.6
  370.2 65.1 reduce-scatter.4
where the time goes:
time: 443 us; the launch traced here: 442 us
  waiting for transfers between devices  296 us (67%)
  blocking collectives  63.6 us (14%)
  matrix products  29 us (7%)
  starting transfers between devices  17.8 us (4%)
  between operations  16.6 us (4%)
  local copies, waits for them, and re-layouts  10.4 us (2%)
  other arithmetic  8.89 us (2%)
    reduce_scatter x1, waiting for transfers between devices, shards(): lax.psum_scatter(inner(features, edge_grad_pre) * edge_scale, ('dom', 'su...  70.1 us
    reduce_scatter x1, waiting for transfers between devices, shards(): lax.psum_scatter(inner(node_input, node_grad_pre) * node_scale, ('dom', '...  65.3 us
    unnamed x1, blocking collectives  63.6 us
    reduce_scatter x1, waiting for transfers between devices, shards(): lax.psum_scatter(inner(edge_act, edge_grad_z) * edge_scale, ('dom', 'sub'...  60.6 us
    reduce_scatter x1, waiting for transfers between devices, shards(): lax.psum_scatter(inner(node_act, node_grad_z) * node_scale, ('dom', 'sub'...  38.9 us
    all_gather x1, waiting for transfers between devices, shards(): lax.all_gather(node_first, ('dom', 'sub'), axis=0, tiled=True)  31.2 us
    all_gather x1, waiting for transfers between devices, shards(): lax.all_gather(edge_first, ('dom', 'sub'), axis=0, tiled=True)  17.1 us
    dot_general x4, matrix products, outer_back(): lax.dot_general(left, right, (((1,), (1,)), ((), ())), precision=lax.Prec...  12.4 us
  transfers between devices with their start and end apart: 16, of which 10 were waited for; matrix products, arithmetic and copies ran while one was open for 11% of the time, Pallas kernels for 0%

commit v1 on v0

--- a/solution.py
+++ b/solution.py
@@ -94,18 +94,26 @@
     sub_side = padded(jnp.stack([outgoing[3], outgoing[2]]), (("sub", 0),), 1)
     ghosts = jnp.stack([dom_side[0], dom_side[3], sub_side[0], sub_side[3]])
     ghosts = ghosts.reshape(4 * ghost, width)
-    full_node_first, full_node_second, full_node_bias, full_node_gain = (
-        lax.all_gather(node_first, ("dom", "sub"), axis=0, tiled=True),
-        lax.all_gather(node_second, ("dom", "sub"), axis=0, tiled=True),
-        lax.all_gather(node_bias, ("dom", "sub"), axis=0, tiled=True),
-        lax.all_gather(node_gain, ("dom", "sub"), axis=0, tiled=True),
-    )
-    full_edge_first, full_edge_second, full_edge_bias, full_edge_gain, full_edge_shift = (
-        lax.all_gather(edge_first, ("dom", "sub"), axis=0, tiled=True),
-        lax.all_gather(edge_second, ("dom", "sub"), axis=0, tiled=True),
-        lax.all_gather(edge_bias, ("dom", "sub"), axis=0, tiled=True),
-        lax.all_gather(edge_gain, ("dom", "sub"), axis=0, tiled=True),
-        lax.all_gather(edge_shift, ("dom", "sub"), axis=0, tiled=True),
+    peers = ("dom", "sub")
+    matrices = (edge_first, edge_second, node_first, node_second)
+    vectors = jnp.concatenate([edge_bias, edge_gain, edge_shift, node_bias, node_gain])
+    vector_rows = -(-vectors.shape[0] // width)
+    vectors = jnp.pad(vectors, (0, vector_rows * width - vectors.shape[0])).reshape(vector_rows, width)
+    packed = jnp.concatenate(list(matrices) + [vectors], axis=0)
+    gathered = lax.all_gather(packed, peers, axis=0, tiled=False)
+    pieces = []
+    offset = 0
+    for rows in [m.shape[0] for m in matrices] + [vector_rows]:
+        pieces.append(gathered[:, offset : offset + rows, :])
+        offset += rows
+    full_edge_first, full_edge_second, full_node_first, full_node_second = (
+        piece.reshape(-1, width) for piece in pieces[:4]
+    )
+    vector_count = edge_bias.shape[0]
+    all_vectors = pieces[4].reshape(pieces[4].shape[0], -1)[:, : 5 * vector_count]
+    all_vectors = all_vectors.reshape(-1, 5, vector_count).transpose(1, 0, 2).reshape(5, -1)
+    full_edge_bias, full_edge_gain, full_edge_shift, full_node_bias, full_node_gain = (
+        all_vectors[i] for i in range(5)
     )
     live_nodes = (jnp.arange(node_rows) < node_counts[0]).astype(jnp.float32)[:, None]
     live_edges = (jnp.arange(edge_rows) < edge_blocks[0] * 128).astype(jnp.float32)[:, None]
@@ -123,20 +131,8 @@
     node_grad_z = norm_back(node_upstream * full_node_gain, node_normed, node_inverse)
     node_grad_pre = outer_back(node_grad_z, full_node_second) * (node_pre > 0).astype(jnp.float32)
     node_input = jnp.concatenate([node_states, aggregate], axis=1)
-    node_first_grad, node_second_grad = (
-        lax.psum_scatter(
-            inner(node_input, node_grad_pre) * node_scale,
-            ("dom", "sub"),
-            scatter_dimension=0,
-            tiled=True,
-        ),
-        lax.psum_scatter(
-            inner(node_act, node_grad_z) * node_scale,
-            ("dom", "sub"),
-            scatter_dimension=0,
-            tiled=True,
-        ),
-    )
+    node_first_part = inner(node_input, node_grad_pre) * node_scale
+    node_second_part = inner(node_act, node_grad_z) * node_scale
     node_grad_input = outer_back(node_grad_pre, full_node_first)
     state_grads = node_upstream + node_grad_input[:, :width]
     edge_upstream = (
@@ -144,17 +140,24 @@
     ) * live_edges
     edge_grad_z = norm_back(edge_upstream * full_edge_gain, edge_normed, edge_inverse)
     edge_grad_pre = outer_back(edge_grad_z, full_edge_second) * (edge_pre > 0).astype(jnp.float32)
-    edge_second_grad = lax.psum_scatter(
-        inner(edge_act, edge_grad_z) * edge_scale, ("dom", "sub"), scatter_dimension=0, tiled=True
-    )
+    edge_second_part = inner(edge_act, edge_grad_z) * edge_scale
     extended = jnp.concatenate([node_states, ghosts], axis=0)
     features = jnp.concatenate(
         [edge_states, jnp.take(extended, source, axis=0), jnp.take(extended, target, axis=0)],
         axis=1,
     )
-    edge_first_grad = lax.psum_scatter(
-        inner(features, edge_grad_pre) * edge_scale, ("dom", "sub"), scatter_dimension=0, tiled=True
-    )
+    edge_first_part = inner(features, edge_grad_pre) * edge_scale
+    parts = (edge_first_part, edge_second_part, node_first_part, node_second_part)
+    blocked = jnp.concatenate(
+        [part.reshape(peer_count, -1, width) for part in parts], axis=1
+    )
+    reduced = lax.psum_scatter(blocked, peers, scatter_dimension=0, tiled=True)[0]
+    grads = []
+    offset = 0
+    for rows in [m.shape[0] for m in matrices]:
+        grads.append(reduced[offset : offset + rows])
+        offset += rows
+    edge_first_grad, edge_second_grad, node_first_grad, node_second_grad = grads
     edge_grad_input = outer_back(edge_grad_pre, full_edge_first)
     edge_grads = (edge_cotangent + edge_grad_input[:, :width]) * live_edges
     extended_grads = jax.ops.segment_sum(

time: 443 us -> 221 us (0.50)
  waiting for transfers between devices: 296 us -> 126 us
  blocking collectives: 63.6 us -> 0 us
  local copies, waits for them, and re-layouts: 10.4 us -> 23.2 us
  matrix products: 29 us -> 23.1 us
  other arithmetic: 8.89 us -> 13.6 us
    reduce_scatter x4 -> x1, waiting for transfers between devices: 235 us -> 71.1 us  [shards(): lax.psum_scatter(blocked, peers, scatter_dimension=0, tiled=True)[0]]
    unnamed x1 -> x0, blocking collectives: 63.6 us -> none
    slice x0 -> x11, local copies, waits for them, and re-layouts: none -> 10.6 us  [the longest x6 5.73 us: shards(): pieces.append(gathered[:, offset:offset + rows, :])]
    all_gather x4 -> x1, waiting for transfers between devices: 51.9 us -> 53.1 us  [shards(): gathered = lax.all_gather(packed, peers, axis=0, tiled=False)]
  transfers between devices with their start and end apart: 16 -> 10, of which waited for: 10 -> 4; matrix products, arithmetic and copies ran while one was open for 11% -> 7% of each run, Pallas kernels for 0% -> 0%
where the time goes in v1:
time: 221 us
  waiting for transfers between devices  126 us (57%)
  local copies, waits for them, and re-layouts  23.2 us (10%)
  matrix products  23.1 us (10%)
  starting transfers between devices  18.8 us (9%)
  between operations  15.9 us (7%)
  other arithmetic  13.6 us (6%)
    reduce_scatter x1, waiting for transfers between devices, shards(): lax.psum_scatter(blocked, peers, scatter_dimension=0, tiled=True)[0]  71.1 us
    all_gather x1, waiting for transfers between devices, shards(): gathered = lax.all_gather(packed, peers, axis=0, tiled=False)  53.1 us
    ppermute x4, starting transfers between devices, padded(): lax.ppermute(tail, axis, [(i, (i + 1) % count) for i in range(ends)])  13.5 us
    dot_general x4, matrix products, inner(): lax.dot_general(left, right, (((0,), (0,)), ((), ())), precision=lax.Prec...  11.3 us
    dot_general x4, matrix products, outer_back(): lax.dot_general(left, right, (((1,), (1,)), ((), ())), precision=lax.Prec...  8.43 us
    slice x6, local copies, waits for them, and re-layouts, shards(): pieces.append(gathered[:, offset:offset + rows, :])  5.73 us
    unnamed x39, local copies, waits for them, and re-layouts  5.69 us
    ppermute x4, starting transfers between devices, padded(): lax.ppermute(head, axis, [((i + 1) % count, i) for i in range(ends)])  5.17 us
  transfers between devices with their start and end apart: 10, of which 4 were waited for; matrix products, arithmetic and copies ran while one was open for 7% of the time, Pallas kernels for 0%

profile of v1, /device:TPU:0, one launch (start us, length us, event | category | flops | bytes accessed | tf_op | source)
XLA Modules:
  0.0 220.7 jit_solution(13132464971501739964)
XLA Ops:
  7.2 1.0 constant_dynamic-update-slice_fusion.3
  8.2 0.8 constant_dynamic-update-slice_fusion.2
  9.1 0.9 constant_dynamic-update-slice_fusion.1
  10.0 0.8 constant_dynamic-update-slice_fusion
  10.8 0.8 concatenate.24
  11.7 0.8 copy-done.15
  12.5 0.8 broadcast_in_dim_reshape_squeeze.3
  13.3 0.8 reshape.258
  14.8 1.8 gather_fusion.1
  16.6 1.3 collective-permute-start.7
  17.9 5.6 %collective-permute-start.6 = (f32[1,16,512]{2,1,0:T(8,128)S(1)}, f32[1,16,512]{2,1,0:T(8,128)S(1)}, u32[]{:S(2)}, u32[]{:S(2)}) collective-permute-start(f32[1,16,512]{2,1,0:T(8,128)S(1)} %get-tuple-element.34), channel_id=1, source_target_pairs={{0,1},{1,2},{2,3},{4,5},{5,6},{6,7},{8,9},{9,10},{10,11},{12,13},{... | collective-permute-start | bytes 98312 | tf_op jit(solution)/shard_map/ppermute | solution.py:19
  23.5 1.3 collective-permute-start.5
  24.8 3.0 %collective-permute-start.4 = (f32[1,16,512]{2,1,0:T(8,128)S(1)}, f32[1,16,512]{2,1,0:T(8,128)S(1)}, u32[]{:S(2)}, u32[]{:S(2)}) collective-permute-start(f32[1,16,512]{2,1,0:T(8,128)S(1)} %get-tuple-element.32), channel_id=1, source_target_pairs={{0,4},{4,8},{8,12},{1,5},{5,9},{9,13},{2,6},{6,10},{10,14},{3,7},{... | collective-permute-start | bytes 98312 | tf_op jit(solution)/shard_map/ppermute | solution.py:19
  29.3 0.8 gather_fusion.3
  30.1 0.8 gather_fusion.2
  30.9 0.8 broadcast_select_fusion
  31.7 0.8 broadcast_select_fusion.1
  32.5 53.1 %all-gather.4.cloned.1.call-done = f32[16,225,512]{2,1,0:T(8,128)} async-done(((f32[1,225,512]{2,1,0:T(8,128)}), f32[16,225,512]{2,1,0:T(8,128)}) %all-gather.4.cloned.1.call-update) | async-done | bytes 7372816 | tf_op jit(solution)/shard_map/all_gather | solution.py:103
  85.6 1.0 slice.191
  87.0 2.9 %fusion.42 = (f32[16,32,512]{2,1,0:T(8,128)S(1)}, f32[16,32,512]{2,1,0:T(8,128)}) fusion(f32[16,225,512]{2,1,0:T(8,128)} %all-gather.4.cloned.1.call-done), kind=kLoop, calls=%fused_computation.126 | loop fusion | bytes 4194304 | tf_op jit(solution)/shard_map/slice | solution.py:107
  89.9 1.1 fusion.45
  91.6 1.2 convolution_select_fusion
  92.8 2.3 %convolution_multiply_fusion.2 = f32[512,512]{1,0:T(8,128)} fusion(f32[256,512]{1,0:T(8,128)S(1)} %copy-done.6, f32[256,512]{1,0:T(8,128)S(1)} %get-tuple-element.45, f32[256,512]{1,0:T(8,128)S(1)} %copy-done.2, f32[256]{0:T(256)S(1)} %get-tuple-element.50, f32[256]{0:T(256)S(1)} %get-tuple-element.51, f32[512]{0:T(512)S(1)} %mul.152, ...), kind=kOutput, calls=%fused_computation.10 | convolution fusion | flops 806748160 | bytes 2628608 | tf_op jit(solution)/shard_map/dot_general | solution.py:33
  95.2 2.2 %fusion.44 = (f32[128]{0:T(128)S(1)}, f32[128,512]{1,0:T(8,128)S(1)}) fusion(f32[512]{0:T(512)S(1)} %add.131, f32[512,512]{1,0:T(8,128)} %bitcast.77, f32[128,512]{1,0:T(8,128)} %param.24), kind=kOutput, calls=%fused_computation.128 | convolution fusion | flops 402849664 | bytes 1575424 | tf_op jit(solution)/shard_map/dot_general | solution.py:29
  97.7 1.9 fusion.46
  99.7 1.0 copy-done.9
  100.7 0.8 gather_fusion
  102.0 1.9 convolution_select_fusion.1
  103.9 2.1 convolution_multiply_fusion.3
  106.1 2.3 %scatter_custom_fusion.2 = f32[256,512]{1,0:T(8,128)} fusion(s32[128]{0:T(128)S(1)} %get-tuple-element.39, f32[]{:T(128)} %constant.40.clone.1, f32[128,512]{1,0:T(8,128)S(1)} %get-tuple-element.43, f32[512]{0:T(512)S(1)} %add.154, f32[512]{0:T(512)S(1)} %mul.165, f32[128]{0:T(128)S(1)} %compare_convert_fusion, f32[128]{0:T(128)S(1)} %add_rsqrt_fusion.1, ...), kind=kCustom, calls=%fused_computation.41 | custom fusion | flops 393216 | bytes 792068 | tf_op jit(solution)/shard_map/scatter-add | solution.py:127
  108.4 3.0 %convolution_multiply_fusion.1 = f32[1024,512]{1,0:T(8,128)S(1)} fusion(f32[256,512]{1,0:T(8,128)S(1)} %copy-done.5, f32[256,512]{1,0:T(8,128)} %scatter_custom_fusion.2, f32[256,512]{1,0:T(8,128)S(1)} %copy-done.1), kind=kOutput, calls=%fused_computation.9 | convolution fusion | flops 1611399168 | bytes 3670016 | tf_op jit(solution)/shard_map/dot_general | solution.py:33
  111.4 3.9 %convolution_multiply_fusion = f32[1536,512]{1,0:T(8,128)S(1)} fusion(f32[128,512]{1,0:T(8,128)S(1)} %copy-done.11, f32[128,512]{1,0:T(8,128)} %broadcast_select_fusion, f32[128,512]{1,0:T(8,128)} %broadcast_select_fusion.1, f32[128,512]{1,0:T(8,128)} %param.23), kind=kOutput, calls=%fused_computation.8 | convolution fusion | flops 1209139200 | bytes 4194304 | tf_op jit(solution)/shard_map/dot_general | solution.py:33
  115.3 3.5 %pad_maximum_fusion = f32[16,224,512]{2,1,0:T(8,128)} fusion(f32[16,32,512]{2,1,0:T(8,128)S(1)} %bitcast.82, f32[16,64,512]{2,1,0:T(8,128)S(1)} %bitcast.81, f32[16,32,512]{2,1,0:T(8,128)S(1)} %bitcast.83, f32[16,96,512]{2,1,0:T(8,128)S(1)} %bitcast.74), kind=kLoop, calls=%fused_computation.7 | loop fusion | flops 5505024 | bytes 14680064 | tf_op jit(solution)/shard_map/concatenate | solution.py:151
  118.9 1.9 slice-done.1
  120.7 3.4 %fusion.47 = f32[128,1536]{1,0:T(8,128)S(1)} fusion(f32[128,512]{1,0:T(8,128)S(1)} %copy-done.11, f32[1536,512]{1,0:T(8,128)S(1)} %bitcast.76), kind=kOutput, calls=%fused_computation.131 | convolution fusion | flops 1207959552 | bytes 4194304 | tf_op jit(solution)/shard_map/dot_general | solution.py:43
  124.1 0.8 fusion.43
  124.9 2.3 %scatter_custom_fusion = f32[320,512]{1,0:T(8,128)S(1)} fusion(s32[256]{0:T(256)S(1)} %bitcast.90, f32[128,512]{1,0:T(8,128)S(1)} %get-tuple-element.24, f32[]{:T(128)} %constant.87, f32[128,512]{1,0:T(8,128)S(1)} %get-tuple-element.23, f32[]{:T(128)} %constant.40.clone.1), kind=kCustom, calls=%fused_computation.27 | custom fusion | flops 262144 | bytes 1179656 | tf_op jit(solution)/shard_map/add | solution.py:166
  127.2 3.0 %collective-permute-start.3 = (f32[1,16,512]{2,1,0:T(8,128)S(1)}, f32[1,16,512]{2,1,0:T(8,128)S(1)}, u32[]{:S(2)}, u32[]{:S(2)}) collective-permute-start(f32[1,16,512]{2,1,0:T(8,128)S(1)} %get-tuple-element.27), channel_id=1, source_target_pairs={{0,1},{1,2},{2,3},{4,5},{5,6},{6,7},{8,9},{9,10},{10,11},{12,13},{... | collective-permute-start | bytes 98312 | tf_op jit(solution)/shard_map/ppermute | solution.py:19
  130.3 1.3 collective-permute-start.2
  131.6 1.9 collective-permute-start.1
  133.5 1.3 collective-permute-start
  134.9 1.1 collective-permute-done.2
  136.1 0.7 collective-permute-done
  136.8 1.2 scatter_fusion
  138.0 71.1 %reduce-scatter.2.cloned.1.call-done = f32[1,224,512]{2,1,0:T(8,128)} async-done(((f32[16,224,512]{2,1,0:T(8,128)}), f32[1,224,512]{2,1,0:T(8,128)}) %reduce-scatter.2.cloned.1.call-update) | async-done | bytes 458768 | tf_op jit(solution)/shard_map/reduce_scatter | solution.py:154
  209.1 1.6 slice_bitcast_fusion
  210.7 1.5 slice_bitcast_fusion.2
  212.3 1.6 slice_bitcast_fusion.1
  (85 shorter events, 3.1 us)
Async XLA Ops:
  7.2 22.0 %copy-start.16 = (s32[2,128]{1,0:T(2,128)S(1)}, s32[2,128]{1,0:T(2,128)}, u32[]{:S(2)}) copy-start(s32[2,128]{1,0:T(2,128)} %param.27) | copy-start | bytes 3076
  7.2 22.1 %copy-start.1 = (f32[256,512]{1,0:T(8,128)S(1)}, f32[256,512]{1,0:T(8,128)}, u32[]{:S(2)}) copy-start(f32[256,512]{1,0:T(8,128)} %param.21) | copy-start | bytes 1572868
  7.2 78.4 %all-gather.4.cloned.1.call-start = ((), (), s32[]{:S(2)}) async-start(), calls=%async_computation.2 | async-start | bytes 8077312 | tf_op jit(solution)/shard_map/all_gather | solution.py:103
  11.7 0.8 copy-start.15
  12.5 196.6 %reduce-scatter.2.cloned.1.call-start = ((), (), s32[]{:S(2)}) async-start(), calls=%async_computation.1 | async-start | bytes 7798784 | tf_op jit(solution)/shard_map/reduce_scatter | solution.py:154
  16.6 12.6 %collective-permute-start.7 = (f32[1,16,512]{2,1,0:T(8,128)S(1)}, f32[1,16,512]{2,1,0:T(8,128)S(1)}, u32[]{:S(2)}, u32[]{:S(2)}) collective-permute-start(f32[1,16,512]{2,1,0:T(8,128)S(1)} %get-tuple-element.33), channel_id=1, source_target_pairs={{1,0},{2,1},{3,2},{5,4},{6,5},{7,6},{9,8},{10,9},{11,10},{13,12},{... | collective-permute-start | bytes 98312 | tf_op jit(solution)/shard_map/ppermute | solution.py:21
  17.9 11.3 %collective-permute-start.6 = (f32[1,16,512]{2,1,0:T(8,128)S(1)}, f32[1,16,512]{2,1,0:T(8,128)S(1)}, u32[]{:S(2)}, u32[]{:S(2)}) collective-permute-start(f32[1,16,512]{2,1,0:T(8,128)S(1)} %get-tuple-element.34), channel_id=1, source_target_pairs={{0,1},{1,2},{2,3},{4,5},{5,6},{6,7},{8,9},{9,10},{10,11},{12,13},{... | collective-permute-start | bytes 98312 | tf_op jit(solution)/shard_map/ppermute | solution.py:19
  23.5 5.7 %collective-permute-start.5 = (f32[1,16,512]{2,1,0:T(8,128)S(1)}, f32[1,16,512]{2,1,0:T(8,128)S(1)}, u32[]{:S(2)}, u32[]{:S(2)}) collective-permute-start(f32[1,16,512]{2,1,0:T(8,128)S(1)} %get-tuple-element.35), channel_id=1, source_target_pairs={{4,0},{8,4},{12,8},{5,1},{9,5},{13,9},{6,2},{10,6},{14,10},{7,3},{... | collective-permute-start | bytes 98312 | tf_op jit(solution)/shard_map/ppermute | solution.py:21
  24.8 4.5 %collective-permute-start.4 = (f32[1,16,512]{2,1,0:T(8,128)S(1)}, f32[1,16,512]{2,1,0:T(8,128)S(1)}, u32[]{:S(2)}, u32[]{:S(2)}) collective-permute-start(f32[1,16,512]{2,1,0:T(8,128)S(1)} %get-tuple-element.32), channel_id=1, source_target_pairs={{0,4},{4,8},{8,12},{1,5},{5,9},{9,13},{2,6},{6,10},{10,14},{3,7},{... | collective-permute-start | bytes 98312 | tf_op jit(solution)/shard_map/ppermute | solution.py:19
  30.9 59.0 %copy-start.6 = (f32[256,512]{1,0:T(8,128)S(1)}, f32[256,512]{1,0:T(8,128)}, u32[]{:S(2)}) copy-start(f32[256,512]{1,0:T(8,128)} %param.22) | copy-start | bytes 1572868
  87.0 4.3 %copy-start.2 = (f32[256,512]{1,0:T(8,128)S(1)}, f32[256,512]{1,0:T(8,128)}, u32[]{:S(2)}) copy-start(f32[256,512]{1,0:T(8,128)} %param.25) | copy-start | bytes 1572868
  92.8 5.0 %copy-start.4 = (f32[256,512]{1,0:T(8,128)}, f32[256,512]{1,0:T(8,128)S(1)}, u32[]{:S(2)}) copy-start(f32[256,512]{1,0:T(8,128)S(1)} %convolution_select_fusion) | copy-start | bytes 1572868
  95.1 2.6 %slice-start = ((f32[16,225,512]{2,1,0:T(8,128)}), f32[16,64,512]{2,1,0:T(8,128)S(1)}, s32[]{:S(2)}) async-start(f32[16,225,512]{2,1,0:T(8,128)} %all-gather.4.cloned.1.call-done), calls=%async_computation.3 | async-start | bytes 4194304 | tf_op jit(solution)/shard_map/slice | solution.py:107
  99.7 1.0 copy-start.9
  100.7 0.9 copy-start.13
  100.7 1.3 copy-start
  100.7 1.3 copy-start.12
  101.5 6.9 %copy-start.5 = (f32[256,512]{1,0:T(8,128)S(1)}, f32[256,512]{1,0:T(8,128)}, u32[]{:S(2)}) copy-start(f32[256,512]{1,0:T(8,128)} %copy-done.4) | copy-start | bytes 1572868
  108.4 3.0 %copy-start.11 = (f32[128,512]{1,0:T(8,128)S(1)}, f32[128,512]{1,0:T(8,128)}, u32[]{:S(2)}) copy-start(f32[128,512]{1,0:T(8,128)} %convolution_select_fusion.1) | copy-start | bytes 786436
  108.4 6.9 %copy-start.8 = (f32[512,512]{1,0:T(8,128)S(1)}, f32[512,512]{1,0:T(8,128)}, u32[]{:S(2)}) copy-start(f32[512,512]{1,0:T(8,128)} %convolution_multiply_fusion.2) | copy-start | bytes 3145732
  118.8 1.9 slice-start.1
  118.8 5.3 %copy-start.14 = (f32[128,512]{1,0:T(8,128)S(1)}, f32[128,512]{1,0:T(8,128)}, u32[]{:S(2)}) copy-start(f32[128,512]{1,0:T(8,128)} %param.26) | copy-start | bytes 786436
  120.7 14.0 %copy-start.3 = (f32[256,512]{1,0:T(8,128)S(1)}, f32[256,512]{1,0:T(8,128)}, u32[]{:S(2)}) copy-start(f32[256,512]{1,0:T(8,128)} %param.25) | copy-start | bytes 1572868
  120.7 14.1 %copy-start.10 = (f32[256,1024]{1,0:T(8,128)S(1)}, f32[256,1024]{1,0:T(8,128)}, u32[]{:S(2)}) copy-start(f32[256,1024]{1,0:T(8,128)} %copy-done.9) | copy-start | bytes 3145732
  127.2 7.7 %collective-permute-start.3 = (f32[1,16,512]{2,1,0:T(8,128)S(1)}, f32[1,16,512]{2,1,0:T(8,128)S(1)}, u32[]{:S(2)}, u32[]{:S(2)}) collective-permute-start(f32[1,16,512]{2,1,0:T(8,128)S(1)} %get-tuple-element.27), channel_id=1, source_target_pairs={{0,1},{1,2},{2,3},{4,5},{5,6},{6,7},{8,9},{9,10},{10,11},{12,13},{... | collective-permute-start | bytes 98312 | tf_op jit(solution)/shard_map/ppermute | solution.py:19
  130.3 5.8 %collective-permute-start.2 = (f32[1,16,512]{2,1,0:T(8,128)S(1)}, f32[1,16,512]{2,1,0:T(8,128)S(1)}, u32[]{:S(2)}, u32[]{:S(2)}) collective-permute-start(f32[1,16,512]{2,1,0:T(8,128)S(1)} %get-tuple-element.28), channel_id=1, source_target_pairs={{1,0},{2,1},{3,2},{5,4},{6,5},{7,6},{9,8},{10,9},{11,10},{13,12},{... | collective-permute-start | bytes 98312 | tf_op jit(solution)/shard_map/ppermute | solution.py:21
  131.6 4.5 %collective-permute-start.1 = (f32[1,16,512]{2,1,0:T(8,128)S(1)}, f32[1,16,512]{2,1,0:T(8,128)S(1)}, u32[]{:S(2)}, u32[]{:S(2)}) collective-permute-start(f32[1,16,512]{2,1,0:T(8,128)S(1)} %get-tuple-element.29), channel_id=1, source_target_pairs={{0,4},{4,8},{8,12},{1,5},{5,9},{9,13},{2,6},{6,10},{10,14},{3,7},{... | collective-permute-start | bytes 98312 | tf_op jit(solution)/shard_map/ppermute | solution.py:19
  133.5 3.3 %collective-permute-start = (f32[1,16,512]{2,1,0:T(8,128)S(1)}, f32[1,16,512]{2,1,0:T(8,128)S(1)}, u32[]{:S(2)}, u32[]{:S(2)}) collective-permute-start(f32[1,16,512]{2,1,0:T(8,128)S(1)} %get-tuple-element.26), channel_id=1, source_target_pairs={{4,0},{8,4},{12,8},{5,1},{9,5},{13,9},{6,2},{10,6},{14,10},{7,3},{... | collective-permute-start | bytes 98312 | tf_op jit(solution)/shard_map/ppermute | solution.py:21
  138.0 75.8 %copy-start.7 = (f32[256,512]{1,0:T(8,128)}, f32[256,512]{1,0:T(8,128)S(1)}, u32[]{:S(2)}) copy-start(f32[256,512]{1,0:T(8,128)S(1)} %scatter_fusion) | copy-start | bytes 1572868
Sparse Core Ops, SparseCore 0:
  12.6 72.9 all-gather.3
  118.9 90.1 reduce-scatter.1

commit v2 on v1

--- a/solution.py
+++ b/solution.py
@@ -3,14 +3,22 @@
 import jax
 import jax.numpy as jnp
 from jax import lax
+from jax.sharding import Mesh
 from jax.sharding import PartitionSpec as P
 
 EPSILON = 1e-05
+DOM = ("domx", "core")
+
+
+def axis_count(axis):
+    if isinstance(axis, tuple):
+        return math.prod(lax.axis_size(name) for name in axis)
+    return lax.axis_size(axis)
 
 
 def padded(cells, sides, width):
     for axis, dim in sides:
-        count = lax.axis_size(axis)
+        count = axis_count(axis)
         ends = count - 1
         head = lax.slice_in_dim(cells, 0, width, axis=dim)
         tail = lax.slice_in_dim(cells, cells.shape[dim] - width, cells.shape[dim], axis=dim)
@@ -85,22 +93,32 @@
     node_rows, width = node_states.shape
     edge_rows = edge_states.shape[0]
     ghost = send_lists.shape[2]
-    dom_count = lax.axis_size("dom")
+    dom_count = axis_count(DOM)
     sub_count = lax.axis_size("sub")
     peer_count = dom_count * sub_count
     lists = send_lists[0]
     outgoing = jnp.take(node_states, lists.reshape(-1), axis=0).reshape(4, ghost, width)
-    dom_side = padded(jnp.stack([outgoing[1], outgoing[0]]), (("dom", 0),), 1)
+    dom_side = padded(jnp.stack([outgoing[1], outgoing[0]]), ((DOM, 0),), 1)
     sub_side = padded(jnp.stack([outgoing[3], outgoing[2]]), (("sub", 0),), 1)
     ghosts = jnp.stack([dom_side[0], dom_side[3], sub_side[0], sub_side[3]])
     ghosts = ghosts.reshape(4 * ghost, width)
-    peers = ("dom", "sub")
+    chips = ("domx", "sub")
+    core = lax.axis_index("core")
+    swap = [(0, 1), (1, 0)]
+    chip_rows = lax.axis_size("domx")
     matrices = (edge_first, edge_second, node_first, node_second)
     vectors = jnp.concatenate([edge_bias, edge_gain, edge_shift, node_bias, node_gain])
     vector_rows = -(-vectors.shape[0] // width)
     vectors = jnp.pad(vectors, (0, vector_rows * width - vectors.shape[0])).reshape(vector_rows, width)
     packed = jnp.concatenate(list(matrices) + [vectors], axis=0)
-    gathered = lax.all_gather(packed, peers, axis=0, tiled=False)
+    mine = lax.all_gather(packed, chips, axis=0, tiled=False)
+    theirs = lax.ppermute(mine, "core", swap)
+    mine = mine.reshape(chip_rows, 1, sub_count, *packed.shape)
+    theirs = theirs.reshape(chip_rows, 1, sub_count, *packed.shape)
+    low = core == 0
+    gathered = jnp.concatenate(
+        [jnp.where(low, mine, theirs), jnp.where(low, theirs, mine)], axis=1
+    ).reshape(peer_count, *packed.shape)
     pieces = []
     offset = 0
     for rows in [m.shape[0] for m in matrices] + [vector_rows]:
@@ -151,7 +169,12 @@
     blocked = jnp.concatenate(
         [part.reshape(peer_count, -1, width) for part in parts], axis=1
     )
-    reduced = lax.psum_scatter(blocked, peers, scatter_dimension=0, tiled=True)[0]
+    blocked = blocked.reshape(chip_rows, 2, sub_count, *blocked.shape[1:])
+    own = jnp.where(low, blocked[:, 0], blocked[:, 1])
+    other = jnp.where(low, blocked[:, 1], blocked[:, 0])
+    own = own + lax.ppermute(other, "core", swap)
+    own = own.reshape(chip_rows * sub_count, *own.shape[2:])
+    reduced = lax.psum_scatter(own, chips, scatter_dimension=0, tiled=True)[0]
     grads = []
     offset = 0
     for rows in [m.shape[0] for m in matrices]:
@@ -168,7 +191,7 @@
     )
     state_grads = state_grads + extended_grads[:node_rows]
     ghost_grads = extended_grads[node_rows:].reshape(4, ghost, width)
-    dom_back = padded(jnp.stack([ghost_grads[0], ghost_grads[1]]), (("dom", 0),), 1)
+    dom_back = padded(jnp.stack([ghost_grads[0], ghost_grads[1]]), ((DOM, 0),), 1)
     sub_back = padded(jnp.stack([ghost_grads[2], ghost_grads[3]]), (("sub", 0),), 1)
     returned = jnp.stack([dom_back[3], dom_back[0], sub_back[3], sub_back[0]])
     state_grads = state_grads + jax.ops.segment_sum(
@@ -214,4 +237,12 @@
         P(("groups", "dom", "sub"), None),
         P(("groups", "dom", "sub"), None),
     )
-    return jax.shard_map(shards, mesh=mesh, in_specs=in_specs, out_specs=out_specs, check_vma=False)
+    groups, doms, subs = mesh.devices.shape
+    split = Mesh(mesh.devices.reshape(groups, doms // 2, 2, subs), ("groups", "domx", "core", "sub"))
+
+    def spec(parts):
+        return P(*[tuple(n for a in p for n in (DOM if a == "dom" else (a,))) if isinstance(p, tuple) else p for p in parts])
+
+    in_specs = tuple(spec(s) for s in in_specs)
+    out_specs = tuple(spec(s) for s in out_specs)
+    return jax.shard_map(shards, mesh=split, in_specs=in_specs, out_specs=out_specs, check_vma=False)

time: 221 us -> 247 us (1.12)
  waiting for transfers between devices: 126 us -> 141 us
  other arithmetic: 13.6 us -> 21.7 us
  local copies, waits for them, and re-layouts: 23.2 us -> 26.5 us
    all_gather x1, waiting for transfers between devices: 53.1 us -> 71.2 us  [shards(): mine = lax.all_gather(packed, chips, axis=0, tiled=False)]
    reduce_scatter x1, waiting for transfers between devices: 71.1 us -> 60.7 us  [shards(): reduced = lax.psum_scatter(own, chips, scatter_dimension=0, tiled=True)[0]]
    select_n x0 -> x2, other arithmetic: none -> 6.47 us  [the longest x1 5.59 us: shards(): jnp.where(low, mine, theirs)]
    all_gather x0 -> x1, local copies, waits for them, and re-layouts: none -> 6.13 us  [shards(): mine = lax.all_gather(packed, chips, axis=0, tiled=False)]
    ppermute x0 -> x2, waiting for transfers between devices: none -> 6.04 us  [the longest x1 6.04 us: shards(): own = own + lax.ppermute(other, 'core', swap)]
    add x0 -> x1, other arithmetic: none -> 3.28 us  [shards(): own = own + lax.ppermute(other, 'core', swap)]
    concatenate x1, other arithmetic: 3.52 us -> 0.86 us  [shards(): jnp.concatenate([part.reshape(peer_count, -1, width) for part in parts],...]
    slice x6 -> x4, local copies, waits for them, and re-layouts: 5.73 us -> 4.09 us  [shards(): pieces.append(gathered[:, offset:offset + rows, :])]
  transfers between devices with their start and end apart: 10 -> 12, of which waited for: 4 -> 5; matrix products, arithmetic and copies ran while one was open for 7% -> 6% of each run, Pallas kernels for 0% -> 0%
where the time goes in v2:
time: 247 us
  waiting for transfers between devices  141 us (57%)
  local copies, waits for them, and re-layouts  26.5 us (11%)
  matrix products  21.9 us (9%)
  other arithmetic  21.7 us (9%)
  starting transfers between devices  19.3 us (8%)
  between operations  16 us (6%)
    all_gather x1, waiting for transfers between devices, shards(): mine = lax.all_gather(packed, chips, axis=0, tiled=False)  71.2 us
    reduce_scatter x1, waiting for transfers between devices, shards(): reduced = lax.psum_scatter(own, chips, scatter_dimension=0, tiled=True)[0]  60.7 us
    ppermute x4, starting transfers between devices, padded(): lax.ppermute(tail, axis, [(i, (i + 1) % count) for i in range(ends)])  12.8 us
    dot_general x4, matrix products, outer_back(): lax.dot_general(left, right, (((1,), (1,)), ((), ())), precision=lax.Prec...  9.78 us
    dot_general x4, matrix products, inner(): lax.dot_general(left, right, (((0,), (0,)), ((), ())), precision=lax.Prec...  9.24 us
    unnamed x47, local copies, waits for them, and re-layouts  7.03 us
    all_gather x1, local copies, waits for them, and re-layouts, shards(): mine = lax.all_gather(packed, chips, axis=0, tiled=False)  6.13 us
    ppermute x1, waiting for transfers between devices, shards(): own = own + lax.ppermute(other, 'core', swap)  6.04 us
  transfers between devices with their start and end apart: 12, of which 5 were waited for; matrix products, arithmetic and copies ran while one was open for 6% of the time, Pallas kernels for 0%

profile of v2, /device:TPU:0, one launch (start us, length us, event | category | flops | bytes accessed | tf_op | source)
XLA Modules:
  0.0 246.5 jit_solution(14595872047931174597)
XLA Ops:
  7.2 0.9 constant_dynamic-update-slice_fusion.3
  8.2 0.8 constant_dynamic-update-slice_fusion.2
  9.0 0.9 constant_dynamic-update-slice_fusion.1
  9.9 0.8 constant_dynamic-update-slice_fusion
  10.8 0.8 concatenate.36
  12.5 71.2 %all-gather.4.cloned.1.call-done = f32[8,225,512]{2,1,0:T(8,128)} async-done(((f32[1,225,512]{2,1,0:T(8,128)}), f32[8,225,512]{2,1,0:T(8,128)}) %all-gather.4.cloned.1.call-update) | async-done | bytes 3686416 | tf_op jit(solution)/shard_map/all_gather | solution.py:114
  83.7 6.1 %copy.35 = f32[8,225,512]{2,0,1:T(8,128)} copy(f32[8,225,512]{2,1,0:T(8,128)} %all-gather.4.cloned.1.call-done) | data formatting | bytes 7372800 | tf_op jit(solution)/shard_map/all_gather | solution.py:114
  90.8 1.3 collective-permute-start.8
  92.1 4.5 %collective-permute-start.7 = (f32[1,16,512]{2,1,0:T(8,128)S(1)}, f32[1,16,512]{2,1,0:T(8,128)S(1)}, u32[]{:S(2)}, u32[]{:S(2)}) collective-permute-start(f32[1,16,512]{2,1,0:T(8,128)S(1)} %get-tuple-element.36), channel_id=1, source_target_pairs={{0,1},{1,2},{2,3},{4,5},{5,6},{6,7},{8,9},{9,10},{10,11},{12,13},{... | collective-permute-start | bytes 98312 | tf_op jit(solution)/shard_map/ppermute | solution.py:27
  96.7 1.3 collective-permute-start.6
  98.0 3.2 %collective-permute-start.5 = (f32[1,16,512]{2,1,0:T(8,128)S(1)}, f32[1,16,512]{2,1,0:T(8,128)S(1)}, u32[]{:S(2)}, u32[]{:S(2)}) collective-permute-start(f32[1,16,512]{2,1,0:T(8,128)S(1)} %get-tuple-element.34), channel_id=1, source_target_pairs={{0,4},{4,8},{8,12},{1,5},{5,9},{9,13},{2,6},{6,10},{10,14},{3,7},{... | collective-permute-start | bytes 98312 | tf_op jit(solution)/shard_map/ppermute | solution.py:27
  104.2 0.8 broadcast_select_fusion
  105.0 0.8 broadcast_select_fusion.1
  105.8 5.6 %copy_select_fusion.1 = (f32[8,225,512]{2,1,0:T(8,128)S(1)}, f32[8,225,512]{2,1,0:T(8,128)S(1)}) fusion(f32[8,225,512]{2,1,0:T(8,128)} %all-gather.4.cloned.1.call-done, f32[8,225,512]{2,0,1:T(8,128)} %collective-permute-done, pred[]{:T(512)S(6)} %eq.3), kind=kLoop, calls=%fused_computation.14 | loop fusion | flops 1843200 | bytes 14745601 | tf_op jit(solution)/shard_map/jit(_where)/select_n | solution.py:120
  111.4 1.4 pad_maximum_fusion
  113.1 1.6 slice.207
  114.8 1.7 copy-done
  116.8 1.1 fusion.47
  118.5 2.0 convolution_select_fusion
  120.5 3.5 %convolution_multiply_fusion.2 = f32[512,512]{1,0:T(8,128)} fusion(f32[256,512]{1,0:T(8,128)S(1)} %copy-done.8, f32[256,512]{1,0:T(8,128)S(1)} %get-tuple-element.47, f32[256,512]{1,0:T(8,128)} %param.25, f32[256]{0:T(256)S(1)} %get-tuple-element.52, f32[256]{0:T(256)S(1)} %get-tuple-element.53, f32[512]{0:T(512)S(1)} %mul.152, ...), kind=kOutput, calls=%fused_computation.17 | convolution fusion | flops 806748160 | bytes 2628608 | tf_op jit(solution)/shard_map/dot_general | solution.py:41
  124.1 1.7 fusion.46
  126.2 3.0 %fusion.48 = f32[256,1024]{1,0:T(8,128)S(1)} fusion(f32[256,512]{1,0:T(8,128)} %convolution_select_fusion, f32[1024,512]{1,0:T(8,128)S(1)} %bitcast.114), kind=kOutput, calls=%fused_computation.137 | convolution fusion | flops 1610612736 | bytes 3670016 | tf_op jit(solution)/shard_map/dot_general | solution.py:51
  129.2 0.9 copy-done.11
  130.9 1.2 fusion.43
  132.1 1.4 convolution_select_fusion.1
  133.5 1.1 convolution_multiply_fusion.3
  134.7 1.6 scatter_custom_fusion.2
  136.4 1.9 convolution_multiply_fusion.1
  138.3 2.8 %convolution_multiply_fusion = f32[1536,512]{1,0:T(8,128)S(1)} fusion(f32[128,512]{1,0:T(8,128)S(1)} %convolution_select_fusion.1, f32[128,512]{1,0:T(8,128)S(1)} %copy-done.14, f32[128,512]{1,0:T(8,128)S(1)} %copy-done.15, f32[128,512]{1,0:T(8,128)S(1)} %copy-done.18), kind=kOutput, calls=%fused_computation.15 | convolution fusion | flops 1209139200 | bytes 4194304 | tf_op jit(solution)/shard_map/dot_general | solution.py:41
  141.0 0.9 pad_maximum_fusion.1
  141.9 0.9 select_bitcast_fusion
  142.8 1.2 collective-permute-start.9
  144.1 6.0 %collective-permute-done.9 = f32[2,4,224,512]{3,2,1,0:T(8,128)S(1)} collective-permute-done((f32[2,4,224,512]{3,2,1,0:T(8,128)S(1)}, f32[2,4,224,512]{3,2,1,0:T(8,128)S(1)}, u32[]{:S(2)}, u32[]{:S(2)}) %collective-permute-start.9) | collective-permute-done | bytes 3670048 | tf_op jit(solution)/shard_map/ppermute | solution.py:175
  150.1 3.3 %fusion.1 = f32[2,4,224,512]{3,2,1,0:T(8,128)} fusion(f32[2,4,224,512]{3,2,1,0:T(8,128)S(1)} %collective-permute-done.9, f32[2,2,4,224,512]{4,3,2,1,0:T(8,128)S(1)} %pad_maximum_fusion.1, pred[]{:T(512)S(6)} %eq.3), kind=kLoop, calls=%fused_computation.11 | loop fusion | flops 1835008 | bytes 14680065 | tf_op jit(solution)/shard_map/add | solution.py:175
  153.4 2.2 slice.210
  155.7 3.4 %fusion.49 = f32[128,1536]{1,0:T(8,128)S(1)} fusion(f32[128,512]{1,0:T(8,128)S(1)} %convolution_select_fusion.1, f32[1536,512]{1,0:T(8,128)S(1)} %bitcast.108), kind=kOutput, calls=%fused_computation.138 | convolution fusion | flops 1207959552 | bytes 4194304 | tf_op jit(solution)/shard_map/dot_general | solution.py:51
  159.0 0.8 fusion.45
  159.8 2.3 scatter_custom_fusion
  162.1 3.0 %collective-permute-start.4 = (f32[1,16,512]{2,1,0:T(8,128)S(1)}, f32[1,16,512]{2,1,0:T(8,128)S(1)}, u32[]{:S(2)}, u32[]{:S(2)}) collective-permute-start(f32[1,16,512]{2,1,0:T(8,128)S(1)} %get-tuple-element.29), channel_id=1, source_target_pairs={{0,1},{1,2},{2,3},{4,5},{5,6},{6,7},{8,9},{9,10},{10,11},{12,13},{... | collective-permute-start | bytes 98312 | tf_op jit(solution)/shard_map/ppermute | solution.py:27
  165.2 1.3 collective-permute-start.3
  166.5 2.0 collective-permute-start.2
  168.5 1.3 collective-permute-start.1
  169.9 2.6 %collective-permute-done.3 = f32[1,16,512]{2,1,0:T(8,128)S(1)} collective-permute-done((f32[1,16,512]{2,1,0:T(8,128)S(1)}, f32[1,16,512]{2,1,0:T(8,128)S(1)}, u32[]{:S(2)}, u32[]{:S(2)}) %collective-permute-start.3) | collective-permute-done | bytes 32800 | tf_op jit(solution)/shard_map/ppermute | solution.py:29
  173.1 1.2 scatter_fusion
  174.3 60.7 %reduce-scatter.2.cloned.1.call-done = f32[1,224,512]{2,1,0:T(8,128)} async-done(((f32[8,224,512]{2,1,0:T(8,128)}), f32[1,224,512]{2,1,0:T(8,128)}) %reduce-scatter.2.cloned.1.call-update) | async-done | bytes 458768 | tf_op jit(solution)/shard_map/reduce_scatter | solution.py:177
  235.0 1.6 slice_bitcast_fusion
  236.6 1.5 slice_bitcast_fusion.2
  238.1 1.6 slice_bitcast_fusion.1
  (100 shorter events, 6.6 us)
Async XLA Ops:
  7.2 76.6 %all-gather.4.cloned.1.call-start = ((), (), s32[]{:S(2)}) async-start(), calls=%async_computation.2 | async-start | bytes 4276224 | tf_op jit(solution)/shard_map/all_gather | solution.py:114
  11.6 0.8 copy-start.17
  12.4 77.4 %copy-start.19 = (s32[1,4,16]{2,1,0:T(4,128)S(1)}, s32[1,4,16]{2,1,0:T(4,128)}, u32[]{:S(2)}) copy-start(s32[1,4,16]{2,1,0:T(4,128)} %param.28) | copy-start | bytes 772
  12.4 77.6 %copy-start.20 = (s32[2,128]{1,0:T(2,128)S(1)}, s32[2,128]{1,0:T(2,128)}, u32[]{:S(2)}) copy-start(s32[2,128]{1,0:T(2,128)} %param.27) | copy-start | bytes 3076
  12.4 77.6 %copy-start.2 = (f32[256,512]{1,0:T(8,128)S(1)}, f32[256,512]{1,0:T(8,128)}, u32[]{:S(2)}) copy-start(f32[256,512]{1,0:T(8,128)} %param.21) | copy-start | bytes 1572868
  12.4 222.5 %reduce-scatter.2.cloned.1.call-start = ((), (), s32[]{:S(2)}) async-start(), calls=%async_computation.1 | async-start | bytes 4128768 | tf_op jit(solution)/shard_map/reduce_scatter | solution.py:177
  89.9 15.9 %collective-permute-start = (f32[8,225,512]{2,0,1:T(8,128)}, f32[8,225,512]{2,0,1:T(8,128)}, u32[]{:S(2)}, u32[]{:S(2)}) collective-permute-start(f32[8,225,512]{2,0,1:T(8,128)} %copy.35), channel_id=1, source_target_pairs={{0,4},{4,0},{1,5},{5,1},{2,6},{6,2},{3,7},{7,3},{8,12},{12,8},{9,1... | collective-permute-start | bytes 11059208 | tf_op jit(solution)/shard_map/ppermute | solution.py:115
  90.8 11.8 %collective-permute-start.8 = (f32[1,16,512]{2,1,0:T(8,128)S(1)}, f32[1,16,512]{2,1,0:T(8,128)S(1)}, u32[]{:S(2)}, u32[]{:S(2)}) collective-permute-start(f32[1,16,512]{2,1,0:T(8,128)S(1)} %get-tuple-element.35), channel_id=1, source_target_pairs={{1,0},{2,1},{3,2},{5,4},{6,5},{7,6},{9,8},{10,9},{11,10},{13,12},{... | collective-permute-start | bytes 98312 | tf_op jit(solution)/shard_map/ppermute | solution.py:29
  92.1 10.5 %collective-permute-start.7 = (f32[1,16,512]{2,1,0:T(8,128)S(1)}, f32[1,16,512]{2,1,0:T(8,128)S(1)}, u32[]{:S(2)}, u32[]{:S(2)}) collective-permute-start(f32[1,16,512]{2,1,0:T(8,128)S(1)} %get-tuple-element.36), channel_id=1, source_target_pairs={{0,1},{1,2},{2,3},{4,5},{5,6},{6,7},{8,9},{9,10},{10,11},{12,13},{... | collective-permute-start | bytes 98312 | tf_op jit(solution)/shard_map/ppermute | solution.py:27
  96.7 5.9 %collective-permute-start.6 = (f32[1,16,512]{2,1,0:T(8,128)S(1)}, f32[1,16,512]{2,1,0:T(8,128)S(1)}, u32[]{:S(2)}, u32[]{:S(2)}) collective-permute-start(f32[1,16,512]{2,1,0:T(8,128)S(1)} %get-tuple-element.37), channel_id=1, source_target_pairs={{4,0},{8,4},{12,8},{5,1},{9,5},{13,9},{6,2},{10,6},{14,10},{7,3},{... | collective-permute-start | bytes 98312 | tf_op jit(solution)/shard_map/ppermute | solution.py:29
  98.0 4.6 %collective-permute-start.5 = (f32[1,16,512]{2,1,0:T(8,128)S(1)}, f32[1,16,512]{2,1,0:T(8,128)S(1)}, u32[]{:S(2)}, u32[]{:S(2)}) collective-permute-start(f32[1,16,512]{2,1,0:T(8,128)S(1)} %get-tuple-element.34), channel_id=1, source_target_pairs={{0,4},{4,8},{8,12},{1,5},{5,9},{9,13},{2,6},{6,10},{10,14},{3,7},{... | collective-permute-start | bytes 98312 | tf_op jit(solution)/shard_map/ppermute | solution.py:27
  112.8 3.7 %copy-start = (f32[2,2,4,225,512]{4,3,2,1,0:T(8,128)}, f32[2,2,4,225,512]{4,3,2,1,0:T(8,128)S(1)}, u32[]{:S(2)}) copy-start(f32[2,2,4,225,512]{4,3,2,1,0:T(8,128)S(1)} %pad_maximum_fusion) | copy-start | bytes 22118404
  112.8 4.0 %copy-start.7 = (f32[256,512]{1,0:T(8,128)S(1)}, f32[256,512]{1,0:T(8,128)}, u32[]{:S(2)}) copy-start(f32[256,512]{1,0:T(8,128)} %param.22) | copy-start | bytes 1572868
  113.1 5.1 %copy-start.4 = (f32[256,512]{1,0:T(8,128)S(1)}, f32[256,512]{1,0:T(8,128)}, u32[]{:S(2)}) copy-start(f32[256,512]{1,0:T(8,128)} %param.25) | copy-start | bytes 1572868
  116.8 3.7 %copy-start.8 = (f32[256,512]{1,0:T(8,128)S(1)}, f32[256,512]{1,0:T(8,128)}, u32[]{:S(2)}) copy-start(f32[256,512]{1,0:T(8,128)} %param.22) | copy-start | bytes 1572868
  120.5 5.6 %copy-start.1 = (f32[16,64,512]{2,1,0:T(8,128)S(1)}, f32[16,64,512]{2,1,0:T(8,128)}, u32[]{:S(2)}) copy-start(f32[16,64,512]{2,1,0:T(8,128)} %slice.207) | copy-start | bytes 6291460
  129.1 1.0 copy-start.11
  129.1 2.9 %copy-start.13 = (f32[128,512]{1,0:T(8,128)S(1)}, f32[128,512]{1,0:T(8,128)}, u32[]{:S(2)}) copy-start(f32[128,512]{1,0:T(8,128)} %param.24) | copy-start | bytes 786436
  130.1 6.2 %copy-start.3 = (f32[256,512]{1,0:T(8,128)S(1)}, f32[256,512]{1,0:T(8,128)}, u32[]{:S(2)}) copy-start(f32[256,512]{1,0:T(8,128)} %param.21) | copy-start | bytes 1572868
  130.1 6.2 %copy-start.6 = (f32[256,512]{1,0:T(8,128)S(1)}, f32[256,512]{1,0:T(8,128)}, u32[]{:S(2)}) copy-start(f32[256,512]{1,0:T(8,128)} %convolution_select_fusion) | copy-start | bytes 1572868
  134.6 3.6 %copy-start.14 = (f32[128,512]{1,0:T(8,128)S(1)}, f32[128,512]{1,0:T(8,128)}, u32[]{:S(2)}) copy-start(f32[128,512]{1,0:T(8,128)} %broadcast_select_fusion) | copy-start | bytes 786436
  136.3 1.9 copy-start.15
  136.3 1.9 copy-start.18
  136.4 4.7 %copy-start.10 = (f32[512,512]{1,0:T(8,128)S(1)}, f32[512,512]{1,0:T(8,128)}, u32[]{:S(2)}) copy-start(f32[512,512]{1,0:T(8,128)} %convolution_multiply_fusion.2) | copy-start | bytes 3145732
  142.8 7.3 %collective-permute-start.9 = (f32[2,4,224,512]{3,2,1,0:T(8,128)S(1)}, f32[2,4,224,512]{3,2,1,0:T(8,128)S(1)}, u32[]{:S(2)}, u32[]{:S(2)}) collective-permute-start(f32[2,4,224,512]{3,2,1,0:T(8,128)S(1)} %select_bitcast_fusion), channel_id=1, source_target_pairs={{0,4},{4,0},{1,5},{5,1},{2,6},{6,2},{3,7},{7,3},{8,12},{12,8},{9,1... | collective-permute-start | bytes 11010056 | tf_op jit(solution)/shard_map/ppermute | solution.py:175
  155.6 3.4 %copy-start.16 = (f32[128,512]{1,0:T(8,128)S(1)}, f32[128,512]{1,0:T(8,128)}, u32[]{:S(2)}) copy-start(f32[128,512]{1,0:T(8,128)} %param.26) | copy-start | bytes 786436
  155.6 14.1 %copy-start.5 = (f32[256,512]{1,0:T(8,128)S(1)}, f32[256,512]{1,0:T(8,128)}, u32[]{:S(2)}) copy-start(f32[256,512]{1,0:T(8,128)} %param.25) | copy-start | bytes 1572868
  155.6 14.1 %copy-start.12 = (f32[256,1024]{1,0:T(8,128)S(1)}, f32[256,1024]{1,0:T(8,128)}, u32[]{:S(2)}) copy-start(f32[256,1024]{1,0:T(8,128)} %copy-done.11) | copy-start | bytes 3145732
  162.1 7.8 %collective-permute-start.4 = (f32[1,16,512]{2,1,0:T(8,128)S(1)}, f32[1,16,512]{2,1,0:T(8,128)S(1)}, u32[]{:S(2)}, u32[]{:S(2)}) collective-permute-start(f32[1,16,512]{2,1,0:T(8,128)S(1)} %get-tuple-element.29), channel_id=1, source_target_pairs={{0,1},{1,2},{2,3},{4,5},{5,6},{6,7},{8,9},{9,10},{10,11},{12,13},{... | collective-permute-start | bytes 98312 | tf_op jit(solution)/shard_map/ppermute | solution.py:27
  165.2 7.4 %collective-permute-start.3 = (f32[1,16,512]{2,1,0:T(8,128)S(1)}, f32[1,16,512]{2,1,0:T(8,128)S(1)}, u32[]{:S(2)}, u32[]{:S(2)}) collective-permute-start(f32[1,16,512]{2,1,0:T(8,128)S(1)} %get-tuple-element.30), channel_id=1, source_target_pairs={{1,0},{2,1},{3,2},{5,4},{6,5},{7,6},{9,8},{10,9},{11,10},{13,12},{... | collective-permute-start | bytes 98312 | tf_op jit(solution)/shard_map/ppermute | solution.py:29
  166.5 6.1 %collective-permute-start.2 = (f32[1,16,512]{2,1,0:T(8,128)S(1)}, f32[1,16,512]{2,1,0:T(8,128)S(1)}, u32[]{:S(2)}, u32[]{:S(2)}) collective-permute-start(f32[1,16,512]{2,1,0:T(8,128)S(1)} %get-tuple-element.31), channel_id=1, source_target_pairs={{0,4},{4,8},{8,12},{1,5},{5,9},{9,13},{2,6},{6,10},{10,14},{3,7},{... | collective-permute-start | bytes 98312 | tf_op jit(solution)/shard_map/ppermute | solution.py:27
  168.5 4.6 %collective-permute-start.1 = (f32[1,16,512]{2,1,0:T(8,128)S(1)}, f32[1,16,512]{2,1,0:T(8,128)S(1)}, u32[]{:S(2)}, u32[]{:S(2)}) collective-permute-start(f32[1,16,512]{2,1,0:T(8,128)S(1)} %get-tuple-element.28), channel_id=1, source_target_pairs={{4,0},{8,4},{12,8},{5,1},{9,5},{13,9},{6,2},{10,6},{14,10},{7,3},{... | collective-permute-start | bytes 98312 | tf_op jit(solution)/shard_map/ppermute | solution.py:29
  174.3 65.4 %copy-start.9 = (f32[256,512]{1,0:T(8,128)}, f32[256,512]{1,0:T(8,128)S(1)}, u32[]{:S(2)}) copy-start(f32[256,512]{1,0:T(8,128)S(1)} %scatter_fusion) | copy-start | bytes 1572868
Sparse Core Ops, SparseCore 0:
  12.5 71.1 all-gather.3
  153.5 81.3 reduce-scatter.1

commit v3 on v1

--- a/solution.py
+++ b/solution.py
@@ -26,7 +26,7 @@
 
 
 def matmul(left, right):
-    return jnp.dot(left, right, precision=lax.Precision.HIGHEST, preferred_element_type=jnp.float32)
+    return jnp.dot(left, right, precision=lax.Precision.HIGH, preferred_element_type=jnp.float32)
 
 
 def inner(left, right):
@@ -34,7 +34,7 @@
         left,
         right,
         (((0,), (0,)), ((), ())),
-        precision=lax.Precision.HIGHEST,
+        precision=lax.Precision.HIGH,
         preferred_element_type=jnp.float32,
     )
 
@@ -44,7 +44,7 @@
         left,
         right,
         (((1,), (1,)), ((), ())),
-        precision=lax.Precision.HIGHEST,
+        precision=lax.Precision.HIGH,
         preferred_element_type=jnp.float32,
     )
 

time: 221 us -> 216 us (0.977)
  matrix products: 23.1 us -> 16 us
    dot_general x4, matrix products: 8.43 us -> 4.95 us  [outer_back(): lax.dot_general(left, right, (((1,), (1,)), ((), ())), precision=lax.Prec...]
    dot_general x4, matrix products: 11.3 us -> 8.36 us  [inner(): lax.dot_general(left, right, (((0,), (0,)), ((), ())), precision=lax.Prec...]
  transfers between devices with their start and end apart: 10 -> 10, of which waited for: 4 -> 4; matrix products, arithmetic and copies ran while one was open for 7% -> 6% of each run, Pallas kernels for 0% -> 0%
where the time goes in v3:
time: 216 us; the launch traced here: 215 us
  waiting for transfers between devices  128 us (59%)
  local copies, waits for them, and re-layouts  23.2 us (11%)
  starting transfers between devices  18.8 us (9%)
  matrix products  16 us (7%)
  between operations  15.9 us (7%)
  other arithmetic  13.6 us (6%)
    reduce_scatter x1, waiting for transfers between devices, shards(): lax.psum_scatter(blocked, peers, scatter_dimension=0, tiled=True)[0]  72.7 us
    all_gather x1, waiting for transfers between devices, shards(): gathered = lax.all_gather(packed, peers, axis=0, tiled=False)  53.1 us
    ppermute x4, starting transfers between devices, padded(): lax.ppermute(tail, axis, [(i, (i + 1) % count) for i in range(ends)])  13.5 us
    dot_general x4, matrix products, inner(): lax.dot_general(left, right, (((0,), (0,)), ((), ())), precision=lax.Prec...  8.36 us
    slice x6, local copies, waits for them, and re-layouts, shards(): pieces.append(gathered[:, offset:offset + rows, :])  5.73 us
    unnamed x39, local copies, waits for them, and re-layouts  5.69 us
    ppermute x4, starting transfers between devices, padded(): lax.ppermute(head, axis, [((i + 1) % count, i) for i in range(ends)])  5.17 us
    dot_general x4, matrix products, outer_back(): lax.dot_general(left, right, (((1,), (1,)), ((), ())), precision=lax.Prec...  4.95 us
  transfers between devices with their start and end apart: 10, of which 4 were waited for; matrix products, arithmetic and copies ran while one was open for 6% of the time, Pallas kernels for 0%

profile of v3, /device:TPU:0, one launch (start us, length us, event | category | flops | bytes accessed | tf_op | source)
XLA Modules:
  0.0 215.1 jit_solution(4365328034385385654)
XLA Ops:
  7.2 1.0 constant_dynamic-update-slice_fusion.3
  8.2 0.8 constant_dynamic-update-slice_fusion.2
  9.1 0.9 constant_dynamic-update-slice_fusion.1
  10.0 0.8 constant_dynamic-update-slice_fusion
  10.8 0.8 concatenate.24
  11.7 0.8 copy-done.15
  12.5 0.8 broadcast_in_dim_reshape_squeeze.3
  13.3 0.8 reshape.258
  14.8 1.8 gather_fusion.1
  16.6 1.3 collective-permute-start.7
  17.9 5.6 %collective-permute-start.6 = (f32[1,16,512]{2,1,0:T(8,128)S(1)}, f32[1,16,512]{2,1,0:T(8,128)S(1)}, u32[]{:S(2)}, u32[]{:S(2)}) collective-permute-start(f32[1,16,512]{2,1,0:T(8,128)S(1)} %get-tuple-element.34), channel_id=1, source_target_pairs={{0,1},{1,2},{2,3},{4,5},{5,6},{6,7},{8,9},{9,10},{10,11},{12,13},{... | collective-permute-start | bytes 98312 | tf_op jit(solution)/shard_map/ppermute | solution.py:19
  23.5 1.3 collective-permute-start.5
  24.8 3.0 %collective-permute-start.4 = (f32[1,16,512]{2,1,0:T(8,128)S(1)}, f32[1,16,512]{2,1,0:T(8,128)S(1)}, u32[]{:S(2)}, u32[]{:S(2)}) collective-permute-start(f32[1,16,512]{2,1,0:T(8,128)S(1)} %get-tuple-element.32), channel_id=1, source_target_pairs={{0,4},{4,8},{8,12},{1,5},{5,9},{9,13},{2,6},{6,10},{10,14},{3,7},{... | collective-permute-start | bytes 98312 | tf_op jit(solution)/shard_map/ppermute | solution.py:19
  29.3 0.8 gather_fusion.3
  30.1 0.8 gather_fusion.2
  30.9 0.8 broadcast_select_fusion
  31.7 0.8 broadcast_select_fusion.1
  32.5 53.1 %all-gather.4.cloned.1.call-done = f32[16,225,512]{2,1,0:T(8,128)} async-done(((f32[1,225,512]{2,1,0:T(8,128)}), f32[16,225,512]{2,1,0:T(8,128)}) %all-gather.4.cloned.1.call-update) | async-done | bytes 7372816 | tf_op jit(solution)/shard_map/all_gather | solution.py:103
  85.6 1.0 slice.191
  87.0 2.9 %fusion.42 = (f32[16,32,512]{2,1,0:T(8,128)S(1)}, f32[16,32,512]{2,1,0:T(8,128)}) fusion(f32[16,225,512]{2,1,0:T(8,128)} %all-gather.4.cloned.1.call-done), kind=kLoop, calls=%fused_computation.126 | loop fusion | bytes 4194304 | tf_op jit(solution)/shard_map/slice | solution.py:107
  89.9 0.7 fusion.45
  91.2 0.8 convolution_select_fusion
  91.9 1.9 convolution_multiply_fusion.2
  93.9 1.9 fusion.44
  96.1 1.1 fusion.46
  97.2 1.0 copy-done.9
  98.2 0.8 gather_fusion
  99.5 1.4 convolution_select_fusion.1
  100.9 1.7 convolution_multiply_fusion.3
  102.6 2.3 %scatter_custom_fusion.2 = f32[256,512]{1,0:T(8,128)} fusion(s32[128]{0:T(128)S(1)} %get-tuple-element.39, f32[]{:T(128)} %constant.40.clone.1, f32[128,512]{1,0:T(8,128)S(1)} %get-tuple-element.43, f32[512]{0:T(512)S(1)} %add.154, f32[512]{0:T(512)S(1)} %mul.165, f32[128]{0:T(128)S(1)} %compare_convert_fusion, f32[128]{0:T(128)S(1)} %add_rsqrt_fusion.1, ...), kind=kCustom, calls=%fused_computation.41 | custom fusion | flops 393216 | bytes 792068 | tf_op jit(solution)/shard_map/scatter-add | solution.py:127
  104.9 2.2 %convolution_multiply_fusion.1 = f32[1024,512]{1,0:T(8,128)S(1)} fusion(f32[256,512]{1,0:T(8,128)S(1)} %copy-done.5, f32[256,512]{1,0:T(8,128)} %scatter_custom_fusion.2, f32[256,512]{1,0:T(8,128)S(1)} %copy-done.1), kind=kOutput, calls=%fused_computation.9 | convolution fusion | flops 806092800 | bytes 3670016 | tf_op jit(solution)/shard_map/dot_general | solution.py:33
  107.1 2.7 %convolution_multiply_fusion = f32[1536,512]{1,0:T(8,128)S(1)} fusion(f32[128,512]{1,0:T(8,128)S(1)} %copy-done.11, f32[128,512]{1,0:T(8,128)} %broadcast_select_fusion, f32[128,512]{1,0:T(8,128)} %broadcast_select_fusion.1, f32[128,512]{1,0:T(8,128)} %param.23), kind=kOutput, calls=%fused_computation.8 | convolution fusion | flops 605159424 | bytes 4194304 | tf_op jit(solution)/shard_map/dot_general | solution.py:33
  109.8 3.5 %pad_maximum_fusion = f32[16,224,512]{2,1,0:T(8,128)} fusion(f32[16,32,512]{2,1,0:T(8,128)S(1)} %bitcast.82, f32[16,64,512]{2,1,0:T(8,128)S(1)} %bitcast.81, f32[16,32,512]{2,1,0:T(8,128)S(1)} %bitcast.83, f32[16,96,512]{2,1,0:T(8,128)S(1)} %bitcast.74), kind=kLoop, calls=%fused_computation.7 | loop fusion | flops 5505024 | bytes 14680064 | tf_op jit(solution)/shard_map/concatenate | solution.py:151
  113.4 1.9 slice-done.1
  115.2 1.7 fusion.47
  117.0 0.8 fusion.43
  117.8 2.3 %scatter_custom_fusion = f32[320,512]{1,0:T(8,128)S(1)} fusion(s32[256]{0:T(256)S(1)} %bitcast.90, f32[128,512]{1,0:T(8,128)S(1)} %get-tuple-element.24, f32[]{:T(128)} %constant.87, f32[128,512]{1,0:T(8,128)S(1)} %get-tuple-element.23, f32[]{:T(128)} %constant.40.clone.1), kind=kCustom, calls=%fused_computation.27 | custom fusion | flops 262144 | bytes 1179656 | tf_op jit(solution)/shard_map/add | solution.py:166
  120.1 3.0 %collective-permute-start.3 = (f32[1,16,512]{2,1,0:T(8,128)S(1)}, f32[1,16,512]{2,1,0:T(8,128)S(1)}, u32[]{:S(2)}, u32[]{:S(2)}) collective-permute-start(f32[1,16,512]{2,1,0:T(8,128)S(1)} %get-tuple-element.27), channel_id=1, source_target_pairs={{0,1},{1,2},{2,3},{4,5},{5,6},{6,7},{8,9},{9,10},{10,11},{12,13},{... | collective-permute-start | bytes 98312 | tf_op jit(solution)/shard_map/ppermute | solution.py:19
  123.1 1.3 collective-permute-start.2
  124.4 1.9 collective-permute-start.1
  126.3 1.3 collective-permute-start
  127.8 1.1 collective-permute-done.2
  128.9 0.7 collective-permute-done
  129.7 1.2 scatter_fusion
  130.9 72.7 %reduce-scatter.2.cloned.1.call-done = f32[1,224,512]{2,1,0:T(8,128)} async-done(((f32[16,224,512]{2,1,0:T(8,128)}), f32[1,224,512]{2,1,0:T(8,128)}) %reduce-scatter.2.cloned.1.call-update) | async-done | bytes 458768 | tf_op jit(solution)/shard_map/reduce_scatter | solution.py:154
  203.6 1.6 slice_bitcast_fusion
  205.2 1.5 slice_bitcast_fusion.2
  206.7 1.6 slice_bitcast_fusion.1
  (85 shorter events, 3.1 us)
Async XLA Ops:
  7.2 22.0 %copy-start.16 = (s32[2,128]{1,0:T(2,128)S(1)}, s32[2,128]{1,0:T(2,128)}, u32[]{:S(2)}) copy-start(s32[2,128]{1,0:T(2,128)} %param.27) | copy-start | bytes 3076
  7.2 22.1 %copy-start.1 = (f32[256,512]{1,0:T(8,128)S(1)}, f32[256,512]{1,0:T(8,128)}, u32[]{:S(2)}) copy-start(f32[256,512]{1,0:T(8,128)} %param.21) | copy-start | bytes 1572868
  7.2 78.4 %all-gather.4.cloned.1.call-start = ((), (), s32[]{:S(2)}) async-start(), calls=%async_computation.2 | async-start | bytes 8077312 | tf_op jit(solution)/shard_map/all_gather | solution.py:103
  11.7 0.8 copy-start.15
  12.5 191.1 %reduce-scatter.2.cloned.1.call-start = ((), (), s32[]{:S(2)}) async-start(), calls=%async_computation.1 | async-start | bytes 7798784 | tf_op jit(solution)/shard_map/reduce_scatter | solution.py:154
  16.6 12.6 %collective-permute-start.7 = (f32[1,16,512]{2,1,0:T(8,128)S(1)}, f32[1,16,512]{2,1,0:T(8,128)S(1)}, u32[]{:S(2)}, u32[]{:S(2)}) collective-permute-start(f32[1,16,512]{2,1,0:T(8,128)S(1)} %get-tuple-element.33), channel_id=1, source_target_pairs={{1,0},{2,1},{3,2},{5,4},{6,5},{7,6},{9,8},{10,9},{11,10},{13,12},{... | collective-permute-start | bytes 98312 | tf_op jit(solution)/shard_map/ppermute | solution.py:21
  17.9 11.3 %collective-permute-start.6 = (f32[1,16,512]{2,1,0:T(8,128)S(1)}, f32[1,16,512]{2,1,0:T(8,128)S(1)}, u32[]{:S(2)}, u32[]{:S(2)}) collective-permute-start(f32[1,16,512]{2,1,0:T(8,128)S(1)} %get-tuple-element.34), channel_id=1, source_target_pairs={{0,1},{1,2},{2,3},{4,5},{5,6},{6,7},{8,9},{9,10},{10,11},{12,13},{... | collective-permute-start | bytes 98312 | tf_op jit(solution)/shard_map/ppermute | solution.py:19
  23.5 5.7 %collective-permute-start.5 = (f32[1,16,512]{2,1,0:T(8,128)S(1)}, f32[1,16,512]{2,1,0:T(8,128)S(1)}, u32[]{:S(2)}, u32[]{:S(2)}) collective-permute-start(f32[1,16,512]{2,1,0:T(8,128)S(1)} %get-tuple-element.35), channel_id=1, source_target_pairs={{4,0},{8,4},{12,8},{5,1},{9,5},{13,9},{6,2},{10,6},{14,10},{7,3},{... | collective-permute-start | bytes 98312 | tf_op jit(solution)/shard_map/ppermute | solution.py:21
  24.8 4.5 %collective-permute-start.4 = (f32[1,16,512]{2,1,0:T(8,128)S(1)}, f32[1,16,512]{2,1,0:T(8,128)S(1)}, u32[]{:S(2)}, u32[]{:S(2)}) collective-permute-start(f32[1,16,512]{2,1,0:T(8,128)S(1)} %get-tuple-element.32), channel_id=1, source_target_pairs={{0,4},{4,8},{8,12},{1,5},{5,9},{9,13},{2,6},{6,10},{10,14},{3,7},{... | collective-permute-start | bytes 98312 | tf_op jit(solution)/shard_map/ppermute | solution.py:19
  30.9 59.0 %copy-start.6 = (f32[256,512]{1,0:T(8,128)S(1)}, f32[256,512]{1,0:T(8,128)}, u32[]{:S(2)}) copy-start(f32[256,512]{1,0:T(8,128)} %param.22) | copy-start | bytes 1572868
  87.0 3.9 %copy-start.2 = (f32[256,512]{1,0:T(8,128)S(1)}, f32[256,512]{1,0:T(8,128)}, u32[]{:S(2)}) copy-start(f32[256,512]{1,0:T(8,128)} %param.25) | copy-start | bytes 1572868
  91.9 4.2 %copy-start.4 = (f32[256,512]{1,0:T(8,128)}, f32[256,512]{1,0:T(8,128)S(1)}, u32[]{:S(2)}) copy-start(f32[256,512]{1,0:T(8,128)S(1)} %convolution_select_fusion) | copy-start | bytes 1572868
  93.8 2.3 %slice-start = ((f32[16,225,512]{2,1,0:T(8,128)}), f32[16,64,512]{2,1,0:T(8,128)S(1)}, s32[]{:S(2)}) async-start(f32[16,225,512]{2,1,0:T(8,128)} %all-gather.4.cloned.1.call-done), calls=%async_computation.3 | async-start | bytes 4194304 | tf_op jit(solution)/shard_map/slice | solution.py:107
  97.2 1.0 copy-start.9
  98.2 0.9 copy-start.13
  98.2 1.3 copy-start
  98.2 1.3 copy-start.12
  99.0 5.9 %copy-start.5 = (f32[256,512]{1,0:T(8,128)S(1)}, f32[256,512]{1,0:T(8,128)}, u32[]{:S(2)}) copy-start(f32[256,512]{1,0:T(8,128)} %copy-done.4) | copy-start | bytes 1572868
  104.9 2.2 %copy-start.11 = (f32[128,512]{1,0:T(8,128)S(1)}, f32[128,512]{1,0:T(8,128)}, u32[]{:S(2)}) copy-start(f32[128,512]{1,0:T(8,128)} %convolution_select_fusion.1) | copy-start | bytes 786436
  104.9 4.9 %copy-start.8 = (f32[512,512]{1,0:T(8,128)S(1)}, f32[512,512]{1,0:T(8,128)}, u32[]{:S(2)}) copy-start(f32[512,512]{1,0:T(8,128)} %convolution_multiply_fusion.2) | copy-start | bytes 3145732
  113.3 1.9 slice-start.1
  113.3 3.6 %copy-start.14 = (f32[128,512]{1,0:T(8,128)S(1)}, f32[128,512]{1,0:T(8,128)}, u32[]{:S(2)}) copy-start(f32[128,512]{1,0:T(8,128)} %param.26) | copy-start | bytes 786436
  115.2 12.4 %copy-start.3 = (f32[256,512]{1,0:T(8,128)S(1)}, f32[256,512]{1,0:T(8,128)}, u32[]{:S(2)}) copy-start(f32[256,512]{1,0:T(8,128)} %param.25) | copy-start | bytes 1572868
  115.2 12.4 %copy-start.10 = (f32[256,1024]{1,0:T(8,128)S(1)}, f32[256,1024]{1,0:T(8,128)}, u32[]{:S(2)}) copy-start(f32[256,1024]{1,0:T(8,128)} %copy-done.9) | copy-start | bytes 3145732
  120.1 7.7 %collective-permute-start.3 = (f32[1,16,512]{2,1,0:T(8,128)S(1)}, f32[1,16,512]{2,1,0:T(8,128)S(1)}, u32[]{:S(2)}, u32[]{:S(2)}) collective-permute-start(f32[1,16,512]{2,1,0:T(8,128)S(1)} %get-tuple-element.27), channel_id=1, source_target_pairs={{0,1},{1,2},{2,3},{4,5},{5,6},{6,7},{8,9},{9,10},{10,11},{12,13},{... | collective-permute-start | bytes 98312 | tf_op jit(solution)/shard_map/ppermute | solution.py:19
  123.1 5.8 %collective-permute-start.2 = (f32[1,16,512]{2,1,0:T(8,128)S(1)}, f32[1,16,512]{2,1,0:T(8,128)S(1)}, u32[]{:S(2)}, u32[]{:S(2)}) collective-permute-start(f32[1,16,512]{2,1,0:T(8,128)S(1)} %get-tuple-element.28), channel_id=1, source_target_pairs={{1,0},{2,1},{3,2},{5,4},{6,5},{7,6},{9,8},{10,9},{11,10},{13,12},{... | collective-permute-start | bytes 98312 | tf_op jit(solution)/shard_map/ppermute | solution.py:21
  124.4 4.5 %collective-permute-start.1 = (f32[1,16,512]{2,1,0:T(8,128)S(1)}, f32[1,16,512]{2,1,0:T(8,128)S(1)}, u32[]{:S(2)}, u32[]{:S(2)}) collective-permute-start(f32[1,16,512]{2,1,0:T(8,128)S(1)} %get-tuple-element.29), channel_id=1, source_target_pairs={{0,4},{4,8},{8,12},{1,5},{5,9},{9,13},{2,6},{6,10},{10,14},{3,7},{... | collective-permute-start | bytes 98312 | tf_op jit(solution)/shard_map/ppermute | solution.py:19
  126.3 3.3 %collective-permute-start = (f32[1,16,512]{2,1,0:T(8,128)S(1)}, f32[1,16,512]{2,1,0:T(8,128)S(1)}, u32[]{:S(2)}, u32[]{:S(2)}) collective-permute-start(f32[1,16,512]{2,1,0:T(8,128)S(1)} %get-tuple-element.26), channel_id=1, source_target_pairs={{4,0},{8,4},{12,8},{5,1},{9,5},{13,9},{6,2},{10,6},{14,10},{7,3},{... | collective-permute-start | bytes 98312 | tf_op jit(solution)/shard_map/ppermute | solution.py:21
  130.9 77.4 %copy-start.7 = (f32[256,512]{1,0:T(8,128)}, f32[256,512]{1,0:T(8,128)S(1)}, u32[]{:S(2)}) copy-start(f32[256,512]{1,0:T(8,128)S(1)} %scatter_fusion) | copy-start | bytes 1572868
Sparse Core Ops, SparseCore 0:
  12.6 72.9 all-gather.3
  113.4 90.0 reduce-scatter.1

commit v4 on v3

--- a/solution.py
+++ b/solution.py
@@ -3,6 +3,7 @@
 import jax
 import jax.numpy as jnp
 from jax import lax
+from jax.experimental import pallas as pl
 from jax.sharding import PartitionSpec as P
 
 EPSILON = 1e-05
@@ -23,6 +24,40 @@
             axis=dim,
         )
     return cells
+
+
+def row_offsets(sizes):
+    offsets = [0]
+    for size in sizes:
+        offsets.append(offsets[-1] + size)
+    return offsets
+
+
+def pack_rows(pieces):
+    offsets = row_offsets([piece.shape[0] for piece in pieces])
+
+    def kernel(*refs):
+        out = refs[-1]
+        for index, ref in enumerate(refs[:-1]):
+            out[offsets[index] : offsets[index + 1], :] = ref[...]
+
+    return pl.pallas_call(
+        kernel,
+        out_shape=jax.ShapeDtypeStruct((offsets[-1], pieces[0].shape[1]), pieces[0].dtype),
+    )(*pieces)
+
+
+def split_rows(packed, sizes):
+    offsets = row_offsets(sizes)
+
+    def kernel(source, *outs):
+        for index, out in enumerate(outs):
+            out[...] = source[offsets[index] : offsets[index + 1], :]
+
+    return pl.pallas_call(
+        kernel,
+        out_shape=tuple(jax.ShapeDtypeStruct((size, packed.shape[1]), packed.dtype) for size in sizes),
+    )(packed)
 
 
 def matmul(left, right):
@@ -99,7 +134,7 @@
     vectors = jnp.concatenate([edge_bias, edge_gain, edge_shift, node_bias, node_gain])
     vector_rows = -(-vectors.shape[0] // width)
     vectors = jnp.pad(vectors, (0, vector_rows * width - vectors.shape[0])).reshape(vector_rows, width)
-    packed = jnp.concatenate(list(matrices) + [vectors], axis=0)
+    packed = pack_rows(list(matrices) + [vectors])
     gathered = lax.all_gather(packed, peers, axis=0, tiled=False)
     pieces = []
     offset = 0
@@ -152,12 +187,9 @@
         [part.reshape(peer_count, -1, width) for part in parts], axis=1
     )
     reduced = lax.psum_scatter(blocked, peers, scatter_dimension=0, tiled=True)[0]
-    grads = []
-    offset = 0
-    for rows in [m.shape[0] for m in matrices]:
-        grads.append(reduced[offset : offset + rows])
-        offset += rows
-    edge_first_grad, edge_second_grad, node_first_grad, node_second_grad = grads
+    edge_first_grad, edge_second_grad, node_first_grad, node_second_grad = split_rows(
+        reduced, [m.shape[0] for m in matrices]
+    )
     edge_grad_input = outer_back(edge_grad_pre, full_edge_first)
     edge_grads = (edge_cotangent + edge_grad_input[:, :width]) * live_edges
     extended_grads = jax.ops.segment_sum(

time: 216 us -> 211 us (0.977)
  local copies, waits for them, and re-layouts: 23.2 us -> 14.7 us
  Pallas kernels: 0 us -> 3.65 us
    slice x3 -> x0, local copies, waits for them, and re-layouts: 4.71 us -> none  [shards(): grads.append(reduced[offset:offset + rows])]
    unnamed x39 -> x33, local copies, waits for them, and re-layouts: 5.69 us -> 1.32 us
    pallas_call x0 -> x2, Pallas kernels: none -> 3.65 us  [the longest x1 1.87 us: pack_rows(): pl.pallas_call(kernel, out_shape=jax.ShapeDtypeStruct((offsets[-1], piece...]
where the time goes in v4:
time: 211 us; the launch traced here: 210 us
  waiting for transfers between devices  129 us (61%)
  starting transfers between devices  18.8 us (9%)
  matrix products  16 us (8%)
  between operations  15.9 us (8%)
  local copies, waits for them, and re-layouts  14.7 us (7%)
  other arithmetic  12.3 us (6%)
  Pallas kernels  3.65 us (2%)
    reduce_scatter x1, waiting for transfers between devices, shards(): lax.psum_scatter(blocked, peers, scatter_dimension=0, tiled=True)[0]  72.7 us
    all_gather x1, waiting for transfers between devices, shards(): gathered = lax.all_gather(packed, peers, axis=0, tiled=False)  54.6 us
    ppermute x4, starting transfers between devices, padded(): lax.ppermute(tail, axis, [(i, (i + 1) % count) for i in range(ends)])  13.5 us
    dot_general x4, matrix products, inner(): lax.dot_general(left, right, (((0,), (0,)), ((), ())), precision=lax.Prec...  8.35 us
    slice x6, local copies, waits for them, and re-layouts, shards(): pieces.append(gathered[:, offset:offset + rows, :])  5.73 us
    ppermute x4, starting transfers between devices, padded(): lax.ppermute(head, axis, [((i + 1) % count, i) for i in range(ends)])  5.17 us
    dot_general x4, matrix products, outer_back(): lax.dot_general(left, right, (((1,), (1,)), ((), ())), precision=lax.Prec...  4.94 us
  transfers between devices with their start and end apart: 10, of which 4 were waited for; matrix products, arithmetic and copies ran while one was open for 6% of the time, Pallas kernels for 0%

profile of v4, /device:TPU:0, one launch (start us, length us, event | category | flops | bytes accessed | tf_op | source)
XLA Modules:
  0.0 210.4 jit_solution(8343598026396165146)
XLA Ops:
  7.2 0.8 concatenate.21
  8.1 0.6 pad.4
  8.7 1.9 shard_map.226
  10.6 0.8 reshape.254
  11.4 0.8 broadcast_in_dim_reshape_squeeze.3
  12.2 1.8 gather_fusion.1
  14.0 1.3 collective-permute-start.7
  15.3 5.6 %collective-permute-start.6 = (f32[1,16,512]{2,1,0:T(8,128)S(1)}, f32[1,16,512]{2,1,0:T(8,128)S(1)}, u32[]{:S(2)}, u32[]{:S(2)}) collective-permute-start(f32[1,16,512]{2,1,0:T(8,128)S(1)} %get-tuple-element.40), channel_id=1, source_target_pairs={{0,1},{1,2},{2,3},{4,5},{5,6},{6,7},{8,9},{9,10},{10,11},{12,13},{... | collective-permute-start | bytes 98312 | tf_op jit(solution)/shard_map/ppermute | solution.py:20
  20.9 1.3 collective-permute-start.5
  22.2 3.0 %collective-permute-start.4 = (f32[1,16,512]{2,1,0:T(8,128)S(1)}, f32[1,16,512]{2,1,0:T(8,128)S(1)}, u32[]{:S(2)}, u32[]{:S(2)}) collective-permute-start(f32[1,16,512]{2,1,0:T(8,128)S(1)} %get-tuple-element.38), channel_id=1, source_target_pairs={{0,4},{4,8},{8,12},{1,5},{5,9},{9,13},{2,6},{6,10},{10,14},{3,7},{... | collective-permute-start | bytes 98312 | tf_op jit(solution)/shard_map/ppermute | solution.py:20
  26.8 0.8 gather_fusion.3
  27.5 0.8 gather_fusion.2
  28.3 0.9 broadcast_select_fusion
  29.2 54.6 %all-gather.4.cloned.1.call-done = f32[16,225,512]{2,1,0:T(8,128)} async-done(((f32[1,225,512]{2,1,0:T(8,128)}), f32[16,225,512]{2,1,0:T(8,128)}) %all-gather.4.cloned.1.call-update) | async-done | bytes 7372816 | tf_op jit(solution)/shard_map/all_gather | solution.py:138
  83.8 1.0 slice.159
  85.2 2.9 %fusion.42 = (f32[16,32,512]{2,1,0:T(8,128)S(1)}, f32[16,32,512]{2,1,0:T(8,128)}) fusion(f32[16,225,512]{2,1,0:T(8,128)} %all-gather.4.cloned.1.call-done), kind=kLoop, calls=%fused_computation.118 | loop fusion | bytes 4194304 | tf_op jit(solution)/shard_map/slice | solution.py:142
  88.1 0.7 fusion.45
  88.8 0.2 multiply_reduce_fusion.1
  89.1 0.3 fusion.14
  89.4 0.8 convolution_select_fusion
  90.2 1.9 convolution_multiply_fusion.2
  92.1 1.9 fusion.44
  94.0 0.2 multiply_reduce_fusion.3
  94.3 1.1 fusion.46
  95.4 1.0 copy-done.9
  96.4 0.8 gather_fusion
  97.2 0.1 copy-done.13
  97.3 0.2 fusion.41
  97.7 1.4 convolution_select_fusion.1
  99.1 1.6 convolution_multiply_fusion.3
  100.8 2.3 %scatter_custom_fusion.2 = f32[256,512]{1,0:T(8,128)} fusion(s32[128]{0:T(128)S(1)} %get-tuple-element.45, f32[]{:T(128)} %constant.40.clone.1, f32[128,512]{1,0:T(8,128)S(1)} %get-tuple-element.49, f32[512]{0:T(512)S(1)} %add.154, f32[512]{0:T(512)S(1)} %mul.165, f32[128]{0:T(128)S(1)} %compare_convert_fusion, f32[128]{0:T(128)S(1)} %add_rsqrt_fusion.1, ...), kind=kCustom, calls=%fused_computation.41 | custom fusion | flops 393216 | bytes 792068 | tf_op jit(solution)/shard_map/scatter-add | solution.py:162
  103.1 2.2 %convolution_multiply_fusion.1 = f32[1024,512]{1,0:T(8,128)S(1)} fusion(f32[256,512]{1,0:T(8,128)S(1)} %copy-done.5, f32[256,512]{1,0:T(8,128)} %scatter_custom_fusion.2, f32[256,512]{1,0:T(8,128)S(1)} %copy-done.1), kind=kOutput, calls=%fused_computation.9 | convolution fusion | flops 806092800 | bytes 3670016 | tf_op jit(solution)/shard_map/dot_general | solution.py:68
  105.3 2.7 %convolution_multiply_fusion = f32[1536,512]{1,0:T(8,128)S(1)} fusion(f32[128,512]{1,0:T(8,128)S(1)} %copy-done.11, f32[128,512]{1,0:T(8,128)} %get-tuple-element.54, f32[128,512]{1,0:T(8,128)} %get-tuple-element.55, f32[128,512]{1,0:T(8,128)} %param.23), kind=kOutput, calls=%fused_computation.8 | convolution fusion | flops 605159424 | bytes 4194304 | tf_op jit(solution)/shard_map/dot_general | solution.py:68
  108.0 3.5 %pad_maximum_fusion = f32[16,224,512]{2,1,0:T(8,128)} fusion(f32[16,32,512]{2,1,0:T(8,128)S(1)} %bitcast.75, f32[16,64,512]{2,1,0:T(8,128)S(1)} %bitcast.74, f32[16,32,512]{2,1,0:T(8,128)S(1)} %bitcast.76, f32[16,96,512]{2,1,0:T(8,128)S(1)} %bitcast.67), kind=kLoop, calls=%fused_computation.7 | loop fusion | flops 5505024 | bytes 14680064 | tf_op jit(solution)/shard_map/concatenate | solution.py:186
  111.6 1.9 slice-done.1
  113.4 1.7 fusion.47
  115.2 0.8 fusion.43
  116.0 2.3 %scatter_custom_fusion = f32[320,512]{1,0:T(8,128)S(1)} fusion(s32[256]{0:T(256)S(1)} %bitcast.84, f32[128,512]{1,0:T(8,128)S(1)} %get-tuple-element.32, f32[]{:T(128)} %constant.87, f32[128,512]{1,0:T(8,128)S(1)} %get-tuple-element.31, f32[]{:T(128)} %constant.40.clone.1), kind=kCustom, calls=%fused_computation.27 | custom fusion | flops 262144 | bytes 1179656 | tf_op jit(solution)/shard_map/add | solution.py:198
  118.3 3.1 %collective-permute-start.3 = (f32[1,16,512]{2,1,0:T(8,128)S(1)}, f32[1,16,512]{2,1,0:T(8,128)S(1)}, u32[]{:S(2)}, u32[]{:S(2)}) collective-permute-start(f32[1,16,512]{2,1,0:T(8,128)S(1)} %get-tuple-element.35), channel_id=1, source_target_pairs={{0,1},{1,2},{2,3},{4,5},{5,6},{6,7},{8,9},{9,10},{10,11},{12,13},{... | collective-permute-start | bytes 98312 | tf_op jit(solution)/shard_map/ppermute | solution.py:20
  121.4 1.3 collective-permute-start.2
  122.7 1.9 collective-permute-start.1
  124.6 1.3 collective-permute-start
  125.9 0.1 slice_add_fusion
  126.0 1.1 collective-permute-done.2
  127.2 0.7 collective-permute-done
  127.9 1.2 scatter_fusion
  129.1 72.7 %reduce-scatter.2.cloned.1.call-done = f32[1,224,512]{2,1,0:T(8,128)} async-done(((f32[16,224,512]{2,1,0:T(8,128)}), f32[1,224,512]{2,1,0:T(8,128)}) %reduce-scatter.2.cloned.1.call-update) | async-done | bytes 458768 | tf_op jit(solution)/shard_map/reduce_scatter | solution.py:189
  201.8 1.8 shard_map.227
  (78 shorter events, 1.3 us)
Async XLA Ops:
  7.2 19.5 %copy-start.1 = (f32[256,512]{1,0:T(8,128)S(1)}, f32[256,512]{1,0:T(8,128)}, u32[]{:S(2)}) copy-start(f32[256,512]{1,0:T(8,128)} %param.21) | copy-start | bytes 1572868
  7.2 19.4 %copy-start.15 = (s32[2,128]{1,0:T(2,128)S(1)}, s32[2,128]{1,0:T(2,128)}, u32[]{:S(2)}) copy-start(s32[2,128]{1,0:T(2,128)} %param.27) | copy-start | bytes 3076
  7.2 76.6 %all-gather.4.cloned.1.call-start = ((), (), s32[]{:S(2)}) async-start(), calls=%async_computation.2 | async-start | bytes 8077312 | tf_op jit(solution)/shard_map/all_gather | solution.py:138
  10.6 191.2 %reduce-scatter.2.cloned.1.call-start = ((), (), s32[]{:S(2)}) async-start(), calls=%async_computation.1 | async-start | bytes 7798784 | tf_op jit(solution)/shard_map/reduce_scatter | solution.py:189
  14.0 12.6 %collective-permute-start.7 = (f32[1,16,512]{2,1,0:T(8,128)S(1)}, f32[1,16,512]{2,1,0:T(8,128)S(1)}, u32[]{:S(2)}, u32[]{:S(2)}) collective-permute-start(f32[1,16,512]{2,1,0:T(8,128)S(1)} %get-tuple-element.39), channel_id=1, source_target_pairs={{1,0},{2,1},{3,2},{5,4},{6,5},{7,6},{9,8},{10,9},{11,10},{13,12},{... | collective-permute-start | bytes 98312 | tf_op jit(solution)/shard_map/ppermute | solution.py:22
  15.3 11.3 %collective-permute-start.6 = (f32[1,16,512]{2,1,0:T(8,128)S(1)}, f32[1,16,512]{2,1,0:T(8,128)S(1)}, u32[]{:S(2)}, u32[]{:S(2)}) collective-permute-start(f32[1,16,512]{2,1,0:T(8,128)S(1)} %get-tuple-element.40), channel_id=1, source_target_pairs={{0,1},{1,2},{2,3},{4,5},{5,6},{6,7},{8,9},{9,10},{10,11},{12,13},{... | collective-permute-start | bytes 98312 | tf_op jit(solution)/shard_map/ppermute | solution.py:20
  20.9 5.8 %collective-permute-start.5 = (f32[1,16,512]{2,1,0:T(8,128)S(1)}, f32[1,16,512]{2,1,0:T(8,128)S(1)}, u32[]{:S(2)}, u32[]{:S(2)}) collective-permute-start(f32[1,16,512]{2,1,0:T(8,128)S(1)} %get-tuple-element.41), channel_id=1, source_target_pairs={{4,0},{8,4},{12,8},{5,1},{9,5},{13,9},{6,2},{10,6},{14,10},{7,3},{... | collective-permute-start | bytes 98312 | tf_op jit(solution)/shard_map/ppermute | solution.py:22
  22.2 4.5 %collective-permute-start.4 = (f32[1,16,512]{2,1,0:T(8,128)S(1)}, f32[1,16,512]{2,1,0:T(8,128)S(1)}, u32[]{:S(2)}, u32[]{:S(2)}) collective-permute-start(f32[1,16,512]{2,1,0:T(8,128)S(1)} %get-tuple-element.38), channel_id=1, source_target_pairs={{0,4},{4,8},{8,12},{1,5},{5,9},{9,13},{2,6},{6,10},{10,14},{3,7},{... | collective-permute-start | bytes 98312 | tf_op jit(solution)/shard_map/ppermute | solution.py:20
  28.3 59.8 %copy-start.6 = (f32[256,512]{1,0:T(8,128)S(1)}, f32[256,512]{1,0:T(8,128)}, u32[]{:S(2)}) copy-start(f32[256,512]{1,0:T(8,128)} %param.22) | copy-start | bytes 1572868
  85.2 3.9 %copy-start.2 = (f32[256,512]{1,0:T(8,128)S(1)}, f32[256,512]{1,0:T(8,128)}, u32[]{:S(2)}) copy-start(f32[256,512]{1,0:T(8,128)} %param.25) | copy-start | bytes 1572868
  90.2 4.2 %copy-start.4 = (f32[256,512]{1,0:T(8,128)}, f32[256,512]{1,0:T(8,128)S(1)}, u32[]{:S(2)}) copy-start(f32[256,512]{1,0:T(8,128)S(1)} %convolution_select_fusion) | copy-start | bytes 1572868
  92.0 2.3 %slice-start = ((f32[16,225,512]{2,1,0:T(8,128)}), f32[16,64,512]{2,1,0:T(8,128)S(1)}, s32[]{:S(2)}) async-start(f32[16,225,512]{2,1,0:T(8,128)} %all-gather.4.cloned.1.call-done), calls=%async_computation.3 | async-start | bytes 4194304 | tf_op jit(solution)/shard_map/slice | solution.py:142
  95.4 1.0 copy-start.9
  96.4 0.9 copy-start.13
  96.4 1.3 copy-start
  96.4 1.3 copy-start.12
  97.2 5.9 %copy-start.5 = (f32[256,512]{1,0:T(8,128)S(1)}, f32[256,512]{1,0:T(8,128)}, u32[]{:S(2)}) copy-start(f32[256,512]{1,0:T(8,128)} %copy-done.4) | copy-start | bytes 1572868
  103.1 2.2 %copy-start.11 = (f32[128,512]{1,0:T(8,128)S(1)}, f32[128,512]{1,0:T(8,128)}, u32[]{:S(2)}) copy-start(f32[128,512]{1,0:T(8,128)} %convolution_select_fusion.1) | copy-start | bytes 786436
  103.1 4.9 %copy-start.8 = (f32[512,512]{1,0:T(8,128)S(1)}, f32[512,512]{1,0:T(8,128)}, u32[]{:S(2)}) copy-start(f32[512,512]{1,0:T(8,128)} %convolution_multiply_fusion.2) | copy-start | bytes 3145732
  111.5 1.9 slice-start.1
  111.6 3.6 %copy-start.14 = (f32[128,512]{1,0:T(8,128)S(1)}, f32[128,512]{1,0:T(8,128)}, u32[]{:S(2)}) copy-start(f32[128,512]{1,0:T(8,128)} %param.26) | copy-start | bytes 786436
  113.4 12.4 %copy-start.3 = (f32[256,512]{1,0:T(8,128)S(1)}, f32[256,512]{1,0:T(8,128)}, u32[]{:S(2)}) copy-start(f32[256,512]{1,0:T(8,128)} %param.25) | copy-start | bytes 1572868
  113.4 12.4 %copy-start.10 = (f32[256,1024]{1,0:T(8,128)S(1)}, f32[256,1024]{1,0:T(8,128)}, u32[]{:S(2)}) copy-start(f32[256,1024]{1,0:T(8,128)} %copy-done.9) | copy-start | bytes 3145732
  118.3 7.7 %collective-permute-start.3 = (f32[1,16,512]{2,1,0:T(8,128)S(1)}, f32[1,16,512]{2,1,0:T(8,128)S(1)}, u32[]{:S(2)}, u32[]{:S(2)}) collective-permute-start(f32[1,16,512]{2,1,0:T(8,128)S(1)} %get-tuple-element.35), channel_id=1, source_target_pairs={{0,1},{1,2},{2,3},{4,5},{5,6},{6,7},{8,9},{9,10},{10,11},{12,13},{... | collective-permute-start | bytes 98312 | tf_op jit(solution)/shard_map/ppermute | solution.py:20
  121.4 5.8 %collective-permute-start.2 = (f32[1,16,512]{2,1,0:T(8,128)S(1)}, f32[1,16,512]{2,1,0:T(8,128)S(1)}, u32[]{:S(2)}, u32[]{:S(2)}) collective-permute-start(f32[1,16,512]{2,1,0:T(8,128)S(1)} %get-tuple-element.36), channel_id=1, source_target_pairs={{1,0},{2,1},{3,2},{5,4},{6,5},{7,6},{9,8},{10,9},{11,10},{13,12},{... | collective-permute-start | bytes 98312 | tf_op jit(solution)/shard_map/ppermute | solution.py:22
  122.7 4.5 %collective-permute-start.1 = (f32[1,16,512]{2,1,0:T(8,128)S(1)}, f32[1,16,512]{2,1,0:T(8,128)S(1)}, u32[]{:S(2)}, u32[]{:S(2)}) collective-permute-start(f32[1,16,512]{2,1,0:T(8,128)S(1)} %get-tuple-element.37), channel_id=1, source_target_pairs={{0,4},{4,8},{8,12},{1,5},{5,9},{9,13},{2,6},{6,10},{10,14},{3,7},{... | collective-permute-start | bytes 98312 | tf_op jit(solution)/shard_map/ppermute | solution.py:20
  124.6 3.3 %collective-permute-start = (f32[1,16,512]{2,1,0:T(8,128)S(1)}, f32[1,16,512]{2,1,0:T(8,128)S(1)}, u32[]{:S(2)}, u32[]{:S(2)}) collective-permute-start(f32[1,16,512]{2,1,0:T(8,128)S(1)} %get-tuple-element.34), channel_id=1, source_target_pairs={{4,0},{8,4},{12,8},{5,1},{9,5},{13,9},{6,2},{10,6},{14,10},{7,3},{... | collective-permute-start | bytes 98312 | tf_op jit(solution)/shard_map/ppermute | solution.py:22
  129.1 74.5 %copy-start.7 = (f32[256,512]{1,0:T(8,128)}, f32[256,512]{1,0:T(8,128)S(1)}, u32[]{:S(2)}) copy-start(f32[256,512]{1,0:T(8,128)S(1)} %scatter_fusion) | copy-start | bytes 1572868
Sparse Core Ops, SparseCore 0:
  10.9 72.8 all-gather.3
  111.7 90.0 reduce-scatter.1

commit v5 on v4

--- a/solution.py
+++ b/solution.py
@@ -33,18 +33,27 @@
     return offsets
 
 
-def pack_rows(pieces):
+def pack_rows(pieces, vectors):
     offsets = row_offsets([piece.shape[0] for piece in pieces])
+    width = pieces[0].shape[1]
+    length = vectors[0].shape[1]
+    count = len(pieces)
 
     def kernel(*refs):
         out = refs[-1]
-        for index, ref in enumerate(refs[:-1]):
-            out[offsets[index] : offsets[index + 1], :] = ref[...]
+        for index, ref in enumerate(refs[:count]):
+            out[0, offsets[index] : offsets[index + 1], :] = ref[...]
+        row = jnp.concatenate(
+            [ref[...] for ref in refs[count:-1]]
+            + [jnp.zeros((1, width - len(vectors) * length), jnp.float32)],
+            axis=1,
+        )
+        out[0, offsets[-1] : offsets[-1] + 1, :] = row
 
     return pl.pallas_call(
         kernel,
-        out_shape=jax.ShapeDtypeStruct((offsets[-1], pieces[0].shape[1]), pieces[0].dtype),
-    )(*pieces)
+        out_shape=jax.ShapeDtypeStruct((1, offsets[-1] + 1, width), pieces[0].dtype),
+    )(*pieces, *vectors)
 
 
 def split_rows(packed, sizes):
@@ -131,11 +140,10 @@
     ghosts = ghosts.reshape(4 * ghost, width)
     peers = ("dom", "sub")
     matrices = (edge_first, edge_second, node_first, node_second)
-    vectors = jnp.concatenate([edge_bias, edge_gain, edge_shift, node_bias, node_gain])
-    vector_rows = -(-vectors.shape[0] // width)
-    vectors = jnp.pad(vectors, (0, vector_rows * width - vectors.shape[0])).reshape(vector_rows, width)
-    packed = pack_rows(list(matrices) + [vectors])
-    gathered = lax.all_gather(packed, peers, axis=0, tiled=False)
+    vectors = [v.reshape(1, -1) for v in (edge_bias, edge_gain, edge_shift, node_bias, node_gain)]
+    vector_rows = 1
+    packed = pack_rows(list(matrices), vectors)
+    gathered = lax.all_gather(packed, peers, axis=0, tiled=True)
     pieces = []
     offset = 0
     for rows in [m.shape[0] for m in matrices] + [vector_rows]:

time: 211 us -> 211 us (level)
  no operation moved by 1% of the time
where the time goes in v5:
time: 211 us; the launch traced here: 210 us
  waiting for transfers between devices  130 us (62%)
  starting transfers between devices  18.8 us (9%)
  matrix products  16 us (8%)
  between operations  15.9 us (8%)
  local copies, waits for them, and re-layouts  13.2 us (6%)
  other arithmetic  12.3 us (6%)
  Pallas kernels  3.78 us (2%)
    reduce_scatter x1, waiting for transfers between devices, shards(): lax.psum_scatter(blocked, peers, scatter_dimension=0, tiled=True)[0]  72.7 us
    all_gather x1, waiting for transfers between devices, shards(): gathered = lax.all_gather(packed, peers, axis=0, tiled=True)  55.7 us
    ppermute x4, starting transfers between devices, padded(): lax.ppermute(tail, axis, [(i, (i + 1) % count) for i in range(ends)])  13.5 us
    dot_general x4, matrix products, inner(): lax.dot_general(left, right, (((0,), (0,)), ((), ())), precision=lax.Prec...  8.36 us
    slice x6, local copies, waits for them, and re-layouts, shards(): pieces.append(gathered[:, offset:offset + rows, :])  5.73 us
    ppermute x4, starting transfers between devices, padded(): lax.ppermute(head, axis, [((i + 1) % count, i) for i in range(ends)])  5.17 us
    dot_general x4, matrix products, outer_back(): lax.dot_general(left, right, (((1,), (1,)), ((), ())), precision=lax.Prec...  4.95 us
  transfers between devices with their start and end apart: 10, of which 4 were waited for; matrix products, arithmetic and copies ran while one was open for 6% of the time, Pallas kernels for 0%

profile of v5, /device:TPU:0, one launch (start us, length us, event | category | flops | bytes accessed | tf_op | source)
XLA Modules:
  0.0 210.2 jit_solution(690605900688418968)
XLA Ops:
  7.2 2.0 shard_map.226
  9.3 0.8 reshape.270
  10.1 0.8 broadcast_in_dim_reshape_squeeze.3
  10.9 1.8 gather_fusion.1
  12.7 1.3 collective-permute-start.7
  14.0 5.6 %collective-permute-start.6 = (f32[1,16,512]{2,1,0:T(8,128)S(1)}, f32[1,16,512]{2,1,0:T(8,128)S(1)}, u32[]{:S(2)}, u32[]{:S(2)}) collective-permute-start(f32[1,16,512]{2,1,0:T(8,128)S(1)} %get-tuple-element.40), channel_id=1, source_target_pairs={{0,1},{1,2},{2,3},{4,5},{5,6},{6,7},{8,9},{9,10},{10,11},{12,13},{... | collective-permute-start | bytes 98312 | tf_op jit(solution)/shard_map/ppermute | solution.py:20
  19.6 1.3 collective-permute-start.5
  20.9 3.0 %collective-permute-start.4 = (f32[1,16,512]{2,1,0:T(8,128)S(1)}, f32[1,16,512]{2,1,0:T(8,128)S(1)}, u32[]{:S(2)}, u32[]{:S(2)}) collective-permute-start(f32[1,16,512]{2,1,0:T(8,128)S(1)} %get-tuple-element.38), channel_id=1, source_target_pairs={{0,4},{4,8},{8,12},{1,5},{5,9},{9,13},{2,6},{6,10},{10,14},{3,7},{... | collective-permute-start | bytes 98312 | tf_op jit(solution)/shard_map/ppermute | solution.py:20
  25.5 0.8 gather_fusion.3
  26.2 0.8 gather_fusion.2
  27.0 0.9 broadcast_select_fusion
  27.9 55.7 %all-gather.2.cloned.1.call-done = f32[16,225,512]{2,1,0:T(8,128)} async-done(((f32[1,225,512]{2,1,0:T(8,128)}), f32[16,225,512]{2,1,0:T(8,128)}) %all-gather.2.cloned.1.call-update) | async-done | bytes 7372816 | tf_op jit(solution)/shard_map/all_gather | solution.py:146
  83.6 1.0 slice.159
  84.6 0.1 slice_reduce_fusion
  84.9 2.9 %fusion.42 = (f32[16,32,512]{2,1,0:T(8,128)S(1)}, f32[16,32,512]{2,1,0:T(8,128)}) fusion(f32[16,225,512]{2,1,0:T(8,128)} %all-gather.2.cloned.1.call-done), kind=kLoop, calls=%fused_computation.118 | loop fusion | bytes 4194304 | tf_op jit(solution)/shard_map/slice | solution.py:150
  87.8 0.7 fusion.45
  88.6 0.2 multiply_reduce_fusion.1
  88.8 0.3 fusion.14
  89.1 0.8 convolution_select_fusion
  89.9 1.9 convolution_multiply_fusion.2
  91.9 1.9 fusion.44
  93.8 0.2 multiply_reduce_fusion.3
  94.1 1.1 fusion.46
  95.2 1.0 copy-done.9
  96.2 0.8 gather_fusion
  97.0 0.1 copy-done.13
  97.1 0.2 fusion.41
  97.3 0.1 copy-done
  97.5 1.4 convolution_select_fusion.1
  98.8 1.7 convolution_multiply_fusion.3
  100.6 2.3 %scatter_custom_fusion.2 = f32[256,512]{1,0:T(8,128)} fusion(s32[128]{0:T(128)S(1)} %get-tuple-element.45, f32[]{:T(128)} %constant.39.clone.1, f32[128,512]{1,0:T(8,128)S(1)} %get-tuple-element.49, f32[512]{0:T(512)S(1)} %add.152, f32[512]{0:T(512)S(1)} %mul.165, f32[128]{0:T(128)S(1)} %compare_convert_fusion, f32[128]{0:T(128)S(1)} %add_rsqrt_fusion.1, ...), kind=kCustom, calls=%fused_computation.41 | custom fusion | flops 393216 | bytes 792068 | tf_op jit(solution)/shard_map/scatter-add | solution.py:170
  102.9 2.2 %convolution_multiply_fusion.1 = f32[1024,512]{1,0:T(8,128)S(1)} fusion(f32[256,512]{1,0:T(8,128)S(1)} %copy-done.5, f32[256,512]{1,0:T(8,128)} %scatter_custom_fusion.2, f32[256,512]{1,0:T(8,128)S(1)} %copy-done.1), kind=kOutput, calls=%fused_computation.9 | convolution fusion | flops 806092800 | bytes 3670016 | tf_op jit(solution)/shard_map/dot_general | solution.py:77
  105.1 2.7 %convolution_multiply_fusion = f32[1536,512]{1,0:T(8,128)S(1)} fusion(f32[128,512]{1,0:T(8,128)S(1)} %copy-done.11, f32[128,512]{1,0:T(8,128)} %get-tuple-element.54, f32[128,512]{1,0:T(8,128)} %get-tuple-element.55, f32[128,512]{1,0:T(8,128)} %param.23), kind=kOutput, calls=%fused_computation.8 | convolution fusion | flops 605159424 | bytes 4194304 | tf_op jit(solution)/shard_map/dot_general | solution.py:77
  107.7 3.5 %pad_maximum_fusion = f32[16,224,512]{2,1,0:T(8,128)} fusion(f32[16,32,512]{2,1,0:T(8,128)S(1)} %bitcast.78, f32[16,64,512]{2,1,0:T(8,128)S(1)} %bitcast.77, f32[16,32,512]{2,1,0:T(8,128)S(1)} %bitcast.79, f32[16,96,512]{2,1,0:T(8,128)S(1)} %bitcast.70), kind=kLoop, calls=%fused_computation.7 | loop fusion | flops 5505024 | bytes 14680064 | tf_op jit(solution)/shard_map/concatenate | solution.py:194
  111.3 1.9 slice-done.1
  113.2 1.7 fusion.47
  114.9 0.8 fusion.43
  115.7 2.3 %scatter_custom_fusion = f32[320,512]{1,0:T(8,128)S(1)} fusion(s32[256]{0:T(256)S(1)} %bitcast.85, f32[128,512]{1,0:T(8,128)S(1)} %get-tuple-element.32, f32[]{:T(128)} %constant.83, f32[128,512]{1,0:T(8,128)S(1)} %get-tuple-element.31, f32[]{:T(128)} %constant.39.clone.1), kind=kCustom, calls=%fused_computation.27 | custom fusion | flops 262144 | bytes 1179656 | tf_op jit(solution)/shard_map/add | solution.py:206
  118.0 3.0 %collective-permute-start.3 = (f32[1,16,512]{2,1,0:T(8,128)S(1)}, f32[1,16,512]{2,1,0:T(8,128)S(1)}, u32[]{:S(2)}, u32[]{:S(2)}) collective-permute-start(f32[1,16,512]{2,1,0:T(8,128)S(1)} %get-tuple-element.35), channel_id=1, source_target_pairs={{0,1},{1,2},{2,3},{4,5},{5,6},{6,7},{8,9},{9,10},{10,11},{12,13},{... | collective-permute-start | bytes 98312 | tf_op jit(solution)/shard_map/ppermute | solution.py:20
  121.1 1.3 collective-permute-start.2
  122.4 1.9 collective-permute-start.1
  124.3 1.3 collective-permute-start
  125.6 0.1 slice_add_fusion
  125.8 1.1 collective-permute-done.2
  126.9 0.7 collective-permute-done
  127.6 1.2 scatter_fusion
  128.8 72.7 %reduce-scatter.2.cloned.1.call-done = f32[1,224,512]{2,1,0:T(8,128)} async-done(((f32[16,224,512]{2,1,0:T(8,128)}), f32[1,224,512]{2,1,0:T(8,128)}) %reduce-scatter.2.cloned.1.call-update) | async-done | bytes 458768 | tf_op jit(solution)/shard_map/reduce_scatter | solution.py:197
  201.6 1.8 shard_map.227
  (76 shorter events, 1.0 us)
Async XLA Ops:
  7.2 18.2 %copy-start.1 = (f32[256,512]{1,0:T(8,128)S(1)}, f32[256,512]{1,0:T(8,128)}, u32[]{:S(2)}) copy-start(f32[256,512]{1,0:T(8,128)} %param.21) | copy-start | bytes 1572868
  7.2 18.1 %copy-start.15 = (s32[2,128]{1,0:T(2,128)S(1)}, s32[2,128]{1,0:T(2,128)}, u32[]{:S(2)}) copy-start(s32[2,128]{1,0:T(2,128)} %param.27) | copy-start | bytes 3076
  7.2 76.4 %all-gather.2.cloned.1.call-start = ((), (), s32[]{:S(2)}) async-start(), calls=%async_computation.1 | async-start | bytes 8077312 | tf_op jit(solution)/shard_map/all_gather | solution.py:146
  9.3 192.3 %reduce-scatter.2.cloned.1.call-start = ((), (), s32[]{:S(2)}) async-start(), calls=%async_computation.2 | async-start | bytes 7798784 | tf_op jit(solution)/shard_map/reduce_scatter | solution.py:197
  12.7 12.6 %collective-permute-start.7 = (f32[1,16,512]{2,1,0:T(8,128)S(1)}, f32[1,16,512]{2,1,0:T(8,128)S(1)}, u32[]{:S(2)}, u32[]{:S(2)}) collective-permute-start(f32[1,16,512]{2,1,0:T(8,128)S(1)} %get-tuple-element.39), channel_id=1, source_target_pairs={{1,0},{2,1},{3,2},{5,4},{6,5},{7,6},{9,8},{10,9},{11,10},{13,12},{... | collective-permute-start | bytes 98312 | tf_op jit(solution)/shard_map/ppermute | solution.py:22
  14.0 11.3 %collective-permute-start.6 = (f32[1,16,512]{2,1,0:T(8,128)S(1)}, f32[1,16,512]{2,1,0:T(8,128)S(1)}, u32[]{:S(2)}, u32[]{:S(2)}) collective-permute-start(f32[1,16,512]{2,1,0:T(8,128)S(1)} %get-tuple-element.40), channel_id=1, source_target_pairs={{0,1},{1,2},{2,3},{4,5},{5,6},{6,7},{8,9},{9,10},{10,11},{12,13},{... | collective-permute-start | bytes 98312 | tf_op jit(solution)/shard_map/ppermute | solution.py:20
  19.6 5.8 %collective-permute-start.5 = (f32[1,16,512]{2,1,0:T(8,128)S(1)}, f32[1,16,512]{2,1,0:T(8,128)S(1)}, u32[]{:S(2)}, u32[]{:S(2)}) collective-permute-start(f32[1,16,512]{2,1,0:T(8,128)S(1)} %get-tuple-element.41), channel_id=1, source_target_pairs={{4,0},{8,4},{12,8},{5,1},{9,5},{13,9},{6,2},{10,6},{14,10},{7,3},{... | collective-permute-start | bytes 98312 | tf_op jit(solution)/shard_map/ppermute | solution.py:22
  20.9 4.5 %collective-permute-start.4 = (f32[1,16,512]{2,1,0:T(8,128)S(1)}, f32[1,16,512]{2,1,0:T(8,128)S(1)}, u32[]{:S(2)}, u32[]{:S(2)}) collective-permute-start(f32[1,16,512]{2,1,0:T(8,128)S(1)} %get-tuple-element.38), channel_id=1, source_target_pairs={{0,4},{4,8},{8,12},{1,5},{5,9},{9,13},{2,6},{6,10},{10,14},{3,7},{... | collective-permute-start | bytes 98312 | tf_op jit(solution)/shard_map/ppermute | solution.py:20
  27.0 60.8 %copy-start.6 = (f32[256,512]{1,0:T(8,128)S(1)}, f32[256,512]{1,0:T(8,128)}, u32[]{:S(2)}) copy-start(f32[256,512]{1,0:T(8,128)} %param.22) | copy-start | bytes 1572868
  84.9 3.9 %copy-start.2 = (f32[256,512]{1,0:T(8,128)S(1)}, f32[256,512]{1,0:T(8,128)}, u32[]{:S(2)}) copy-start(f32[256,512]{1,0:T(8,128)} %param.25) | copy-start | bytes 1572868
  89.9 4.2 %copy-start.4 = (f32[256,512]{1,0:T(8,128)}, f32[256,512]{1,0:T(8,128)S(1)}, u32[]{:S(2)}) copy-start(f32[256,512]{1,0:T(8,128)S(1)} %convolution_select_fusion) | copy-start | bytes 1572868
  91.8 2.3 %slice-start = ((f32[16,225,512]{2,1,0:T(8,128)}), f32[16,64,512]{2,1,0:T(8,128)S(1)}, s32[]{:S(2)}) async-start(f32[16,225,512]{2,1,0:T(8,128)} %all-gather.2.cloned.1.call-done), calls=%async_computation.3 | async-start | bytes 4194304 | tf_op jit(solution)/shard_map/slice | solution.py:150
  95.2 1.0 copy-start.9
  96.1 0.9 copy-start.13
  96.1 1.3 copy-start
  96.1 1.3 copy-start.12
  97.0 5.9 %copy-start.5 = (f32[256,512]{1,0:T(8,128)S(1)}, f32[256,512]{1,0:T(8,128)}, u32[]{:S(2)}) copy-start(f32[256,512]{1,0:T(8,128)} %copy-done.4) | copy-start | bytes 1572868
  102.9 2.2 %copy-start.11 = (f32[128,512]{1,0:T(8,128)S(1)}, f32[128,512]{1,0:T(8,128)}, u32[]{:S(2)}) copy-start(f32[128,512]{1,0:T(8,128)} %convolution_select_fusion.1) | copy-start | bytes 786436
  102.9 4.9 %copy-start.8 = (f32[512,512]{1,0:T(8,128)S(1)}, f32[512,512]{1,0:T(8,128)}, u32[]{:S(2)}) copy-start(f32[512,512]{1,0:T(8,128)} %convolution_multiply_fusion.2) | copy-start | bytes 3145732
  111.3 1.9 slice-start.1
  111.3 3.6 %copy-start.14 = (f32[128,512]{1,0:T(8,128)S(1)}, f32[128,512]{1,0:T(8,128)}, u32[]{:S(2)}) copy-start(f32[128,512]{1,0:T(8,128)} %param.26) | copy-start | bytes 786436
  113.2 12.4 %copy-start.3 = (f32[256,512]{1,0:T(8,128)S(1)}, f32[256,512]{1,0:T(8,128)}, u32[]{:S(2)}) copy-start(f32[256,512]{1,0:T(8,128)} %param.25) | copy-start | bytes 1572868
  113.2 12.4 %copy-start.10 = (f32[256,1024]{1,0:T(8,128)S(1)}, f32[256,1024]{1,0:T(8,128)}, u32[]{:S(2)}) copy-start(f32[256,1024]{1,0:T(8,128)} %copy-done.9) | copy-start | bytes 3145732
  118.0 7.7 %collective-permute-start.3 = (f32[1,16,512]{2,1,0:T(8,128)S(1)}, f32[1,16,512]{2,1,0:T(8,128)S(1)}, u32[]{:S(2)}, u32[]{:S(2)}) collective-permute-start(f32[1,16,512]{2,1,0:T(8,128)S(1)} %get-tuple-element.35), channel_id=1, source_target_pairs={{0,1},{1,2},{2,3},{4,5},{5,6},{6,7},{8,9},{9,10},{10,11},{12,13},{... | collective-permute-start | bytes 98312 | tf_op jit(solution)/shard_map/ppermute | solution.py:20
  121.1 5.8 %collective-permute-start.2 = (f32[1,16,512]{2,1,0:T(8,128)S(1)}, f32[1,16,512]{2,1,0:T(8,128)S(1)}, u32[]{:S(2)}, u32[]{:S(2)}) collective-permute-start(f32[1,16,512]{2,1,0:T(8,128)S(1)} %get-tuple-element.36), channel_id=1, source_target_pairs={{1,0},{2,1},{3,2},{5,4},{6,5},{7,6},{9,8},{10,9},{11,10},{13,12},{... | collective-permute-start | bytes 98312 | tf_op jit(solution)/shard_map/ppermute | solution.py:22
  122.4 4.5 %collective-permute-start.1 = (f32[1,16,512]{2,1,0:T(8,128)S(1)}, f32[1,16,512]{2,1,0:T(8,128)S(1)}, u32[]{:S(2)}, u32[]{:S(2)}) collective-permute-start(f32[1,16,512]{2,1,0:T(8,128)S(1)} %get-tuple-element.37), channel_id=1, source_target_pairs={{0,4},{4,8},{8,12},{1,5},{5,9},{9,13},{2,6},{6,10},{10,14},{3,7},{... | collective-permute-start | bytes 98312 | tf_op jit(solution)/shard_map/ppermute | solution.py:20
  124.3 3.3 %collective-permute-start = (f32[1,16,512]{2,1,0:T(8,128)S(1)}, f32[1,16,512]{2,1,0:T(8,128)S(1)}, u32[]{:S(2)}, u32[]{:S(2)}) collective-permute-start(f32[1,16,512]{2,1,0:T(8,128)S(1)} %get-tuple-element.34), channel_id=1, source_target_pairs={{4,0},{8,4},{12,8},{5,1},{9,5},{13,9},{6,2},{10,6},{14,10},{7,3},{... | collective-permute-start | bytes 98312 | tf_op jit(solution)/shard_map/ppermute | solution.py:22
  128.8 74.5 %copy-start.7 = (f32[256,512]{1,0:T(8,128)}, f32[256,512]{1,0:T(8,128)S(1)}, u32[]{:S(2)}) copy-start(f32[256,512]{1,0:T(8,128)S(1)} %scatter_fusion) | copy-start | bytes 1572868
Sparse Core Ops, SparseCore 0:
  10.9 72.6 all-gather.1
  111.4 90.1 reduce-scatter.1

commit v6 on v5

--- a/solution.py
+++ b/solution.py
@@ -167,20 +167,21 @@
     edge_act = jnp.maximum(edge_pre, 0.0)
     edge_normed, edge_inverse = layer_norm(matmul(edge_act, full_edge_second) + full_edge_bias)
     message = (edge_normed * full_edge_gain + full_edge_shift) * live_edges
-    aggregate = jax.ops.segment_sum(message, target, node_rows)
     node_act = jnp.maximum(node_pre, 0.0)
     node_normed, node_inverse = layer_norm(matmul(node_act, full_node_second) + full_node_bias)
     node_upstream = node_cotangent * live_nodes
     node_grad_z = norm_back(node_upstream * full_node_gain, node_normed, node_inverse)
     node_grad_pre = outer_back(node_grad_z, full_node_second) * (node_pre > 0).astype(jnp.float32)
-    node_input = jnp.concatenate([node_states, aggregate], axis=1)
-    node_first_part = inner(node_input, node_grad_pre) * node_scale
+    node_first_part = jnp.concatenate(
+        [
+            inner(node_states, node_grad_pre),
+            inner(message, jnp.take(node_grad_pre, target, axis=0)),
+        ],
+        axis=0,
+    ) * node_scale
     node_second_part = inner(node_act, node_grad_z) * node_scale
-    node_grad_input = outer_back(node_grad_pre, full_node_first)
-    state_grads = node_upstream + node_grad_input[:, :width]
-    edge_upstream = (
-        edge_cotangent + jnp.take(node_grad_input[:, width:], target, axis=0)
-    ) * live_edges
+    aggregate_grads = outer_back(node_grad_pre, full_node_first[width:])
+    edge_upstream = (edge_cotangent + jnp.take(aggregate_grads, target, axis=0)) * live_edges
     edge_grad_z = norm_back(edge_upstream * full_edge_gain, edge_normed, edge_inverse)
     edge_grad_pre = outer_back(edge_grad_z, full_edge_second) * (edge_pre > 0).astype(jnp.float32)
     edge_second_part = inner(edge_act, edge_grad_z) * edge_scale
@@ -206,6 +207,7 @@
     extended_grads = extended_grads + jax.ops.segment_sum(
         edge_grad_input[:, 2 * width :], target, node_rows + 4 * ghost
     )
+    state_grads = node_upstream + outer_back(node_grad_pre, full_node_first[:width])
     state_grads = state_grads + extended_grads[:node_rows]
     ghost_grads = extended_grads[node_rows:].reshape(4, ghost, width)
     dom_back = padded(jnp.stack([ghost_grads[0], ghost_grads[1]]), (("dom", 0),), 1)

time: 211 us -> 212 us (level)
    slice x1, local copies, waits for them, and re-layouts: 0.04 us -> 2.74 us  [shards(): full_node_first[:width]]
    scatter-add x1 -> x0, other arithmetic: 2.27 us -> none  [shards(): aggregate = jax.ops.segment_sum(message, target, node_rows)]
    slice x6 -> x4, local copies, waits for them, and re-layouts: 5.73 us -> 4.62 us  [shards(): pieces.append(gathered[:, offset:offset + rows, :])]
    dot_general x4 -> x5, matrix products: 8.36 us -> 7.5 us  [inner(): lax.dot_general(left, right, (((0,), (0,)), ((), ())), precision=lax.Prec...]
    dot_general x4 -> x5, matrix products: 4.95 us -> 5.41 us  [outer_back(): lax.dot_general(left, right, (((1,), (1,)), ((), ())), precision=lax.Prec...]
where the time goes in v6:
time: 212 us; the launch traced here: 211 us
  waiting for transfers between devices  130 us (61%)
  starting transfers between devices  18.8 us (9%)
  between operations  15.9 us (8%)
  local copies, waits for them, and re-layouts  15.1 us (7%)
  matrix products  15.1 us (7%)
  other arithmetic  12.5 us (6%)
  Pallas kernels  3.78 us (2%)
    reduce_scatter x1, waiting for transfers between devices, shards(): lax.psum_scatter(blocked, peers, scatter_dimension=0, tiled=True)[0]  72.7 us
    all_gather x1, waiting for transfers between devices, shards(): gathered = lax.all_gather(packed, peers, axis=0, tiled=True)  55.7 us
    ppermute x4, starting transfers between devices, padded(): lax.ppermute(tail, axis, [(i, (i + 1) % count) for i in range(ends)])  13.5 us
    dot_general x5, matrix products, inner(): lax.dot_general(left, right, (((0,), (0,)), ((), ())), precision=lax.Prec...  7.5 us
    dot_general x5, matrix products, outer_back(): lax.dot_general(left, right, (((1,), (1,)), ((), ())), precision=lax.Prec...  5.41 us
    ppermute x4, starting transfers between devices, padded(): lax.ppermute(head, axis, [((i + 1) % count, i) for i in range(ends)])  5.17 us
    slice x4, local copies, waits for them, and re-layouts, shards(): pieces.append(gathered[:, offset:offset + rows, :])  4.62 us
  transfers between devices with their start and end apart: 10, of which 4 were waited for; matrix products, arithmetic and copies ran while one was open for 6% of the time, Pallas kernels for 0%

profile of v6, /device:TPU:0, one launch (start us, length us, event | category | flops | bytes accessed | tf_op | source)
XLA Modules:
  0.0 211.0 jit_solution(6389696873913593224)
XLA Ops:
  7.2 2.0 shard_map.226
  9.3 0.8 reshape.248
  10.1 0.8 broadcast_in_dim_reshape_squeeze.3
  10.9 1.8 gather_fusion
  12.7 1.3 collective-permute-start.7
  14.0 5.6 %collective-permute-start.6 = (f32[1,16,512]{2,1,0:T(8,128)S(1)}, f32[1,16,512]{2,1,0:T(8,128)S(1)}, u32[]{:S(2)}, u32[]{:S(2)}) collective-permute-start(f32[1,16,512]{2,1,0:T(8,128)S(1)} %get-tuple-element.45), channel_id=1, source_target_pairs={{0,1},{1,2},{2,3},{4,5},{5,6},{6,7},{8,9},{9,10},{10,11},{12,13},{... | collective-permute-start | bytes 98312 | tf_op jit(solution)/shard_map/ppermute | solution.py:20
  19.6 1.3 collective-permute-start.5
  20.9 3.0 %collective-permute-start.4 = (f32[1,16,512]{2,1,0:T(8,128)S(1)}, f32[1,16,512]{2,1,0:T(8,128)S(1)}, u32[]{:S(2)}, u32[]{:S(2)}) collective-permute-start(f32[1,16,512]{2,1,0:T(8,128)S(1)} %get-tuple-element.43), channel_id=1, source_target_pairs={{0,4},{4,8},{8,12},{1,5},{5,9},{9,13},{2,6},{6,10},{10,14},{3,7},{... | collective-permute-start | bytes 98312 | tf_op jit(solution)/shard_map/ppermute | solution.py:20
  25.4 0.8 gather_fusion.3
  26.2 0.8 gather_fusion.2
  27.0 0.9 broadcast_select_fusion
  27.9 55.7 %all-gather.2.cloned.1.call-done = f32[16,225,512]{2,1,0:T(8,128)} async-done(((f32[1,225,512]{2,1,0:T(8,128)}), f32[16,225,512]{2,1,0:T(8,128)}) %all-gather.2.cloned.1.call-update) | async-done | bytes 7372816 | tf_op jit(solution)/shard_map/all_gather | solution.py:146
  83.6 1.0 slice.168
  84.6 0.1 slice_reduce_fusion
  84.9 1.8 fusion.45
  86.7 0.7 fusion.48
  87.5 0.2 multiply_reduce_fusion.1
  87.7 0.3 fusion.12
  88.0 0.8 convolution_select_fusion
  88.8 1.8 convolution_multiply_fusion.1
  90.7 1.4 fusion.47
  92.2 0.2 multiply_reduce_fusion.3
  92.5 1.7 convolution_bitcast_fusion
  94.2 2.7 %fusion.44 = (f32[8,64,512]{2,1,0:T(8,128)}, f32[8,64,512]{2,1,0:T(8,128)S(1)}) fusion(f32[16,225,512]{2,1,0:T(8,128)} %all-gather.2.cloned.1.call-done), kind=kLoop, calls=%fused_computation.117 | loop fusion | bytes 4194304 | tf_op jit(solution)/shard_map/slice | solution.py:210
  96.9 0.7 fusion.49
  97.6 1.5 gather_fusion.4
  99.0 0.8 gather_fusion.1
  99.8 1.2 fusion.42
  101.0 1.6 convolution_select_fusion.1
  102.7 0.7 convolution_multiply_fusion.2
  103.5 1.7 fusion.15
  105.2 1.5 maximum_multiply_fusion
  106.8 1.5 convolution_multiply_fusion
  108.3 3.7 %pad_maximum_fusion = f32[16,224,512]{2,1,0:T(8,128)} fusion(f32[16,32,512]{2,1,0:T(8,128)S(1)} %bitcast.77, f32[16,64,512]{2,1,0:T(8,128)S(1)} %bitcast.76, f32[16,32,512]{2,1,0:T(8,128)S(1)} %bitcast.78, f32[16,96,512]{2,1,0:T(8,128)S(1)} %bitcast.70), kind=kLoop, calls=%fused_computation.7 | loop fusion | flops 5505024 | bytes 14680064 | tf_op jit(solution)/shard_map/concatenate | solution.py:195
  112.1 1.9 slice-done
  114.0 1.7 fusion.50
  115.7 0.8 fusion.46
  116.5 2.3 %scatter_custom_fusion = f32[320,512]{1,0:T(8,128)S(1)} fusion(s32[256]{0:T(256)S(1)} %bitcast.86, f32[128,512]{1,0:T(8,128)S(1)} %get-tuple-element.37, f32[]{:T(128)} %constant.81, f32[128,512]{1,0:T(8,128)S(1)} %get-tuple-element.36, f32[]{:T(128)} %constant.31.clone.1), kind=kCustom, calls=%fused_computation.25 | custom fusion | flops 262144 | bytes 1179656 | tf_op jit(solution)/shard_map/add | solution.py:207
  118.8 3.1 %collective-permute-start.3 = (f32[1,16,512]{2,1,0:T(8,128)S(1)}, f32[1,16,512]{2,1,0:T(8,128)S(1)}, u32[]{:S(2)}, u32[]{:S(2)}) collective-permute-start(f32[1,16,512]{2,1,0:T(8,128)S(1)} %get-tuple-element.40), channel_id=1, source_target_pairs={{0,1},{1,2},{2,3},{4,5},{5,6},{6,7},{8,9},{9,10},{10,11},{12,13},{... | collective-permute-start | bytes 98312 | tf_op jit(solution)/shard_map/ppermute | solution.py:20
  121.9 1.3 collective-permute-start.2
  123.2 1.9 collective-permute-start.1
  125.1 1.3 collective-permute-start
  126.4 0.6 fusion
  127.1 0.7 collective-permute-done.2
  127.7 0.7 collective-permute-done
  128.4 1.2 scatter_fusion
  129.6 72.7 %reduce-scatter.2.cloned.1.call-done = f32[1,224,512]{2,1,0:T(8,128)} async-done(((f32[16,224,512]{2,1,0:T(8,128)}), f32[1,224,512]{2,1,0:T(8,128)}) %reduce-scatter.2.cloned.1.call-update) | async-done | bytes 458768 | tf_op jit(solution)/shard_map/reduce_scatter | solution.py:198
  202.3 1.8 shard_map.227
  (71 shorter events, 1.0 us)
Async XLA Ops:
  7.2 18.2 %copy-start = (f32[256,512]{1,0:T(8,128)S(1)}, f32[256,512]{1,0:T(8,128)}, u32[]{:S(2)}) copy-start(f32[256,512]{1,0:T(8,128)} %param.23) | copy-start | bytes 1572868
  7.2 18.1 %copy-start.13 = (s32[2,128]{1,0:T(2,128)S(1)}, s32[2,128]{1,0:T(2,128)}, u32[]{:S(2)}) copy-start(s32[2,128]{1,0:T(2,128)} %param.29) | copy-start | bytes 3076
  7.2 76.4 %all-gather.2.cloned.1.call-start = ((), (), s32[]{:S(2)}) async-start(), calls=%async_computation.1 | async-start | bytes 8077312 | tf_op jit(solution)/shard_map/all_gather | solution.py:146
  9.3 193.1 %reduce-scatter.2.cloned.1.call-start = ((), (), s32[]{:S(2)}) async-start(), calls=%async_computation.2 | async-start | bytes 7798784 | tf_op jit(solution)/shard_map/reduce_scatter | solution.py:198
  12.7 12.6 %collective-permute-start.7 = (f32[1,16,512]{2,1,0:T(8,128)S(1)}, f32[1,16,512]{2,1,0:T(8,128)S(1)}, u32[]{:S(2)}, u32[]{:S(2)}) collective-permute-start(f32[1,16,512]{2,1,0:T(8,128)S(1)} %get-tuple-element.44), channel_id=1, source_target_pairs={{1,0},{2,1},{3,2},{5,4},{6,5},{7,6},{9,8},{10,9},{11,10},{13,12},{... | collective-permute-start | bytes 98312 | tf_op jit(solution)/shard_map/ppermute | solution.py:22
  14.0 11.3 %collective-permute-start.6 = (f32[1,16,512]{2,1,0:T(8,128)S(1)}, f32[1,16,512]{2,1,0:T(8,128)S(1)}, u32[]{:S(2)}, u32[]{:S(2)}) collective-permute-start(f32[1,16,512]{2,1,0:T(8,128)S(1)} %get-tuple-element.45), channel_id=1, source_target_pairs={{0,1},{1,2},{2,3},{4,5},{5,6},{6,7},{8,9},{9,10},{10,11},{12,13},{... | collective-permute-start | bytes 98312 | tf_op jit(solution)/shard_map/ppermute | solution.py:20
  19.6 5.8 %collective-permute-start.5 = (f32[1,16,512]{2,1,0:T(8,128)S(1)}, f32[1,16,512]{2,1,0:T(8,128)S(1)}, u32[]{:S(2)}, u32[]{:S(2)}) collective-permute-start(f32[1,16,512]{2,1,0:T(8,128)S(1)} %get-tuple-element.46), channel_id=1, source_target_pairs={{4,0},{8,4},{12,8},{5,1},{9,5},{13,9},{6,2},{10,6},{14,10},{7,3},{... | collective-permute-start | bytes 98312 | tf_op jit(solution)/shard_map/ppermute | solution.py:22
  20.9 4.5 %collective-permute-start.4 = (f32[1,16,512]{2,1,0:T(8,128)S(1)}, f32[1,16,512]{2,1,0:T(8,128)S(1)}, u32[]{:S(2)}, u32[]{:S(2)}) collective-permute-start(f32[1,16,512]{2,1,0:T(8,128)S(1)} %get-tuple-element.43), channel_id=1, source_target_pairs={{0,4},{4,8},{8,12},{1,5},{5,9},{9,13},{2,6},{6,10},{10,14},{3,7},{... | collective-permute-start | bytes 98312 | tf_op jit(solution)/shard_map/ppermute | solution.py:20
  27.0 59.8 %copy-start.2 = (f32[256,512]{1,0:T(8,128)S(1)}, f32[256,512]{1,0:T(8,128)}, u32[]{:S(2)}) copy-start(f32[256,512]{1,0:T(8,128)} %param.24) | copy-start | bytes 1572868
  84.9 2.8 %copy-start.1 = (f32[256,512]{1,0:T(8,128)S(1)}, f32[256,512]{1,0:T(8,128)}, u32[]{:S(2)}) copy-start(f32[256,512]{1,0:T(8,128)} %param.27) | copy-start | bytes 1572868
  99.8 2.9 %copy-start.8 = (f32[128,512]{1,0:T(8,128)S(1)}, f32[128,512]{1,0:T(8,128)}, u32[]{:S(2)}) copy-start(f32[128,512]{1,0:T(8,128)} %param.26) | copy-start | bytes 786436
  102.7 4.1 %copy-start.6 = (f32[128,512]{1,0:T(8,128)}, f32[128,512]{1,0:T(8,128)S(1)}, u32[]{:S(2)}) copy-start(f32[128,512]{1,0:T(8,128)S(1)} %convolution_select_fusion.1) | copy-start | bytes 786436
  103.4 3.4 %copy-start.9 = (f32[128,512]{1,0:T(8,128)S(1)}, f32[128,512]{1,0:T(8,128)}, u32[]{:S(2)}) copy-start(f32[128,512]{1,0:T(8,128)} %get-tuple-element.59) | copy-start | bytes 786436
  103.4 3.4 %copy-start.10 = (f32[128,512]{1,0:T(8,128)S(1)}, f32[128,512]{1,0:T(8,128)}, u32[]{:S(2)}) copy-start(f32[128,512]{1,0:T(8,128)} %get-tuple-element.60) | copy-start | bytes 786436
  103.4 3.4 %copy-start.12 = (f32[128,512]{1,0:T(8,128)S(1)}, f32[128,512]{1,0:T(8,128)}, u32[]{:S(2)}) copy-start(f32[128,512]{1,0:T(8,128)} %param.25) | copy-start | bytes 786436
  106.7 1.6 copy-start.4
  112.1 1.9 slice-start
  112.1 1.9 copy-start.7
  112.1 3.6 %copy-start.11 = (f32[128,512]{1,0:T(8,128)S(1)}, f32[128,512]{1,0:T(8,128)}, u32[]{:S(2)}) copy-start(f32[128,512]{1,0:T(8,128)} %param.28) | copy-start | bytes 786436
  114.0 12.4 %copy-start.5 = (f32[8,64,512]{2,1,0:T(8,128)S(1)}, f32[8,64,512]{2,1,0:T(8,128)}, u32[]{:S(2)}) copy-start(f32[8,64,512]{2,1,0:T(8,128)} %get-tuple-element.32) | copy-start | bytes 3145732
  118.8 8.2 %collective-permute-start.3 = (f32[1,16,512]{2,1,0:T(8,128)S(1)}, f32[1,16,512]{2,1,0:T(8,128)S(1)}, u32[]{:S(2)}, u32[]{:S(2)}) collective-permute-start(f32[1,16,512]{2,1,0:T(8,128)S(1)} %get-tuple-element.40), channel_id=1, source_target_pairs={{0,1},{1,2},{2,3},{4,5},{5,6},{6,7},{8,9},{9,10},{10,11},{12,13},{... | collective-permute-start | bytes 98312 | tf_op jit(solution)/shard_map/ppermute | solution.py:20
  121.9 5.8 %collective-permute-start.2 = (f32[1,16,512]{2,1,0:T(8,128)S(1)}, f32[1,16,512]{2,1,0:T(8,128)S(1)}, u32[]{:S(2)}, u32[]{:S(2)}) collective-permute-start(f32[1,16,512]{2,1,0:T(8,128)S(1)} %get-tuple-element.41), channel_id=1, source_target_pairs={{1,0},{2,1},{3,2},{5,4},{6,5},{7,6},{9,8},{10,9},{11,10},{13,12},{... | collective-permute-start | bytes 98312 | tf_op jit(solution)/shard_map/ppermute | solution.py:22
  123.2 4.5 %collective-permute-start.1 = (f32[1,16,512]{2,1,0:T(8,128)S(1)}, f32[1,16,512]{2,1,0:T(8,128)S(1)}, u32[]{:S(2)}, u32[]{:S(2)}) collective-permute-start(f32[1,16,512]{2,1,0:T(8,128)S(1)} %get-tuple-element.42), channel_id=1, source_target_pairs={{0,4},{4,8},{8,12},{1,5},{5,9},{9,13},{2,6},{6,10},{10,14},{3,7},{... | collective-permute-start | bytes 98312 | tf_op jit(solution)/shard_map/ppermute | solution.py:20
  125.1 3.3 %collective-permute-start = (f32[1,16,512]{2,1,0:T(8,128)S(1)}, f32[1,16,512]{2,1,0:T(8,128)S(1)}, u32[]{:S(2)}, u32[]{:S(2)}) collective-permute-start(f32[1,16,512]{2,1,0:T(8,128)S(1)} %get-tuple-element.39), channel_id=1, source_target_pairs={{4,0},{8,4},{12,8},{5,1},{9,5},{13,9},{6,2},{10,6},{14,10},{7,3},{... | collective-permute-start | bytes 98312 | tf_op jit(solution)/shard_map/ppermute | solution.py:22
  129.6 74.5 %copy-start.3 = (f32[256,512]{1,0:T(8,128)}, f32[256,512]{1,0:T(8,128)S(1)}, u32[]{:S(2)}) copy-start(f32[256,512]{1,0:T(8,128)S(1)} %scatter_fusion) | copy-start | bytes 1572868
Sparse Core Ops, SparseCore 0:
  10.9 72.6 all-gather.1
  112.2 90.1 reduce-scatter.1

commit v7 on v5

--- a/solution.py
+++ b/solution.py
@@ -67,6 +67,53 @@
         kernel,
         out_shape=tuple(jax.ShapeDtypeStruct((size, packed.shape[1]), packed.dtype) for size in sizes),
     )(packed)
+
+
+def split_bf16(values):
+    high = values.astype(jnp.bfloat16)
+    low = (values - high.astype(jnp.float32)).astype(jnp.bfloat16)
+    return high, low
+
+
+def inner_three(left, right):
+    left_high, left_low = split_bf16(left.T)
+    right_high, right_low = split_bf16(right)
+
+    def dot(a, b):
+        return jnp.dot(a, b, preferred_element_type=jnp.float32)
+
+    return dot(left_high, right_high) + dot(left_low, right_high) + dot(left_high, right_low)
+
+
+def blocked_grads(edge_terms, node_terms, blocks, edge_scale, node_scale):
+    terms = [(pieces, right, edge_scale) for pieces, right in edge_terms] + [
+        (pieces, right, node_scale) for pieces, right in node_terms
+    ]
+    rows = [sum(p.shape[1] for p in pieces) // blocks for pieces, _, _ in terms]
+    offsets = row_offsets(rows)
+    inputs = []
+    layout = []
+    for pieces, right, scale in terms:
+        layout.append((len(inputs), len(pieces), scale))
+        inputs.extend(pieces)
+        inputs.append(right)
+    width = terms[0][1].shape[1]
+
+    def kernel(*refs):
+        out = refs[-1]
+        for index, (start, count, scale) in enumerate(layout):
+            right = refs[start + count][...]
+            product = jnp.concatenate(
+                [inner_three(refs[start + k][...], right) for k in range(count)], axis=0
+            ) * scale
+            size = rows[index]
+            for block in range(blocks):
+                out[block, offsets[index] : offsets[index + 1], :] = product[block * size : (block + 1) * size]
+
+    return pl.pallas_call(
+        kernel,
+        out_shape=jax.ShapeDtypeStruct((blocks, offsets[-1], width), jnp.float32),
+    )(*inputs)
 
 
 def matmul(left, right):
@@ -173,9 +220,7 @@
     node_upstream = node_cotangent * live_nodes
     node_grad_z = norm_back(node_upstream * full_node_gain, node_normed, node_inverse)
     node_grad_pre = outer_back(node_grad_z, full_node_second) * (node_pre > 0).astype(jnp.float32)
-    node_input = jnp.concatenate([node_states, aggregate], axis=1)
-    node_first_part = inner(node_input, node_grad_pre) * node_scale
-    node_second_part = inner(node_act, node_grad_z) * node_scale
+    node_terms = [([node_states, aggregate], node_grad_pre), ([node_act], node_grad_z)]
     node_grad_input = outer_back(node_grad_pre, full_node_first)
     state_grads = node_upstream + node_grad_input[:, :width]
     edge_upstream = (
@@ -183,17 +228,22 @@
     ) * live_edges
     edge_grad_z = norm_back(edge_upstream * full_edge_gain, edge_normed, edge_inverse)
     edge_grad_pre = outer_back(edge_grad_z, full_edge_second) * (edge_pre > 0).astype(jnp.float32)
-    edge_second_part = inner(edge_act, edge_grad_z) * edge_scale
     extended = jnp.concatenate([node_states, ghosts], axis=0)
-    features = jnp.concatenate(
-        [edge_states, jnp.take(extended, source, axis=0), jnp.take(extended, target, axis=0)],
-        axis=1,
-    )
-    edge_first_part = inner(features, edge_grad_pre) * edge_scale
-    parts = (edge_first_part, edge_second_part, node_first_part, node_second_part)
-    blocked = jnp.concatenate(
-        [part.reshape(peer_count, -1, width) for part in parts], axis=1
-    )
+    sent = jnp.take(extended, source, axis=0)
+    received = jnp.take(extended, target, axis=0)
+    edge_terms = [([edge_states, sent, received], edge_grad_pre), ([edge_act], edge_grad_z)]
+    if all(m.shape[0] % 8 == 0 for m in matrices):
+        blocked = blocked_grads(edge_terms, node_terms, peer_count, edge_scale, node_scale)
+    else:
+        parts = [
+            jnp.concatenate([inner(p, right) for p in pieces], axis=0) * scale
+            for (pieces, right), scale in zip(
+                edge_terms + node_terms, [edge_scale] * 2 + [node_scale] * 2
+            )
+        ]
+        blocked = jnp.concatenate(
+            [part.reshape(peer_count, -1, width) for part in parts], axis=1
+        )
     reduced = lax.psum_scatter(blocked, peers, scatter_dimension=0, tiled=True)[0]
     edge_first_grad, edge_second_grad, node_first_grad, node_second_grad = split_rows(
         reduced, [m.shape[0] for m in matrices]

time: 211 us -> 208 us (0.986)
  matrix products: 16 us -> 7.55 us
  Pallas kernels: 3.78 us -> 12 us
    dot_general x4 -> x0, matrix products: 8.36 us -> none  [inner(): lax.dot_general(left, right, (((0,), (0,)), ((), ())), precision=lax.Prec...]
    pallas_call x0 -> x1, Pallas kernels: none -> 8.21 us  [blocked_grads(): pl.pallas_call(kernel, out_shape=jax.ShapeDtypeStruct((blocks, offsets[-1...]
    concatenate x2 -> x1, other arithmetic: 3.52 us -> 0.01 us  [the longest x1 3.52 us: shards(): jnp.concatenate([part.reshape(peer_count, -1, width) for part in parts],...]
  transfers between devices with their start and end apart: 10 -> 10, of which waited for: 4 -> 4; matrix products, arithmetic and copies ran while one was open for 6% -> 7% of each run, Pallas kernels for 0% -> 0%
where the time goes in v7:
time: 208 us; the launch traced here: 207 us
  waiting for transfers between devices  129 us (62%)
  starting transfers between devices  18.8 us (9%)
  between operations  15.9 us (8%)
  local copies, waits for them, and re-layouts  13.8 us (7%)
  Pallas kernels  12 us (6%)
  other arithmetic  10.7 us (5%)
  matrix products  7.55 us (4%)
    reduce_scatter x1, waiting for transfers between devices, shards(): lax.psum_scatter(blocked, peers, scatter_dimension=0, tiled=True)[0]  72.7 us
    all_gather x1, waiting for transfers between devices, shards(): gathered = lax.all_gather(packed, peers, axis=0, tiled=True)  54 us
    ppermute x4, starting transfers between devices, padded(): lax.ppermute(tail, axis, [(i, (i + 1) % count) for i in range(ends)])  13.5 us
    pallas_call x1, Pallas kernels, blocked_grads(): pl.pallas_call(kernel, out_shape=jax.ShapeDtypeStruct((blocks, offsets[-1...  8.21 us
    dot_general x4, matrix products, outer_back(): lax.dot_general(left, right, (((1,), (1,)), ((), ())), precision=lax.Prec...  6.28 us
    ppermute x4, starting transfers between devices, padded(): lax.ppermute(head, axis, [((i + 1) % count, i) for i in range(ends)])  5.17 us
    slice x6, local copies, waits for them, and re-layouts, shards(): pieces.append(gathered[:, offset:offset + rows, :])  4.58 us
  transfers between devices with their start and end apart: 10, of which 4 were waited for; matrix products, arithmetic and copies ran while one was open for 7% of the time, Pallas kernels for 0%

profile of v7, /device:TPU:0, one launch (start us, length us, event | category | flops | bytes accessed | tf_op | source)
XLA Modules:
  0.0 207.4 jit_solution(9145105536558056645)
XLA Ops:
  7.3 2.0 shard_map.226
  9.4 0.8 reshape.254
  10.1 0.8 broadcast_in_dim_reshape_squeeze.3
  10.9 1.8 gather_fusion.1
  12.8 1.3 collective-permute-start.7
  14.1 5.6 %collective-permute-start.6 = (f32[1,16,512]{2,1,0:T(8,128)S(1)}, f32[1,16,512]{2,1,0:T(8,128)S(1)}, u32[]{:S(2)}, u32[]{:S(2)}) collective-permute-start(f32[1,16,512]{2,1,0:T(8,128)S(1)} %get-tuple-element.40), channel_id=1, source_target_pairs={{0,1},{1,2},{2,3},{4,5},{5,6},{6,7},{8,9},{9,10},{10,11},{12,13},{... | collective-permute-start | bytes 98312 | tf_op jit(solution)/shard_map/ppermute | solution.py:20
  19.7 1.3 collective-permute-start.5
  21.0 3.0 %collective-permute-start.4 = (f32[1,16,512]{2,1,0:T(8,128)S(1)}, f32[1,16,512]{2,1,0:T(8,128)S(1)}, u32[]{:S(2)}, u32[]{:S(2)}) collective-permute-start(f32[1,16,512]{2,1,0:T(8,128)S(1)} %get-tuple-element.38), channel_id=1, source_target_pairs={{0,4},{4,8},{8,12},{1,5},{5,9},{9,13},{2,6},{6,10},{10,14},{3,7},{... | collective-permute-start | bytes 98312 | tf_op jit(solution)/shard_map/ppermute | solution.py:20
  25.4 0.7 broadcast_maximum_fusion.1.refs_4_
  26.2 0.9 broadcast_maximum_fusion.refs_9_
  27.1 0.8 gather_fusion.3
  27.9 0.8 gather_fusion.2
  28.7 0.9 broadcast_select_fusion
  29.6 54.0 %all-gather.2.cloned.1.call-done = f32[16,225,512]{2,1,0:T(8,128)} async-done(((f32[1,225,512]{2,1,0:T(8,128)}), f32[16,225,512]{2,1,0:T(8,128)}) %all-gather.2.cloned.1.call-update) | async-done | bytes 7372816 | tf_op jit(solution)/shard_map/all_gather | solution.py:193
  83.6 1.0 slice.159
  84.9 1.7 fusion.20
  86.7 1.0 copy-done
  87.6 0.6 fusion.22
  88.2 0.2 multiply_reduce_fusion.3
  88.6 0.7 fusion.23
  89.4 0.2 multiply_reduce_fusion.1
  89.6 0.3 fusion.4
  89.9 0.3 subtract_multiply_fusion.refs_10_
  90.2 0.8 copy-done.6
  91.0 2.1 %convolution_select_fusion.refs_8_ = f32[256,512]{1,0:T(8,128)S(1)} fusion(f32[256,512]{1,0:T(8,128)S(1)} %subtract_multiply_fusion.refs_10_, f32[512,512]{1,0:T(8,128)} %bitcast.71, f32[256,512]{1,0:T(8,128)} %param.22), kind=kOutput, calls=%fused_computation.8 | convolution fusion | flops 402915328 | bytes 2621440 | tf_op jit(solution)/shard_map/dot_general | solution.py:134
  93.1 1.1 fusion.24
  94.2 1.0 copy-done.10
  95.2 0.8 gather_fusion
  96.0 0.1 copy-done.16
  96.1 0.2 fusion.19
  96.4 0.1 subtract_multiply_fusion.1.refs_5_
  96.6 1.4 convolution_select_fusion.1.refs_3_
  98.0 2.2 %scatter_custom_fusion.2.refs_7_ = f32[256,512]{1,0:T(8,128)} fusion(s32[128]{0:T(128)S(1)} %get-tuple-element.42, f32[]{:T(128)} %constant.39.clone.1, f32[128,512]{1,0:T(8,128)S(1)} %get-tuple-element.49, f32[512]{0:T(512)S(1)} %add.152, f32[512]{0:T(512)S(1)} %mul.141, f32[128]{0:T(128)S(1)} %compare_convert_fusion, f32[128]{0:T(128)S(1)} %add_rsqrt_fusion.1, ...), kind=kCustom, calls=%fused_computation.26 | custom fusion | flops 393216 | bytes 792068 | tf_op jit(solution)/shard_map/scatter-add | solution.py:217
  100.2 8.2 %shard_map.227 = f32[16,224,512]{2,1,0:T(8,128)} custom-call(f32[128,512]{1,0:T(8,128)} %refs_0_.3, f32[128,512]{1,0:T(8,128)} %get-tuple-element.55.refs_1_, f32[128,512]{1,0:T(8,128)} %get-tuple-element.54.refs_2_, f32[128,512]{1,0:T(8,128)} %convolution_select_fusion.1.refs_3_, f32[128,512]{1,0:T(8,128)} %broadcast_maximum_fusion.1.refs_4_, ...), custom_call_target="tpu_custom_call" | custom-call | tf_op jit(solution)/shard_map/pallas_call | solution.py:113
  108.5 1.9 slice-done.1
  110.4 1.7 fusion.25
  112.1 0.8 fusion.21
  112.9 2.3 %scatter_custom_fusion = f32[320,512]{1,0:T(8,128)S(1)} fusion(s32[256]{0:T(256)S(1)} %bitcast.77, f32[128,512]{1,0:T(8,128)S(1)} %get-tuple-element.32, f32[]{:T(128)} %constant.77, f32[128,512]{1,0:T(8,128)S(1)} %get-tuple-element.31, f32[]{:T(128)} %constant.39.clone.1), kind=kCustom, calls=%fused_computation.14 | custom fusion | flops 262144 | bytes 1179656 | tf_op jit(solution)/shard_map/add | solution.py:256
  115.2 3.1 %collective-permute-start.3 = (f32[1,16,512]{2,1,0:T(8,128)S(1)}, f32[1,16,512]{2,1,0:T(8,128)S(1)}, u32[]{:S(2)}, u32[]{:S(2)}) collective-permute-start(f32[1,16,512]{2,1,0:T(8,128)S(1)} %get-tuple-element.35), channel_id=1, source_target_pairs={{0,1},{1,2},{2,3},{4,5},{5,6},{6,7},{8,9},{9,10},{10,11},{12,13},{... | collective-permute-start | bytes 98312 | tf_op jit(solution)/shard_map/ppermute | solution.py:20
  118.3 1.3 collective-permute-start.2
  119.6 1.9 collective-permute-start.1
  121.5 1.3 collective-permute-start
  122.8 0.1 slice_add_fusion
  123.0 1.1 collective-permute-done.2
  124.1 0.7 collective-permute-done
  124.8 1.2 scatter_fusion
  126.0 72.7 %reduce-scatter.2.cloned.1.call-done = f32[1,224,512]{2,1,0:T(8,128)} async-done(((f32[16,224,512]{2,1,0:T(8,128)}), f32[1,224,512]{2,1,0:T(8,128)}) %reduce-scatter.2.cloned.1.call-update) | async-done | bytes 458768 | tf_op jit(solution)/shard_map/reduce_scatter | solution.py:247
  198.7 1.8 shard_map.228
  (80 shorter events, 1.1 us)
Async XLA Ops:
  7.2 19.9 %copy-start.3 = (f32[256,512]{1,0:T(8,128)S(1)}, f32[256,512]{1,0:T(8,128)}, u32[]{:S(2)}) copy-start(f32[256,512]{1,0:T(8,128)} %refs_6_.1) | copy-start | bytes 1572868
  7.2 18.1 %copy-start.17 = (s32[2,128]{1,0:T(2,128)S(1)}, s32[2,128]{1,0:T(2,128)}, u32[]{:S(2)}) copy-start(s32[2,128]{1,0:T(2,128)} %param.27) | copy-start | bytes 3076
  7.2 18.2 %copy-start.14 = (f32[128,512]{1,0:T(8,128)S(1)}, f32[128,512]{1,0:T(8,128)}, u32[]{:S(2)}) copy-start(f32[128,512]{1,0:T(8,128)} %param.24) | copy-start | bytes 786436
  7.2 19.0 %copy-start.5 = (f32[256,512]{1,0:T(8,128)S(1)}, f32[256,512]{1,0:T(8,128)}, u32[]{:S(2)}) copy-start(f32[256,512]{1,0:T(8,128)} %param.22) | copy-start | bytes 1572868
  7.2 76.4 %all-gather.2.cloned.1.call-start = ((), (), s32[]{:S(2)}) async-start(), calls=%async_computation.1 | async-start | bytes 8077312 | tf_op jit(solution)/shard_map/all_gather | solution.py:193
  9.3 189.4 %reduce-scatter.2.cloned.1.call-start = ((), (), s32[]{:S(2)}) async-start(), calls=%async_computation.2 | async-start | bytes 7798784 | tf_op jit(solution)/shard_map/reduce_scatter | solution.py:247
  12.8 14.2 %collective-permute-start.7 = (f32[1,16,512]{2,1,0:T(8,128)S(1)}, f32[1,16,512]{2,1,0:T(8,128)S(1)}, u32[]{:S(2)}, u32[]{:S(2)}) collective-permute-start(f32[1,16,512]{2,1,0:T(8,128)S(1)} %get-tuple-element.39), channel_id=1, source_target_pairs={{1,0},{2,1},{3,2},{5,4},{6,5},{7,6},{9,8},{10,9},{11,10},{13,12},{... | collective-permute-start | bytes 98312 | tf_op jit(solution)/shard_map/ppermute | solution.py:22
  14.1 12.9 %collective-permute-start.6 = (f32[1,16,512]{2,1,0:T(8,128)S(1)}, f32[1,16,512]{2,1,0:T(8,128)S(1)}, u32[]{:S(2)}, u32[]{:S(2)}) collective-permute-start(f32[1,16,512]{2,1,0:T(8,128)S(1)} %get-tuple-element.40), channel_id=1, source_target_pairs={{0,1},{1,2},{2,3},{4,5},{5,6},{6,7},{8,9},{9,10},{10,11},{12,13},{... | collective-permute-start | bytes 98312 | tf_op jit(solution)/shard_map/ppermute | solution.py:20
  19.7 7.4 %collective-permute-start.5 = (f32[1,16,512]{2,1,0:T(8,128)S(1)}, f32[1,16,512]{2,1,0:T(8,128)S(1)}, u32[]{:S(2)}, u32[]{:S(2)}) collective-permute-start(f32[1,16,512]{2,1,0:T(8,128)S(1)} %get-tuple-element.41), channel_id=1, source_target_pairs={{4,0},{8,4},{12,8},{5,1},{9,5},{13,9},{6,2},{10,6},{14,10},{7,3},{... | collective-permute-start | bytes 98312 | tf_op jit(solution)/shard_map/ppermute | solution.py:22
  21.0 6.1 %collective-permute-start.4 = (f32[1,16,512]{2,1,0:T(8,128)S(1)}, f32[1,16,512]{2,1,0:T(8,128)S(1)}, u32[]{:S(2)}, u32[]{:S(2)}) collective-permute-start(f32[1,16,512]{2,1,0:T(8,128)S(1)} %get-tuple-element.38), channel_id=1, source_target_pairs={{0,4},{4,8},{8,12},{1,5},{5,9},{9,13},{2,6},{6,10},{10,14},{3,7},{... | collective-permute-start | bytes 98312 | tf_op jit(solution)/shard_map/ppermute | solution.py:20
  86.6 1.0 copy-start
  86.6 3.3 %copy-start.2 = (f32[16,32,512]{2,1,0:T(8,128)}, f32[16,32,512]{2,1,0:T(8,128)S(1)}, u32[]{:S(2)}) copy-start(f32[16,32,512]{2,1,0:T(8,128)S(1)} %get-tuple-element.29) | copy-start | bytes 3145732
  86.6 2.9 %copy-start.8 = (f32[256,512]{1,0:T(8,128)S(1)}, f32[256,512]{1,0:T(8,128)}, u32[]{:S(2)}) copy-start(f32[256,512]{1,0:T(8,128)} %param.25) | copy-start | bytes 1572868
  90.2 0.8 copy-start.6
  91.0 2.1 %slice-start = ((f32[16,225,512]{2,1,0:T(8,128)}), f32[16,64,512]{2,1,0:T(8,128)S(1)}, s32[]{:S(2)}) async-start(f32[16,225,512]{2,1,0:T(8,128)} %all-gather.2.cloned.1.call-done), calls=%async_computation.3 | async-start | bytes 4194304 | tf_op jit(solution)/shard_map/slice | solution.py:197
  93.1 1.1 copy-start.4
  94.2 1.0 copy-start.10
  95.2 0.9 copy-start.16
  95.2 1.3 copy-start.1
  95.2 1.4 copy-start.15
  96.6 3.7 %copy-start.13 = (f32[128,512]{1,0:T(8,128)}, f32[128,512]{1,0:T(8,128)S(1)}, u32[]{:S(2)}) copy-start(f32[128,512]{1,0:T(8,128)S(1)} %subtract_multiply_fusion.1.refs_5_) | copy-start | bytes 786436
  108.5 1.9 slice-start.1
  108.5 1.9 copy-start.12
  110.4 12.4 %copy-start.9 = (f32[256,512]{1,0:T(8,128)S(1)}, f32[256,512]{1,0:T(8,128)}, u32[]{:S(2)}) copy-start(f32[256,512]{1,0:T(8,128)} %param.25) | copy-start | bytes 1572868
  110.4 12.4 %copy-start.11 = (f32[256,1024]{1,0:T(8,128)S(1)}, f32[256,1024]{1,0:T(8,128)}, u32[]{:S(2)}) copy-start(f32[256,1024]{1,0:T(8,128)} %copy-done.10) | copy-start | bytes 3145732
  115.2 7.7 %collective-permute-start.3 = (f32[1,16,512]{2,1,0:T(8,128)S(1)}, f32[1,16,512]{2,1,0:T(8,128)S(1)}, u32[]{:S(2)}, u32[]{:S(2)}) collective-permute-start(f32[1,16,512]{2,1,0:T(8,128)S(1)} %get-tuple-element.35), channel_id=1, source_target_pairs={{0,1},{1,2},{2,3},{4,5},{5,6},{6,7},{8,9},{9,10},{10,11},{12,13},{... | collective-permute-start | bytes 98312 | tf_op jit(solution)/shard_map/ppermute | solution.py:20
  118.3 5.8 %collective-permute-start.2 = (f32[1,16,512]{2,1,0:T(8,128)S(1)}, f32[1,16,512]{2,1,0:T(8,128)S(1)}, u32[]{:S(2)}, u32[]{:S(2)}) collective-permute-start(f32[1,16,512]{2,1,0:T(8,128)S(1)} %get-tuple-element.36), channel_id=1, source_target_pairs={{1,0},{2,1},{3,2},{5,4},{6,5},{7,6},{9,8},{10,9},{11,10},{13,12},{... | collective-permute-start | bytes 98312 | tf_op jit(solution)/shard_map/ppermute | solution.py:22
  119.6 4.5 %collective-permute-start.1 = (f32[1,16,512]{2,1,0:T(8,128)S(1)}, f32[1,16,512]{2,1,0:T(8,128)S(1)}, u32[]{:S(2)}, u32[]{:S(2)}) collective-permute-start(f32[1,16,512]{2,1,0:T(8,128)S(1)} %get-tuple-element.37), channel_id=1, source_target_pairs={{0,4},{4,8},{8,12},{1,5},{5,9},{9,13},{2,6},{6,10},{10,14},{3,7},{... | collective-permute-start | bytes 98312 | tf_op jit(solution)/shard_map/ppermute | solution.py:20
  121.5 3.3 %collective-permute-start = (f32[1,16,512]{2,1,0:T(8,128)S(1)}, f32[1,16,512]{2,1,0:T(8,128)S(1)}, u32[]{:S(2)}, u32[]{:S(2)}) collective-permute-start(f32[1,16,512]{2,1,0:T(8,128)S(1)} %get-tuple-element.34), channel_id=1, source_target_pairs={{4,0},{8,4},{12,8},{5,1},{9,5},{13,9},{6,2},{10,6},{14,10},{7,3},{... | collective-permute-start | bytes 98312 | tf_op jit(solution)/shard_map/ppermute | solution.py:22
  126.0 74.5 %copy-start.7 = (f32[256,512]{1,0:T(8,128)}, f32[256,512]{1,0:T(8,128)S(1)}, u32[]{:S(2)}) copy-start(f32[256,512]{1,0:T(8,128)S(1)} %scatter_fusion) | copy-start | bytes 1572868
Sparse Core Ops, SparseCore 0:
  10.9 72.6 all-gather.1
  108.6 90.1 reduce-scatter.1

commit v8 on v7

--- a/solution.py
+++ b/solution.py
@@ -4,6 +4,7 @@
 import jax.numpy as jnp
 from jax import lax
 from jax.experimental import pallas as pl
+from jax.experimental.pallas import tpu as pltpu
 from jax.sharding import PartitionSpec as P
 
 EPSILON = 1e-05
@@ -99,20 +100,48 @@
         inputs.append(right)
     width = terms[0][1].shape[1]
 
+    order = sorted(range(len(terms)), key=lambda index: -rows[index] * terms[index][1].shape[0])
+    count_in = len(inputs)
+
     def kernel(*refs):
-        out = refs[-1]
-        for index, (start, count, scale) in enumerate(layout):
-            right = refs[start + count][...]
+        sources = refs[:count_in]
+        out = refs[count_in]
+        staged = refs[count_in + 1 : 2 * count_in + 1]
+        results = refs[2 * count_in + 1 : 2 * count_in + 1 + len(terms)]
+        in_sems = refs[-2]
+        out_sems = refs[-1]
+        loads = [
+            pltpu.make_async_copy(sources[k], staged[k], in_sems.at[k]) for k in range(count_in)
+        ]
+        for load in loads:
+            load.start()
+        stores = []
+        for index in order:
+            start, count, scale = layout[index]
+            for k in range(start, start + count + 1):
+                loads[k].wait()
+            right = staged[start + count][...]
             product = jnp.concatenate(
-                [inner_three(refs[start + k][...], right) for k in range(count)], axis=0
+                [inner_three(staged[start + k][...], right) for k in range(count)], axis=0
             ) * scale
-            size = rows[index]
-            for block in range(blocks):
-                out[block, offsets[index] : offsets[index + 1], :] = product[block * size : (block + 1) * size]
-
+            results[index][...] = product.reshape(blocks, rows[index], width)
+            store = pltpu.make_async_copy(
+                results[index], out.at[:, offsets[index] : offsets[index + 1], :], out_sems.at[index]
+            )
+            store.start()
+            stores.append(store)
+        for store in stores:
+            store.wait()
+
+    any_space = pl.BlockSpec(memory_space=pl.ANY)
     return pl.pallas_call(
         kernel,
         out_shape=jax.ShapeDtypeStruct((blocks, offsets[-1], width), jnp.float32),
+        in_specs=[any_space] * count_in,
+        out_specs=any_space,
+        scratch_shapes=[pltpu.VMEM(x.shape, x.dtype) for x in inputs]
+        + [pltpu.VMEM((blocks, size, width), jnp.float32) for size in rows]
+        + [pltpu.SemaphoreType.DMA((count_in,)), pltpu.SemaphoreType.DMA((len(terms),))],
     )(*inputs)
 
 

time: 208 us -> 206 us (level)
  no operation moved by 1% of the time
where the time goes in v8:
time: 206 us
  waiting for transfers between devices  129 us (63%)
  starting transfers between devices  18.8 us (9%)
  between operations  15.9 us (8%)
  local copies, waits for them, and re-layouts  13.8 us (7%)
  other arithmetic  10.7 us (5%)
  Pallas kernels  10.5 us (5%)
  matrix products  7.55 us (4%)
    reduce_scatter x1, waiting for transfers between devices, shards(): lax.psum_scatter(blocked, peers, scatter_dimension=0, tiled=True)[0]  72.7 us
    all_gather x1, waiting for transfers between devices, shards(): gathered = lax.all_gather(packed, peers, axis=0, tiled=True)  54 us
    ppermute x4, starting transfers between devices, padded(): lax.ppermute(tail, axis, [(i, (i + 1) % count) for i in range(ends)])  13.5 us
    pallas_call x1, Pallas kernels, blocked_grads(): pl.pallas_call(kernel, out_shape=jax.ShapeDtypeStruct((blocks, offsets[-1...  6.72 us
    dot_general x4, matrix products, outer_back(): lax.dot_general(left, right, (((1,), (1,)), ((), ())), precision=lax.Prec...  6.28 us
    ppermute x4, starting transfers between devices, padded(): lax.ppermute(head, axis, [((i + 1) % count, i) for i in range(ends)])  5.17 us
    slice x6, local copies, waits for them, and re-layouts, shards(): pieces.append(gathered[:, offset:offset + rows, :])  4.58 us
  transfers between devices with their start and end apart: 10, of which 4 were waited for; matrix products, arithmetic and copies ran while one was open for 7% of the time, Pallas kernels for 0%

profile of v8, /device:TPU:0, one launch (start us, length us, event | category | flops | bytes accessed | tf_op | source)
XLA Modules:
  0.0 205.9 jit_solution(87072031858471426)
XLA Ops:
  7.3 2.0 shard_map.226
  9.4 0.8 reshape.254
  10.1 0.8 broadcast_in_dim_reshape_squeeze.3
  10.9 1.8 gather_fusion.1
  12.8 1.3 collective-permute-start.7
  14.1 5.6 %collective-permute-start.6 = (f32[1,16,512]{2,1,0:T(8,128)S(1)}, f32[1,16,512]{2,1,0:T(8,128)S(1)}, u32[]{:S(2)}, u32[]{:S(2)}) collective-permute-start(f32[1,16,512]{2,1,0:T(8,128)S(1)} %get-tuple-element.40), channel_id=1, source_target_pairs={{0,1},{1,2},{2,3},{4,5},{5,6},{6,7},{8,9},{9,10},{10,11},{12,13},{... | collective-permute-start | bytes 98312 | tf_op jit(solution)/shard_map/ppermute | solution.py:21
  19.7 1.3 collective-permute-start.5
  21.0 3.0 %collective-permute-start.4 = (f32[1,16,512]{2,1,0:T(8,128)S(1)}, f32[1,16,512]{2,1,0:T(8,128)S(1)}, u32[]{:S(2)}, u32[]{:S(2)}) collective-permute-start(f32[1,16,512]{2,1,0:T(8,128)S(1)} %get-tuple-element.38), channel_id=1, source_target_pairs={{0,4},{4,8},{8,12},{1,5},{5,9},{9,13},{2,6},{6,10},{10,14},{3,7},{... | collective-permute-start | bytes 98312 | tf_op jit(solution)/shard_map/ppermute | solution.py:21
  25.4 0.7 broadcast_maximum_fusion.1.refs_4_
  26.2 0.9 broadcast_maximum_fusion.refs_9_
  27.1 0.8 gather_fusion.3
  27.9 0.8 gather_fusion.2
  28.7 0.9 broadcast_select_fusion
  29.6 54.0 %all-gather.2.cloned.1.call-done = f32[16,225,512]{2,1,0:T(8,128)} async-done(((f32[1,225,512]{2,1,0:T(8,128)}), f32[16,225,512]{2,1,0:T(8,128)}) %all-gather.2.cloned.1.call-update) | async-done | bytes 7372816 | tf_op jit(solution)/shard_map/all_gather | solution.py:222
  83.6 1.0 slice.159
  84.9 1.7 fusion.20
  86.7 1.0 copy-done
  87.6 0.6 fusion.22
  88.2 0.2 multiply_reduce_fusion.3
  88.6 0.7 fusion.23
  89.4 0.2 multiply_reduce_fusion.1
  89.6 0.3 fusion.4
  89.9 0.3 subtract_multiply_fusion.refs_10_
  90.2 0.8 copy-done.6
  91.0 2.1 %convolution_select_fusion.refs_8_ = f32[256,512]{1,0:T(8,128)S(1)} fusion(f32[256,512]{1,0:T(8,128)S(1)} %subtract_multiply_fusion.refs_10_, f32[512,512]{1,0:T(8,128)} %bitcast.71, f32[256,512]{1,0:T(8,128)} %param.22), kind=kOutput, calls=%fused_computation.8 | convolution fusion | flops 402915328 | bytes 2621440 | tf_op jit(solution)/shard_map/dot_general | solution.py:163
  93.1 1.1 fusion.24
  94.2 1.0 copy-done.10
  95.2 0.8 gather_fusion
  96.0 0.1 copy-done.16
  96.1 0.2 fusion.19
  96.4 0.1 subtract_multiply_fusion.1.refs_5_
  96.6 1.4 convolution_select_fusion.1.refs_3_
  98.0 2.2 %scatter_custom_fusion.2.refs_7_ = f32[256,512]{1,0:T(8,128)} fusion(s32[128]{0:T(128)S(1)} %get-tuple-element.42, f32[]{:T(128)} %constant.39.clone.1, f32[128,512]{1,0:T(8,128)S(1)} %get-tuple-element.49, f32[512]{0:T(512)S(1)} %add.152, f32[512]{0:T(512)S(1)} %mul.141, f32[128]{0:T(128)S(1)} %compare_convert_fusion, f32[128]{0:T(128)S(1)} %add_rsqrt_fusion.1, ...), kind=kCustom, calls=%fused_computation.26 | custom fusion | flops 393216 | bytes 792068 | tf_op jit(solution)/shard_map/scatter-add | solution.py:246
  100.2 6.7 %shard_map.227 = f32[16,224,512]{2,1,0:T(8,128)} custom-call(f32[128,512]{1,0:T(8,128)} %refs_0_.3, f32[128,512]{1,0:T(8,128)} %get-tuple-element.55.refs_1_, f32[128,512]{1,0:T(8,128)} %get-tuple-element.54.refs_2_, f32[128,512]{1,0:T(8,128)} %convolution_select_fusion.1.refs_3_, f32[128,512]{1,0:T(8,128)} %broadcast_maximum_fusion.1.refs_4_, ...), custom_call_target="tpu_custom_call" | custom-call | tf_op jit(solution)/shard_map/pallas_call | solution.py:137
  107.0 1.9 slice-done.1
  108.9 1.7 fusion.25
  110.7 0.8 fusion.21
  111.5 2.3 %scatter_custom_fusion = f32[320,512]{1,0:T(8,128)S(1)} fusion(s32[256]{0:T(256)S(1)} %bitcast.77, f32[128,512]{1,0:T(8,128)S(1)} %get-tuple-element.32, f32[]{:T(128)} %constant.77, f32[128,512]{1,0:T(8,128)S(1)} %get-tuple-element.31, f32[]{:T(128)} %constant.39.clone.1), kind=kCustom, calls=%fused_computation.14 | custom fusion | flops 262144 | bytes 1179656 | tf_op jit(solution)/shard_map/add | solution.py:285
  113.8 3.1 %collective-permute-start.3 = (f32[1,16,512]{2,1,0:T(8,128)S(1)}, f32[1,16,512]{2,1,0:T(8,128)S(1)}, u32[]{:S(2)}, u32[]{:S(2)}) collective-permute-start(f32[1,16,512]{2,1,0:T(8,128)S(1)} %get-tuple-element.35), channel_id=1, source_target_pairs={{0,1},{1,2},{2,3},{4,5},{5,6},{6,7},{8,9},{9,10},{10,11},{12,13},{... | collective-permute-start | bytes 98312 | tf_op jit(solution)/shard_map/ppermute | solution.py:21
  116.8 1.3 collective-permute-start.2
  118.1 1.9 collective-permute-start.1
  120.0 1.3 collective-permute-start
  121.3 0.1 slice_add_fusion
  121.5 1.1 collective-permute-done.2
  122.6 0.7 collective-permute-done
  123.3 1.2 scatter_fusion
  124.5 72.7 %reduce-scatter.2.cloned.1.call-done = f32[1,224,512]{2,1,0:T(8,128)} async-done(((f32[16,224,512]{2,1,0:T(8,128)}), f32[1,224,512]{2,1,0:T(8,128)}) %reduce-scatter.2.cloned.1.call-update) | async-done | bytes 458768 | tf_op jit(solution)/shard_map/reduce_scatter | solution.py:276
  197.3 1.8 shard_map.228
  (80 shorter events, 1.1 us)
Async XLA Ops:
  7.2 19.9 %copy-start.3 = (f32[256,512]{1,0:T(8,128)S(1)}, f32[256,512]{1,0:T(8,128)}, u32[]{:S(2)}) copy-start(f32[256,512]{1,0:T(8,128)} %refs_6_.1) | copy-start | bytes 1572868
  7.2 18.1 %copy-start.17 = (s32[2,128]{1,0:T(2,128)S(1)}, s32[2,128]{1,0:T(2,128)}, u32[]{:S(2)}) copy-start(s32[2,128]{1,0:T(2,128)} %param.27) | copy-start | bytes 3076
  7.2 18.2 %copy-start.14 = (f32[128,512]{1,0:T(8,128)S(1)}, f32[128,512]{1,0:T(8,128)}, u32[]{:S(2)}) copy-start(f32[128,512]{1,0:T(8,128)} %param.24) | copy-start | bytes 786436
  7.2 19.0 %copy-start.5 = (f32[256,512]{1,0:T(8,128)S(1)}, f32[256,512]{1,0:T(8,128)}, u32[]{:S(2)}) copy-start(f32[256,512]{1,0:T(8,128)} %param.22) | copy-start | bytes 1572868
  7.2 76.4 %all-gather.2.cloned.1.call-start = ((), (), s32[]{:S(2)}) async-start(), calls=%async_computation.1 | async-start | bytes 8077312 | tf_op jit(solution)/shard_map/all_gather | solution.py:222
  9.3 187.9 %reduce-scatter.2.cloned.1.call-start = ((), (), s32[]{:S(2)}) async-start(), calls=%async_computation.2 | async-start | bytes 7798784 | tf_op jit(solution)/shard_map/reduce_scatter | solution.py:276
  12.8 14.2 %collective-permute-start.7 = (f32[1,16,512]{2,1,0:T(8,128)S(1)}, f32[1,16,512]{2,1,0:T(8,128)S(1)}, u32[]{:S(2)}, u32[]{:S(2)}) collective-permute-start(f32[1,16,512]{2,1,0:T(8,128)S(1)} %get-tuple-element.39), channel_id=1, source_target_pairs={{1,0},{2,1},{3,2},{5,4},{6,5},{7,6},{9,8},{10,9},{11,10},{13,12},{... | collective-permute-start | bytes 98312 | tf_op jit(solution)/shard_map/ppermute | solution.py:23
  14.1 12.9 %collective-permute-start.6 = (f32[1,16,512]{2,1,0:T(8,128)S(1)}, f32[1,16,512]{2,1,0:T(8,128)S(1)}, u32[]{:S(2)}, u32[]{:S(2)}) collective-permute-start(f32[1,16,512]{2,1,0:T(8,128)S(1)} %get-tuple-element.40), channel_id=1, source_target_pairs={{0,1},{1,2},{2,3},{4,5},{5,6},{6,7},{8,9},{9,10},{10,11},{12,13},{... | collective-permute-start | bytes 98312 | tf_op jit(solution)/shard_map/ppermute | solution.py:21
  19.7 7.4 %collective-permute-start.5 = (f32[1,16,512]{2,1,0:T(8,128)S(1)}, f32[1,16,512]{2,1,0:T(8,128)S(1)}, u32[]{:S(2)}, u32[]{:S(2)}) collective-permute-start(f32[1,16,512]{2,1,0:T(8,128)S(1)} %get-tuple-element.41), channel_id=1, source_target_pairs={{4,0},{8,4},{12,8},{5,1},{9,5},{13,9},{6,2},{10,6},{14,10},{7,3},{... | collective-permute-start | bytes 98312 | tf_op jit(solution)/shard_map/ppermute | solution.py:23
  21.0 6.1 %collective-permute-start.4 = (f32[1,16,512]{2,1,0:T(8,128)S(1)}, f32[1,16,512]{2,1,0:T(8,128)S(1)}, u32[]{:S(2)}, u32[]{:S(2)}) collective-permute-start(f32[1,16,512]{2,1,0:T(8,128)S(1)} %get-tuple-element.38), channel_id=1, source_target_pairs={{0,4},{4,8},{8,12},{1,5},{5,9},{9,13},{2,6},{6,10},{10,14},{3,7},{... | collective-permute-start | bytes 98312 | tf_op jit(solution)/shard_map/ppermute | solution.py:21
  86.6 1.0 copy-start
  86.6 3.3 %copy-start.2 = (f32[16,32,512]{2,1,0:T(8,128)}, f32[16,32,512]{2,1,0:T(8,128)S(1)}, u32[]{:S(2)}) copy-start(f32[16,32,512]{2,1,0:T(8,128)S(1)} %get-tuple-element.29) | copy-start | bytes 3145732
  86.6 2.9 %copy-start.8 = (f32[256,512]{1,0:T(8,128)S(1)}, f32[256,512]{1,0:T(8,128)}, u32[]{:S(2)}) copy-start(f32[256,512]{1,0:T(8,128)} %param.25) | copy-start | bytes 1572868
  90.2 0.8 copy-start.6
  91.0 2.1 %slice-start = ((f32[16,225,512]{2,1,0:T(8,128)}), f32[16,64,512]{2,1,0:T(8,128)S(1)}, s32[]{:S(2)}) async-start(f32[16,225,512]{2,1,0:T(8,128)} %all-gather.2.cloned.1.call-done), calls=%async_computation.3 | async-start | bytes 4194304 | tf_op jit(solution)/shard_map/slice | solution.py:226
  93.1 1.1 copy-start.4
  94.2 1.0 copy-start.10
  95.2 0.9 copy-start.16
  95.2 1.3 copy-start.1
  95.2 1.4 copy-start.15
  96.6 3.7 %copy-start.13 = (f32[128,512]{1,0:T(8,128)}, f32[128,512]{1,0:T(8,128)S(1)}, u32[]{:S(2)}) copy-start(f32[128,512]{1,0:T(8,128)S(1)} %subtract_multiply_fusion.1.refs_5_) | copy-start | bytes 786436
  107.0 1.9 slice-start.1
  107.0 1.9 copy-start.12
  108.9 12.4 %copy-start.9 = (f32[256,512]{1,0:T(8,128)S(1)}, f32[256,512]{1,0:T(8,128)}, u32[]{:S(2)}) copy-start(f32[256,512]{1,0:T(8,128)} %param.25) | copy-start | bytes 1572868
  108.9 12.4 %copy-start.11 = (f32[256,1024]{1,0:T(8,128)S(1)}, f32[256,1024]{1,0:T(8,128)}, u32[]{:S(2)}) copy-start(f32[256,1024]{1,0:T(8,128)} %copy-done.10) | copy-start | bytes 3145732
  113.8 7.7 %collective-permute-start.3 = (f32[1,16,512]{2,1,0:T(8,128)S(1)}, f32[1,16,512]{2,1,0:T(8,128)S(1)}, u32[]{:S(2)}, u32[]{:S(2)}) collective-permute-start(f32[1,16,512]{2,1,0:T(8,128)S(1)} %get-tuple-element.35), channel_id=1, source_target_pairs={{0,1},{1,2},{2,3},{4,5},{5,6},{6,7},{8,9},{9,10},{10,11},{12,13},{... | collective-permute-start | bytes 98312 | tf_op jit(solution)/shard_map/ppermute | solution.py:21
  116.8 5.8 %collective-permute-start.2 = (f32[1,16,512]{2,1,0:T(8,128)S(1)}, f32[1,16,512]{2,1,0:T(8,128)S(1)}, u32[]{:S(2)}, u32[]{:S(2)}) collective-permute-start(f32[1,16,512]{2,1,0:T(8,128)S(1)} %get-tuple-element.36), channel_id=1, source_target_pairs={{1,0},{2,1},{3,2},{5,4},{6,5},{7,6},{9,8},{10,9},{11,10},{13,12},{... | collective-permute-start | bytes 98312 | tf_op jit(solution)/shard_map/ppermute | solution.py:23
  118.1 4.5 %collective-permute-start.1 = (f32[1,16,512]{2,1,0:T(8,128)S(1)}, f32[1,16,512]{2,1,0:T(8,128)S(1)}, u32[]{:S(2)}, u32[]{:S(2)}) collective-permute-start(f32[1,16,512]{2,1,0:T(8,128)S(1)} %get-tuple-element.37), channel_id=1, source_target_pairs={{0,4},{4,8},{8,12},{1,5},{5,9},{9,13},{2,6},{6,10},{10,14},{3,7},{... | collective-permute-start | bytes 98312 | tf_op jit(solution)/shard_map/ppermute | solution.py:21
  120.0 3.3 %collective-permute-start = (f32[1,16,512]{2,1,0:T(8,128)S(1)}, f32[1,16,512]{2,1,0:T(8,128)S(1)}, u32[]{:S(2)}, u32[]{:S(2)}) collective-permute-start(f32[1,16,512]{2,1,0:T(8,128)S(1)} %get-tuple-element.34), channel_id=1, source_target_pairs={{4,0},{8,4},{12,8},{5,1},{9,5},{13,9},{6,2},{10,6},{14,10},{7,3},{... | collective-permute-start | bytes 98312 | tf_op jit(solution)/shard_map/ppermute | solution.py:23
  124.5 74.5 %copy-start.7 = (f32[256,512]{1,0:T(8,128)}, f32[256,512]{1,0:T(8,128)S(1)}, u32[]{:S(2)}) copy-start(f32[256,512]{1,0:T(8,128)S(1)} %scatter_fusion) | copy-start | bytes 1572868
Sparse Core Ops, SparseCore 0:
  10.9 72.6 all-gather.1
  107.1 90.1 reduce-scatter.1

commit v9 on v8

--- a/solution.py
+++ b/solution.py
@@ -76,12 +76,13 @@
     return high, low
 
 
-def inner_three(left, right):
-    left_high, left_low = split_bf16(left.T)
-    right_high, right_low = split_bf16(right)
+def inner_three(left, right_high, right_low):
+    left_high, left_low = split_bf16(left)
 
     def dot(a, b):
-        return jnp.dot(a, b, preferred_element_type=jnp.float32)
+        return lax.dot_general(
+            a, b, (((0,), (0,)), ((), ())), preferred_element_type=jnp.float32
+        )
 
     return dot(left_high, right_high) + dot(left_low, right_high) + dot(left_high, right_low)
 
@@ -120,9 +121,10 @@
             start, count, scale = layout[index]
             for k in range(start, start + count + 1):
                 loads[k].wait()
-            right = staged[start + count][...]
+            right_high, right_low = split_bf16(staged[start + count][...])
             product = jnp.concatenate(
-                [inner_three(staged[start + k][...], right) for k in range(count)], axis=0
+                [inner_three(staged[start + k][...], right_high, right_low) for k in range(count)],
+                axis=0,
             ) * scale
             results[index][...] = product.reshape(blocks, rows[index], width)
             store = pltpu.make_async_copy(

time: 206 us -> 206 us (level)
  no operation moved by 1% of the time
where the time goes in v9:
time: 206 us
  waiting for transfers between devices  129 us (63%)
  starting transfers between devices  18.8 us (9%)
  between operations  15.9 us (8%)
  local copies, waits for them, and re-layouts  13.8 us (7%)
  other arithmetic  10.7 us (5%)
  Pallas kernels  10.5 us (5%)
  matrix products  7.55 us (4%)
    reduce_scatter x1, waiting for transfers between devices, shards(): lax.psum_scatter(blocked, peers, scatter_dimension=0, tiled=True)[0]  72.7 us
    all_gather x1, waiting for transfers between devices, shards(): gathered = lax.all_gather(packed, peers, axis=0, tiled=True)  54 us
    ppermute x4, starting transfers between devices, padded(): lax.ppermute(tail, axis, [(i, (i + 1) % count) for i in range(ends)])  13.5 us
    pallas_call x1, Pallas kernels, blocked_grads(): pl.pallas_call(kernel, out_shape=jax.ShapeDtypeStruct((blocks, offsets[-1...  6.69 us
    dot_general x4, matrix products, outer_back(): lax.dot_general(left, right, (((1,), (1,)), ((), ())), precision=lax.Prec...  6.28 us
    ppermute x4, starting transfers between devices, padded(): lax.ppermute(head, axis, [((i + 1) % count, i) for i in range(ends)])  5.17 us
    slice x6, local copies, waits for them, and re-layouts, shards(): pieces.append(gathered[:, offset:offset + rows, :])  4.58 us
  transfers between devices with their start and end apart: 10, of which 4 were waited for; matrix products, arithmetic and copies ran while one was open for 7% of the time, Pallas kernels for 0%

profile of v9, /device:TPU:0, one launch (start us, length us, event | category | flops | bytes accessed | tf_op | source)
XLA Modules:
  0.0 205.9 jit_solution(9041533905538855597)
XLA Ops:
  7.3 2.0 shard_map.226
  9.4 0.8 reshape.254
  10.1 0.8 broadcast_in_dim_reshape_squeeze.3
  10.9 1.8 gather_fusion.1
  12.8 1.3 collective-permute-start.7
  14.1 5.6 %collective-permute-start.6 = (f32[1,16,512]{2,1,0:T(8,128)S(1)}, f32[1,16,512]{2,1,0:T(8,128)S(1)}, u32[]{:S(2)}, u32[]{:S(2)}) collective-permute-start(f32[1,16,512]{2,1,0:T(8,128)S(1)} %get-tuple-element.40), channel_id=1, source_target_pairs={{0,1},{1,2},{2,3},{4,5},{5,6},{6,7},{8,9},{9,10},{10,11},{12,13},{... | collective-permute-start | bytes 98312 | tf_op jit(solution)/shard_map/ppermute | solution.py:21
  19.7 1.3 collective-permute-start.5
  21.0 3.0 %collective-permute-start.4 = (f32[1,16,512]{2,1,0:T(8,128)S(1)}, f32[1,16,512]{2,1,0:T(8,128)S(1)}, u32[]{:S(2)}, u32[]{:S(2)}) collective-permute-start(f32[1,16,512]{2,1,0:T(8,128)S(1)} %get-tuple-element.38), channel_id=1, source_target_pairs={{0,4},{4,8},{8,12},{1,5},{5,9},{9,13},{2,6},{6,10},{10,14},{3,7},{... | collective-permute-start | bytes 98312 | tf_op jit(solution)/shard_map/ppermute | solution.py:21
  25.4 0.7 broadcast_maximum_fusion.1.refs_4_
  26.2 0.9 broadcast_maximum_fusion.refs_9_
  27.1 0.8 gather_fusion.3
  27.9 0.8 gather_fusion.2
  28.7 0.9 broadcast_select_fusion
  29.6 54.0 %all-gather.2.cloned.1.call-done = f32[16,225,512]{2,1,0:T(8,128)} async-done(((f32[1,225,512]{2,1,0:T(8,128)}), f32[16,225,512]{2,1,0:T(8,128)}) %all-gather.2.cloned.1.call-update) | async-done | bytes 7372816 | tf_op jit(solution)/shard_map/all_gather | solution.py:224
  83.6 1.0 slice.159
  84.9 1.7 fusion.20
  86.7 1.0 copy-done
  87.6 0.6 fusion.22
  88.2 0.2 multiply_reduce_fusion.3
  88.6 0.7 fusion.23
  89.4 0.2 multiply_reduce_fusion.1
  89.6 0.3 fusion.4
  89.9 0.3 subtract_multiply_fusion.refs_10_
  90.2 0.8 copy-done.6
  91.0 2.1 %convolution_select_fusion.refs_8_ = f32[256,512]{1,0:T(8,128)S(1)} fusion(f32[256,512]{1,0:T(8,128)S(1)} %subtract_multiply_fusion.refs_10_, f32[512,512]{1,0:T(8,128)} %bitcast.71, f32[256,512]{1,0:T(8,128)} %param.22), kind=kOutput, calls=%fused_computation.8 | convolution fusion | flops 402915328 | bytes 2621440 | tf_op jit(solution)/shard_map/dot_general | solution.py:165
  93.1 1.1 fusion.24
  94.2 1.0 copy-done.10
  95.2 0.8 gather_fusion
  96.0 0.1 copy-done.16
  96.1 0.2 fusion.19
  96.4 0.1 subtract_multiply_fusion.1.refs_5_
  96.6 1.4 convolution_select_fusion.1.refs_3_
  98.0 2.2 %scatter_custom_fusion.2.refs_7_ = f32[256,512]{1,0:T(8,128)} fusion(s32[128]{0:T(128)S(1)} %get-tuple-element.42, f32[]{:T(128)} %constant.39.clone.1, f32[128,512]{1,0:T(8,128)S(1)} %get-tuple-element.49, f32[512]{0:T(512)S(1)} %add.152, f32[512]{0:T(512)S(1)} %mul.141, f32[128]{0:T(128)S(1)} %compare_convert_fusion, f32[128]{0:T(128)S(1)} %add_rsqrt_fusion.1, ...), kind=kCustom, calls=%fused_computation.26 | custom fusion | flops 393216 | bytes 792068 | tf_op jit(solution)/shard_map/scatter-add | solution.py:248
  100.2 6.7 %shard_map.227 = f32[16,224,512]{2,1,0:T(8,128)} custom-call(f32[128,512]{1,0:T(8,128)} %refs_0_.3, f32[128,512]{1,0:T(8,128)} %get-tuple-element.55.refs_1_, f32[128,512]{1,0:T(8,128)} %get-tuple-element.54.refs_2_, f32[128,512]{1,0:T(8,128)} %convolution_select_fusion.1.refs_3_, f32[128,512]{1,0:T(8,128)} %broadcast_maximum_fusion.1.refs_4_, ...), custom_call_target="tpu_custom_call" | custom-call | tf_op jit(solution)/shard_map/pallas_call | solution.py:139
  107.0 1.9 slice-done.1
  108.9 1.7 fusion.25
  110.6 0.8 fusion.21
  111.4 2.3 %scatter_custom_fusion = f32[320,512]{1,0:T(8,128)S(1)} fusion(s32[256]{0:T(256)S(1)} %bitcast.77, f32[128,512]{1,0:T(8,128)S(1)} %get-tuple-element.32, f32[]{:T(128)} %constant.77, f32[128,512]{1,0:T(8,128)S(1)} %get-tuple-element.31, f32[]{:T(128)} %constant.39.clone.1), kind=kCustom, calls=%fused_computation.14 | custom fusion | flops 262144 | bytes 1179656 | tf_op jit(solution)/shard_map/add | solution.py:287
  113.7 3.1 %collective-permute-start.3 = (f32[1,16,512]{2,1,0:T(8,128)S(1)}, f32[1,16,512]{2,1,0:T(8,128)S(1)}, u32[]{:S(2)}, u32[]{:S(2)}) collective-permute-start(f32[1,16,512]{2,1,0:T(8,128)S(1)} %get-tuple-element.35), channel_id=1, source_target_pairs={{0,1},{1,2},{2,3},{4,5},{5,6},{6,7},{8,9},{9,10},{10,11},{12,13},{... | collective-permute-start | bytes 98312 | tf_op jit(solution)/shard_map/ppermute | solution.py:21
  116.8 1.3 collective-permute-start.2
  118.1 1.9 collective-permute-start.1
  120.0 1.3 collective-permute-start
  121.3 0.1 slice_add_fusion
  121.5 1.1 collective-permute-done.2
  122.6 0.7 collective-permute-done
  123.3 1.2 scatter_fusion
  124.5 72.7 %reduce-scatter.2.cloned.1.call-done = f32[1,224,512]{2,1,0:T(8,128)} async-done(((f32[16,224,512]{2,1,0:T(8,128)}), f32[1,224,512]{2,1,0:T(8,128)}) %reduce-scatter.2.cloned.1.call-update) | async-done | bytes 458768 | tf_op jit(solution)/shard_map/reduce_scatter | solution.py:278
  197.2 1.8 shard_map.228
  (80 shorter events, 1.1 us)
Async XLA Ops:
  7.2 19.9 %copy-start.3 = (f32[256,512]{1,0:T(8,128)S(1)}, f32[256,512]{1,0:T(8,128)}, u32[]{:S(2)}) copy-start(f32[256,512]{1,0:T(8,128)} %refs_6_.1) | copy-start | bytes 1572868
  7.2 18.1 %copy-start.17 = (s32[2,128]{1,0:T(2,128)S(1)}, s32[2,128]{1,0:T(2,128)}, u32[]{:S(2)}) copy-start(s32[2,128]{1,0:T(2,128)} %param.27) | copy-start | bytes 3076
  7.2 18.2 %copy-start.14 = (f32[128,512]{1,0:T(8,128)S(1)}, f32[128,512]{1,0:T(8,128)}, u32[]{:S(2)}) copy-start(f32[128,512]{1,0:T(8,128)} %param.24) | copy-start | bytes 786436
  7.2 19.0 %copy-start.5 = (f32[256,512]{1,0:T(8,128)S(1)}, f32[256,512]{1,0:T(8,128)}, u32[]{:S(2)}) copy-start(f32[256,512]{1,0:T(8,128)} %param.22) | copy-start | bytes 1572868
  7.2 76.4 %all-gather.2.cloned.1.call-start = ((), (), s32[]{:S(2)}) async-start(), calls=%async_computation.1 | async-start | bytes 8077312 | tf_op jit(solution)/shard_map/all_gather | solution.py:224
  9.3 187.9 %reduce-scatter.2.cloned.1.call-start = ((), (), s32[]{:S(2)}) async-start(), calls=%async_computation.2 | async-start | bytes 7798784 | tf_op jit(solution)/shard_map/reduce_scatter | solution.py:278
  12.8 14.2 %collective-permute-start.7 = (f32[1,16,512]{2,1,0:T(8,128)S(1)}, f32[1,16,512]{2,1,0:T(8,128)S(1)}, u32[]{:S(2)}, u32[]{:S(2)}) collective-permute-start(f32[1,16,512]{2,1,0:T(8,128)S(1)} %get-tuple-element.39), channel_id=1, source_target_pairs={{1,0},{2,1},{3,2},{5,4},{6,5},{7,6},{9,8},{10,9},{11,10},{13,12},{... | collective-permute-start | bytes 98312 | tf_op jit(solution)/shard_map/ppermute | solution.py:23
  14.1 12.9 %collective-permute-start.6 = (f32[1,16,512]{2,1,0:T(8,128)S(1)}, f32[1,16,512]{2,1,0:T(8,128)S(1)}, u32[]{:S(2)}, u32[]{:S(2)}) collective-permute-start(f32[1,16,512]{2,1,0:T(8,128)S(1)} %get-tuple-element.40), channel_id=1, source_target_pairs={{0,1},{1,2},{2,3},{4,5},{5,6},{6,7},{8,9},{9,10},{10,11},{12,13},{... | collective-permute-start | bytes 98312 | tf_op jit(solution)/shard_map/ppermute | solution.py:21
  19.7 7.4 %collective-permute-start.5 = (f32[1,16,512]{2,1,0:T(8,128)S(1)}, f32[1,16,512]{2,1,0:T(8,128)S(1)}, u32[]{:S(2)}, u32[]{:S(2)}) collective-permute-start(f32[1,16,512]{2,1,0:T(8,128)S(1)} %get-tuple-element.41), channel_id=1, source_target_pairs={{4,0},{8,4},{12,8},{5,1},{9,5},{13,9},{6,2},{10,6},{14,10},{7,3},{... | collective-permute-start | bytes 98312 | tf_op jit(solution)/shard_map/ppermute | solution.py:23
  21.0 6.1 %collective-permute-start.4 = (f32[1,16,512]{2,1,0:T(8,128)S(1)}, f32[1,16,512]{2,1,0:T(8,128)S(1)}, u32[]{:S(2)}, u32[]{:S(2)}) collective-permute-start(f32[1,16,512]{2,1,0:T(8,128)S(1)} %get-tuple-element.38), channel_id=1, source_target_pairs={{0,4},{4,8},{8,12},{1,5},{5,9},{9,13},{2,6},{6,10},{10,14},{3,7},{... | collective-permute-start | bytes 98312 | tf_op jit(solution)/shard_map/ppermute | solution.py:21
  86.6 1.0 copy-start
  86.6 3.3 %copy-start.2 = (f32[16,32,512]{2,1,0:T(8,128)}, f32[16,32,512]{2,1,0:T(8,128)S(1)}, u32[]{:S(2)}) copy-start(f32[16,32,512]{2,1,0:T(8,128)S(1)} %get-tuple-element.29) | copy-start | bytes 3145732
  86.6 2.9 %copy-start.8 = (f32[256,512]{1,0:T(8,128)S(1)}, f32[256,512]{1,0:T(8,128)}, u32[]{:S(2)}) copy-start(f32[256,512]{1,0:T(8,128)} %param.25) | copy-start | bytes 1572868
  90.2 0.8 copy-start.6
  91.0 2.1 %slice-start = ((f32[16,225,512]{2,1,0:T(8,128)}), f32[16,64,512]{2,1,0:T(8,128)S(1)}, s32[]{:S(2)}) async-start(f32[16,225,512]{2,1,0:T(8,128)} %all-gather.2.cloned.1.call-done), calls=%async_computation.3 | async-start | bytes 4194304 | tf_op jit(solution)/shard_map/slice | solution.py:228
  93.1 1.1 copy-start.4
  94.2 1.0 copy-start.10
  95.2 0.9 copy-start.16
  95.2 1.3 copy-start.1
  95.2 1.4 copy-start.15
  96.6 3.7 %copy-start.13 = (f32[128,512]{1,0:T(8,128)}, f32[128,512]{1,0:T(8,128)S(1)}, u32[]{:S(2)}) copy-start(f32[128,512]{1,0:T(8,128)S(1)} %subtract_multiply_fusion.1.refs_5_) | copy-start | bytes 786436
  107.0 1.9 slice-start.1
  107.0 1.9 copy-start.12
  108.9 12.4 %copy-start.9 = (f32[256,512]{1,0:T(8,128)S(1)}, f32[256,512]{1,0:T(8,128)}, u32[]{:S(2)}) copy-start(f32[256,512]{1,0:T(8,128)} %param.25) | copy-start | bytes 1572868
  108.9 12.4 %copy-start.11 = (f32[256,1024]{1,0:T(8,128)S(1)}, f32[256,1024]{1,0:T(8,128)}, u32[]{:S(2)}) copy-start(f32[256,1024]{1,0:T(8,128)} %copy-done.10) | copy-start | bytes 3145732
  113.7 7.7 %collective-permute-start.3 = (f32[1,16,512]{2,1,0:T(8,128)S(1)}, f32[1,16,512]{2,1,0:T(8,128)S(1)}, u32[]{:S(2)}, u32[]{:S(2)}) collective-permute-start(f32[1,16,512]{2,1,0:T(8,128)S(1)} %get-tuple-element.35), channel_id=1, source_target_pairs={{0,1},{1,2},{2,3},{4,5},{5,6},{6,7},{8,9},{9,10},{10,11},{12,13},{... | collective-permute-start | bytes 98312 | tf_op jit(solution)/shard_map/ppermute | solution.py:21
  116.8 5.8 %collective-permute-start.2 = (f32[1,16,512]{2,1,0:T(8,128)S(1)}, f32[1,16,512]{2,1,0:T(8,128)S(1)}, u32[]{:S(2)}, u32[]{:S(2)}) collective-permute-start(f32[1,16,512]{2,1,0:T(8,128)S(1)} %get-tuple-element.36), channel_id=1, source_target_pairs={{1,0},{2,1},{3,2},{5,4},{6,5},{7,6},{9,8},{10,9},{11,10},{13,12},{... | collective-permute-start | bytes 98312 | tf_op jit(solution)/shard_map/ppermute | solution.py:23
  118.1 4.5 %collective-permute-start.1 = (f32[1,16,512]{2,1,0:T(8,128)S(1)}, f32[1,16,512]{2,1,0:T(8,128)S(1)}, u32[]{:S(2)}, u32[]{:S(2)}) collective-permute-start(f32[1,16,512]{2,1,0:T(8,128)S(1)} %get-tuple-element.37), channel_id=1, source_target_pairs={{0,4},{4,8},{8,12},{1,5},{5,9},{9,13},{2,6},{6,10},{10,14},{3,7},{... | collective-permute-start | bytes 98312 | tf_op jit(solution)/shard_map/ppermute | solution.py:21
  120.0 3.3 %collective-permute-start = (f32[1,16,512]{2,1,0:T(8,128)S(1)}, f32[1,16,512]{2,1,0:T(8,128)S(1)}, u32[]{:S(2)}, u32[]{:S(2)}) collective-permute-start(f32[1,16,512]{2,1,0:T(8,128)S(1)} %get-tuple-element.34), channel_id=1, source_target_pairs={{4,0},{8,4},{12,8},{5,1},{9,5},{13,9},{6,2},{10,6},{14,10},{7,3},{... | collective-permute-start | bytes 98312 | tf_op jit(solution)/shard_map/ppermute | solution.py:23
  124.5 74.5 %copy-start.7 = (f32[256,512]{1,0:T(8,128)}, f32[256,512]{1,0:T(8,128)S(1)}, u32[]{:S(2)}) copy-start(f32[256,512]{1,0:T(8,128)S(1)} %scatter_fusion) | copy-start | bytes 1572868
Sparse Core Ops, SparseCore 0:
  10.9 72.6 all-gather.1
  107.1 90.0 reduce-scatter.1

commit v10 on v9

--- a/solution.py
+++ b/solution.py
@@ -88,20 +88,18 @@
 
 
 def blocked_grads(edge_terms, node_terms, blocks, edge_scale, node_scale):
-    terms = [(pieces, right, edge_scale) for pieces, right in edge_terms] + [
-        (pieces, right, node_scale) for pieces, right in node_terms
-    ]
-    rows = [sum(p.shape[1] for p in pieces) // blocks for pieces, _, _ in terms]
+    terms = [(pairs, edge_scale) for pairs in edge_terms] + [(pairs, node_scale) for pairs in node_terms]
+    rows = [sum(left.shape[1] for left, _ in pairs) // blocks for pairs, _ in terms]
     offsets = row_offsets(rows)
     inputs = []
     layout = []
-    for pieces, right, scale in terms:
-        layout.append((len(inputs), len(pieces), scale))
-        inputs.extend(pieces)
-        inputs.append(right)
-    width = terms[0][1].shape[1]
-
-    order = sorted(range(len(terms)), key=lambda index: -rows[index] * terms[index][1].shape[0])
+    for pairs, scale in terms:
+        layout.append((len(inputs), len(pairs), scale))
+        for pair in pairs:
+            inputs.extend(pair)
+    width = terms[0][0][0][1].shape[1]
+
+    order = sorted(range(len(terms)), key=lambda index: -rows[index] * terms[index][0][0][0].shape[0])
     count_in = len(inputs)
 
     def kernel(*refs):
@@ -119,13 +117,13 @@
         stores = []
         for index in order:
             start, count, scale = layout[index]
-            for k in range(start, start + count + 1):
+            for k in range(start, start + 2 * count):
                 loads[k].wait()
-            right_high, right_low = split_bf16(staged[start + count][...])
-            product = jnp.concatenate(
-                [inner_three(staged[start + k][...], right_high, right_low) for k in range(count)],
-                axis=0,
-            ) * scale
+            pieces = []
+            for k in range(count):
+                right_high, right_low = split_bf16(staged[start + 2 * k + 1][...])
+                pieces.append(inner_three(staged[start + 2 * k][...], right_high, right_low))
+            product = jnp.concatenate(pieces, axis=0) * scale
             results[index][...] = product.reshape(blocks, rows[index], width)
             store = pltpu.make_async_copy(
                 results[index], out.at[:, offsets[index] : offsets[index + 1], :], out_sems.at[index]
@@ -245,13 +243,15 @@
     edge_act = jnp.maximum(edge_pre, 0.0)
     edge_normed, edge_inverse = layer_norm(matmul(edge_act, full_edge_second) + full_edge_bias)
     message = (edge_normed * full_edge_gain + full_edge_shift) * live_edges
-    aggregate = jax.ops.segment_sum(message, target, node_rows)
     node_act = jnp.maximum(node_pre, 0.0)
     node_normed, node_inverse = layer_norm(matmul(node_act, full_node_second) + full_node_bias)
     node_upstream = node_cotangent * live_nodes
     node_grad_z = norm_back(node_upstream * full_node_gain, node_normed, node_inverse)
     node_grad_pre = outer_back(node_grad_z, full_node_second) * (node_pre > 0).astype(jnp.float32)
-    node_terms = [([node_states, aggregate], node_grad_pre), ([node_act], node_grad_z)]
+    node_terms = [
+        [(node_states, node_grad_pre), (message, jnp.take(node_grad_pre, target, axis=0))],
+        [(node_act, node_grad_z)],
+    ]
     node_grad_input = outer_back(node_grad_pre, full_node_first)
     state_grads = node_upstream + node_grad_input[:, :width]
     edge_upstream = (
@@ -262,15 +262,16 @@
     extended = jnp.concatenate([node_states, ghosts], axis=0)
     sent = jnp.take(extended, source, axis=0)
     received = jnp.take(extended, target, axis=0)
-    edge_terms = [([edge_states, sent, received], edge_grad_pre), ([edge_act], edge_grad_z)]
+    edge_terms = [
+        [(edge_states, edge_grad_pre), (sent, edge_grad_pre), (received, edge_grad_pre)],
+        [(edge_act, edge_grad_z)],
+    ]
     if all(m.shape[0] % 8 == 0 for m in matrices):
         blocked = blocked_grads(edge_terms, node_terms, peer_count, edge_scale, node_scale)
     else:
         parts = [
-            jnp.concatenate([inner(p, right) for p in pieces], axis=0) * scale
-            for (pieces, right), scale in zip(
-                edge_terms + node_terms, [edge_scale] * 2 + [node_scale] * 2
-            )
+            jnp.concatenate([inner(left, right) for left, right in pairs], axis=0) * scale
+            for pairs, scale in zip(edge_terms + node_terms, [edge_scale] * 2 + [node_scale] * 2)
         ]
         blocked = jnp.concatenate(
             [part.reshape(peer_count, -1, width) for part in parts], axis=1

time: 206 us -> 206 us (level)
    scatter-add x1 -> x0, other arithmetic: 2.23 us -> none  [shards(): aggregate = jax.ops.segment_sum(message, target, node_rows)]
where the time goes in v10:
time: 206 us; the launch traced here: 205 us
  waiting for transfers between devices  129 us (63%)
  starting transfers between devices  18.8 us (9%)
  between operations  15.9 us (8%)
  local copies, waits for them, and re-layouts  14.4 us (7%)
  Pallas kernels  10.7 us (5%)
  other arithmetic  9.18 us (4%)
  matrix products  7.56 us (4%)
    reduce_scatter x1, waiting for transfers between devices, shards(): lax.psum_scatter(blocked, peers, scatter_dimension=0, tiled=True)[0]  72.6 us
    all_gather x1, waiting for transfers between devices, shards(): gathered = lax.all_gather(packed, peers, axis=0, tiled=True)  54.1 us
    ppermute x4, starting transfers between devices, padded(): lax.ppermute(tail, axis, [(i, (i + 1) % count) for i in range(ends)])  13.5 us
    pallas_call x1, Pallas kernels, blocked_grads(): pl.pallas_call(kernel, out_shape=jax.ShapeDtypeStruct((blocks, offsets[-1...  6.92 us
    dot_general x4, matrix products, outer_back(): lax.dot_general(left, right, (((1,), (1,)), ((), ())), precision=lax.Prec...  6.29 us
    ppermute x4, starting transfers between devices, padded(): lax.ppermute(head, axis, [((i + 1) % count, i) for i in range(ends)])  5.17 us
    slice x6, local copies, waits for them, and re-layouts, shards(): pieces.append(gathered[:, offset:offset + rows, :])  4.58 us
  transfers between devices with their start and end apart: 10, of which 4 were waited for; matrix products, arithmetic and copies ran while one was open for 7% of the time, Pallas kernels for 0%

profile of v10, /device:TPU:0, one launch (start us, length us, event | category | flops | bytes accessed | tf_op | source)
XLA Modules:
  0.0 205.2 jit_solution(9378156836526177178)
XLA Ops:
  7.3 2.0 shard_map.226
  9.4 0.8 reshape.233
  10.1 0.8 broadcast_in_dim_reshape_squeeze.3
  10.9 1.8 gather_fusion
  12.8 1.3 collective-permute-start.7
  14.1 5.6 %collective-permute-start.6 = (f32[1,16,512]{2,1,0:T(8,128)S(1)}, f32[1,16,512]{2,1,0:T(8,128)S(1)}, u32[]{:S(2)}, u32[]{:S(2)}) collective-permute-start(f32[1,16,512]{2,1,0:T(8,128)S(1)} %get-tuple-element.44), channel_id=1, source_target_pairs={{0,1},{1,2},{2,3},{4,5},{5,6},{6,7},{8,9},{9,10},{10,11},{12,13},{... | collective-permute-start | bytes 98312 | tf_op jit(solution)/shard_map/ppermute | solution.py:21
  19.7 1.3 collective-permute-start.5
  21.0 3.0 %collective-permute-start.4 = (f32[1,16,512]{2,1,0:T(8,128)S(1)}, f32[1,16,512]{2,1,0:T(8,128)S(1)}, u32[]{:S(2)}, u32[]{:S(2)}) collective-permute-start(f32[1,16,512]{2,1,0:T(8,128)S(1)} %get-tuple-element.42), channel_id=1, source_target_pairs={{0,4},{4,8},{8,12},{1,5},{5,9},{9,13},{2,6},{6,10},{10,14},{3,7},{... | collective-permute-start | bytes 98312 | tf_op jit(solution)/shard_map/ppermute | solution.py:21
  25.4 0.7 broadcast_maximum_fusion.1.refs_6_
  26.1 0.9 broadcast_maximum_fusion.refs_12_
  27.1 0.8 gather_fusion.3
  27.9 0.8 gather_fusion.2
  28.6 0.9 broadcast_select_fusion.1
  29.5 54.1 %all-gather.2.cloned.1.call-done = f32[16,225,512]{2,1,0:T(8,128)} async-done(((f32[1,225,512]{2,1,0:T(8,128)}), f32[16,225,512]{2,1,0:T(8,128)}) %all-gather.2.cloned.1.call-update) | async-done | bytes 7372816 | tf_op jit(solution)/shard_map/all_gather | solution.py:222
  83.6 1.0 slice.161
  84.7 0.1 slice_reduce_fusion
  84.9 1.7 fusion.12
  86.6 1.0 copy-done.1
  87.6 0.6 fusion.14
  88.2 0.2 multiply_reduce_fusion.3
  88.6 0.7 fusion.15
  89.4 0.2 multiply_reduce_fusion.1
  89.6 0.3 fusion.4
  89.9 0.3 subtract_multiply_fusion.refs_13_
  90.2 0.8 copy-done.7
  91.0 2.1 %convolution_select_fusion.refs_9_ = f32[256,512]{1,0:T(8,128)S(1)} fusion(f32[256,512]{1,0:T(8,128)S(1)} %subtract_multiply_fusion.refs_13_, f32[512,512]{1,0:T(8,128)} %bitcast.65, f32[256,512]{1,0:T(8,128)} %param.24), kind=kOutput, calls=%fused_computation.8 | convolution fusion | flops 402915328 | bytes 2621440 | tf_op jit(solution)/shard_map/dot_general | solution.py:163
  93.1 1.1 fusion.16
  94.2 1.0 copy-done.11
  95.3 0.8 gather_fusion.4
  96.0 0.8 gather_fusion.1
  96.9 1.0 fusion.10
  97.9 0.1 subtract_multiply_fusion.1.refs_7_
  98.0 1.4 convolution_select_fusion.1.refs_1_.refs_3_.refs_5_
  99.4 6.9 %shard_map.227 = f32[16,224,512]{2,1,0:T(8,128)} custom-call(f32[128,512]{1,0:T(8,128)} %refs_0_.3, f32[128,512]{1,0:T(8,128)} %convolution_select_fusion.1.refs_1_.refs_3_.refs_5_, f32[128,512]{1,0:T(8,128)} %get-tuple-element.60.refs_2_, f32[128,512]{1,0:T(8,128)} %convolution_select_fusion.1.refs_1_.refs_3_.refs_5_, ...), custom_call_target="tpu_custom_call" | custom-call | tf_op jit(solution)/shard_map/pallas_call | solution.py:137
  106.4 1.9 slice-done.1
  108.3 1.7 fusion.17
  110.0 0.8 fusion.13
  110.8 2.3 %scatter_custom_fusion = f32[320,512]{1,0:T(8,128)S(1)} fusion(s32[256]{0:T(256)S(1)} %bitcast.71, f32[128,512]{1,0:T(8,128)S(1)} %get-tuple-element.35, f32[]{:T(128)} %constant.75, f32[128,512]{1,0:T(8,128)S(1)} %get-tuple-element.34, f32[]{:T(128)} %constant.37.clone.1), kind=kCustom, calls=%fused_computation.14 | custom fusion | flops 262144 | bytes 1179656 | tf_op jit(solution)/shard_map/add | solution.py:288
  113.1 3.0 %collective-permute-start.3 = (f32[1,16,512]{2,1,0:T(8,128)S(1)}, f32[1,16,512]{2,1,0:T(8,128)S(1)}, u32[]{:S(2)}, u32[]{:S(2)}) collective-permute-start(f32[1,16,512]{2,1,0:T(8,128)S(1)} %get-tuple-element.38), channel_id=1, source_target_pairs={{0,1},{1,2},{2,3},{4,5},{5,6},{6,7},{8,9},{9,10},{10,11},{12,13},{... | collective-permute-start | bytes 98312 | tf_op jit(solution)/shard_map/ppermute | solution.py:21
  116.2 1.3 collective-permute-start.2
  117.5 1.9 collective-permute-start.1
  119.4 1.3 collective-permute-start
  120.7 0.1 slice_add_fusion
  120.9 1.1 collective-permute-done.2
  122.0 0.7 collective-permute-done
  122.7 1.2 scatter_fusion
  123.9 72.6 %reduce-scatter.2.cloned.1.call-done = f32[1,224,512]{2,1,0:T(8,128)} async-done(((f32[16,224,512]{2,1,0:T(8,128)}), f32[1,224,512]{2,1,0:T(8,128)}) %reduce-scatter.2.cloned.1.call-update) | async-done | bytes 458768 | tf_op jit(solution)/shard_map/reduce_scatter | solution.py:279
  196.5 1.8 shard_map.228
  (79 shorter events, 1.0 us)
Async XLA Ops:
  7.2 19.9 %copy-start.4 = (f32[256,512]{1,0:T(8,128)S(1)}, f32[256,512]{1,0:T(8,128)}, u32[]{:S(2)}) copy-start(f32[256,512]{1,0:T(8,128)} %refs_8_.1) | copy-start | bytes 1572868
  7.2 18.1 %copy-start.17 = (s32[2,128]{1,0:T(2,128)S(1)}, s32[2,128]{1,0:T(2,128)}, u32[]{:S(2)}) copy-start(s32[2,128]{1,0:T(2,128)} %param.29) | copy-start | bytes 3076
  7.2 18.2 %copy-start.14 = (f32[128,512]{1,0:T(8,128)S(1)}, f32[128,512]{1,0:T(8,128)}, u32[]{:S(2)}) copy-start(f32[128,512]{1,0:T(8,128)} %param.26) | copy-start | bytes 786436
  7.2 18.9 %copy-start.6 = (f32[256,512]{1,0:T(8,128)S(1)}, f32[256,512]{1,0:T(8,128)}, u32[]{:S(2)}) copy-start(f32[256,512]{1,0:T(8,128)} %param.24) | copy-start | bytes 1572868
  7.2 76.4 %all-gather.2.cloned.1.call-start = ((), (), s32[]{:S(2)}) async-start(), calls=%async_computation.1 | async-start | bytes 8077312 | tf_op jit(solution)/shard_map/all_gather | solution.py:222
  9.3 187.2 %reduce-scatter.2.cloned.1.call-start = ((), (), s32[]{:S(2)}) async-start(), calls=%async_computation.2 | async-start | bytes 7798784 | tf_op jit(solution)/shard_map/reduce_scatter | solution.py:279
  12.8 14.2 %collective-permute-start.7 = (f32[1,16,512]{2,1,0:T(8,128)S(1)}, f32[1,16,512]{2,1,0:T(8,128)S(1)}, u32[]{:S(2)}, u32[]{:S(2)}) collective-permute-start(f32[1,16,512]{2,1,0:T(8,128)S(1)} %get-tuple-element.43), channel_id=1, source_target_pairs={{1,0},{2,1},{3,2},{5,4},{6,5},{7,6},{9,8},{10,9},{11,10},{13,12},{... | collective-permute-start | bytes 98312 | tf_op jit(solution)/shard_map/ppermute | solution.py:23
  14.1 12.9 %collective-permute-start.6 = (f32[1,16,512]{2,1,0:T(8,128)S(1)}, f32[1,16,512]{2,1,0:T(8,128)S(1)}, u32[]{:S(2)}, u32[]{:S(2)}) collective-permute-start(f32[1,16,512]{2,1,0:T(8,128)S(1)} %get-tuple-element.44), channel_id=1, source_target_pairs={{0,1},{1,2},{2,3},{4,5},{5,6},{6,7},{8,9},{9,10},{10,11},{12,13},{... | collective-permute-start | bytes 98312 | tf_op jit(solution)/shard_map/ppermute | solution.py:21
  19.7 7.3 %collective-permute-start.5 = (f32[1,16,512]{2,1,0:T(8,128)S(1)}, f32[1,16,512]{2,1,0:T(8,128)S(1)}, u32[]{:S(2)}, u32[]{:S(2)}) collective-permute-start(f32[1,16,512]{2,1,0:T(8,128)S(1)} %get-tuple-element.45), channel_id=1, source_target_pairs={{4,0},{8,4},{12,8},{5,1},{9,5},{13,9},{6,2},{10,6},{14,10},{7,3},{... | collective-permute-start | bytes 98312 | tf_op jit(solution)/shard_map/ppermute | solution.py:23
  21.0 6.0 %collective-permute-start.4 = (f32[1,16,512]{2,1,0:T(8,128)S(1)}, f32[1,16,512]{2,1,0:T(8,128)S(1)}, u32[]{:S(2)}, u32[]{:S(2)}) collective-permute-start(f32[1,16,512]{2,1,0:T(8,128)S(1)} %get-tuple-element.42), channel_id=1, source_target_pairs={{0,4},{4,8},{8,12},{1,5},{5,9},{9,13},{2,6},{6,10},{10,14},{3,7},{... | collective-permute-start | bytes 98312 | tf_op jit(solution)/shard_map/ppermute | solution.py:21
  86.6 1.0 copy-start.1
  86.6 3.3 %copy-start.3 = (f32[16,32,512]{2,1,0:T(8,128)}, f32[16,32,512]{2,1,0:T(8,128)S(1)}, u32[]{:S(2)}) copy-start(f32[16,32,512]{2,1,0:T(8,128)S(1)} %get-tuple-element.32) | copy-start | bytes 3145732
  86.6 3.0 %copy-start.9 = (f32[256,512]{1,0:T(8,128)S(1)}, f32[256,512]{1,0:T(8,128)}, u32[]{:S(2)}) copy-start(f32[256,512]{1,0:T(8,128)} %param.27) | copy-start | bytes 1572868
  90.2 0.8 copy-start.7
  91.0 2.1 %slice-start = ((f32[16,225,512]{2,1,0:T(8,128)}), f32[16,64,512]{2,1,0:T(8,128)S(1)}, s32[]{:S(2)}) async-start(f32[16,225,512]{2,1,0:T(8,128)} %all-gather.2.cloned.1.call-done), calls=%async_computation.3 | async-start | bytes 4194304 | tf_op jit(solution)/shard_map/slice | solution.py:226
  93.1 2.1 %copy-start = (f32[256,512]{1,0:T(8,128)}, f32[256,512]{1,0:T(8,128)S(1)}, u32[]{:S(2)}) copy-start(f32[256,512]{1,0:T(8,128)S(1)} %convolution_select_fusion.refs_9_) | copy-start | bytes 1572868
  94.2 1.0 copy-start.11
  95.2 1.7 copy-start.16
  95.3 2.8 %copy-start.2 = (f32[16,32,512]{2,1,0:T(8,128)S(1)}, f32[16,32,512]{2,1,0:T(8,128)}, u32[]{:S(2)}) copy-start(f32[16,32,512]{2,1,0:T(8,128)} %copy-done.1) | copy-start | bytes 3145732
  95.3 2.8 %copy-start.15 = (f32[128,512]{1,0:T(8,128)S(1)}, f32[128,512]{1,0:T(8,128)}, u32[]{:S(2)}) copy-start(f32[128,512]{1,0:T(8,128)} %param.26) | copy-start | bytes 786436
  98.0 1.4 copy-start.13
  106.4 1.9 slice-start.1
  106.4 1.9 copy-start.5
  108.3 12.4 %copy-start.10 = (f32[256,512]{1,0:T(8,128)S(1)}, f32[256,512]{1,0:T(8,128)}, u32[]{:S(2)}) copy-start(f32[256,512]{1,0:T(8,128)} %param.27) | copy-start | bytes 1572868
  108.3 12.4 %copy-start.12 = (f32[256,1024]{1,0:T(8,128)S(1)}, f32[256,1024]{1,0:T(8,128)}, u32[]{:S(2)}) copy-start(f32[256,1024]{1,0:T(8,128)} %copy-done.11) | copy-start | bytes 3145732
  113.1 7.7 %collective-permute-start.3 = (f32[1,16,512]{2,1,0:T(8,128)S(1)}, f32[1,16,512]{2,1,0:T(8,128)S(1)}, u32[]{:S(2)}, u32[]{:S(2)}) collective-permute-start(f32[1,16,512]{2,1,0:T(8,128)S(1)} %get-tuple-element.38), channel_id=1, source_target_pairs={{0,1},{1,2},{2,3},{4,5},{5,6},{6,7},{8,9},{9,10},{10,11},{12,13},{... | collective-permute-start | bytes 98312 | tf_op jit(solution)/shard_map/ppermute | solution.py:21
  116.2 5.8 %collective-permute-start.2 = (f32[1,16,512]{2,1,0:T(8,128)S(1)}, f32[1,16,512]{2,1,0:T(8,128)S(1)}, u32[]{:S(2)}, u32[]{:S(2)}) collective-permute-start(f32[1,16,512]{2,1,0:T(8,128)S(1)} %get-tuple-element.39), channel_id=1, source_target_pairs={{1,0},{2,1},{3,2},{5,4},{6,5},{7,6},{9,8},{10,9},{11,10},{13,12},{... | collective-permute-start | bytes 98312 | tf_op jit(solution)/shard_map/ppermute | solution.py:23
  117.5 4.5 %collective-permute-start.1 = (f32[1,16,512]{2,1,0:T(8,128)S(1)}, f32[1,16,512]{2,1,0:T(8,128)S(1)}, u32[]{:S(2)}, u32[]{:S(2)}) collective-permute-start(f32[1,16,512]{2,1,0:T(8,128)S(1)} %get-tuple-element.40), channel_id=1, source_target_pairs={{0,4},{4,8},{8,12},{1,5},{5,9},{9,13},{2,6},{6,10},{10,14},{3,7},{... | collective-permute-start | bytes 98312 | tf_op jit(solution)/shard_map/ppermute | solution.py:21
  119.4 3.3 %collective-permute-start = (f32[1,16,512]{2,1,0:T(8,128)S(1)}, f32[1,16,512]{2,1,0:T(8,128)S(1)}, u32[]{:S(2)}, u32[]{:S(2)}) collective-permute-start(f32[1,16,512]{2,1,0:T(8,128)S(1)} %get-tuple-element.37), channel_id=1, source_target_pairs={{4,0},{8,4},{12,8},{5,1},{9,5},{13,9},{6,2},{10,6},{14,10},{7,3},{... | collective-permute-start | bytes 98312 | tf_op jit(solution)/shard_map/ppermute | solution.py:23
  123.9 74.4 %copy-start.8 = (f32[256,512]{1,0:T(8,128)}, f32[256,512]{1,0:T(8,128)S(1)}, u32[]{:S(2)}) copy-start(f32[256,512]{1,0:T(8,128)S(1)} %scatter_fusion) | copy-start | bytes 1572868
Sparse Core Ops, SparseCore 0:
  10.9 72.6 all-gather.1
  106.5 90.0 reduce-scatter.1

commit v11 on v10

--- a/solution.py
+++ b/solution.py
@@ -252,11 +252,8 @@
         [(node_states, node_grad_pre), (message, jnp.take(node_grad_pre, target, axis=0))],
         [(node_act, node_grad_z)],
     ]
-    node_grad_input = outer_back(node_grad_pre, full_node_first)
-    state_grads = node_upstream + node_grad_input[:, :width]
-    edge_upstream = (
-        edge_cotangent + jnp.take(node_grad_input[:, width:], target, axis=0)
-    ) * live_edges
+    aggregate_grads = outer_back(node_grad_pre, full_node_first[width:])
+    edge_upstream = (edge_cotangent + jnp.take(aggregate_grads, target, axis=0)) * live_edges
     edge_grad_z = norm_back(edge_upstream * full_edge_gain, edge_normed, edge_inverse)
     edge_grad_pre = outer_back(edge_grad_z, full_edge_second) * (edge_pre > 0).astype(jnp.float32)
     extended = jnp.concatenate([node_states, ghosts], axis=0)
@@ -276,7 +273,9 @@
         blocked = jnp.concatenate(
             [part.reshape(peer_count, -1, width) for part in parts], axis=1
         )
+    blocked, late_grad_pre = lax.optimization_barrier((blocked, node_grad_pre))
     reduced = lax.psum_scatter(blocked, peers, scatter_dimension=0, tiled=True)[0]
+    state_grads = node_upstream + outer_back(late_grad_pre, full_node_first[:width])
     edge_first_grad, edge_second_grad, node_first_grad, node_second_grad = split_rows(
         reduced, [m.shape[0] for m in matrices]
     )

time: 206 us -> 209 us (1.015)
  waiting for transfers between devices: 129 us -> 121 us
  other arithmetic: 9.18 us -> 16.7 us
  local copies, waits for them, and re-layouts: 14.4 us -> 17.1 us
    reduce_scatter x1, waiting for transfers between devices: 72.6 us -> 68.3 us  [shards(): lax.psum_scatter(blocked, peers, scatter_dimension=0, tiled=True)[0]]
    reduce_sum x2, other arithmetic: 1.27 us -> 3.41 us  [norm_back(): first = jnp.mean(upstream, axis=-1, keepdims=True)]
    slice x6 -> x3, local copies, waits for them, and re-layouts: 4.58 us -> 5.02 us  [shards(): pieces.append(gathered[:, offset:offset + rows, :])]
    dot_general x4 -> x5, matrix products: 6.29 us -> 6.14 us  [outer_back(): lax.dot_general(left, right, (((1,), (1,)), ((), ())), precision=lax.Prec...]
  transfers between devices with their start and end apart: 10 -> 10, of which waited for: 4 -> 3; matrix products, arithmetic and copies ran while one was open for 7% -> 11% of each run, Pallas kernels for 0% -> 0%
where the time goes in v11:
time: 209 us; the launch traced here: 208 us
  waiting for transfers between devices  121 us (58%)
  starting transfers between devices  19.5 us (9%)
  local copies, waits for them, and re-layouts  17.1 us (8%)
  other arithmetic  16.7 us (8%)
  between operations  15.8 us (8%)
  Pallas kernels  10.6 us (5%)
  matrix products  7.35 us (4%)
    reduce_scatter x1, waiting for transfers between devices, shards(): lax.psum_scatter(blocked, peers, scatter_dimension=0, tiled=True)[0]  68.3 us
    all_gather x1, waiting for transfers between devices, shards(): gathered = lax.all_gather(packed, peers, axis=0, tiled=True)  52.7 us
    ppermute x4, starting transfers between devices, padded(): lax.ppermute(tail, axis, [(i, (i + 1) % count) for i in range(ends)])  14.2 us
    pallas_call x1, Pallas kernels, blocked_grads(): pl.pallas_call(kernel, out_shape=jax.ShapeDtypeStruct((blocks, offsets[-1...  6.88 us
    dot_general x5, matrix products, outer_back(): lax.dot_general(left, right, (((1,), (1,)), ((), ())), precision=lax.Prec...  6.14 us
    ppermute x4, starting transfers between devices, padded(): lax.ppermute(head, axis, [((i + 1) % count, i) for i in range(ends)])  5.17 us
    slice x3, local copies, waits for them, and re-layouts, shards(): pieces.append(gathered[:, offset:offset + rows, :])  5.02 us
  transfers between devices with their start and end apart: 10, of which 3 were waited for; matrix products, arithmetic and copies ran while one was open for 11% of the time, Pallas kernels for 0%

profile of v11, /device:TPU:0, one launch (start us, length us, event | category | flops | bytes accessed | tf_op | source)
XLA Modules:
  0.0 208.5 jit_solution(3099624514490770764)
XLA Ops:
  7.2 2.0 shard_map.226
  9.2 0.8 reshape_squeeze.5
  10.0 0.8 reshape_squeeze.6
  10.8 1.8 gather_fusion
  12.7 2.4 %collective-permute-start = (f32[1,16,512]{2,1,0:T(8,128)S(1)}, f32[1,16,512]{2,1,0:T(8,128)S(1)}, u32[]{:S(2)}, u32[]{:S(2)}) collective-permute-start(f32[1,16,512]{2,1,0:T(8,128)S(1)} %get-tuple-element.48), channel_id=1, source_target_pairs={{0,4},{4,8},{8,12},{1,5},{5,9},{9,13},{2,6},{6,10},{10,14},{3,7},{... | collective-permute-start | bytes 98312 | tf_op jit(solution)/shard_map/ppermute | solution.py:21
  15.1 1.3 collective-permute-start.1
  16.4 4.3 %collective-permute-start.2 = (f32[1,16,512]{2,1,0:T(8,128)S(1)}, f32[1,16,512]{2,1,0:T(8,128)S(1)}, u32[]{:S(2)}, u32[]{:S(2)}) collective-permute-start(f32[1,16,512]{2,1,0:T(8,128)S(1)} %get-tuple-element.50), channel_id=1, source_target_pairs={{0,1},{1,2},{2,3},{4,5},{5,6},{6,7},{8,9},{9,10},{10,11},{12,13},{... | collective-permute-start | bytes 98312 | tf_op jit(solution)/shard_map/ppermute | solution.py:21
  20.7 1.3 collective-permute-start.3
  23.3 0.8 compare_and_fusion
  24.1 1.7 broadcast_maximum_fusion.1.refs_6_
  25.8 1.9 broadcast_maximum_fusion.refs_12_
  27.7 0.3 collective-permute-done.3
  28.0 1.1 pad_maximum_fusion
  29.1 0.8 gather_fusion.2
  29.9 0.8 gather_fusion.3
  30.6 0.9 broadcast_select_fusion.1
  31.5 52.7 %all-gather.2.cloned.1.call-done = f32[16,225,512]{2,1,0:T(8,128)} async-done(((f32[1,225,512]{2,1,0:T(8,128)}), f32[16,225,512]{2,1,0:T(8,128)}) %all-gather.2.cloned.1.call-update) | async-done | bytes 7372816 | tf_op jit(solution)/shard_map/all_gather | solution.py:222
  84.3 1.0 slice.168
  85.5 1.8 fusion.14
  87.3 0.7 fusion.17
  88.0 0.2 multiply_reduce_fusion.1
  88.3 1.3 fusion.5
  89.7 1.3 subtract_multiply_fusion.refs_13_
  91.0 0.8 copy-done.4
  91.8 0.6 convolution_select_fusion.refs_9_
  92.5 2.0 fusion.13
  94.5 0.7 fusion.18
  95.1 1.5 gather_fusion.4
  96.6 1.4 gather_fusion.1
  98.1 0.5 fusion.16
  98.6 0.2 multiply_reduce_fusion.3
  99.0 2.1 fusion.11
  101.1 0.1 subtract_multiply_fusion.1.refs_7_
  101.2 1.4 convolution_select_fusion.1.refs_1_.refs_3_.refs_5_
  102.6 6.9 %shard_map.227 = f32[16,224,512]{2,1,0:T(8,128)} custom-call(f32[128,512]{1,0:T(8,128)} %refs_0_.3, f32[128,512]{1,0:T(8,128)} %convolution_select_fusion.1.refs_1_.refs_3_.refs_5_, f32[128,512]{1,0:T(8,128)} %get-tuple-element.66.refs_2_, f32[128,512]{1,0:T(8,128)} %convolution_select_fusion.1.refs_1_.refs_3_.refs_5_, ...), custom_call_target="tpu_custom_call" | custom-call | tf_op jit(solution)/shard_map/pallas_call | solution.py:137
  109.6 2.3 %slice.176 = f32[16,96,512]{2,1,0:T(8,128)S(1)} slice(f32[16,225,512]{2,1,0:T(8,128)} %all-gather.2.cloned.1.call-done), slice={[0:16], [0:96], [0:512]} | slice | bytes 6291456 | tf_op jit(solution)/shard_map/slice | solution.py:226
  111.9 1.7 fusion.19
  113.7 0.8 fusion.15
  114.5 2.9 %scatter_custom_fusion = f32[320,512]{1,0:T(8,128)} fusion(s32[256]{0:T(256)S(1)} %bitcast.75, f32[128,512]{1,0:T(8,128)S(1)} %get-tuple-element.41, f32[]{:T(128)} %constant.75, f32[128,512]{1,0:T(8,128)S(1)} %get-tuple-element.40, f32[]{:T(128)} %constant.37.clone.1), kind=kCustom, calls=%fused_computation.14 | custom fusion | flops 262144 | bytes 1179656 | tf_op jit(solution)/shard_map/add | solution.py:287
  117.4 0.8 slice_bitcast_fusion.3
  118.3 1.3 collective-permute-start.4
  119.6 3.0 %collective-permute-start.5 = (f32[1,16,512]{2,1,0:T(8,128)S(1)}, f32[1,16,512]{2,1,0:T(8,128)S(1)}, u32[]{:S(2)}, u32[]{:S(2)}) collective-permute-start(f32[1,16,512]{2,1,0:T(8,128)S(1)} %get-tuple-element.46), channel_id=1, source_target_pairs={{0,4},{4,8},{8,12},{1,5},{5,9},{9,13},{2,6},{6,10},{10,14},{3,7},{... | collective-permute-start | bytes 98312 | tf_op jit(solution)/shard_map/ppermute | solution.py:21
  122.6 1.3 collective-permute-start.6
  123.9 4.5 %collective-permute-start.7 = (f32[1,16,512]{2,1,0:T(8,128)S(1)}, f32[1,16,512]{2,1,0:T(8,128)S(1)}, u32[]{:S(2)}, u32[]{:S(2)}) collective-permute-start(f32[1,16,512]{2,1,0:T(8,128)S(1)} %get-tuple-element.44), channel_id=1, source_target_pairs={{0,1},{1,2},{2,3},{4,5},{5,6},{6,7},{8,9},{9,10},{10,11},{12,13},{... | collective-permute-start | bytes 98312 | tf_op jit(solution)/shard_map/ppermute | solution.py:21
  128.5 1.7 fusion
  130.3 1.2 scatter_fusion
  131.5 68.3 %reduce-scatter.2.cloned.1.call-done = f32[1,224,512]{2,1,0:T(8,128)} async-done(((f32[16,224,512]{2,1,0:T(8,128)}), f32[1,224,512]{2,1,0:T(8,128)}) %reduce-scatter.2.cloned.1.call-update) | async-done | bytes 458768 | tf_op jit(solution)/shard_map/reduce_scatter | solution.py:277
  199.8 1.8 shard_map.228
  (62 shorter events, 1.0 us)
Async XLA Ops:
  7.2 77.1 %all-gather.2.cloned.1.call-start = ((), (), s32[]{:S(2)}) async-start(), calls=%async_computation.1 | async-start | bytes 8077312 | tf_op jit(solution)/shard_map/all_gather | solution.py:222
  9.2 190.6 %reduce-scatter.2.cloned.1.call-start = ((), (), s32[]{:S(2)}) async-start(), calls=%async_computation.2 | async-start | bytes 7798784 | tf_op jit(solution)/shard_map/reduce_scatter | solution.py:277
  10.8 76.5 %copy-start.3 = (f32[256,512]{1,0:T(8,128)S(1)}, f32[256,512]{1,0:T(8,128)}, u32[]{:S(2)}) copy-start(f32[256,512]{1,0:T(8,128)} %param.24) | copy-start | bytes 1572868
  12.7 14.9 %collective-permute-start = (f32[1,16,512]{2,1,0:T(8,128)S(1)}, f32[1,16,512]{2,1,0:T(8,128)S(1)}, u32[]{:S(2)}, u32[]{:S(2)}) collective-permute-start(f32[1,16,512]{2,1,0:T(8,128)S(1)} %get-tuple-element.48), channel_id=1, source_target_pairs={{0,4},{4,8},{8,12},{1,5},{5,9},{9,13},{2,6},{6,10},{10,14},{3,7},{... | collective-permute-start | bytes 98312 | tf_op jit(solution)/shard_map/ppermute | solution.py:21
  15.1 12.6 %collective-permute-start.1 = (f32[1,16,512]{2,1,0:T(8,128)S(1)}, f32[1,16,512]{2,1,0:T(8,128)S(1)}, u32[]{:S(2)}, u32[]{:S(2)}) collective-permute-start(f32[1,16,512]{2,1,0:T(8,128)S(1)} %get-tuple-element.51), channel_id=1, source_target_pairs={{4,0},{8,4},{12,8},{5,1},{9,5},{13,9},{6,2},{10,6},{14,10},{7,3},{... | collective-permute-start | bytes 98312 | tf_op jit(solution)/shard_map/ppermute | solution.py:23
  16.4 11.3 %collective-permute-start.2 = (f32[1,16,512]{2,1,0:T(8,128)S(1)}, f32[1,16,512]{2,1,0:T(8,128)S(1)}, u32[]{:S(2)}, u32[]{:S(2)}) collective-permute-start(f32[1,16,512]{2,1,0:T(8,128)S(1)} %get-tuple-element.50), channel_id=1, source_target_pairs={{0,1},{1,2},{2,3},{4,5},{5,6},{6,7},{8,9},{9,10},{10,11},{12,13},{... | collective-permute-start | bytes 98312 | tf_op jit(solution)/shard_map/ppermute | solution.py:21
  20.7 7.3 %collective-permute-start.3 = (f32[1,16,512]{2,1,0:T(8,128)S(1)}, f32[1,16,512]{2,1,0:T(8,128)S(1)}, u32[]{:S(2)}, u32[]{:S(2)}) collective-permute-start(f32[1,16,512]{2,1,0:T(8,128)S(1)} %get-tuple-element.49), channel_id=1, source_target_pairs={{1,0},{2,1},{3,2},{5,4},{6,5},{7,6},{9,8},{10,9},{11,10},{13,12},{... | collective-permute-start | bytes 98312 | tf_op jit(solution)/shard_map/ppermute | solution.py:23
  89.7 8.5 %copy-start.8 = (f32[128,512]{1,0:T(8,128)S(1)}, f32[128,512]{1,0:T(8,128)}, u32[]{:S(2)}) copy-start(f32[128,512]{1,0:T(8,128)} %param.26) | copy-start | bytes 786436
  91.0 0.8 copy-start.4
  92.5 8.6 %copy-start = (f32[256,512]{1,0:T(8,128)}, f32[256,512]{1,0:T(8,128)S(1)}, u32[]{:S(2)}) copy-start(f32[256,512]{1,0:T(8,128)S(1)} %convolution_select_fusion.refs_9_) | copy-start | bytes 1572868
  101.2 1.4 copy-start.7
  102.6 6.9 %copy-start.10 = (s32[2,128]{1,0:T(2,128)S(1)}, s32[2,128]{1,0:T(2,128)}, u32[]{:S(2)}) copy-start(s32[2,128]{1,0:T(2,128)} %param.29) | copy-start | bytes 3076
  109.5 2.4 %copy-start.2 = (f32[128,512]{1,0:T(8,128)S(1)}, f32[128,512]{1,0:T(8,128)}, u32[]{:S(2)}) copy-start(f32[128,512]{1,0:T(8,128)} %convolution_select_fusion.1.refs_1_.refs_3_.refs_5_) | copy-start | bytes 786436
  109.5 4.2 %copy-start.9 = (f32[128,512]{1,0:T(8,128)S(1)}, f32[128,512]{1,0:T(8,128)}, u32[]{:S(2)}) copy-start(f32[128,512]{1,0:T(8,128)} %param.28) | copy-start | bytes 786436
  109.6 18.9 %copy-start.1 = (f32[256,512]{1,0:T(8,128)S(1)}, f32[256,512]{1,0:T(8,128)}, u32[]{:S(2)}) copy-start(f32[256,512]{1,0:T(8,128)} %copy-done) | copy-start | bytes 1572868
  109.6 18.9 %copy-start.6 = (f32[256,512]{1,0:T(8,128)S(1)}, f32[256,512]{1,0:T(8,128)}, u32[]{:S(2)}) copy-start(f32[256,512]{1,0:T(8,128)} %param.27) | copy-start | bytes 1572868
  118.3 12.0 %collective-permute-start.4 = (f32[1,16,512]{2,1,0:T(8,128)S(1)}, f32[1,16,512]{2,1,0:T(8,128)S(1)}, u32[]{:S(2)}, u32[]{:S(2)}) collective-permute-start(f32[1,16,512]{2,1,0:T(8,128)S(1)} %get-tuple-element.43), channel_id=1, source_target_pairs={{4,0},{8,4},{12,8},{5,1},{9,5},{13,9},{6,2},{10,6},{14,10},{7,3},{... | collective-permute-start | bytes 98312 | tf_op jit(solution)/shard_map/ppermute | solution.py:23
  119.6 10.7 %collective-permute-start.5 = (f32[1,16,512]{2,1,0:T(8,128)S(1)}, f32[1,16,512]{2,1,0:T(8,128)S(1)}, u32[]{:S(2)}, u32[]{:S(2)}) collective-permute-start(f32[1,16,512]{2,1,0:T(8,128)S(1)} %get-tuple-element.46), channel_id=1, source_target_pairs={{0,4},{4,8},{8,12},{1,5},{5,9},{9,13},{2,6},{6,10},{10,14},{3,7},{... | collective-permute-start | bytes 98312 | tf_op jit(solution)/shard_map/ppermute | solution.py:21
  122.6 7.7 %collective-permute-start.6 = (f32[1,16,512]{2,1,0:T(8,128)S(1)}, f32[1,16,512]{2,1,0:T(8,128)S(1)}, u32[]{:S(2)}, u32[]{:S(2)}) collective-permute-start(f32[1,16,512]{2,1,0:T(8,128)S(1)} %get-tuple-element.45), channel_id=1, source_target_pairs={{1,0},{2,1},{3,2},{5,4},{6,5},{7,6},{9,8},{10,9},{11,10},{13,12},{... | collective-permute-start | bytes 98312 | tf_op jit(solution)/shard_map/ppermute | solution.py:23
  123.9 6.4 %collective-permute-start.7 = (f32[1,16,512]{2,1,0:T(8,128)S(1)}, f32[1,16,512]{2,1,0:T(8,128)S(1)}, u32[]{:S(2)}, u32[]{:S(2)}) collective-permute-start(f32[1,16,512]{2,1,0:T(8,128)S(1)} %get-tuple-element.44), channel_id=1, source_target_pairs={{0,1},{1,2},{2,3},{4,5},{5,6},{6,7},{8,9},{9,10},{10,11},{12,13},{... | collective-permute-start | bytes 98312 | tf_op jit(solution)/shard_map/ppermute | solution.py:21
  131.5 70.1 %copy-start.5 = (f32[256,512]{1,0:T(8,128)}, f32[256,512]{1,0:T(8,128)S(1)}, u32[]{:S(2)}) copy-start(f32[256,512]{1,0:T(8,128)S(1)} %scatter_fusion) | copy-start | bytes 1572868
Sparse Core Ops, SparseCore 0:
  10.9 73.3 all-gather.1
  109.7 90.0 reduce-scatter.1

commit v12 on v10

--- a/solution.py
+++ b/solution.py
@@ -112,8 +112,10 @@
         loads = [
             pltpu.make_async_copy(sources[k], staged[k], in_sems.at[k]) for k in range(count_in)
         ]
-        for load in loads:
-            load.start()
+        for index in order:
+            start, count, _ = layout[index]
+            for k in range(start, start + 2 * count):
+                loads[k].start()
         stores = []
         for index in order:
             start, count, scale = layout[index]

time: 206 us -> 205 us (level)
  no operation moved by 1% of the time
where the time goes in v12:
time: 205 us
  waiting for transfers between devices  129 us (63%)
  starting transfers between devices  18.8 us (9%)
  between operations  15.9 us (8%)
  local copies, waits for them, and re-layouts  14.4 us (7%)
  Pallas kernels  10.1 us (5%)
  other arithmetic  9.18 us (4%)
  matrix products  7.56 us (4%)
    reduce_scatter x1, waiting for transfers between devices, shards(): lax.psum_scatter(blocked, peers, scatter_dimension=0, tiled=True)[0]  72.7 us
    all_gather x1, waiting for transfers between devices, shards(): gathered = lax.all_gather(packed, peers, axis=0, tiled=True)  54.1 us
    ppermute x4, starting transfers between devices, padded(): lax.ppermute(tail, axis, [(i, (i + 1) % count) for i in range(ends)])  13.5 us
    dot_general x4, matrix products, outer_back(): lax.dot_general(left, right, (((1,), (1,)), ((), ())), precision=lax.Prec...  6.29 us
    pallas_call x1, Pallas kernels, blocked_grads(): pl.pallas_call(kernel, out_shape=jax.ShapeDtypeStruct((blocks, offsets[-1...  6.28 us
    ppermute x4, starting transfers between devices, padded(): lax.ppermute(head, axis, [((i + 1) % count, i) for i in range(ends)])  5.17 us
    slice x6, local copies, waits for them, and re-layouts, shards(): pieces.append(gathered[:, offset:offset + rows, :])  4.58 us
  transfers between devices with their start and end apart: 10, of which 4 were waited for; matrix products, arithmetic and copies ran while one was open for 7% of the time, Pallas kernels for 0%

profile of v12, /device:TPU:0, one launch (start us, length us, event | category | flops | bytes accessed | tf_op | source)
XLA Modules:
  0.0 204.6 jit_solution(17464084319239205814)
XLA Ops:
  7.3 2.0 shard_map.226
  9.4 0.8 reshape.233
  10.1 0.8 broadcast_in_dim_reshape_squeeze.3
  10.9 1.8 gather_fusion
  12.8 1.3 collective-permute-start.7
  14.1 5.6 %collective-permute-start.6 = (f32[1,16,512]{2,1,0:T(8,128)S(1)}, f32[1,16,512]{2,1,0:T(8,128)S(1)}, u32[]{:S(2)}, u32[]{:S(2)}) collective-permute-start(f32[1,16,512]{2,1,0:T(8,128)S(1)} %get-tuple-element.44), channel_id=1, source_target_pairs={{0,1},{1,2},{2,3},{4,5},{5,6},{6,7},{8,9},{9,10},{10,11},{12,13},{... | collective-permute-start | bytes 98312 | tf_op jit(solution)/shard_map/ppermute | solution.py:21
  19.7 1.3 collective-permute-start.5
  21.0 3.0 %collective-permute-start.4 = (f32[1,16,512]{2,1,0:T(8,128)S(1)}, f32[1,16,512]{2,1,0:T(8,128)S(1)}, u32[]{:S(2)}, u32[]{:S(2)}) collective-permute-start(f32[1,16,512]{2,1,0:T(8,128)S(1)} %get-tuple-element.42), channel_id=1, source_target_pairs={{0,4},{4,8},{8,12},{1,5},{5,9},{9,13},{2,6},{6,10},{10,14},{3,7},{... | collective-permute-start | bytes 98312 | tf_op jit(solution)/shard_map/ppermute | solution.py:21
  25.4 0.7 broadcast_maximum_fusion.1.refs_6_
  26.1 0.9 broadcast_maximum_fusion.refs_12_
  27.1 0.8 gather_fusion.3
  27.9 0.8 gather_fusion.2
  28.6 0.9 broadcast_select_fusion.1
  29.5 54.1 %all-gather.2.cloned.1.call-done = f32[16,225,512]{2,1,0:T(8,128)} async-done(((f32[1,225,512]{2,1,0:T(8,128)}), f32[16,225,512]{2,1,0:T(8,128)}) %all-gather.2.cloned.1.call-update) | async-done | bytes 7372816 | tf_op jit(solution)/shard_map/all_gather | solution.py:224
  83.6 1.0 slice.161
  84.7 0.1 slice_reduce_fusion
  84.9 1.7 fusion.12
  86.6 1.0 copy-done.1
  87.6 0.6 fusion.14
  88.2 0.2 multiply_reduce_fusion.3
  88.6 0.7 fusion.15
  89.4 0.2 multiply_reduce_fusion.1
  89.6 0.3 fusion.4
  89.9 0.3 subtract_multiply_fusion.refs_13_
  90.2 0.8 copy-done.7
  91.0 2.1 %convolution_select_fusion.refs_9_ = f32[256,512]{1,0:T(8,128)S(1)} fusion(f32[256,512]{1,0:T(8,128)S(1)} %subtract_multiply_fusion.refs_13_, f32[512,512]{1,0:T(8,128)} %bitcast.65, f32[256,512]{1,0:T(8,128)} %param.24), kind=kOutput, calls=%fused_computation.8 | convolution fusion | flops 402915328 | bytes 2621440 | tf_op jit(solution)/shard_map/dot_general | solution.py:165
  93.1 1.1 fusion.16
  94.2 1.0 copy-done.11
  95.3 0.8 gather_fusion.4
  96.0 0.8 gather_fusion.1
  96.9 1.0 fusion.10
  97.9 0.1 subtract_multiply_fusion.1.refs_7_
  98.0 1.4 convolution_select_fusion.1.refs_1_.refs_3_.refs_5_
  99.4 6.3 %shard_map.227 = f32[16,224,512]{2,1,0:T(8,128)} custom-call(f32[128,512]{1,0:T(8,128)} %refs_0_.3, f32[128,512]{1,0:T(8,128)} %convolution_select_fusion.1.refs_1_.refs_3_.refs_5_, f32[128,512]{1,0:T(8,128)} %get-tuple-element.60.refs_2_, f32[128,512]{1,0:T(8,128)} %convolution_select_fusion.1.refs_1_.refs_3_.refs_5_, ...), custom_call_target="tpu_custom_call" | custom-call | tf_op jit(solution)/shard_map/pallas_call | solution.py:139
  105.8 1.9 slice-done.1
  107.7 1.7 fusion.17
  109.4 0.8 fusion.13
  110.2 2.3 %scatter_custom_fusion = f32[320,512]{1,0:T(8,128)S(1)} fusion(s32[256]{0:T(256)S(1)} %bitcast.71, f32[128,512]{1,0:T(8,128)S(1)} %get-tuple-element.35, f32[]{:T(128)} %constant.75, f32[128,512]{1,0:T(8,128)S(1)} %get-tuple-element.34, f32[]{:T(128)} %constant.37.clone.1), kind=kCustom, calls=%fused_computation.14 | custom fusion | flops 262144 | bytes 1179656 | tf_op jit(solution)/shard_map/add | solution.py:290
  112.5 3.1 %collective-permute-start.3 = (f32[1,16,512]{2,1,0:T(8,128)S(1)}, f32[1,16,512]{2,1,0:T(8,128)S(1)}, u32[]{:S(2)}, u32[]{:S(2)}) collective-permute-start(f32[1,16,512]{2,1,0:T(8,128)S(1)} %get-tuple-element.38), channel_id=1, source_target_pairs={{0,1},{1,2},{2,3},{4,5},{5,6},{6,7},{8,9},{9,10},{10,11},{12,13},{... | collective-permute-start | bytes 98312 | tf_op jit(solution)/shard_map/ppermute | solution.py:21
  115.6 1.3 collective-permute-start.2
  116.9 1.9 collective-permute-start.1
  118.8 1.3 collective-permute-start
  120.1 0.1 slice_add_fusion
  120.2 1.1 collective-permute-done.2
  121.4 0.7 collective-permute-done
  122.1 1.2 scatter_fusion
  123.3 72.7 %reduce-scatter.2.cloned.1.call-done = f32[1,224,512]{2,1,0:T(8,128)} async-done(((f32[16,224,512]{2,1,0:T(8,128)}), f32[1,224,512]{2,1,0:T(8,128)}) %reduce-scatter.2.cloned.1.call-update) | async-done | bytes 458768 | tf_op jit(solution)/shard_map/reduce_scatter | solution.py:281
  196.0 1.8 shard_map.228
  (79 shorter events, 1.0 us)
Async XLA Ops:
  7.2 19.9 %copy-start.4 = (f32[256,512]{1,0:T(8,128)S(1)}, f32[256,512]{1,0:T(8,128)}, u32[]{:S(2)}) copy-start(f32[256,512]{1,0:T(8,128)} %refs_8_.1) | copy-start | bytes 1572868
  7.2 18.1 %copy-start.17 = (s32[2,128]{1,0:T(2,128)S(1)}, s32[2,128]{1,0:T(2,128)}, u32[]{:S(2)}) copy-start(s32[2,128]{1,0:T(2,128)} %param.29) | copy-start | bytes 3076
  7.2 18.2 %copy-start.14 = (f32[128,512]{1,0:T(8,128)S(1)}, f32[128,512]{1,0:T(8,128)}, u32[]{:S(2)}) copy-start(f32[128,512]{1,0:T(8,128)} %param.26) | copy-start | bytes 786436
  7.2 18.9 %copy-start.6 = (f32[256,512]{1,0:T(8,128)S(1)}, f32[256,512]{1,0:T(8,128)}, u32[]{:S(2)}) copy-start(f32[256,512]{1,0:T(8,128)} %param.24) | copy-start | bytes 1572868
  7.2 76.4 %all-gather.2.cloned.1.call-start = ((), (), s32[]{:S(2)}) async-start(), calls=%async_computation.1 | async-start | bytes 8077312 | tf_op jit(solution)/shard_map/all_gather | solution.py:224
  9.3 186.7 %reduce-scatter.2.cloned.1.call-start = ((), (), s32[]{:S(2)}) async-start(), calls=%async_computation.2 | async-start | bytes 7798784 | tf_op jit(solution)/shard_map/reduce_scatter | solution.py:281
  12.8 14.2 %collective-permute-start.7 = (f32[1,16,512]{2,1,0:T(8,128)S(1)}, f32[1,16,512]{2,1,0:T(8,128)S(1)}, u32[]{:S(2)}, u32[]{:S(2)}) collective-permute-start(f32[1,16,512]{2,1,0:T(8,128)S(1)} %get-tuple-element.43), channel_id=1, source_target_pairs={{1,0},{2,1},{3,2},{5,4},{6,5},{7,6},{9,8},{10,9},{11,10},{13,12},{... | collective-permute-start | bytes 98312 | tf_op jit(solution)/shard_map/ppermute | solution.py:23
  14.1 12.9 %collective-permute-start.6 = (f32[1,16,512]{2,1,0:T(8,128)S(1)}, f32[1,16,512]{2,1,0:T(8,128)S(1)}, u32[]{:S(2)}, u32[]{:S(2)}) collective-permute-start(f32[1,16,512]{2,1,0:T(8,128)S(1)} %get-tuple-element.44), channel_id=1, source_target_pairs={{0,1},{1,2},{2,3},{4,5},{5,6},{6,7},{8,9},{9,10},{10,11},{12,13},{... | collective-permute-start | bytes 98312 | tf_op jit(solution)/shard_map/ppermute | solution.py:21
  19.7 7.3 %collective-permute-start.5 = (f32[1,16,512]{2,1,0:T(8,128)S(1)}, f32[1,16,512]{2,1,0:T(8,128)S(1)}, u32[]{:S(2)}, u32[]{:S(2)}) collective-permute-start(f32[1,16,512]{2,1,0:T(8,128)S(1)} %get-tuple-element.45), channel_id=1, source_target_pairs={{4,0},{8,4},{12,8},{5,1},{9,5},{13,9},{6,2},{10,6},{14,10},{7,3},{... | collective-permute-start | bytes 98312 | tf_op jit(solution)/shard_map/ppermute | solution.py:23
  21.0 6.0 %collective-permute-start.4 = (f32[1,16,512]{2,1,0:T(8,128)S(1)}, f32[1,16,512]{2,1,0:T(8,128)S(1)}, u32[]{:S(2)}, u32[]{:S(2)}) collective-permute-start(f32[1,16,512]{2,1,0:T(8,128)S(1)} %get-tuple-element.42), channel_id=1, source_target_pairs={{0,4},{4,8},{8,12},{1,5},{5,9},{9,13},{2,6},{6,10},{10,14},{3,7},{... | collective-permute-start | bytes 98312 | tf_op jit(solution)/shard_map/ppermute | solution.py:21
  86.6 1.0 copy-start.1
  86.6 3.3 %copy-start.3 = (f32[16,32,512]{2,1,0:T(8,128)}, f32[16,32,512]{2,1,0:T(8,128)S(1)}, u32[]{:S(2)}) copy-start(f32[16,32,512]{2,1,0:T(8,128)S(1)} %get-tuple-element.32) | copy-start | bytes 3145732
  86.6 3.0 %copy-start.9 = (f32[256,512]{1,0:T(8,128)S(1)}, f32[256,512]{1,0:T(8,128)}, u32[]{:S(2)}) copy-start(f32[256,512]{1,0:T(8,128)} %param.27) | copy-start | bytes 1572868
  90.2 0.8 copy-start.7
  91.0 2.1 %slice-start = ((f32[16,225,512]{2,1,0:T(8,128)}), f32[16,64,512]{2,1,0:T(8,128)S(1)}, s32[]{:S(2)}) async-start(f32[16,225,512]{2,1,0:T(8,128)} %all-gather.2.cloned.1.call-done), calls=%async_computation.3 | async-start | bytes 4194304 | tf_op jit(solution)/shard_map/slice | solution.py:228
  93.1 2.1 %copy-start = (f32[256,512]{1,0:T(8,128)}, f32[256,512]{1,0:T(8,128)S(1)}, u32[]{:S(2)}) copy-start(f32[256,512]{1,0:T(8,128)S(1)} %convolution_select_fusion.refs_9_) | copy-start | bytes 1572868
  94.2 1.0 copy-start.11
  95.2 1.7 copy-start.16
  95.3 2.8 %copy-start.2 = (f32[16,32,512]{2,1,0:T(8,128)S(1)}, f32[16,32,512]{2,1,0:T(8,128)}, u32[]{:S(2)}) copy-start(f32[16,32,512]{2,1,0:T(8,128)} %copy-done.1) | copy-start | bytes 3145732
  95.3 2.8 %copy-start.15 = (f32[128,512]{1,0:T(8,128)S(1)}, f32[128,512]{1,0:T(8,128)}, u32[]{:S(2)}) copy-start(f32[128,512]{1,0:T(8,128)} %param.26) | copy-start | bytes 786436
  98.0 1.4 copy-start.13
  105.7 1.9 slice-start.1
  105.8 1.9 copy-start.5
  107.6 12.4 %copy-start.10 = (f32[256,512]{1,0:T(8,128)S(1)}, f32[256,512]{1,0:T(8,128)}, u32[]{:S(2)}) copy-start(f32[256,512]{1,0:T(8,128)} %param.27) | copy-start | bytes 1572868
  107.6 12.4 %copy-start.12 = (f32[256,1024]{1,0:T(8,128)S(1)}, f32[256,1024]{1,0:T(8,128)}, u32[]{:S(2)}) copy-start(f32[256,1024]{1,0:T(8,128)} %copy-done.11) | copy-start | bytes 3145732
  112.5 7.7 %collective-permute-start.3 = (f32[1,16,512]{2,1,0:T(8,128)S(1)}, f32[1,16,512]{2,1,0:T(8,128)S(1)}, u32[]{:S(2)}, u32[]{:S(2)}) collective-permute-start(f32[1,16,512]{2,1,0:T(8,128)S(1)} %get-tuple-element.38), channel_id=1, source_target_pairs={{0,1},{1,2},{2,3},{4,5},{5,6},{6,7},{8,9},{9,10},{10,11},{12,13},{... | collective-permute-start | bytes 98312 | tf_op jit(solution)/shard_map/ppermute | solution.py:21
  115.6 5.8 %collective-permute-start.2 = (f32[1,16,512]{2,1,0:T(8,128)S(1)}, f32[1,16,512]{2,1,0:T(8,128)S(1)}, u32[]{:S(2)}, u32[]{:S(2)}) collective-permute-start(f32[1,16,512]{2,1,0:T(8,128)S(1)} %get-tuple-element.39), channel_id=1, source_target_pairs={{1,0},{2,1},{3,2},{5,4},{6,5},{7,6},{9,8},{10,9},{11,10},{13,12},{... | collective-permute-start | bytes 98312 | tf_op jit(solution)/shard_map/ppermute | solution.py:23
  116.9 4.5 %collective-permute-start.1 = (f32[1,16,512]{2,1,0:T(8,128)S(1)}, f32[1,16,512]{2,1,0:T(8,128)S(1)}, u32[]{:S(2)}, u32[]{:S(2)}) collective-permute-start(f32[1,16,512]{2,1,0:T(8,128)S(1)} %get-tuple-element.40), channel_id=1, source_target_pairs={{0,4},{4,8},{8,12},{1,5},{5,9},{9,13},{2,6},{6,10},{10,14},{3,7},{... | collective-permute-start | bytes 98312 | tf_op jit(solution)/shard_map/ppermute | solution.py:21
  118.8 3.3 %collective-permute-start = (f32[1,16,512]{2,1,0:T(8,128)S(1)}, f32[1,16,512]{2,1,0:T(8,128)S(1)}, u32[]{:S(2)}, u32[]{:S(2)}) collective-permute-start(f32[1,16,512]{2,1,0:T(8,128)S(1)} %get-tuple-element.37), channel_id=1, source_target_pairs={{4,0},{8,4},{12,8},{5,1},{9,5},{13,9},{6,2},{10,6},{14,10},{7,3},{... | collective-permute-start | bytes 98312 | tf_op jit(solution)/shard_map/ppermute | solution.py:23
  123.3 74.5 %copy-start.8 = (f32[256,512]{1,0:T(8,128)}, f32[256,512]{1,0:T(8,128)S(1)}, u32[]{:S(2)}) copy-start(f32[256,512]{1,0:T(8,128)S(1)} %scatter_fusion) | copy-start | bytes 1572868
Sparse Core Ops, SparseCore 0:
  10.9 72.6 all-gather.1
  105.8 90.0 reduce-scatter.1

commit v13 on v12

--- a/solution.py
+++ b/solution.py
@@ -93,10 +93,16 @@
     offsets = row_offsets(rows)
     inputs = []
     layout = []
+
+    def slot(value):
+        for index, known in enumerate(inputs):
+            if known is value:
+                return index
+        inputs.append(value)
+        return len(inputs) - 1
+
     for pairs, scale in terms:
-        layout.append((len(inputs), len(pairs), scale))
-        for pair in pairs:
-            inputs.extend(pair)
+        layout.append(([(slot(left), slot(right)) for left, right in pairs], scale))
     width = terms[0][0][0][1].shape[1]
 
     order = sorted(range(len(terms)), key=lambda index: -rows[index] * terms[index][0][0][0].shape[0])
@@ -112,19 +118,28 @@
         loads = [
             pltpu.make_async_copy(sources[k], staged[k], in_sems.at[k]) for k in range(count_in)
         ]
+        started = []
         for index in order:
-            start, count, _ = layout[index]
-            for k in range(start, start + 2 * count):
-                loads[k].start()
+            for pair in layout[index][0]:
+                for k in pair:
+                    if k not in started:
+                        loads[k].start()
+                        started.append(k)
+        waited = []
         stores = []
         for index in order:
-            start, count, scale = layout[index]
-            for k in range(start, start + 2 * count):
-                loads[k].wait()
+            pairs, scale = layout[index]
+            for pair in pairs:
+                for k in pair:
+                    if k not in waited:
+                        loads[k].wait()
+                        waited.append(k)
+            halves = {}
             pieces = []
-            for k in range(count):
-                right_high, right_low = split_bf16(staged[start + 2 * k + 1][...])
-                pieces.append(inner_three(staged[start + 2 * k][...], right_high, right_low))
+            for left, right in pairs:
+                if right not in halves:
+                    halves[right] = split_bf16(staged[right][...])
+                pieces.append(inner_three(staged[left][...], *halves[right]))
             product = jnp.concatenate(pieces, axis=0) * scale
             results[index][...] = product.reshape(blocks, rows[index], width)
             store = pltpu.make_async_copy(

time: 205 us -> 205 us (level)
  no operation moved by 1% of the time
where the time goes in v13:
time: 205 us
  waiting for transfers between devices  129 us (63%)
  starting transfers between devices  18.8 us (9%)
  between operations  15.9 us (8%)
  local copies, waits for them, and re-layouts  14.4 us (7%)
  Pallas kernels  10.1 us (5%)
  other arithmetic  9.18 us (4%)
  matrix products  7.56 us (4%)
    reduce_scatter x1, waiting for transfers between devices, shards(): lax.psum_scatter(blocked, peers, scatter_dimension=0, tiled=True)[0]  72.6 us
    all_gather x1, waiting for transfers between devices, shards(): gathered = lax.all_gather(packed, peers, axis=0, tiled=True)  54.1 us
    ppermute x4, starting transfers between devices, padded(): lax.ppermute(tail, axis, [(i, (i + 1) % count) for i in range(ends)])  13.5 us
    dot_general x4, matrix products, outer_back(): lax.dot_general(left, right, (((1,), (1,)), ((), ())), precision=lax.Prec...  6.29 us
    pallas_call x1, Pallas kernels, blocked_grads(): pl.pallas_call(kernel, out_shape=jax.ShapeDtypeStruct((blocks, offsets[-1...  6.26 us
    ppermute x4, starting transfers between devices, padded(): lax.ppermute(head, axis, [((i + 1) % count, i) for i in range(ends)])  5.17 us
    slice x6, local copies, waits for them, and re-layouts, shards(): pieces.append(gathered[:, offset:offset + rows, :])  4.58 us
  transfers between devices with their start and end apart: 10, of which 4 were waited for; matrix products, arithmetic and copies ran while one was open for 7% of the time, Pallas kernels for 0%

profile of v13, /device:TPU:0, one launch (start us, length us, event | category | flops | bytes accessed | tf_op | source)
XLA Modules:
  0.0 204.5 jit_solution(9332401346554847152)
XLA Ops:
  7.3 2.0 shard_map.226
  9.4 0.8 reshape.233
  10.1 0.8 broadcast_in_dim_reshape_squeeze.3
  10.9 1.8 gather_fusion
  12.8 1.3 collective-permute-start.7
  14.1 5.6 %collective-permute-start.6 = (f32[1,16,512]{2,1,0:T(8,128)S(1)}, f32[1,16,512]{2,1,0:T(8,128)S(1)}, u32[]{:S(2)}, u32[]{:S(2)}) collective-permute-start(f32[1,16,512]{2,1,0:T(8,128)S(1)} %get-tuple-element.44), channel_id=1, source_target_pairs={{0,1},{1,2},{2,3},{4,5},{5,6},{6,7},{8,9},{9,10},{10,11},{12,13},{... | collective-permute-start | bytes 98312 | tf_op jit(solution)/shard_map/ppermute | solution.py:21
  19.7 1.3 collective-permute-start.5
  21.0 3.0 %collective-permute-start.4 = (f32[1,16,512]{2,1,0:T(8,128)S(1)}, f32[1,16,512]{2,1,0:T(8,128)S(1)}, u32[]{:S(2)}, u32[]{:S(2)}) collective-permute-start(f32[1,16,512]{2,1,0:T(8,128)S(1)} %get-tuple-element.42), channel_id=1, source_target_pairs={{0,4},{4,8},{8,12},{1,5},{5,9},{9,13},{2,6},{6,10},{10,14},{3,7},{... | collective-permute-start | bytes 98312 | tf_op jit(solution)/shard_map/ppermute | solution.py:21
  25.4 0.7 broadcast_maximum_fusion.1.refs_4_
  26.1 0.9 broadcast_maximum_fusion.refs_10_
  27.1 0.8 gather_fusion.3
  27.9 0.8 gather_fusion.2
  28.6 0.9 broadcast_select_fusion.1
  29.5 54.1 %all-gather.2.cloned.1.call-done = f32[16,225,512]{2,1,0:T(8,128)} async-done(((f32[1,225,512]{2,1,0:T(8,128)}), f32[16,225,512]{2,1,0:T(8,128)}) %all-gather.2.cloned.1.call-update) | async-done | bytes 7372816 | tf_op jit(solution)/shard_map/all_gather | solution.py:239
  83.6 1.0 slice.161
  84.7 0.1 slice_reduce_fusion
  84.9 1.7 fusion.12
  86.6 1.0 copy-done.1
  87.6 0.6 fusion.14
  88.2 0.2 multiply_reduce_fusion.3
  88.6 0.7 fusion.15
  89.4 0.2 multiply_reduce_fusion.1
  89.6 0.3 fusion.4
  89.9 0.3 subtract_multiply_fusion.refs_11_
  90.2 0.8 copy-done.6
  91.0 2.1 %convolution_select_fusion.refs_7_ = f32[256,512]{1,0:T(8,128)S(1)} fusion(f32[256,512]{1,0:T(8,128)S(1)} %subtract_multiply_fusion.refs_11_, f32[512,512]{1,0:T(8,128)} %bitcast.65, f32[256,512]{1,0:T(8,128)} %param.24), kind=kOutput, calls=%fused_computation.8 | convolution fusion | flops 402915328 | bytes 2621440 | tf_op jit(solution)/shard_map/dot_general | solution.py:180
  93.1 1.1 fusion.16
  94.2 1.0 copy-done.10
  95.3 0.8 gather_fusion.4
  96.0 0.8 gather_fusion.1
  96.9 1.0 fusion.10
  97.9 0.1 subtract_multiply_fusion.1.refs_5_
  98.0 1.4 convolution_select_fusion.1.refs_1_
  99.4 6.3 %shard_map.227 = f32[16,224,512]{2,1,0:T(8,128)} custom-call(f32[128,512]{1,0:T(8,128)} %refs_0_.3, f32[128,512]{1,0:T(8,128)} %convolution_select_fusion.1.refs_1_, f32[128,512]{1,0:T(8,128)} %get-tuple-element.60.refs_2_, f32[128,512]{1,0:T(8,128)} %get-tuple-element.59.refs_3_, f32[128,512]{1,0:T(8,128)} %broadcast_maximum_fusion.1.refs_4_, ...), custom_call_target="tpu_custom_call" | custom-call | tf_op jit(solution)/shard_map/pallas_call | solution.py:154
  105.7 1.9 slice-done.1
  107.6 1.7 fusion.17
  109.4 0.8 fusion.13
  110.2 2.3 %scatter_custom_fusion = f32[320,512]{1,0:T(8,128)S(1)} fusion(s32[256]{0:T(256)S(1)} %bitcast.71, f32[128,512]{1,0:T(8,128)S(1)} %get-tuple-element.35, f32[]{:T(128)} %constant.75, f32[128,512]{1,0:T(8,128)S(1)} %get-tuple-element.34, f32[]{:T(128)} %constant.37.clone.1), kind=kCustom, calls=%fused_computation.14 | custom fusion | flops 262144 | bytes 1179656 | tf_op jit(solution)/shard_map/add | solution.py:305
  112.5 3.0 %collective-permute-start.3 = (f32[1,16,512]{2,1,0:T(8,128)S(1)}, f32[1,16,512]{2,1,0:T(8,128)S(1)}, u32[]{:S(2)}, u32[]{:S(2)}) collective-permute-start(f32[1,16,512]{2,1,0:T(8,128)S(1)} %get-tuple-element.38), channel_id=1, source_target_pairs={{0,1},{1,2},{2,3},{4,5},{5,6},{6,7},{8,9},{9,10},{10,11},{12,13},{... | collective-permute-start | bytes 98312 | tf_op jit(solution)/shard_map/ppermute | solution.py:21
  115.5 1.3 collective-permute-start.2
  116.8 1.9 collective-permute-start.1
  118.7 1.3 collective-permute-start
  120.1 0.1 slice_add_fusion
  120.2 1.1 collective-permute-done.2
  121.3 0.7 collective-permute-done
  122.1 1.2 scatter_fusion
  123.3 72.6 %reduce-scatter.2.cloned.1.call-done = f32[1,224,512]{2,1,0:T(8,128)} async-done(((f32[16,224,512]{2,1,0:T(8,128)}), f32[1,224,512]{2,1,0:T(8,128)}) %reduce-scatter.2.cloned.1.call-update) | async-done | bytes 458768 | tf_op jit(solution)/shard_map/reduce_scatter | solution.py:296
  195.9 1.8 shard_map.228
  (79 shorter events, 1.0 us)
Async XLA Ops:
  7.2 19.9 %copy-start.4 = (f32[256,512]{1,0:T(8,128)S(1)}, f32[256,512]{1,0:T(8,128)}, u32[]{:S(2)}) copy-start(f32[256,512]{1,0:T(8,128)} %refs_6_.1) | copy-start | bytes 1572868
  7.2 18.1 %copy-start.17 = (s32[2,128]{1,0:T(2,128)S(1)}, s32[2,128]{1,0:T(2,128)}, u32[]{:S(2)}) copy-start(s32[2,128]{1,0:T(2,128)} %param.29) | copy-start | bytes 3076
  7.2 18.2 %copy-start.14 = (f32[128,512]{1,0:T(8,128)S(1)}, f32[128,512]{1,0:T(8,128)}, u32[]{:S(2)}) copy-start(f32[128,512]{1,0:T(8,128)} %param.26) | copy-start | bytes 786436
  7.2 18.9 %copy-start.5 = (f32[256,512]{1,0:T(8,128)S(1)}, f32[256,512]{1,0:T(8,128)}, u32[]{:S(2)}) copy-start(f32[256,512]{1,0:T(8,128)} %param.24) | copy-start | bytes 1572868
  7.2 76.4 %all-gather.2.cloned.1.call-start = ((), (), s32[]{:S(2)}) async-start(), calls=%async_computation.1 | async-start | bytes 8077312 | tf_op jit(solution)/shard_map/all_gather | solution.py:239
  9.3 186.6 %reduce-scatter.2.cloned.1.call-start = ((), (), s32[]{:S(2)}) async-start(), calls=%async_computation.2 | async-start | bytes 7798784 | tf_op jit(solution)/shard_map/reduce_scatter | solution.py:296
  12.8 14.2 %collective-permute-start.7 = (f32[1,16,512]{2,1,0:T(8,128)S(1)}, f32[1,16,512]{2,1,0:T(8,128)S(1)}, u32[]{:S(2)}, u32[]{:S(2)}) collective-permute-start(f32[1,16,512]{2,1,0:T(8,128)S(1)} %get-tuple-element.43), channel_id=1, source_target_pairs={{1,0},{2,1},{3,2},{5,4},{6,5},{7,6},{9,8},{10,9},{11,10},{13,12},{... | collective-permute-start | bytes 98312 | tf_op jit(solution)/shard_map/ppermute | solution.py:23
  14.1 12.9 %collective-permute-start.6 = (f32[1,16,512]{2,1,0:T(8,128)S(1)}, f32[1,16,512]{2,1,0:T(8,128)S(1)}, u32[]{:S(2)}, u32[]{:S(2)}) collective-permute-start(f32[1,16,512]{2,1,0:T(8,128)S(1)} %get-tuple-element.44), channel_id=1, source_target_pairs={{0,1},{1,2},{2,3},{4,5},{5,6},{6,7},{8,9},{9,10},{10,11},{12,13},{... | collective-permute-start | bytes 98312 | tf_op jit(solution)/shard_map/ppermute | solution.py:21
  19.7 7.3 %collective-permute-start.5 = (f32[1,16,512]{2,1,0:T(8,128)S(1)}, f32[1,16,512]{2,1,0:T(8,128)S(1)}, u32[]{:S(2)}, u32[]{:S(2)}) collective-permute-start(f32[1,16,512]{2,1,0:T(8,128)S(1)} %get-tuple-element.45), channel_id=1, source_target_pairs={{4,0},{8,4},{12,8},{5,1},{9,5},{13,9},{6,2},{10,6},{14,10},{7,3},{... | collective-permute-start | bytes 98312 | tf_op jit(solution)/shard_map/ppermute | solution.py:23
  21.0 6.0 %collective-permute-start.4 = (f32[1,16,512]{2,1,0:T(8,128)S(1)}, f32[1,16,512]{2,1,0:T(8,128)S(1)}, u32[]{:S(2)}, u32[]{:S(2)}) collective-permute-start(f32[1,16,512]{2,1,0:T(8,128)S(1)} %get-tuple-element.42), channel_id=1, source_target_pairs={{0,4},{4,8},{8,12},{1,5},{5,9},{9,13},{2,6},{6,10},{10,14},{3,7},{... | collective-permute-start | bytes 98312 | tf_op jit(solution)/shard_map/ppermute | solution.py:21
  86.6 1.0 copy-start.1
  86.6 3.3 %copy-start.3 = (f32[16,32,512]{2,1,0:T(8,128)}, f32[16,32,512]{2,1,0:T(8,128)S(1)}, u32[]{:S(2)}) copy-start(f32[16,32,512]{2,1,0:T(8,128)S(1)} %get-tuple-element.32) | copy-start | bytes 3145732
  86.6 3.0 %copy-start.8 = (f32[256,512]{1,0:T(8,128)S(1)}, f32[256,512]{1,0:T(8,128)}, u32[]{:S(2)}) copy-start(f32[256,512]{1,0:T(8,128)} %param.27) | copy-start | bytes 1572868
  90.2 0.8 copy-start.6
  91.0 2.1 %slice-start = ((f32[16,225,512]{2,1,0:T(8,128)}), f32[16,64,512]{2,1,0:T(8,128)S(1)}, s32[]{:S(2)}) async-start(f32[16,225,512]{2,1,0:T(8,128)} %all-gather.2.cloned.1.call-done), calls=%async_computation.3 | async-start | bytes 4194304 | tf_op jit(solution)/shard_map/slice | solution.py:243
  93.1 2.1 %copy-start = (f32[256,512]{1,0:T(8,128)}, f32[256,512]{1,0:T(8,128)S(1)}, u32[]{:S(2)}) copy-start(f32[256,512]{1,0:T(8,128)S(1)} %convolution_select_fusion.refs_7_) | copy-start | bytes 1572868
  94.2 1.0 copy-start.10
  95.2 1.7 copy-start.16
  95.3 2.8 %copy-start.2 = (f32[16,32,512]{2,1,0:T(8,128)S(1)}, f32[16,32,512]{2,1,0:T(8,128)}, u32[]{:S(2)}) copy-start(f32[16,32,512]{2,1,0:T(8,128)} %copy-done.1) | copy-start | bytes 3145732
  95.3 2.8 %copy-start.15 = (f32[128,512]{1,0:T(8,128)S(1)}, f32[128,512]{1,0:T(8,128)}, u32[]{:S(2)}) copy-start(f32[128,512]{1,0:T(8,128)} %param.26) | copy-start | bytes 786436
  98.0 1.4 copy-start.13
  105.7 1.9 slice-start.1
  105.7 1.9 copy-start.12
  107.6 12.4 %copy-start.9 = (f32[256,512]{1,0:T(8,128)S(1)}, f32[256,512]{1,0:T(8,128)}, u32[]{:S(2)}) copy-start(f32[256,512]{1,0:T(8,128)} %param.27) | copy-start | bytes 1572868
  107.6 12.4 %copy-start.11 = (f32[256,1024]{1,0:T(8,128)S(1)}, f32[256,1024]{1,0:T(8,128)}, u32[]{:S(2)}) copy-start(f32[256,1024]{1,0:T(8,128)} %copy-done.10) | copy-start | bytes 3145732
  112.5 7.7 %collective-permute-start.3 = (f32[1,16,512]{2,1,0:T(8,128)S(1)}, f32[1,16,512]{2,1,0:T(8,128)S(1)}, u32[]{:S(2)}, u32[]{:S(2)}) collective-permute-start(f32[1,16,512]{2,1,0:T(8,128)S(1)} %get-tuple-element.38), channel_id=1, source_target_pairs={{0,1},{1,2},{2,3},{4,5},{5,6},{6,7},{8,9},{9,10},{10,11},{12,13},{... | collective-permute-start | bytes 98312 | tf_op jit(solution)/shard_map/ppermute | solution.py:21
  115.5 5.8 %collective-permute-start.2 = (f32[1,16,512]{2,1,0:T(8,128)S(1)}, f32[1,16,512]{2,1,0:T(8,128)S(1)}, u32[]{:S(2)}, u32[]{:S(2)}) collective-permute-start(f32[1,16,512]{2,1,0:T(8,128)S(1)} %get-tuple-element.39), channel_id=1, source_target_pairs={{1,0},{2,1},{3,2},{5,4},{6,5},{7,6},{9,8},{10,9},{11,10},{13,12},{... | collective-permute-start | bytes 98312 | tf_op jit(solution)/shard_map/ppermute | solution.py:23
  116.8 4.5 %collective-permute-start.1 = (f32[1,16,512]{2,1,0:T(8,128)S(1)}, f32[1,16,512]{2,1,0:T(8,128)S(1)}, u32[]{:S(2)}, u32[]{:S(2)}) collective-permute-start(f32[1,16,512]{2,1,0:T(8,128)S(1)} %get-tuple-element.40), channel_id=1, source_target_pairs={{0,4},{4,8},{8,12},{1,5},{5,9},{9,13},{2,6},{6,10},{10,14},{3,7},{... | collective-permute-start | bytes 98312 | tf_op jit(solution)/shard_map/ppermute | solution.py:21
  118.7 3.3 %collective-permute-start = (f32[1,16,512]{2,1,0:T(8,128)S(1)}, f32[1,16,512]{2,1,0:T(8,128)S(1)}, u32[]{:S(2)}, u32[]{:S(2)}) collective-permute-start(f32[1,16,512]{2,1,0:T(8,128)S(1)} %get-tuple-element.37), channel_id=1, source_target_pairs={{4,0},{8,4},{12,8},{5,1},{9,5},{13,9},{6,2},{10,6},{14,10},{7,3},{... | collective-permute-start | bytes 98312 | tf_op jit(solution)/shard_map/ppermute | solution.py:23
  123.3 74.4 %copy-start.7 = (f32[256,512]{1,0:T(8,128)}, f32[256,512]{1,0:T(8,128)S(1)}, u32[]{:S(2)}) copy-start(f32[256,512]{1,0:T(8,128)S(1)} %scatter_fusion) | copy-start | bytes 1572868
Sparse Core Ops, SparseCore 0:
  10.9 72.6 all-gather.1
  105.8 90.0 reduce-scatter.1

commit v14 on v13

--- a/solution.py
+++ b/solution.py
@@ -135,18 +135,22 @@
                         loads[k].wait()
                         waited.append(k)
             halves = {}
-            pieces = []
+            top = 0
             for left, right in pairs:
                 if right not in halves:
                     halves[right] = split_bf16(staged[right][...])
-                pieces.append(inner_three(staged[left][...], *halves[right]))
-            product = jnp.concatenate(pieces, axis=0) * scale
-            results[index][...] = product.reshape(blocks, rows[index], width)
-            store = pltpu.make_async_copy(
-                results[index], out.at[:, offsets[index] : offsets[index + 1], :], out_sems.at[index]
-            )
-            store.start()
-            stores.append(store)
+                piece = inner_three(staged[left][...], *halves[right]) * scale
+                results[index][top : top + piece.shape[0], :] = piece
+                top += piece.shape[0]
+            size = rows[index]
+            for block in range(blocks):
+                store = pltpu.make_async_copy(
+                    results[index].at[block * size : (block + 1) * size, :],
+                    out.at[block, offsets[index] : offsets[index + 1], :],
+                    out_sems.at[index * blocks + block],
+                )
+                store.start()
+                stores.append(store)
         for store in stores:
             store.wait()
 
@@ -157,8 +161,8 @@
         in_specs=[any_space] * count_in,
         out_specs=any_space,
         scratch_shapes=[pltpu.VMEM(x.shape, x.dtype) for x in inputs]
-        + [pltpu.VMEM((blocks, size, width), jnp.float32) for size in rows]
-        + [pltpu.SemaphoreType.DMA((count_in,)), pltpu.SemaphoreType.DMA((len(terms),))],
+        + [pltpu.VMEM((blocks * size, width), jnp.float32) for size in rows]
+        + [pltpu.SemaphoreType.DMA((count_in,)), pltpu.SemaphoreType.DMA((len(terms) * blocks,))],
     )(*inputs)
 
 

time: 205 us -> 206 us (level)
  no operation moved by 1% of the time
where the time goes in v14:
time: 206 us; the launch traced here: 205 us
  waiting for transfers between devices  129 us (63%)
  starting transfers between devices  18.8 us (9%)
  between operations  15.9 us (8%)
  local copies, waits for them, and re-layouts  14.4 us (7%)
  Pallas kernels  10.6 us (5%)
  other arithmetic  9.18 us (4%)
  matrix products  7.56 us (4%)
    reduce_scatter x1, waiting for transfers between devices, shards(): lax.psum_scatter(blocked, peers, scatter_dimension=0, tiled=True)[0]  72.6 us
    all_gather x1, waiting for transfers between devices, shards(): gathered = lax.all_gather(packed, peers, axis=0, tiled=True)  54.1 us
    ppermute x4, starting transfers between devices, padded(): lax.ppermute(tail, axis, [(i, (i + 1) % count) for i in range(ends)])  13.5 us
    pallas_call x1, Pallas kernels, blocked_grads(): pl.pallas_call(kernel, out_shape=jax.ShapeDtypeStruct((blocks, offsets[-1...  6.8 us
    dot_general x4, matrix products, outer_back(): lax.dot_general(left, right, (((1,), (1,)), ((), ())), precision=lax.Prec...  6.29 us
    ppermute x4, starting transfers between devices, padded(): lax.ppermute(head, axis, [((i + 1) % count, i) for i in range(ends)])  5.17 us
    slice x6, local copies, waits for them, and re-layouts, shards(): pieces.append(gathered[:, offset:offset + rows, :])  4.58 us
  transfers between devices with their start and end apart: 10, of which 4 were waited for; matrix products, arithmetic and copies ran while one was open for 7% of the time, Pallas kernels for 0%

profile of v14, /device:TPU:0, one launch (start us, length us, event | category | flops | bytes accessed | tf_op | source)
XLA Modules:
  0.0 205.1 jit_solution(14041100936636430415)
XLA Ops:
  7.3 2.0 shard_map.226
  9.4 0.8 reshape.233
  10.1 0.8 broadcast_in_dim_reshape_squeeze.3
  10.9 1.8 gather_fusion
  12.8 1.3 collective-permute-start.7
  14.1 5.6 %collective-permute-start.6 = (f32[1,16,512]{2,1,0:T(8,128)S(1)}, f32[1,16,512]{2,1,0:T(8,128)S(1)}, u32[]{:S(2)}, u32[]{:S(2)}) collective-permute-start(f32[1,16,512]{2,1,0:T(8,128)S(1)} %get-tuple-element.44), channel_id=1, source_target_pairs={{0,1},{1,2},{2,3},{4,5},{5,6},{6,7},{8,9},{9,10},{10,11},{12,13},{... | collective-permute-start | bytes 98312 | tf_op jit(solution)/shard_map/ppermute | solution.py:21
  19.7 1.3 collective-permute-start.5
  21.0 3.0 %collective-permute-start.4 = (f32[1,16,512]{2,1,0:T(8,128)S(1)}, f32[1,16,512]{2,1,0:T(8,128)S(1)}, u32[]{:S(2)}, u32[]{:S(2)}) collective-permute-start(f32[1,16,512]{2,1,0:T(8,128)S(1)} %get-tuple-element.42), channel_id=1, source_target_pairs={{0,4},{4,8},{8,12},{1,5},{5,9},{9,13},{2,6},{6,10},{10,14},{3,7},{... | collective-permute-start | bytes 98312 | tf_op jit(solution)/shard_map/ppermute | solution.py:21
  25.4 0.7 broadcast_maximum_fusion.1.refs_4_
  26.1 0.9 broadcast_maximum_fusion.refs_10_
  27.1 0.8 gather_fusion.3
  27.9 0.8 gather_fusion.2
  28.6 0.9 broadcast_select_fusion.1
  29.5 54.1 %all-gather.2.cloned.1.call-done = f32[16,225,512]{2,1,0:T(8,128)} async-done(((f32[1,225,512]{2,1,0:T(8,128)}), f32[16,225,512]{2,1,0:T(8,128)}) %all-gather.2.cloned.1.call-update) | async-done | bytes 7372816 | tf_op jit(solution)/shard_map/all_gather | solution.py:243
  83.6 1.0 slice.161
  84.7 0.1 slice_reduce_fusion
  84.9 1.7 fusion.12
  86.6 1.0 copy-done.1
  87.6 0.6 fusion.14
  88.2 0.2 multiply_reduce_fusion.3
  88.6 0.7 fusion.15
  89.4 0.2 multiply_reduce_fusion.1
  89.6 0.3 fusion.4
  89.9 0.3 subtract_multiply_fusion.refs_11_
  90.2 0.8 copy-done.6
  91.0 2.1 %convolution_select_fusion.refs_7_ = f32[256,512]{1,0:T(8,128)S(1)} fusion(f32[256,512]{1,0:T(8,128)S(1)} %subtract_multiply_fusion.refs_11_, f32[512,512]{1,0:T(8,128)} %bitcast.65, f32[256,512]{1,0:T(8,128)} %param.24), kind=kOutput, calls=%fused_computation.8 | convolution fusion | flops 402915328 | bytes 2621440 | tf_op jit(solution)/shard_map/dot_general | solution.py:184
  93.1 1.1 fusion.16
  94.2 1.0 copy-done.10
  95.3 0.8 gather_fusion.4
  96.0 0.8 gather_fusion.1
  96.9 1.0 fusion.10
  97.9 0.1 subtract_multiply_fusion.1.refs_5_
  98.0 1.4 convolution_select_fusion.1.refs_1_
  99.4 6.8 %shard_map.227 = f32[16,224,512]{2,1,0:T(8,128)} custom-call(f32[128,512]{1,0:T(8,128)} %refs_0_.3, f32[128,512]{1,0:T(8,128)} %convolution_select_fusion.1.refs_1_, f32[128,512]{1,0:T(8,128)} %get-tuple-element.60.refs_2_, f32[128,512]{1,0:T(8,128)} %get-tuple-element.59.refs_3_, f32[128,512]{1,0:T(8,128)} %broadcast_maximum_fusion.1.refs_4_, ...), custom_call_target="tpu_custom_call" | custom-call | tf_op jit(solution)/shard_map/pallas_call | solution.py:158
  106.3 1.9 slice-done.1
  108.2 1.7 fusion.17
  109.9 0.8 fusion.13
  110.7 2.3 %scatter_custom_fusion = f32[320,512]{1,0:T(8,128)S(1)} fusion(s32[256]{0:T(256)S(1)} %bitcast.71, f32[128,512]{1,0:T(8,128)S(1)} %get-tuple-element.35, f32[]{:T(128)} %constant.75, f32[128,512]{1,0:T(8,128)S(1)} %get-tuple-element.34, f32[]{:T(128)} %constant.37.clone.1), kind=kCustom, calls=%fused_computation.14 | custom fusion | flops 262144 | bytes 1179656 | tf_op jit(solution)/shard_map/add | solution.py:309
  113.0 3.1 %collective-permute-start.3 = (f32[1,16,512]{2,1,0:T(8,128)S(1)}, f32[1,16,512]{2,1,0:T(8,128)S(1)}, u32[]{:S(2)}, u32[]{:S(2)}) collective-permute-start(f32[1,16,512]{2,1,0:T(8,128)S(1)} %get-tuple-element.38), channel_id=1, source_target_pairs={{0,1},{1,2},{2,3},{4,5},{5,6},{6,7},{8,9},{9,10},{10,11},{12,13},{... | collective-permute-start | bytes 98312 | tf_op jit(solution)/shard_map/ppermute | solution.py:21
  116.1 1.3 collective-permute-start.2
  117.4 1.9 collective-permute-start.1
  119.3 1.3 collective-permute-start
  120.6 0.1 slice_add_fusion
  120.7 1.1 collective-permute-done.2
  121.9 0.7 collective-permute-done
  122.6 1.2 scatter_fusion
  123.8 72.6 %reduce-scatter.2.cloned.1.call-done = f32[1,224,512]{2,1,0:T(8,128)} async-done(((f32[16,224,512]{2,1,0:T(8,128)}), f32[1,224,512]{2,1,0:T(8,128)}) %reduce-scatter.2.cloned.1.call-update) | async-done | bytes 458768 | tf_op jit(solution)/shard_map/reduce_scatter | solution.py:300
  196.4 1.8 shard_map.228
  (79 shorter events, 1.0 us)
Async XLA Ops:
  7.2 19.9 %copy-start.4 = (f32[256,512]{1,0:T(8,128)S(1)}, f32[256,512]{1,0:T(8,128)}, u32[]{:S(2)}) copy-start(f32[256,512]{1,0:T(8,128)} %refs_6_.1) | copy-start | bytes 1572868
  7.2 18.1 %copy-start.17 = (s32[2,128]{1,0:T(2,128)S(1)}, s32[2,128]{1,0:T(2,128)}, u32[]{:S(2)}) copy-start(s32[2,128]{1,0:T(2,128)} %param.29) | copy-start | bytes 3076
  7.2 18.2 %copy-start.14 = (f32[128,512]{1,0:T(8,128)S(1)}, f32[128,512]{1,0:T(8,128)}, u32[]{:S(2)}) copy-start(f32[128,512]{1,0:T(8,128)} %param.26) | copy-start | bytes 786436
  7.2 18.9 %copy-start.5 = (f32[256,512]{1,0:T(8,128)S(1)}, f32[256,512]{1,0:T(8,128)}, u32[]{:S(2)}) copy-start(f32[256,512]{1,0:T(8,128)} %param.24) | copy-start | bytes 1572868
  7.2 76.4 %all-gather.2.cloned.1.call-start = ((), (), s32[]{:S(2)}) async-start(), calls=%async_computation.1 | async-start | bytes 8077312 | tf_op jit(solution)/shard_map/all_gather | solution.py:243
  9.3 187.1 %reduce-scatter.2.cloned.1.call-start = ((), (), s32[]{:S(2)}) async-start(), calls=%async_computation.2 | async-start | bytes 7798784 | tf_op jit(solution)/shard_map/reduce_scatter | solution.py:300
  12.8 14.2 %collective-permute-start.7 = (f32[1,16,512]{2,1,0:T(8,128)S(1)}, f32[1,16,512]{2,1,0:T(8,128)S(1)}, u32[]{:S(2)}, u32[]{:S(2)}) collective-permute-start(f32[1,16,512]{2,1,0:T(8,128)S(1)} %get-tuple-element.43), channel_id=1, source_target_pairs={{1,0},{2,1},{3,2},{5,4},{6,5},{7,6},{9,8},{10,9},{11,10},{13,12},{... | collective-permute-start | bytes 98312 | tf_op jit(solution)/shard_map/ppermute | solution.py:23
  14.1 12.9 %collective-permute-start.6 = (f32[1,16,512]{2,1,0:T(8,128)S(1)}, f32[1,16,512]{2,1,0:T(8,128)S(1)}, u32[]{:S(2)}, u32[]{:S(2)}) collective-permute-start(f32[1,16,512]{2,1,0:T(8,128)S(1)} %get-tuple-element.44), channel_id=1, source_target_pairs={{0,1},{1,2},{2,3},{4,5},{5,6},{6,7},{8,9},{9,10},{10,11},{12,13},{... | collective-permute-start | bytes 98312 | tf_op jit(solution)/shard_map/ppermute | solution.py:21
  19.7 7.3 %collective-permute-start.5 = (f32[1,16,512]{2,1,0:T(8,128)S(1)}, f32[1,16,512]{2,1,0:T(8,128)S(1)}, u32[]{:S(2)}, u32[]{:S(2)}) collective-permute-start(f32[1,16,512]{2,1,0:T(8,128)S(1)} %get-tuple-element.45), channel_id=1, source_target_pairs={{4,0},{8,4},{12,8},{5,1},{9,5},{13,9},{6,2},{10,6},{14,10},{7,3},{... | collective-permute-start | bytes 98312 | tf_op jit(solution)/shard_map/ppermute | solution.py:23
  21.0 6.0 %collective-permute-start.4 = (f32[1,16,512]{2,1,0:T(8,128)S(1)}, f32[1,16,512]{2,1,0:T(8,128)S(1)}, u32[]{:S(2)}, u32[]{:S(2)}) collective-permute-start(f32[1,16,512]{2,1,0:T(8,128)S(1)} %get-tuple-element.42), channel_id=1, source_target_pairs={{0,4},{4,8},{8,12},{1,5},{5,9},{9,13},{2,6},{6,10},{10,14},{3,7},{... | collective-permute-start | bytes 98312 | tf_op jit(solution)/shard_map/ppermute | solution.py:21
  86.6 1.0 copy-start.1
  86.6 3.3 %copy-start.3 = (f32[16,32,512]{2,1,0:T(8,128)}, f32[16,32,512]{2,1,0:T(8,128)S(1)}, u32[]{:S(2)}) copy-start(f32[16,32,512]{2,1,0:T(8,128)S(1)} %get-tuple-element.32) | copy-start | bytes 3145732
  86.6 3.0 %copy-start.8 = (f32[256,512]{1,0:T(8,128)S(1)}, f32[256,512]{1,0:T(8,128)}, u32[]{:S(2)}) copy-start(f32[256,512]{1,0:T(8,128)} %param.27) | copy-start | bytes 1572868
  90.2 0.8 copy-start.6
  91.0 2.1 %slice-start = ((f32[16,225,512]{2,1,0:T(8,128)}), f32[16,64,512]{2,1,0:T(8,128)S(1)}, s32[]{:S(2)}) async-start(f32[16,225,512]{2,1,0:T(8,128)} %all-gather.2.cloned.1.call-done), calls=%async_computation.3 | async-start | bytes 4194304 | tf_op jit(solution)/shard_map/slice | solution.py:247
  93.1 2.1 %copy-start = (f32[256,512]{1,0:T(8,128)}, f32[256,512]{1,0:T(8,128)S(1)}, u32[]{:S(2)}) copy-start(f32[256,512]{1,0:T(8,128)S(1)} %convolution_select_fusion.refs_7_) | copy-start | bytes 1572868
  94.2 1.0 copy-start.10
  95.2 1.7 copy-start.16
  95.3 2.8 %copy-start.2 = (f32[16,32,512]{2,1,0:T(8,128)S(1)}, f32[16,32,512]{2,1,0:T(8,128)}, u32[]{:S(2)}) copy-start(f32[16,32,512]{2,1,0:T(8,128)} %copy-done.1) | copy-start | bytes 3145732
  95.3 2.8 %copy-start.15 = (f32[128,512]{1,0:T(8,128)S(1)}, f32[128,512]{1,0:T(8,128)}, u32[]{:S(2)}) copy-start(f32[128,512]{1,0:T(8,128)} %param.26) | copy-start | bytes 786436
  98.0 1.4 copy-start.13
  106.3 1.9 slice-start.1
  106.3 1.9 copy-start.12
  108.2 12.4 %copy-start.9 = (f32[256,512]{1,0:T(8,128)S(1)}, f32[256,512]{1,0:T(8,128)}, u32[]{:S(2)}) copy-start(f32[256,512]{1,0:T(8,128)} %param.27) | copy-start | bytes 1572868
  108.2 12.4 %copy-start.11 = (f32[256,1024]{1,0:T(8,128)S(1)}, f32[256,1024]{1,0:T(8,128)}, u32[]{:S(2)}) copy-start(f32[256,1024]{1,0:T(8,128)} %copy-done.10) | copy-start | bytes 3145732
  113.0 7.7 %collective-permute-start.3 = (f32[1,16,512]{2,1,0:T(8,128)S(1)}, f32[1,16,512]{2,1,0:T(8,128)S(1)}, u32[]{:S(2)}, u32[]{:S(2)}) collective-permute-start(f32[1,16,512]{2,1,0:T(8,128)S(1)} %get-tuple-element.38), channel_id=1, source_target_pairs={{0,1},{1,2},{2,3},{4,5},{5,6},{6,7},{8,9},{9,10},{10,11},{12,13},{... | collective-permute-start | bytes 98312 | tf_op jit(solution)/shard_map/ppermute | solution.py:21
  116.1 5.8 %collective-permute-start.2 = (f32[1,16,512]{2,1,0:T(8,128)S(1)}, f32[1,16,512]{2,1,0:T(8,128)S(1)}, u32[]{:S(2)}, u32[]{:S(2)}) collective-permute-start(f32[1,16,512]{2,1,0:T(8,128)S(1)} %get-tuple-element.39), channel_id=1, source_target_pairs={{1,0},{2,1},{3,2},{5,4},{6,5},{7,6},{9,8},{10,9},{11,10},{13,12},{... | collective-permute-start | bytes 98312 | tf_op jit(solution)/shard_map/ppermute | solution.py:23
  117.4 4.5 %collective-permute-start.1 = (f32[1,16,512]{2,1,0:T(8,128)S(1)}, f32[1,16,512]{2,1,0:T(8,128)S(1)}, u32[]{:S(2)}, u32[]{:S(2)}) collective-permute-start(f32[1,16,512]{2,1,0:T(8,128)S(1)} %get-tuple-element.40), channel_id=1, source_target_pairs={{0,4},{4,8},{8,12},{1,5},{5,9},{9,13},{2,6},{6,10},{10,14},{3,7},{... | collective-permute-start | bytes 98312 | tf_op jit(solution)/shard_map/ppermute | solution.py:21
  119.3 3.3 %collective-permute-start = (f32[1,16,512]{2,1,0:T(8,128)S(1)}, f32[1,16,512]{2,1,0:T(8,128)S(1)}, u32[]{:S(2)}, u32[]{:S(2)}) collective-permute-start(f32[1,16,512]{2,1,0:T(8,128)S(1)} %get-tuple-element.37), channel_id=1, source_target_pairs={{4,0},{8,4},{12,8},{5,1},{9,5},{13,9},{6,2},{10,6},{14,10},{7,3},{... | collective-permute-start | bytes 98312 | tf_op jit(solution)/shard_map/ppermute | solution.py:23
  123.8 74.4 %copy-start.7 = (f32[256,512]{1,0:T(8,128)}, f32[256,512]{1,0:T(8,128)S(1)}, u32[]{:S(2)}) copy-start(f32[256,512]{1,0:T(8,128)S(1)} %scatter_fusion) | copy-start | bytes 1572868
Sparse Core Ops, SparseCore 0:
  10.9 72.6 all-gather.1
  106.4 90.0 reduce-scatter.1

commit v15 on v12

--- a/solution.py
+++ b/solution.py
@@ -123,9 +123,9 @@
                 loads[k].wait()
             pieces = []
             for k in range(count):
-                right_high, right_low = split_bf16(staged[start + 2 * k + 1][...])
+                right_high, right_low = split_bf16(staged[start + 2 * k + 1][...] * scale)
                 pieces.append(inner_three(staged[start + 2 * k][...], right_high, right_low))
-            product = jnp.concatenate(pieces, axis=0) * scale
+            product = jnp.concatenate(pieces, axis=0)
             results[index][...] = product.reshape(blocks, rows[index], width)
             store = pltpu.make_async_copy(
                 results[index], out.at[:, offsets[index] : offsets[index + 1], :], out_sems.at[index]

time: 205 us -> 205 us (level)
  no operation moved by 1% of the time
where the time goes in v15:
time: 205 us
  waiting for transfers between devices  129 us (63%)
  starting transfers between devices  18.8 us (9%)
  between operations  15.9 us (8%)
  local copies, waits for them, and re-layouts  14.4 us (7%)
  Pallas kernels  10.1 us (5%)
  other arithmetic  9.18 us (4%)
  matrix products  7.56 us (4%)
    reduce_scatter x1, waiting for transfers between devices, shards(): lax.psum_scatter(blocked, peers, scatter_dimension=0, tiled=True)[0]  72.7 us
    all_gather x1, waiting for transfers between devices, shards(): gathered = lax.all_gather(packed, peers, axis=0, tiled=True)  54.1 us
    ppermute x4, starting transfers between devices, padded(): lax.ppermute(tail, axis, [(i, (i + 1) % count) for i in range(ends)])  13.5 us
    pallas_call x1, Pallas kernels, blocked_grads(): pl.pallas_call(kernel, out_shape=jax.ShapeDtypeStruct((blocks, offsets[-1...  6.3 us
    dot_general x4, matrix products, outer_back(): lax.dot_general(left, right, (((1,), (1,)), ((), ())), precision=lax.Prec...  6.29 us
    ppermute x4, starting transfers between devices, padded(): lax.ppermute(head, axis, [((i + 1) % count, i) for i in range(ends)])  5.17 us
    slice x6, local copies, waits for them, and re-layouts, shards(): pieces.append(gathered[:, offset:offset + rows, :])  4.58 us
  transfers between devices with their start and end apart: 10, of which 4 were waited for; matrix products, arithmetic and copies ran while one was open for 7% of the time, Pallas kernels for 0%

profile of v15, /device:TPU:0, one launch (start us, length us, event | category | flops | bytes accessed | tf_op | source)
XLA Modules:
  0.0 204.6 jit_solution(17017728387708937711)
XLA Ops:
  7.3 2.0 shard_map.226
  9.4 0.8 reshape.233
  10.1 0.8 broadcast_in_dim_reshape_squeeze.3
  10.9 1.8 gather_fusion
  12.8 1.3 collective-permute-start.7
  14.1 5.6 %collective-permute-start.6 = (f32[1,16,512]{2,1,0:T(8,128)S(1)}, f32[1,16,512]{2,1,0:T(8,128)S(1)}, u32[]{:S(2)}, u32[]{:S(2)}) collective-permute-start(f32[1,16,512]{2,1,0:T(8,128)S(1)} %get-tuple-element.44), channel_id=1, source_target_pairs={{0,1},{1,2},{2,3},{4,5},{5,6},{6,7},{8,9},{9,10},{10,11},{12,13},{... | collective-permute-start | bytes 98312 | tf_op jit(solution)/shard_map/ppermute | solution.py:21
  19.7 1.3 collective-permute-start.5
  21.0 3.0 %collective-permute-start.4 = (f32[1,16,512]{2,1,0:T(8,128)S(1)}, f32[1,16,512]{2,1,0:T(8,128)S(1)}, u32[]{:S(2)}, u32[]{:S(2)}) collective-permute-start(f32[1,16,512]{2,1,0:T(8,128)S(1)} %get-tuple-element.42), channel_id=1, source_target_pairs={{0,4},{4,8},{8,12},{1,5},{5,9},{9,13},{2,6},{6,10},{10,14},{3,7},{... | collective-permute-start | bytes 98312 | tf_op jit(solution)/shard_map/ppermute | solution.py:21
  25.4 0.7 broadcast_maximum_fusion.1.refs_6_
  26.1 0.9 broadcast_maximum_fusion.refs_12_
  27.1 0.8 gather_fusion.3
  27.9 0.8 gather_fusion.2
  28.6 0.9 broadcast_select_fusion.1
  29.5 54.1 %all-gather.2.cloned.1.call-done = f32[16,225,512]{2,1,0:T(8,128)} async-done(((f32[1,225,512]{2,1,0:T(8,128)}), f32[16,225,512]{2,1,0:T(8,128)}) %all-gather.2.cloned.1.call-update) | async-done | bytes 7372816 | tf_op jit(solution)/shard_map/all_gather | solution.py:224
  83.6 1.0 slice.161
  84.7 0.1 slice_reduce_fusion
  84.9 1.7 fusion.12
  86.6 1.0 copy-done.1
  87.6 0.6 fusion.14
  88.2 0.2 multiply_reduce_fusion.3
  88.6 0.7 fusion.15
  89.4 0.2 multiply_reduce_fusion.1
  89.6 0.3 fusion.4
  89.9 0.3 subtract_multiply_fusion.refs_13_
  90.2 0.8 copy-done.7
  91.0 2.1 %convolution_select_fusion.refs_9_ = f32[256,512]{1,0:T(8,128)S(1)} fusion(f32[256,512]{1,0:T(8,128)S(1)} %subtract_multiply_fusion.refs_13_, f32[512,512]{1,0:T(8,128)} %bitcast.65, f32[256,512]{1,0:T(8,128)} %param.24), kind=kOutput, calls=%fused_computation.8 | convolution fusion | flops 402915328 | bytes 2621440 | tf_op jit(solution)/shard_map/dot_general | solution.py:165
  93.1 1.1 fusion.16
  94.2 1.0 copy-done.11
  95.3 0.8 gather_fusion.4
  96.0 0.8 gather_fusion.1
  96.9 1.0 fusion.10
  97.9 0.1 subtract_multiply_fusion.1.refs_7_
  98.0 1.4 convolution_select_fusion.1.refs_1_.refs_3_.refs_5_
  99.4 6.3 %shard_map.227 = f32[16,224,512]{2,1,0:T(8,128)} custom-call(f32[128,512]{1,0:T(8,128)} %refs_0_.3, f32[128,512]{1,0:T(8,128)} %convolution_select_fusion.1.refs_1_.refs_3_.refs_5_, f32[128,512]{1,0:T(8,128)} %get-tuple-element.60.refs_2_, f32[128,512]{1,0:T(8,128)} %convolution_select_fusion.1.refs_1_.refs_3_.refs_5_, ...), custom_call_target="tpu_custom_call" | custom-call | tf_op jit(solution)/shard_map/pallas_call | solution.py:139
  105.8 1.9 slice-done.1
  107.7 1.7 fusion.17
  109.4 0.8 fusion.13
  110.2 2.3 %scatter_custom_fusion = f32[320,512]{1,0:T(8,128)S(1)} fusion(s32[256]{0:T(256)S(1)} %bitcast.71, f32[128,512]{1,0:T(8,128)S(1)} %get-tuple-element.35, f32[]{:T(128)} %constant.75, f32[128,512]{1,0:T(8,128)S(1)} %get-tuple-element.34, f32[]{:T(128)} %constant.37.clone.1), kind=kCustom, calls=%fused_computation.14 | custom fusion | flops 262144 | bytes 1179656 | tf_op jit(solution)/shard_map/add | solution.py:290
  112.5 3.0 %collective-permute-start.3 = (f32[1,16,512]{2,1,0:T(8,128)S(1)}, f32[1,16,512]{2,1,0:T(8,128)S(1)}, u32[]{:S(2)}, u32[]{:S(2)}) collective-permute-start(f32[1,16,512]{2,1,0:T(8,128)S(1)} %get-tuple-element.38), channel_id=1, source_target_pairs={{0,1},{1,2},{2,3},{4,5},{5,6},{6,7},{8,9},{9,10},{10,11},{12,13},{... | collective-permute-start | bytes 98312 | tf_op jit(solution)/shard_map/ppermute | solution.py:21
  115.6 1.3 collective-permute-start.2
  116.9 1.9 collective-permute-start.1
  118.8 1.3 collective-permute-start
  120.1 0.1 slice_add_fusion
  120.2 1.2 collective-permute-done.2
  121.4 0.7 collective-permute-done
  122.1 1.2 scatter_fusion
  123.3 72.7 %reduce-scatter.2.cloned.1.call-done = f32[1,224,512]{2,1,0:T(8,128)} async-done(((f32[16,224,512]{2,1,0:T(8,128)}), f32[1,224,512]{2,1,0:T(8,128)}) %reduce-scatter.2.cloned.1.call-update) | async-done | bytes 458768 | tf_op jit(solution)/shard_map/reduce_scatter | solution.py:281
  196.0 1.8 shard_map.228
  (79 shorter events, 1.0 us)
Async XLA Ops:
  7.2 19.9 %copy-start.4 = (f32[256,512]{1,0:T(8,128)S(1)}, f32[256,512]{1,0:T(8,128)}, u32[]{:S(2)}) copy-start(f32[256,512]{1,0:T(8,128)} %refs_8_.1) | copy-start | bytes 1572868
  7.2 18.1 %copy-start.17 = (s32[2,128]{1,0:T(2,128)S(1)}, s32[2,128]{1,0:T(2,128)}, u32[]{:S(2)}) copy-start(s32[2,128]{1,0:T(2,128)} %param.29) | copy-start | bytes 3076
  7.2 18.2 %copy-start.14 = (f32[128,512]{1,0:T(8,128)S(1)}, f32[128,512]{1,0:T(8,128)}, u32[]{:S(2)}) copy-start(f32[128,512]{1,0:T(8,128)} %param.26) | copy-start | bytes 786436
  7.2 18.9 %copy-start.6 = (f32[256,512]{1,0:T(8,128)S(1)}, f32[256,512]{1,0:T(8,128)}, u32[]{:S(2)}) copy-start(f32[256,512]{1,0:T(8,128)} %param.24) | copy-start | bytes 1572868
  7.2 76.4 %all-gather.2.cloned.1.call-start = ((), (), s32[]{:S(2)}) async-start(), calls=%async_computation.1 | async-start | bytes 8077312 | tf_op jit(solution)/shard_map/all_gather | solution.py:224
  9.3 186.7 %reduce-scatter.2.cloned.1.call-start = ((), (), s32[]{:S(2)}) async-start(), calls=%async_computation.2 | async-start | bytes 7798784 | tf_op jit(solution)/shard_map/reduce_scatter | solution.py:281
  12.8 14.2 %collective-permute-start.7 = (f32[1,16,512]{2,1,0:T(8,128)S(1)}, f32[1,16,512]{2,1,0:T(8,128)S(1)}, u32[]{:S(2)}, u32[]{:S(2)}) collective-permute-start(f32[1,16,512]{2,1,0:T(8,128)S(1)} %get-tuple-element.43), channel_id=1, source_target_pairs={{1,0},{2,1},{3,2},{5,4},{6,5},{7,6},{9,8},{10,9},{11,10},{13,12},{... | collective-permute-start | bytes 98312 | tf_op jit(solution)/shard_map/ppermute | solution.py:23
  14.1 12.9 %collective-permute-start.6 = (f32[1,16,512]{2,1,0:T(8,128)S(1)}, f32[1,16,512]{2,1,0:T(8,128)S(1)}, u32[]{:S(2)}, u32[]{:S(2)}) collective-permute-start(f32[1,16,512]{2,1,0:T(8,128)S(1)} %get-tuple-element.44), channel_id=1, source_target_pairs={{0,1},{1,2},{2,3},{4,5},{5,6},{6,7},{8,9},{9,10},{10,11},{12,13},{... | collective-permute-start | bytes 98312 | tf_op jit(solution)/shard_map/ppermute | solution.py:21
  19.7 7.3 %collective-permute-start.5 = (f32[1,16,512]{2,1,0:T(8,128)S(1)}, f32[1,16,512]{2,1,0:T(8,128)S(1)}, u32[]{:S(2)}, u32[]{:S(2)}) collective-permute-start(f32[1,16,512]{2,1,0:T(8,128)S(1)} %get-tuple-element.45), channel_id=1, source_target_pairs={{4,0},{8,4},{12,8},{5,1},{9,5},{13,9},{6,2},{10,6},{14,10},{7,3},{... | collective-permute-start | bytes 98312 | tf_op jit(solution)/shard_map/ppermute | solution.py:23
  21.0 6.0 %collective-permute-start.4 = (f32[1,16,512]{2,1,0:T(8,128)S(1)}, f32[1,16,512]{2,1,0:T(8,128)S(1)}, u32[]{:S(2)}, u32[]{:S(2)}) collective-permute-start(f32[1,16,512]{2,1,0:T(8,128)S(1)} %get-tuple-element.42), channel_id=1, source_target_pairs={{0,4},{4,8},{8,12},{1,5},{5,9},{9,13},{2,6},{6,10},{10,14},{3,7},{... | collective-permute-start | bytes 98312 | tf_op jit(solution)/shard_map/ppermute | solution.py:21
  86.6 1.0 copy-start.1
  86.6 3.3 %copy-start.3 = (f32[16,32,512]{2,1,0:T(8,128)}, f32[16,32,512]{2,1,0:T(8,128)S(1)}, u32[]{:S(2)}) copy-start(f32[16,32,512]{2,1,0:T(8,128)S(1)} %get-tuple-element.32) | copy-start | bytes 3145732
  86.6 3.0 %copy-start.9 = (f32[256,512]{1,0:T(8,128)S(1)}, f32[256,512]{1,0:T(8,128)}, u32[]{:S(2)}) copy-start(f32[256,512]{1,0:T(8,128)} %param.27) | copy-start | bytes 1572868
  90.2 0.8 copy-start.7
  91.0 2.1 %slice-start = ((f32[16,225,512]{2,1,0:T(8,128)}), f32[16,64,512]{2,1,0:T(8,128)S(1)}, s32[]{:S(2)}) async-start(f32[16,225,512]{2,1,0:T(8,128)} %all-gather.2.cloned.1.call-done), calls=%async_computation.3 | async-start | bytes 4194304 | tf_op jit(solution)/shard_map/slice | solution.py:228
  93.1 2.1 %copy-start = (f32[256,512]{1,0:T(8,128)}, f32[256,512]{1,0:T(8,128)S(1)}, u32[]{:S(2)}) copy-start(f32[256,512]{1,0:T(8,128)S(1)} %convolution_select_fusion.refs_9_) | copy-start | bytes 1572868
  94.2 1.0 copy-start.11
  95.2 1.7 copy-start.16
  95.3 2.8 %copy-start.2 = (f32[16,32,512]{2,1,0:T(8,128)S(1)}, f32[16,32,512]{2,1,0:T(8,128)}, u32[]{:S(2)}) copy-start(f32[16,32,512]{2,1,0:T(8,128)} %copy-done.1) | copy-start | bytes 3145732
  95.3 2.8 %copy-start.15 = (f32[128,512]{1,0:T(8,128)S(1)}, f32[128,512]{1,0:T(8,128)}, u32[]{:S(2)}) copy-start(f32[128,512]{1,0:T(8,128)} %param.26) | copy-start | bytes 786436
  98.0 1.4 copy-start.13
  105.8 1.9 slice-start.1
  105.8 1.9 copy-start.5
  107.7 12.4 %copy-start.10 = (f32[256,512]{1,0:T(8,128)S(1)}, f32[256,512]{1,0:T(8,128)}, u32[]{:S(2)}) copy-start(f32[256,512]{1,0:T(8,128)} %param.27) | copy-start | bytes 1572868
  107.7 12.4 %copy-start.12 = (f32[256,1024]{1,0:T(8,128)S(1)}, f32[256,1024]{1,0:T(8,128)}, u32[]{:S(2)}) copy-start(f32[256,1024]{1,0:T(8,128)} %copy-done.11) | copy-start | bytes 3145732
  112.5 7.7 %collective-permute-start.3 = (f32[1,16,512]{2,1,0:T(8,128)S(1)}, f32[1,16,512]{2,1,0:T(8,128)S(1)}, u32[]{:S(2)}, u32[]{:S(2)}) collective-permute-start(f32[1,16,512]{2,1,0:T(8,128)S(1)} %get-tuple-element.38), channel_id=1, source_target_pairs={{0,1},{1,2},{2,3},{4,5},{5,6},{6,7},{8,9},{9,10},{10,11},{12,13},{... | collective-permute-start | bytes 98312 | tf_op jit(solution)/shard_map/ppermute | solution.py:21
  115.6 5.8 %collective-permute-start.2 = (f32[1,16,512]{2,1,0:T(8,128)S(1)}, f32[1,16,512]{2,1,0:T(8,128)S(1)}, u32[]{:S(2)}, u32[]{:S(2)}) collective-permute-start(f32[1,16,512]{2,1,0:T(8,128)S(1)} %get-tuple-element.39), channel_id=1, source_target_pairs={{1,0},{2,1},{3,2},{5,4},{6,5},{7,6},{9,8},{10,9},{11,10},{13,12},{... | collective-permute-start | bytes 98312 | tf_op jit(solution)/shard_map/ppermute | solution.py:23
  116.9 4.5 %collective-permute-start.1 = (f32[1,16,512]{2,1,0:T(8,128)S(1)}, f32[1,16,512]{2,1,0:T(8,128)S(1)}, u32[]{:S(2)}, u32[]{:S(2)}) collective-permute-start(f32[1,16,512]{2,1,0:T(8,128)S(1)} %get-tuple-element.40), channel_id=1, source_target_pairs={{0,4},{4,8},{8,12},{1,5},{5,9},{9,13},{2,6},{6,10},{10,14},{3,7},{... | collective-permute-start | bytes 98312 | tf_op jit(solution)/shard_map/ppermute | solution.py:21
  118.8 3.3 %collective-permute-start = (f32[1,16,512]{2,1,0:T(8,128)S(1)}, f32[1,16,512]{2,1,0:T(8,128)S(1)}, u32[]{:S(2)}, u32[]{:S(2)}) collective-permute-start(f32[1,16,512]{2,1,0:T(8,128)S(1)} %get-tuple-element.37), channel_id=1, source_target_pairs={{4,0},{8,4},{12,8},{5,1},{9,5},{13,9},{6,2},{10,6},{14,10},{7,3},{... | collective-permute-start | bytes 98312 | tf_op jit(solution)/shard_map/ppermute | solution.py:23
  123.3 74.5 %copy-start.8 = (f32[256,512]{1,0:T(8,128)}, f32[256,512]{1,0:T(8,128)S(1)}, u32[]{:S(2)}) copy-start(f32[256,512]{1,0:T(8,128)S(1)} %scatter_fusion) | copy-start | bytes 1572868
Sparse Core Ops, SparseCore 0:
  10.9 72.6 all-gather.1
  105.9 90.0 reduce-scatter.1

commit v16 on v12

--- a/solution.py
+++ b/solution.py
@@ -60,13 +60,36 @@
 def split_rows(packed, sizes):
     offsets = row_offsets(sizes)
 
-    def kernel(source, *outs):
-        for index, out in enumerate(outs):
-            out[...] = source[offsets[index] : offsets[index + 1], :]
-
+    if any(size % 8 for size in sizes):
+
+        def staged(source, *outs):
+            for index, out in enumerate(outs):
+                out[...] = source[offsets[index] : offsets[index + 1], :]
+
+        return pl.pallas_call(
+            staged,
+            out_shape=tuple(jax.ShapeDtypeStruct((size, packed.shape[1]), packed.dtype) for size in sizes),
+        )(packed)
+
+    def kernel(source, *refs):
+        outs = refs[:-1]
+        sems = refs[-1]
+        copies = [
+            pltpu.make_async_copy(source.at[offsets[index] : offsets[index + 1], :], out, sems.at[index])
+            for index, out in enumerate(outs)
+        ]
+        for copy in copies:
+            copy.start()
+        for copy in copies:
+            copy.wait()
+
+    any_space = pl.BlockSpec(memory_space=pl.ANY)
     return pl.pallas_call(
         kernel,
         out_shape=tuple(jax.ShapeDtypeStruct((size, packed.shape[1]), packed.dtype) for size in sizes),
+        in_specs=[any_space],
+        out_specs=tuple(any_space for _ in sizes),
+        scratch_shapes=[pltpu.SemaphoreType.DMA((len(sizes),))],
     )(packed)
 
 

time: 205 us -> 218 us (1.063)
  Pallas kernels: 10.1 us -> 23.3 us
    pallas_call x1, Pallas kernels: 1.78 us -> 15 us  [split_rows(): pl.pallas_call(kernel, out_shape=tuple((jax.ShapeDtypeStruct((size, packe...]
  transfers between devices with their start and end apart: 10 -> 10, of which waited for: 4 -> 4; matrix products, arithmetic and copies ran while one was open for 7% -> 6% of each run, Pallas kernels for 0% -> 0%
where the time goes in v16:
time: 218 us
  waiting for transfers between devices  129 us (59%)
  Pallas kernels  23.3 us (11%)
  starting transfers between devices  18.8 us (9%)
  between operations  15.9 us (7%)
  local copies, waits for them, and re-layouts  14.4 us (7%)
  other arithmetic  9.18 us (4%)
  matrix products  7.56 us (3%)
    reduce_scatter x1, waiting for transfers between devices, shards(): lax.psum_scatter(blocked, peers, scatter_dimension=0, tiled=True)[0]  72.7 us
    all_gather x1, waiting for transfers between devices, shards(): gathered = lax.all_gather(packed, peers, axis=0, tiled=True)  54.1 us
    pallas_call x1, Pallas kernels, split_rows(): pl.pallas_call(kernel, out_shape=tuple((jax.ShapeDtypeStruct((size, packe...  15 us
    ppermute x4, starting transfers between devices, padded(): lax.ppermute(tail, axis, [(i, (i + 1) % count) for i in range(ends)])  13.5 us
    dot_general x4, matrix products, outer_back(): lax.dot_general(left, right, (((1,), (1,)), ((), ())), precision=lax.Prec...  6.29 us
    pallas_call x1, Pallas kernels, blocked_grads(): pl.pallas_call(kernel, out_shape=jax.ShapeDtypeStruct((blocks, offsets[-1...  6.28 us
    ppermute x4, starting transfers between devices, padded(): lax.ppermute(head, axis, [((i + 1) % count, i) for i in range(ends)])  5.17 us
    slice x6, local copies, waits for them, and re-layouts, shards(): pieces.append(gathered[:, offset:offset + rows, :])  4.58 us
  transfers between devices with their start and end apart: 10, of which 4 were waited for; matrix products, arithmetic and copies ran while one was open for 6% of the time, Pallas kernels for 0%

profile of v16, /device:TPU:0, one launch (start us, length us, event | category | flops | bytes accessed | tf_op | source)
XLA Modules:
  0.0 217.9 jit_solution(4612065528932652236)
XLA Ops:
  7.3 2.0 shard_map.226
  9.4 0.8 reshape.233
  10.1 0.8 broadcast_in_dim_reshape_squeeze.3
  10.9 1.8 gather_fusion
  12.8 1.3 collective-permute-start.7
  14.1 5.6 %collective-permute-start.6 = (f32[1,16,512]{2,1,0:T(8,128)S(1)}, f32[1,16,512]{2,1,0:T(8,128)S(1)}, u32[]{:S(2)}, u32[]{:S(2)}) collective-permute-start(f32[1,16,512]{2,1,0:T(8,128)S(1)} %get-tuple-element.44), channel_id=1, source_target_pairs={{0,1},{1,2},{2,3},{4,5},{5,6},{6,7},{8,9},{9,10},{10,11},{12,13},{... | collective-permute-start | bytes 98312 | tf_op jit(solution)/shard_map/ppermute | solution.py:21
  19.7 1.3 collective-permute-start.5
  21.0 3.0 %collective-permute-start.4 = (f32[1,16,512]{2,1,0:T(8,128)S(1)}, f32[1,16,512]{2,1,0:T(8,128)S(1)}, u32[]{:S(2)}, u32[]{:S(2)}) collective-permute-start(f32[1,16,512]{2,1,0:T(8,128)S(1)} %get-tuple-element.42), channel_id=1, source_target_pairs={{0,4},{4,8},{8,12},{1,5},{5,9},{9,13},{2,6},{6,10},{10,14},{3,7},{... | collective-permute-start | bytes 98312 | tf_op jit(solution)/shard_map/ppermute | solution.py:21
  25.4 0.7 broadcast_maximum_fusion.1.refs_6_
  26.1 0.9 broadcast_maximum_fusion.refs_12_
  27.1 0.8 gather_fusion.3
  27.9 0.8 gather_fusion.2
  28.6 0.9 broadcast_select_fusion.1
  29.5 54.1 %all-gather.2.cloned.1.call-done = f32[16,225,512]{2,1,0:T(8,128)} async-done(((f32[1,225,512]{2,1,0:T(8,128)}), f32[16,225,512]{2,1,0:T(8,128)}) %all-gather.2.cloned.1.call-update) | async-done | bytes 7372816 | tf_op jit(solution)/shard_map/all_gather | solution.py:247
  83.6 1.0 slice.161
  84.7 0.1 slice_reduce_fusion
  84.9 1.7 fusion.12
  86.6 1.0 copy-done.1
  87.6 0.6 fusion.14
  88.2 0.2 multiply_reduce_fusion.3
  88.6 0.7 fusion.15
  89.4 0.2 multiply_reduce_fusion.1
  89.6 0.3 fusion.4
  89.9 0.3 subtract_multiply_fusion.refs_13_
  90.2 0.8 copy-done.7
  91.0 2.1 convolution_select_fusion.refs_9_
  93.1 1.1 fusion.16
  94.2 1.0 copy-done.11
  95.3 0.8 gather_fusion.4
  96.0 0.8 gather_fusion.1
  96.9 1.0 fusion.10
  97.9 0.1 subtract_multiply_fusion.1.refs_7_
  98.0 1.4 convolution_select_fusion.1.refs_1_.refs_3_.refs_5_
  99.4 6.3 %shard_map.227 = f32[16,224,512]{2,1,0:T(8,128)} custom-call(f32[128,512]{1,0:T(8,128)} %refs_0_.3, f32[128,512]{1,0:T(8,128)} %convolution_select_fusion.1.refs_1_.refs_3_.refs_5_, f32[128,512]{1,0:T(8,128)} %get-tuple-element.60.refs_2_, f32[128,512]{1,0:T(8,128)} %convolution_select_fusion.1.refs_1_.refs_3_.refs_5_, ...), custom_call_target="tpu_custom_call" | custom-call | tf_op jit(solution)/shard_map/pallas_call | solution.py:162
  105.8 1.9 slice-done.1
  107.7 1.7 fusion.17
  109.4 0.8 fusion.13
  110.2 2.3 %scatter_custom_fusion = f32[320,512]{1,0:T(8,128)S(1)} fusion(s32[256]{0:T(256)S(1)} %bitcast.71, f32[128,512]{1,0:T(8,128)S(1)} %get-tuple-element.35, f32[]{:T(128)} %constant.75, f32[128,512]{1,0:T(8,128)S(1)} %get-tuple-element.34, f32[]{:T(128)} %constant.37.clone.1), kind=kCustom, calls=%fused_computation.14 | custom fusion | flops 262144 | bytes 1179656 | tf_op jit(solution)/shard_map/add | solution.py:313
  112.5 3.1 %collective-permute-start.3 = (f32[1,16,512]{2,1,0:T(8,128)S(1)}, f32[1,16,512]{2,1,0:T(8,128)S(1)}, u32[]{:S(2)}, u32[]{:S(2)}) collective-permute-start(f32[1,16,512]{2,1,0:T(8,128)S(1)} %get-tuple-element.38), channel_id=1, source_target_pairs={{0,1},{1,2},{2,3},{4,5},{5,6},{6,7},{8,9},{9,10},{10,11},{12,13},{... | collective-permute-start | bytes 98312 | tf_op jit(solution)/shard_map/ppermute | solution.py:21
  115.6 1.3 collective-permute-start.2
  116.9 1.9 collective-permute-start.1
  118.8 1.3 collective-permute-start
  120.1 0.1 slice_add_fusion
  120.2 1.1 collective-permute-done.2
  121.4 0.7 collective-permute-done
  122.1 1.2 scatter_fusion
  123.3 72.7 %reduce-scatter.2.cloned.1.call-done = f32[1,224,512]{2,1,0:T(8,128)} async-done(((f32[16,224,512]{2,1,0:T(8,128)}), f32[1,224,512]{2,1,0:T(8,128)}) %reduce-scatter.2.cloned.1.call-update) | async-done | bytes 458768 | tf_op jit(solution)/shard_map/reduce_scatter | solution.py:304
  196.0 15.0 %shard_map.228 = (f32[96,512]{1,0:T(8,128)}, f32[32,512]{1,0:T(8,128)}, f32[64,512]{1,0:T(8,128)}, f32[32,512]{1,0:T(8,128)}) custom-call(f32[224,512]{1,0:T(8,128)} %bitcast.68), custom_call_target="tpu_custom_call" | custom-call | tf_op jit(solution)/shard_map/pallas_call | solution.py:87
  (79 shorter events, 1.0 us)
Async XLA Ops:
  7.2 19.9 %copy-start.4 = (f32[256,512]{1,0:T(8,128)S(1)}, f32[256,512]{1,0:T(8,128)}, u32[]{:S(2)}) copy-start(f32[256,512]{1,0:T(8,128)} %refs_8_.1) | copy-start | bytes 1572868
  7.2 18.1 %copy-start.17 = (s32[2,128]{1,0:T(2,128)S(1)}, s32[2,128]{1,0:T(2,128)}, u32[]{:S(2)}) copy-start(s32[2,128]{1,0:T(2,128)} %param.29) | copy-start | bytes 3076
  7.2 18.2 %copy-start.14 = (f32[128,512]{1,0:T(8,128)S(1)}, f32[128,512]{1,0:T(8,128)}, u32[]{:S(2)}) copy-start(f32[128,512]{1,0:T(8,128)} %param.26) | copy-start | bytes 786436
  7.2 18.9 %copy-start.6 = (f32[256,512]{1,0:T(8,128)S(1)}, f32[256,512]{1,0:T(8,128)}, u32[]{:S(2)}) copy-start(f32[256,512]{1,0:T(8,128)} %param.24) | copy-start | bytes 1572868
  7.2 76.4 %all-gather.2.cloned.1.call-start = ((), (), s32[]{:S(2)}) async-start(), calls=%async_computation.1 | async-start | bytes 8077312 | tf_op jit(solution)/shard_map/all_gather | solution.py:247
  9.3 186.7 %reduce-scatter.2.cloned.1.call-start = ((), (), s32[]{:S(2)}) async-start(), calls=%async_computation.2 | async-start | bytes 7798784 | tf_op jit(solution)/shard_map/reduce_scatter | solution.py:304
  12.8 14.2 %collective-permute-start.7 = (f32[1,16,512]{2,1,0:T(8,128)S(1)}, f32[1,16,512]{2,1,0:T(8,128)S(1)}, u32[]{:S(2)}, u32[]{:S(2)}) collective-permute-start(f32[1,16,512]{2,1,0:T(8,128)S(1)} %get-tuple-element.43), channel_id=1, source_target_pairs={{1,0},{2,1},{3,2},{5,4},{6,5},{7,6},{9,8},{10,9},{11,10},{13,12},{... | collective-permute-start | bytes 98312 | tf_op jit(solution)/shard_map/ppermute | solution.py:23
  14.1 12.9 %collective-permute-start.6 = (f32[1,16,512]{2,1,0:T(8,128)S(1)}, f32[1,16,512]{2,1,0:T(8,128)S(1)}, u32[]{:S(2)}, u32[]{:S(2)}) collective-permute-start(f32[1,16,512]{2,1,0:T(8,128)S(1)} %get-tuple-element.44), channel_id=1, source_target_pairs={{0,1},{1,2},{2,3},{4,5},{5,6},{6,7},{8,9},{9,10},{10,11},{12,13},{... | collective-permute-start | bytes 98312 | tf_op jit(solution)/shard_map/ppermute | solution.py:21
  19.7 7.3 %collective-permute-start.5 = (f32[1,16,512]{2,1,0:T(8,128)S(1)}, f32[1,16,512]{2,1,0:T(8,128)S(1)}, u32[]{:S(2)}, u32[]{:S(2)}) collective-permute-start(f32[1,16,512]{2,1,0:T(8,128)S(1)} %get-tuple-element.45), channel_id=1, source_target_pairs={{4,0},{8,4},{12,8},{5,1},{9,5},{13,9},{6,2},{10,6},{14,10},{7,3},{... | collective-permute-start | bytes 98312 | tf_op jit(solution)/shard_map/ppermute | solution.py:23
  21.0 6.0 %collective-permute-start.4 = (f32[1,16,512]{2,1,0:T(8,128)S(1)}, f32[1,16,512]{2,1,0:T(8,128)S(1)}, u32[]{:S(2)}, u32[]{:S(2)}) collective-permute-start(f32[1,16,512]{2,1,0:T(8,128)S(1)} %get-tuple-element.42), channel_id=1, source_target_pairs={{0,4},{4,8},{8,12},{1,5},{5,9},{9,13},{2,6},{6,10},{10,14},{3,7},{... | collective-permute-start | bytes 98312 | tf_op jit(solution)/shard_map/ppermute | solution.py:21
  86.6 1.0 copy-start.1
  86.6 3.3 %copy-start.3 = (f32[16,32,512]{2,1,0:T(8,128)}, f32[16,32,512]{2,1,0:T(8,128)S(1)}, u32[]{:S(2)}) copy-start(f32[16,32,512]{2,1,0:T(8,128)S(1)} %get-tuple-element.32) | copy-start | bytes 3145732
  86.6 3.0 %copy-start.9 = (f32[256,512]{1,0:T(8,128)S(1)}, f32[256,512]{1,0:T(8,128)}, u32[]{:S(2)}) copy-start(f32[256,512]{1,0:T(8,128)} %param.27) | copy-start | bytes 1572868
  90.2 0.8 copy-start.7
  91.0 2.1 slice-start
  93.1 2.1 copy-start
  94.2 1.0 copy-start.11
  95.2 1.7 copy-start.16
  95.3 2.8 %copy-start.2 = (f32[16,32,512]{2,1,0:T(8,128)S(1)}, f32[16,32,512]{2,1,0:T(8,128)}, u32[]{:S(2)}) copy-start(f32[16,32,512]{2,1,0:T(8,128)} %copy-done.1) | copy-start | bytes 3145732
  95.3 2.8 %copy-start.15 = (f32[128,512]{1,0:T(8,128)S(1)}, f32[128,512]{1,0:T(8,128)}, u32[]{:S(2)}) copy-start(f32[128,512]{1,0:T(8,128)} %param.26) | copy-start | bytes 786436
  98.0 1.4 copy-start.13
  105.7 1.9 slice-start.1
  105.8 1.9 copy-start.5
  107.6 12.4 %copy-start.10 = (f32[256,512]{1,0:T(8,128)S(1)}, f32[256,512]{1,0:T(8,128)}, u32[]{:S(2)}) copy-start(f32[256,512]{1,0:T(8,128)} %param.27) | copy-start | bytes 1572868
  107.6 12.4 %copy-start.12 = (f32[256,1024]{1,0:T(8,128)S(1)}, f32[256,1024]{1,0:T(8,128)}, u32[]{:S(2)}) copy-start(f32[256,1024]{1,0:T(8,128)} %copy-done.11) | copy-start | bytes 3145732
  112.5 7.7 %collective-permute-start.3 = (f32[1,16,512]{2,1,0:T(8,128)S(1)}, f32[1,16,512]{2,1,0:T(8,128)S(1)}, u32[]{:S(2)}, u32[]{:S(2)}) collective-permute-start(f32[1,16,512]{2,1,0:T(8,128)S(1)} %get-tuple-element.38), channel_id=1, source_target_pairs={{0,1},{1,2},{2,3},{4,5},{5,6},{6,7},{8,9},{9,10},{10,11},{12,13},{... | collective-permute-start | bytes 98312 | tf_op jit(solution)/shard_map/ppermute | solution.py:21
  115.6 5.8 %collective-permute-start.2 = (f32[1,16,512]{2,1,0:T(8,128)S(1)}, f32[1,16,512]{2,1,0:T(8,128)S(1)}, u32[]{:S(2)}, u32[]{:S(2)}) collective-permute-start(f32[1,16,512]{2,1,0:T(8,128)S(1)} %get-tuple-element.39), channel_id=1, source_target_pairs={{1,0},{2,1},{3,2},{5,4},{6,5},{7,6},{9,8},{10,9},{11,10},{13,12},{... | collective-permute-start | bytes 98312 | tf_op jit(solution)/shard_map/ppermute | solution.py:23
  116.9 4.5 %collective-permute-start.1 = (f32[1,16,512]{2,1,0:T(8,128)S(1)}, f32[1,16,512]{2,1,0:T(8,128)S(1)}, u32[]{:S(2)}, u32[]{:S(2)}) collective-permute-start(f32[1,16,512]{2,1,0:T(8,128)S(1)} %get-tuple-element.40), channel_id=1, source_target_pairs={{0,4},{4,8},{8,12},{1,5},{5,9},{9,13},{2,6},{6,10},{10,14},{3,7},{... | collective-permute-start | bytes 98312 | tf_op jit(solution)/shard_map/ppermute | solution.py:21
  118.8 3.3 %collective-permute-start = (f32[1,16,512]{2,1,0:T(8,128)S(1)}, f32[1,16,512]{2,1,0:T(8,128)S(1)}, u32[]{:S(2)}, u32[]{:S(2)}) collective-permute-start(f32[1,16,512]{2,1,0:T(8,128)S(1)} %get-tuple-element.37), channel_id=1, source_target_pairs={{4,0},{8,4},{12,8},{5,1},{9,5},{13,9},{6,2},{10,6},{14,10},{7,3},{... | collective-permute-start | bytes 98312 | tf_op jit(solution)/shard_map/ppermute | solution.py:23
  123.3 87.7 %copy-start.8 = (f32[256,512]{1,0:T(8,128)}, f32[256,512]{1,0:T(8,128)S(1)}, u32[]{:S(2)}) copy-start(f32[256,512]{1,0:T(8,128)S(1)} %scatter_fusion) | copy-start | bytes 1572868
Sparse Core Ops, SparseCore 0:
  10.9 72.6 all-gather.1
  105.8 90.0 reduce-scatter.1

commit v17 on v12

--- a/solution.py
+++ b/solution.py
@@ -100,6 +100,7 @@
     width = terms[0][0][0][1].shape[1]
 
     order = sorted(range(len(terms)), key=lambda index: -rows[index] * terms[index][0][0][0].shape[0])
+    order = order[-1:] + order[:-1]
     count_in = len(inputs)
 
     def kernel(*refs):

time: 205 us -> 205 us (level)
  no operation moved by 1% of the time
where the time goes in v17:
time: 205 us; the launch traced here: 204 us
  waiting for transfers between devices  129 us (63%)
  starting transfers between devices  18.8 us (9%)
  between operations  15.9 us (8%)
  local copies, waits for them, and re-layouts  14.4 us (7%)
  Pallas kernels  10.1 us (5%)
  other arithmetic  9.18 us (4%)
  matrix products  7.56 us (4%)
    reduce_scatter x1, waiting for transfers between devices, shards(): lax.psum_scatter(blocked, peers, scatter_dimension=0, tiled=True)[0]  72.6 us
    all_gather x1, waiting for transfers between devices, shards(): gathered = lax.all_gather(packed, peers, axis=0, tiled=True)  54.1 us
    ppermute x4, starting transfers between devices, padded(): lax.ppermute(tail, axis, [(i, (i + 1) % count) for i in range(ends)])  13.5 us
    dot_general x4, matrix products, outer_back(): lax.dot_general(left, right, (((1,), (1,)), ((), ())), precision=lax.Prec...  6.29 us
    pallas_call x1, Pallas kernels, blocked_grads(): pl.pallas_call(kernel, out_shape=jax.ShapeDtypeStruct((blocks, offsets[-1...  6.24 us
    ppermute x4, starting transfers between devices, padded(): lax.ppermute(head, axis, [((i + 1) % count, i) for i in range(ends)])  5.17 us
    slice x6, local copies, waits for them, and re-layouts, shards(): pieces.append(gathered[:, offset:offset + rows, :])  4.58 us
  transfers between devices with their start and end apart: 10, of which 4 were waited for; matrix products, arithmetic and copies ran while one was open for 7% of the time, Pallas kernels for 0%

profile of v17, /device:TPU:0, one launch (start us, length us, event | category | flops | bytes accessed | tf_op | source)
XLA Modules:
  0.0 204.5 jit_solution(3896107487671506635)
XLA Ops:
  7.3 2.0 shard_map.226
  9.4 0.8 reshape.233
  10.1 0.8 broadcast_in_dim_reshape_squeeze.3
  10.9 1.8 gather_fusion
  12.8 1.3 collective-permute-start.7
  14.1 5.6 %collective-permute-start.6 = (f32[1,16,512]{2,1,0:T(8,128)S(1)}, f32[1,16,512]{2,1,0:T(8,128)S(1)}, u32[]{:S(2)}, u32[]{:S(2)}) collective-permute-start(f32[1,16,512]{2,1,0:T(8,128)S(1)} %get-tuple-element.44), channel_id=1, source_target_pairs={{0,1},{1,2},{2,3},{4,5},{5,6},{6,7},{8,9},{9,10},{10,11},{12,13},{... | collective-permute-start | bytes 98312 | tf_op jit(solution)/shard_map/ppermute | solution.py:21
  19.7 1.3 collective-permute-start.5
  21.0 3.0 %collective-permute-start.4 = (f32[1,16,512]{2,1,0:T(8,128)S(1)}, f32[1,16,512]{2,1,0:T(8,128)S(1)}, u32[]{:S(2)}, u32[]{:S(2)}) collective-permute-start(f32[1,16,512]{2,1,0:T(8,128)S(1)} %get-tuple-element.42), channel_id=1, source_target_pairs={{0,4},{4,8},{8,12},{1,5},{5,9},{9,13},{2,6},{6,10},{10,14},{3,7},{... | collective-permute-start | bytes 98312 | tf_op jit(solution)/shard_map/ppermute | solution.py:21
  25.4 0.7 broadcast_maximum_fusion.1.refs_6_
  26.1 0.9 broadcast_maximum_fusion.refs_12_
  27.1 0.8 gather_fusion.3
  27.9 0.8 gather_fusion.2
  28.6 0.9 broadcast_select_fusion.1
  29.5 54.1 %all-gather.2.cloned.1.call-done = f32[16,225,512]{2,1,0:T(8,128)} async-done(((f32[1,225,512]{2,1,0:T(8,128)}), f32[16,225,512]{2,1,0:T(8,128)}) %all-gather.2.cloned.1.call-update) | async-done | bytes 7372816 | tf_op jit(solution)/shard_map/all_gather | solution.py:225
  83.6 1.0 slice.161
  84.7 0.1 slice_reduce_fusion
  84.9 1.7 fusion.12
  86.6 1.0 copy-done.1
  87.6 0.6 fusion.14
  88.2 0.2 multiply_reduce_fusion.3
  88.6 0.7 fusion.15
  89.4 0.2 multiply_reduce_fusion.1
  89.6 0.3 fusion.4
  89.9 0.3 subtract_multiply_fusion.refs_13_
  90.2 0.8 copy-done.7
  91.0 2.1 %convolution_select_fusion.refs_9_ = f32[256,512]{1,0:T(8,128)S(1)} fusion(f32[256,512]{1,0:T(8,128)S(1)} %subtract_multiply_fusion.refs_13_, f32[512,512]{1,0:T(8,128)} %bitcast.65, f32[256,512]{1,0:T(8,128)} %param.24), kind=kOutput, calls=%fused_computation.8 | convolution fusion | flops 402915328 | bytes 2621440 | tf_op jit(solution)/shard_map/dot_general | solution.py:166
  93.1 1.1 fusion.16
  94.2 1.0 copy-done.11
  95.3 0.8 gather_fusion.4
  96.0 0.8 gather_fusion.1
  96.9 1.0 fusion.10
  97.9 0.1 subtract_multiply_fusion.1.refs_7_
  98.0 1.4 convolution_select_fusion.1.refs_1_.refs_3_.refs_5_
  99.4 6.2 %shard_map.227 = f32[16,224,512]{2,1,0:T(8,128)} custom-call(f32[128,512]{1,0:T(8,128)} %refs_0_.3, f32[128,512]{1,0:T(8,128)} %convolution_select_fusion.1.refs_1_.refs_3_.refs_5_, f32[128,512]{1,0:T(8,128)} %get-tuple-element.60.refs_2_, f32[128,512]{1,0:T(8,128)} %convolution_select_fusion.1.refs_1_.refs_3_.refs_5_, ...), custom_call_target="tpu_custom_call" | custom-call | tf_op jit(solution)/shard_map/pallas_call | solution.py:140
  105.7 1.9 slice-done.1
  107.6 1.7 fusion.17
  109.4 0.8 fusion.13
  110.2 2.3 %scatter_custom_fusion = f32[320,512]{1,0:T(8,128)S(1)} fusion(s32[256]{0:T(256)S(1)} %bitcast.71, f32[128,512]{1,0:T(8,128)S(1)} %get-tuple-element.35, f32[]{:T(128)} %constant.75, f32[128,512]{1,0:T(8,128)S(1)} %get-tuple-element.34, f32[]{:T(128)} %constant.37.clone.1), kind=kCustom, calls=%fused_computation.14 | custom fusion | flops 262144 | bytes 1179656 | tf_op jit(solution)/shard_map/add | solution.py:291
  112.5 3.0 %collective-permute-start.3 = (f32[1,16,512]{2,1,0:T(8,128)S(1)}, f32[1,16,512]{2,1,0:T(8,128)S(1)}, u32[]{:S(2)}, u32[]{:S(2)}) collective-permute-start(f32[1,16,512]{2,1,0:T(8,128)S(1)} %get-tuple-element.38), channel_id=1, source_target_pairs={{0,1},{1,2},{2,3},{4,5},{5,6},{6,7},{8,9},{9,10},{10,11},{12,13},{... | collective-permute-start | bytes 98312 | tf_op jit(solution)/shard_map/ppermute | solution.py:21
  115.5 1.3 collective-permute-start.2
  116.8 1.9 collective-permute-start.1
  118.7 1.3 collective-permute-start
  120.0 0.1 slice_add_fusion
  120.2 1.1 collective-permute-done.2
  121.3 0.7 collective-permute-done
  122.1 1.2 scatter_fusion
  123.3 72.6 %reduce-scatter.2.cloned.1.call-done = f32[1,224,512]{2,1,0:T(8,128)} async-done(((f32[16,224,512]{2,1,0:T(8,128)}), f32[1,224,512]{2,1,0:T(8,128)}) %reduce-scatter.2.cloned.1.call-update) | async-done | bytes 458768 | tf_op jit(solution)/shard_map/reduce_scatter | solution.py:282
  195.9 1.8 shard_map.228
  (79 shorter events, 1.0 us)
Async XLA Ops:
  7.2 19.9 %copy-start.4 = (f32[256,512]{1,0:T(8,128)S(1)}, f32[256,512]{1,0:T(8,128)}, u32[]{:S(2)}) copy-start(f32[256,512]{1,0:T(8,128)} %refs_8_.1) | copy-start | bytes 1572868
  7.2 18.1 %copy-start.17 = (s32[2,128]{1,0:T(2,128)S(1)}, s32[2,128]{1,0:T(2,128)}, u32[]{:S(2)}) copy-start(s32[2,128]{1,0:T(2,128)} %param.29) | copy-start | bytes 3076
  7.2 18.2 %copy-start.14 = (f32[128,512]{1,0:T(8,128)S(1)}, f32[128,512]{1,0:T(8,128)}, u32[]{:S(2)}) copy-start(f32[128,512]{1,0:T(8,128)} %param.26) | copy-start | bytes 786436
  7.2 18.9 %copy-start.6 = (f32[256,512]{1,0:T(8,128)S(1)}, f32[256,512]{1,0:T(8,128)}, u32[]{:S(2)}) copy-start(f32[256,512]{1,0:T(8,128)} %param.24) | copy-start | bytes 1572868
  7.2 76.4 %all-gather.2.cloned.1.call-start = ((), (), s32[]{:S(2)}) async-start(), calls=%async_computation.1 | async-start | bytes 8077312 | tf_op jit(solution)/shard_map/all_gather | solution.py:225
  9.3 186.5 %reduce-scatter.2.cloned.1.call-start = ((), (), s32[]{:S(2)}) async-start(), calls=%async_computation.2 | async-start | bytes 7798784 | tf_op jit(solution)/shard_map/reduce_scatter | solution.py:282
  12.8 14.2 %collective-permute-start.7 = (f32[1,16,512]{2,1,0:T(8,128)S(1)}, f32[1,16,512]{2,1,0:T(8,128)S(1)}, u32[]{:S(2)}, u32[]{:S(2)}) collective-permute-start(f32[1,16,512]{2,1,0:T(8,128)S(1)} %get-tuple-element.43), channel_id=1, source_target_pairs={{1,0},{2,1},{3,2},{5,4},{6,5},{7,6},{9,8},{10,9},{11,10},{13,12},{... | collective-permute-start | bytes 98312 | tf_op jit(solution)/shard_map/ppermute | solution.py:23
  14.1 12.9 %collective-permute-start.6 = (f32[1,16,512]{2,1,0:T(8,128)S(1)}, f32[1,16,512]{2,1,0:T(8,128)S(1)}, u32[]{:S(2)}, u32[]{:S(2)}) collective-permute-start(f32[1,16,512]{2,1,0:T(8,128)S(1)} %get-tuple-element.44), channel_id=1, source_target_pairs={{0,1},{1,2},{2,3},{4,5},{5,6},{6,7},{8,9},{9,10},{10,11},{12,13},{... | collective-permute-start | bytes 98312 | tf_op jit(solution)/shard_map/ppermute | solution.py:21
  19.7 7.3 %collective-permute-start.5 = (f32[1,16,512]{2,1,0:T(8,128)S(1)}, f32[1,16,512]{2,1,0:T(8,128)S(1)}, u32[]{:S(2)}, u32[]{:S(2)}) collective-permute-start(f32[1,16,512]{2,1,0:T(8,128)S(1)} %get-tuple-element.45), channel_id=1, source_target_pairs={{4,0},{8,4},{12,8},{5,1},{9,5},{13,9},{6,2},{10,6},{14,10},{7,3},{... | collective-permute-start | bytes 98312 | tf_op jit(solution)/shard_map/ppermute | solution.py:23
  21.0 6.0 %collective-permute-start.4 = (f32[1,16,512]{2,1,0:T(8,128)S(1)}, f32[1,16,512]{2,1,0:T(8,128)S(1)}, u32[]{:S(2)}, u32[]{:S(2)}) collective-permute-start(f32[1,16,512]{2,1,0:T(8,128)S(1)} %get-tuple-element.42), channel_id=1, source_target_pairs={{0,4},{4,8},{8,12},{1,5},{5,9},{9,13},{2,6},{6,10},{10,14},{3,7},{... | collective-permute-start | bytes 98312 | tf_op jit(solution)/shard_map/ppermute | solution.py:21
  86.6 1.0 copy-start.1
  86.6 3.3 %copy-start.3 = (f32[16,32,512]{2,1,0:T(8,128)}, f32[16,32,512]{2,1,0:T(8,128)S(1)}, u32[]{:S(2)}) copy-start(f32[16,32,512]{2,1,0:T(8,128)S(1)} %get-tuple-element.32) | copy-start | bytes 3145732
  86.6 3.0 %copy-start.9 = (f32[256,512]{1,0:T(8,128)S(1)}, f32[256,512]{1,0:T(8,128)}, u32[]{:S(2)}) copy-start(f32[256,512]{1,0:T(8,128)} %param.27) | copy-start | bytes 1572868
  90.2 0.8 copy-start.7
  91.0 2.1 %slice-start = ((f32[16,225,512]{2,1,0:T(8,128)}), f32[16,64,512]{2,1,0:T(8,128)S(1)}, s32[]{:S(2)}) async-start(f32[16,225,512]{2,1,0:T(8,128)} %all-gather.2.cloned.1.call-done), calls=%async_computation.3 | async-start | bytes 4194304 | tf_op jit(solution)/shard_map/slice | solution.py:229
  93.1 2.1 %copy-start = (f32[256,512]{1,0:T(8,128)}, f32[256,512]{1,0:T(8,128)S(1)}, u32[]{:S(2)}) copy-start(f32[256,512]{1,0:T(8,128)S(1)} %convolution_select_fusion.refs_9_) | copy-start | bytes 1572868
  94.2 1.0 copy-start.11
  95.2 1.7 copy-start.16
  95.3 2.8 %copy-start.2 = (f32[16,32,512]{2,1,0:T(8,128)S(1)}, f32[16,32,512]{2,1,0:T(8,128)}, u32[]{:S(2)}) copy-start(f32[16,32,512]{2,1,0:T(8,128)} %copy-done.1) | copy-start | bytes 3145732
  95.3 2.8 %copy-start.15 = (f32[128,512]{1,0:T(8,128)S(1)}, f32[128,512]{1,0:T(8,128)}, u32[]{:S(2)}) copy-start(f32[128,512]{1,0:T(8,128)} %param.26) | copy-start | bytes 786436
  98.0 1.4 copy-start.13
  105.7 1.9 slice-start.1
  105.7 1.9 copy-start.5
  107.6 12.4 %copy-start.10 = (f32[256,512]{1,0:T(8,128)S(1)}, f32[256,512]{1,0:T(8,128)}, u32[]{:S(2)}) copy-start(f32[256,512]{1,0:T(8,128)} %param.27) | copy-start | bytes 1572868
  107.6 12.4 %copy-start.12 = (f32[256,1024]{1,0:T(8,128)S(1)}, f32[256,1024]{1,0:T(8,128)}, u32[]{:S(2)}) copy-start(f32[256,1024]{1,0:T(8,128)} %copy-done.11) | copy-start | bytes 3145732
  112.5 7.7 %collective-permute-start.3 = (f32[1,16,512]{2,1,0:T(8,128)S(1)}, f32[1,16,512]{2,1,0:T(8,128)S(1)}, u32[]{:S(2)}, u32[]{:S(2)}) collective-permute-start(f32[1,16,512]{2,1,0:T(8,128)S(1)} %get-tuple-element.38), channel_id=1, source_target_pairs={{0,1},{1,2},{2,3},{4,5},{5,6},{6,7},{8,9},{9,10},{10,11},{12,13},{... | collective-permute-start | bytes 98312 | tf_op jit(solution)/shard_map/ppermute | solution.py:21
  115.5 5.8 %collective-permute-start.2 = (f32[1,16,512]{2,1,0:T(8,128)S(1)}, f32[1,16,512]{2,1,0:T(8,128)S(1)}, u32[]{:S(2)}, u32[]{:S(2)}) collective-permute-start(f32[1,16,512]{2,1,0:T(8,128)S(1)} %get-tuple-element.39), channel_id=1, source_target_pairs={{1,0},{2,1},{3,2},{5,4},{6,5},{7,6},{9,8},{10,9},{11,10},{13,12},{... | collective-permute-start | bytes 98312 | tf_op jit(solution)/shard_map/ppermute | solution.py:23
  116.8 4.5 %collective-permute-start.1 = (f32[1,16,512]{2,1,0:T(8,128)S(1)}, f32[1,16,512]{2,1,0:T(8,128)S(1)}, u32[]{:S(2)}, u32[]{:S(2)}) collective-permute-start(f32[1,16,512]{2,1,0:T(8,128)S(1)} %get-tuple-element.40), channel_id=1, source_target_pairs={{0,4},{4,8},{8,12},{1,5},{5,9},{9,13},{2,6},{6,10},{10,14},{3,7},{... | collective-permute-start | bytes 98312 | tf_op jit(solution)/shard_map/ppermute | solution.py:21
  118.7 3.3 %collective-permute-start = (f32[1,16,512]{2,1,0:T(8,128)S(1)}, f32[1,16,512]{2,1,0:T(8,128)S(1)}, u32[]{:S(2)}, u32[]{:S(2)}) collective-permute-start(f32[1,16,512]{2,1,0:T(8,128)S(1)} %get-tuple-element.37), channel_id=1, source_target_pairs={{4,0},{8,4},{12,8},{5,1},{9,5},{13,9},{6,2},{10,6},{14,10},{7,3},{... | collective-permute-start | bytes 98312 | tf_op jit(solution)/shard_map/ppermute | solution.py:23
  123.3 74.4 %copy-start.8 = (f32[256,512]{1,0:T(8,128)}, f32[256,512]{1,0:T(8,128)S(1)}, u32[]{:S(2)}) copy-start(f32[256,512]{1,0:T(8,128)S(1)} %scatter_fusion) | copy-start | bytes 1572868
Sparse Core Ops, SparseCore 0:
  10.9 72.6 all-gather.1
  105.8 90.0 reduce-scatter.1

commit v18 on v12

--- a/solution.py
+++ b/solution.py
@@ -99,7 +99,7 @@
             inputs.extend(pair)
     width = terms[0][0][0][1].shape[1]
 
-    order = sorted(range(len(terms)), key=lambda index: -rows[index] * terms[index][0][0][0].shape[0])
+    order = sorted(range(len(terms)), key=lambda index: -rows[index] * width)
     count_in = len(inputs)
 
     def kernel(*refs):

time: 205 us -> 206 us (level)
  no operation moved by 1% of the time
where the time goes in v18:
time: 206 us; the launch traced here: 205 us
  waiting for transfers between devices  129 us (63%)
  starting transfers between devices  18.8 us (9%)
  between operations  15.9 us (8%)
  local copies, waits for them, and re-layouts  14.4 us (7%)
  Pallas kernels  10.7 us (5%)
  other arithmetic  9.18 us (4%)
  matrix products  7.56 us (4%)
    reduce_scatter x1, waiting for transfers between devices, shards(): lax.psum_scatter(blocked, peers, scatter_dimension=0, tiled=True)[0]  72.7 us
    all_gather x1, waiting for transfers between devices, shards(): gathered = lax.all_gather(packed, peers, axis=0, tiled=True)  54.1 us
    ppermute x4, starting transfers between devices, padded(): lax.ppermute(tail, axis, [(i, (i + 1) % count) for i in range(ends)])  13.5 us
    pallas_call x1, Pallas kernels, blocked_grads(): pl.pallas_call(kernel, out_shape=jax.ShapeDtypeStruct((blocks, offsets[-1...  6.88 us
    dot_general x4, matrix products, outer_back(): lax.dot_general(left, right, (((1,), (1,)), ((), ())), precision=lax.Prec...  6.29 us
    ppermute x4, starting transfers between devices, padded(): lax.ppermute(head, axis, [((i + 1) % count, i) for i in range(ends)])  5.17 us
    slice x6, local copies, waits for them, and re-layouts, shards(): pieces.append(gathered[:, offset:offset + rows, :])  4.58 us
  transfers between devices with their start and end apart: 10, of which 4 were waited for; matrix products, arithmetic and copies ran while one was open for 7% of the time, Pallas kernels for 0%

profile of v18, /device:TPU:0, one launch (start us, length us, event | category | flops | bytes accessed | tf_op | source)
XLA Modules:
  0.0 205.2 jit_solution(2332474447273019725)
XLA Ops:
  7.3 2.0 shard_map.226
  9.4 0.8 reshape.233
  10.1 0.8 broadcast_in_dim_reshape_squeeze.3
  10.9 1.8 gather_fusion
  12.8 1.3 collective-permute-start.7
  14.1 5.6 %collective-permute-start.6 = (f32[1,16,512]{2,1,0:T(8,128)S(1)}, f32[1,16,512]{2,1,0:T(8,128)S(1)}, u32[]{:S(2)}, u32[]{:S(2)}) collective-permute-start(f32[1,16,512]{2,1,0:T(8,128)S(1)} %get-tuple-element.44), channel_id=1, source_target_pairs={{0,1},{1,2},{2,3},{4,5},{5,6},{6,7},{8,9},{9,10},{10,11},{12,13},{... | collective-permute-start | bytes 98312 | tf_op jit(solution)/shard_map/ppermute | solution.py:21
  19.7 1.3 collective-permute-start.5
  21.0 3.0 %collective-permute-start.4 = (f32[1,16,512]{2,1,0:T(8,128)S(1)}, f32[1,16,512]{2,1,0:T(8,128)S(1)}, u32[]{:S(2)}, u32[]{:S(2)}) collective-permute-start(f32[1,16,512]{2,1,0:T(8,128)S(1)} %get-tuple-element.42), channel_id=1, source_target_pairs={{0,4},{4,8},{8,12},{1,5},{5,9},{9,13},{2,6},{6,10},{10,14},{3,7},{... | collective-permute-start | bytes 98312 | tf_op jit(solution)/shard_map/ppermute | solution.py:21
  25.4 0.7 broadcast_maximum_fusion.1.refs_6_
  26.1 0.9 broadcast_maximum_fusion.refs_12_
  27.1 0.8 gather_fusion.3
  27.9 0.8 gather_fusion.2
  28.6 0.9 broadcast_select_fusion.1
  29.5 54.1 %all-gather.2.cloned.1.call-done = f32[16,225,512]{2,1,0:T(8,128)} async-done(((f32[1,225,512]{2,1,0:T(8,128)}), f32[16,225,512]{2,1,0:T(8,128)}) %all-gather.2.cloned.1.call-update) | async-done | bytes 7372816 | tf_op jit(solution)/shard_map/all_gather | solution.py:224
  83.6 1.0 slice.161
  84.7 0.1 slice_reduce_fusion
  84.9 1.7 fusion.12
  86.6 1.0 copy-done.1
  87.6 0.6 fusion.14
  88.2 0.2 multiply_reduce_fusion.3
  88.6 0.7 fusion.15
  89.4 0.2 multiply_reduce_fusion.1
  89.6 0.3 fusion.4
  89.9 0.3 subtract_multiply_fusion.refs_13_
  90.2 0.8 copy-done.7
  91.0 2.1 %convolution_select_fusion.refs_9_ = f32[256,512]{1,0:T(8,128)S(1)} fusion(f32[256,512]{1,0:T(8,128)S(1)} %subtract_multiply_fusion.refs_13_, f32[512,512]{1,0:T(8,128)} %bitcast.65, f32[256,512]{1,0:T(8,128)} %param.24), kind=kOutput, calls=%fused_computation.8 | convolution fusion | flops 402915328 | bytes 2621440 | tf_op jit(solution)/shard_map/dot_general | solution.py:165
  93.1 1.1 fusion.16
  94.2 1.0 copy-done.11
  95.3 0.8 gather_fusion.4
  96.0 0.8 gather_fusion.1
  96.9 1.0 fusion.10
  97.9 0.1 subtract_multiply_fusion.1.refs_7_
  98.0 1.4 convolution_select_fusion.1.refs_1_.refs_3_.refs_5_
  99.4 6.9 %shard_map.227 = f32[16,224,512]{2,1,0:T(8,128)} custom-call(f32[128,512]{1,0:T(8,128)} %refs_0_.3, f32[128,512]{1,0:T(8,128)} %convolution_select_fusion.1.refs_1_.refs_3_.refs_5_, f32[128,512]{1,0:T(8,128)} %get-tuple-element.60.refs_2_, f32[128,512]{1,0:T(8,128)} %convolution_select_fusion.1.refs_1_.refs_3_.refs_5_, ...), custom_call_target="tpu_custom_call" | custom-call | tf_op jit(solution)/shard_map/pallas_call | solution.py:139
  106.4 1.9 slice-done.1
  108.3 1.7 fusion.17
  110.0 0.8 fusion.13
  110.8 2.3 %scatter_custom_fusion = f32[320,512]{1,0:T(8,128)S(1)} fusion(s32[256]{0:T(256)S(1)} %bitcast.71, f32[128,512]{1,0:T(8,128)S(1)} %get-tuple-element.35, f32[]{:T(128)} %constant.75, f32[128,512]{1,0:T(8,128)S(1)} %get-tuple-element.34, f32[]{:T(128)} %constant.37.clone.1), kind=kCustom, calls=%fused_computation.14 | custom fusion | flops 262144 | bytes 1179656 | tf_op jit(solution)/shard_map/add | solution.py:290
  113.1 3.0 %collective-permute-start.3 = (f32[1,16,512]{2,1,0:T(8,128)S(1)}, f32[1,16,512]{2,1,0:T(8,128)S(1)}, u32[]{:S(2)}, u32[]{:S(2)}) collective-permute-start(f32[1,16,512]{2,1,0:T(8,128)S(1)} %get-tuple-element.38), channel_id=1, source_target_pairs={{0,1},{1,2},{2,3},{4,5},{5,6},{6,7},{8,9},{9,10},{10,11},{12,13},{... | collective-permute-start | bytes 98312 | tf_op jit(solution)/shard_map/ppermute | solution.py:21
  116.2 1.3 collective-permute-start.2
  117.5 1.9 collective-permute-start.1
  119.4 1.3 collective-permute-start
  120.7 0.1 slice_add_fusion
  120.8 1.1 collective-permute-done.2
  122.0 0.7 collective-permute-done
  122.7 1.2 scatter_fusion
  123.9 72.7 %reduce-scatter.2.cloned.1.call-done = f32[1,224,512]{2,1,0:T(8,128)} async-done(((f32[16,224,512]{2,1,0:T(8,128)}), f32[1,224,512]{2,1,0:T(8,128)}) %reduce-scatter.2.cloned.1.call-update) | async-done | bytes 458768 | tf_op jit(solution)/shard_map/reduce_scatter | solution.py:281
  196.6 1.8 shard_map.228
  (79 shorter events, 1.0 us)
Async XLA Ops:
  7.2 19.9 %copy-start.4 = (f32[256,512]{1,0:T(8,128)S(1)}, f32[256,512]{1,0:T(8,128)}, u32[]{:S(2)}) copy-start(f32[256,512]{1,0:T(8,128)} %refs_8_.1) | copy-start | bytes 1572868
  7.2 18.1 %copy-start.17 = (s32[2,128]{1,0:T(2,128)S(1)}, s32[2,128]{1,0:T(2,128)}, u32[]{:S(2)}) copy-start(s32[2,128]{1,0:T(2,128)} %param.29) | copy-start | bytes 3076
  7.2 18.2 %copy-start.14 = (f32[128,512]{1,0:T(8,128)S(1)}, f32[128,512]{1,0:T(8,128)}, u32[]{:S(2)}) copy-start(f32[128,512]{1,0:T(8,128)} %param.26) | copy-start | bytes 786436
  7.2 18.9 %copy-start.6 = (f32[256,512]{1,0:T(8,128)S(1)}, f32[256,512]{1,0:T(8,128)}, u32[]{:S(2)}) copy-start(f32[256,512]{1,0:T(8,128)} %param.24) | copy-start | bytes 1572868
  7.2 76.4 %all-gather.2.cloned.1.call-start = ((), (), s32[]{:S(2)}) async-start(), calls=%async_computation.1 | async-start | bytes 8077312 | tf_op jit(solution)/shard_map/all_gather | solution.py:224
  9.3 187.3 %reduce-scatter.2.cloned.1.call-start = ((), (), s32[]{:S(2)}) async-start(), calls=%async_computation.2 | async-start | bytes 7798784 | tf_op jit(solution)/shard_map/reduce_scatter | solution.py:281
  12.8 14.2 %collective-permute-start.7 = (f32[1,16,512]{2,1,0:T(8,128)S(1)}, f32[1,16,512]{2,1,0:T(8,128)S(1)}, u32[]{:S(2)}, u32[]{:S(2)}) collective-permute-start(f32[1,16,512]{2,1,0:T(8,128)S(1)} %get-tuple-element.43), channel_id=1, source_target_pairs={{1,0},{2,1},{3,2},{5,4},{6,5},{7,6},{9,8},{10,9},{11,10},{13,12},{... | collective-permute-start | bytes 98312 | tf_op jit(solution)/shard_map/ppermute | solution.py:23
  14.1 12.9 %collective-permute-start.6 = (f32[1,16,512]{2,1,0:T(8,128)S(1)}, f32[1,16,512]{2,1,0:T(8,128)S(1)}, u32[]{:S(2)}, u32[]{:S(2)}) collective-permute-start(f32[1,16,512]{2,1,0:T(8,128)S(1)} %get-tuple-element.44), channel_id=1, source_target_pairs={{0,1},{1,2},{2,3},{4,5},{5,6},{6,7},{8,9},{9,10},{10,11},{12,13},{... | collective-permute-start | bytes 98312 | tf_op jit(solution)/shard_map/ppermute | solution.py:21
  19.7 7.3 %collective-permute-start.5 = (f32[1,16,512]{2,1,0:T(8,128)S(1)}, f32[1,16,512]{2,1,0:T(8,128)S(1)}, u32[]{:S(2)}, u32[]{:S(2)}) collective-permute-start(f32[1,16,512]{2,1,0:T(8,128)S(1)} %get-tuple-element.45), channel_id=1, source_target_pairs={{4,0},{8,4},{12,8},{5,1},{9,5},{13,9},{6,2},{10,6},{14,10},{7,3},{... | collective-permute-start | bytes 98312 | tf_op jit(solution)/shard_map/ppermute | solution.py:23
  21.0 6.0 %collective-permute-start.4 = (f32[1,16,512]{2,1,0:T(8,128)S(1)}, f32[1,16,512]{2,1,0:T(8,128)S(1)}, u32[]{:S(2)}, u32[]{:S(2)}) collective-permute-start(f32[1,16,512]{2,1,0:T(8,128)S(1)} %get-tuple-element.42), channel_id=1, source_target_pairs={{0,4},{4,8},{8,12},{1,5},{5,9},{9,13},{2,6},{6,10},{10,14},{3,7},{... | collective-permute-start | bytes 98312 | tf_op jit(solution)/shard_map/ppermute | solution.py:21
  86.6 1.0 copy-start.1
  86.6 3.3 %copy-start.3 = (f32[16,32,512]{2,1,0:T(8,128)}, f32[16,32,512]{2,1,0:T(8,128)S(1)}, u32[]{:S(2)}) copy-start(f32[16,32,512]{2,1,0:T(8,128)S(1)} %get-tuple-element.32) | copy-start | bytes 3145732
  86.6 3.0 %copy-start.9 = (f32[256,512]{1,0:T(8,128)S(1)}, f32[256,512]{1,0:T(8,128)}, u32[]{:S(2)}) copy-start(f32[256,512]{1,0:T(8,128)} %param.27) | copy-start | bytes 1572868
  90.2 0.8 copy-start.7
  91.0 2.1 %slice-start = ((f32[16,225,512]{2,1,0:T(8,128)}), f32[16,64,512]{2,1,0:T(8,128)S(1)}, s32[]{:S(2)}) async-start(f32[16,225,512]{2,1,0:T(8,128)} %all-gather.2.cloned.1.call-done), calls=%async_computation.3 | async-start | bytes 4194304 | tf_op jit(solution)/shard_map/slice | solution.py:228
  93.1 2.1 %copy-start = (f32[256,512]{1,0:T(8,128)}, f32[256,512]{1,0:T(8,128)S(1)}, u32[]{:S(2)}) copy-start(f32[256,512]{1,0:T(8,128)S(1)} %convolution_select_fusion.refs_9_) | copy-start | bytes 1572868
  94.2 1.0 copy-start.11
  95.2 1.7 copy-start.16
  95.3 2.8 %copy-start.2 = (f32[16,32,512]{2,1,0:T(8,128)S(1)}, f32[16,32,512]{2,1,0:T(8,128)}, u32[]{:S(2)}) copy-start(f32[16,32,512]{2,1,0:T(8,128)} %copy-done.1) | copy-start | bytes 3145732
  95.3 2.8 %copy-start.15 = (f32[128,512]{1,0:T(8,128)S(1)}, f32[128,512]{1,0:T(8,128)}, u32[]{:S(2)}) copy-start(f32[128,512]{1,0:T(8,128)} %param.26) | copy-start | bytes 786436
  98.0 1.4 copy-start.13
  106.4 1.9 slice-start.1
  106.4 1.9 copy-start.5
  108.3 12.4 %copy-start.10 = (f32[256,512]{1,0:T(8,128)S(1)}, f32[256,512]{1,0:T(8,128)}, u32[]{:S(2)}) copy-start(f32[256,512]{1,0:T(8,128)} %param.27) | copy-start | bytes 1572868
  108.3 12.4 %copy-start.12 = (f32[256,1024]{1,0:T(8,128)S(1)}, f32[256,1024]{1,0:T(8,128)}, u32[]{:S(2)}) copy-start(f32[256,1024]{1,0:T(8,128)} %copy-done.11) | copy-start | bytes 3145732
  113.1 7.7 %collective-permute-start.3 = (f32[1,16,512]{2,1,0:T(8,128)S(1)}, f32[1,16,512]{2,1,0:T(8,128)S(1)}, u32[]{:S(2)}, u32[]{:S(2)}) collective-permute-start(f32[1,16,512]{2,1,0:T(8,128)S(1)} %get-tuple-element.38), channel_id=1, source_target_pairs={{0,1},{1,2},{2,3},{4,5},{5,6},{6,7},{8,9},{9,10},{10,11},{12,13},{... | collective-permute-start | bytes 98312 | tf_op jit(solution)/shard_map/ppermute | solution.py:21
  116.2 5.8 %collective-permute-start.2 = (f32[1,16,512]{2,1,0:T(8,128)S(1)}, f32[1,16,512]{2,1,0:T(8,128)S(1)}, u32[]{:S(2)}, u32[]{:S(2)}) collective-permute-start(f32[1,16,512]{2,1,0:T(8,128)S(1)} %get-tuple-element.39), channel_id=1, source_target_pairs={{1,0},{2,1},{3,2},{5,4},{6,5},{7,6},{9,8},{10,9},{11,10},{13,12},{... | collective-permute-start | bytes 98312 | tf_op jit(solution)/shard_map/ppermute | solution.py:23
  117.5 4.5 %collective-permute-start.1 = (f32[1,16,512]{2,1,0:T(8,128)S(1)}, f32[1,16,512]{2,1,0:T(8,128)S(1)}, u32[]{:S(2)}, u32[]{:S(2)}) collective-permute-start(f32[1,16,512]{2,1,0:T(8,128)S(1)} %get-tuple-element.40), channel_id=1, source_target_pairs={{0,4},{4,8},{8,12},{1,5},{5,9},{9,13},{2,6},{6,10},{10,14},{3,7},{... | collective-permute-start | bytes 98312 | tf_op jit(solution)/shard_map/ppermute | solution.py:21
  119.4 3.3 %collective-permute-start = (f32[1,16,512]{2,1,0:T(8,128)S(1)}, f32[1,16,512]{2,1,0:T(8,128)S(1)}, u32[]{:S(2)}, u32[]{:S(2)}) collective-permute-start(f32[1,16,512]{2,1,0:T(8,128)S(1)} %get-tuple-element.37), channel_id=1, source_target_pairs={{4,0},{8,4},{12,8},{5,1},{9,5},{13,9},{6,2},{10,6},{14,10},{7,3},{... | collective-permute-start | bytes 98312 | tf_op jit(solution)/shard_map/ppermute | solution.py:23
  123.9 74.5 %copy-start.8 = (f32[256,512]{1,0:T(8,128)}, f32[256,512]{1,0:T(8,128)S(1)}, u32[]{:S(2)}) copy-start(f32[256,512]{1,0:T(8,128)S(1)} %scatter_fusion) | copy-start | bytes 1572868
Sparse Core Ops, SparseCore 0:
  10.9 72.6 all-gather.1
  106.5 90.1 reduce-scatter.1
